TPU v7x, 256 devices: a whole 4x4x8 slice. The times are simulated.
256 devices in a mesh: ctx: 32 (over y, z), head: 8 (over x, core).
Axes of the slice: x: 4, y: 4, z: 8, core: 2. Of those that a mesh axis runs over, the one named last changes fastest.
Arguments:
- queries: bfloat16 [4096, 4096], P('ctx', 'head'), may hold values from -30 to 30
- key_proj: bfloat16 [4096, 1024], P('ctx', 'head'), may hold values from -6 to 6
- value_proj: bfloat16 [4096, 1024], P('ctx', 'head'), may hold values from -6 to 6
- lengths: int32 [32], replicated, may hold values from 1 to 2048, 4096 in all
- out_weight: bfloat16 [4096, 8192], P(None, 'head'), may hold values from -0.09375 to 0.09375
Outputs:
- mixed_out: bfloat16 [4096, 8192], P('ctx', 'head')
Inputs may be any that keep to these rules, and one draw needn't show every extreme that they name: Document lengths in pack order; they sum to 4096 and the longest is exactly 2048.
All inputs are finite; a program needn't handle non-finite values.
Results may differ from a plain program's by a relative error of at most 0.005.
The roundings to bfloat16 on the way count: a program that leaves them out, or rounds other values in their place, can miss the bound.
Values may be sent and summed in bfloat16 or wider, within the bound.
No kernel may reach another device: no remote copies, remote signals or barrier semaphores. Data moves between devices by JAX's collectives and lax.ppermute only.
A program may use at most 64 MiB of HBM per device.

v0:
```python
import jax
import jax.numpy as jnp
from jax import lax
from jax.sharding import PartitionSpec as P

HD = 128


rope_theta = 500000.0


def doc_starts(lengths, positions):
    doc_ends = jnp.cumsum(lengths)
    picked = jnp.where(doc_ends[None, :] <= positions[:, None], lengths[None, :], 0)
    return jnp.sum(picked, axis=1)


def rotary(projected, offsets, head_dim):
    token_count = projected.shape[0]
    heads_grid = projected.astype(jnp.float32).reshape(token_count, -1, head_dim)
    half_dim = head_dim // 2
    inverse = rope_theta ** (-2.0 * jnp.arange(half_dim).astype(jnp.float32) / head_dim)
    angles = offsets.astype(jnp.float32)[:, None] * inverse[None, :]
    cosine = jnp.cos(angles)[:, None, :]
    sine_part = jnp.sin(angles)[:, None, :]
    first_half = heads_grid[..., :half_dim]
    second_half = heads_grid[..., half_dim:]
    rotated = jnp.concatenate(
        [
            first_half * cosine - second_half * sine_part,
            second_half * cosine + first_half * sine_part,
        ],
        axis=-1,
    )
    return rotated.reshape(token_count, -1).astype(jnp.bfloat16)


def on_device(queries, key_proj, value_proj, lengths, out_weight):
    tok_rows = queries.shape[0]
    kv_local = key_proj.shape[1] // HD
    query_group = queries.shape[1] // key_proj.shape[1]
    first_row = lax.axis_index("ctx") * tok_rows
    positions = first_row + jnp.arange(tok_rows, dtype=jnp.int32)
    starts = doc_starts(lengths, positions)
    offsets = positions - starts
    q_rot = rotary(queries, offsets, HD).reshape(tok_rows, kv_local, query_group, HD)
    k_rot = rotary(key_proj, offsets, HD)
    lowest = starts[0]
    initial = (
        jnp.full((kv_local, query_group, tok_rows), -1e30, jnp.float32),
        jnp.zeros((kv_local, query_group, tok_rows), jnp.float32),
        jnp.zeros((kv_local, query_group, tok_rows, HD), jnp.float32),
    )
    begin_row = jnp.int32(0)
    key_part = lax.all_gather(k_rot, "ctx", axis=0, tiled=True)
    value_part = lax.all_gather(value_proj, "ctx", axis=0, tiled=True)
    key_count = key_part.shape[0]

    def update(state):
        running_max, running_sum, weighted = state
        key_block = key_part.reshape(key_count, kv_local, HD)
        value_block = value_part.reshape(key_count, kv_local, HD)
        scores = jnp.einsum(
            "tkgd,nkd->kgtn", q_rot, key_block, preferred_element_type=jnp.float32
        ) / jnp.sqrt(jnp.float32(HD))
        key_pos = jnp.arange(key_count, dtype=jnp.int32)
        allowed = (key_pos[None, :] <= positions[:, None]) & (key_pos[None, :] >= starts[:, None])
        scores = jnp.where(allowed, scores, -1e30)
        new_max = jnp.maximum(running_max, jnp.max(scores, axis=-1))
        weights = jnp.where(allowed, jnp.exp(scores - new_max[..., None]), 0.0)
        new_sum = jnp.sum(weights, axis=-1)
        product = jnp.einsum(
            "kgtn,nkd->kgtd",
            weights.astype(jnp.bfloat16),
            value_block,
            preferred_element_type=jnp.float32,
        )
        return (new_max, new_sum, product)

    needed = (begin_row <= first_row + tok_rows - 1) & (begin_row + key_count - 1 >= lowest)
    state = lax.cond(needed, update, lambda state: state, initial)
    running_max, running_sum, weighted = state
    normed = (weighted / running_sum[..., None]).astype(jnp.bfloat16)
    attended = jnp.transpose(normed, (2, 0, 1, 3)).reshape(tok_rows, kv_local * query_group * HD)
    mixed_out = jnp.dot(
        lax.all_gather(attended, "head", axis=1, tiled=True),
        out_weight,
        preferred_element_type=jnp.float32,
    )
    return mixed_out.astype(jnp.bfloat16)


def solution(mesh):
    placed = (P("ctx", "head"), P("ctx", "head"), P("ctx", "head"), P(), P(None, "head"))
    return jax.shard_map(
        on_device, mesh=mesh, in_specs=placed, out_specs=P("ctx", "head"), check_vma=False
    )
```

profile of v0, /device:TPU:1, one launch (start us, length us, event | category | flops | bytes accessed | tf_op | source)
XLA Modules:
  0.0 206.3 jit_solution(5268036091979652018)
XLA Ops:
  6.5 0.7 all-gather.5.cloned.1.call-update
  7.3 0.0 all-gather.9.cloned.1.call-start
  7.3 0.7 copy.19
  8.0 0.1 reduce-window.8
  8.1 0.1 reduce.2
  8.2 0.9 copy.21
  9.1 0.7 select_reduce_fusion
  9.9 0.2 fusion.23
  10.1 0.6 pad_maximum_fusion.1
  10.7 0.0 all-gather.9.cloned.1.call-update
  10.7 0.0 all-gather.7.cloned.1.call-start
  10.8 1.0 copy.20
  11.9 0.2 multiply_cosine_fusion.1
  12.2 72.9 %all-gather.5.cloned.1.call-done = bf16[4096,128]{1,0:T(8,128)(2,1)} async-done(((bf16[128,128]{1,0:T(8,128)(2,1)}), bf16[4096,128]{1,0:T(8,128)(2,1)}) %all-gather.5.cloned.1.call-update) | async-done | bytes 1048592 | tf_op jit(solution)/shard_map/all_gather | solution.py:56
  85.0 71.6 %all-gather.9.cloned.1.call-done = bf16[4096,1,128]{0,2,1:T(8,128)(2,1)} async-done(((bf16[128,1,128]{0,2,1:T(8,128)(2,1)}), bf16[4096,1,128]{0,2,1:T(8,128)(2,1)}) %all-gather.9.cloned.1.call-update) | async-done | bytes 1048592 | tf_op jit(solution)/shard_map/all_gather | solution.py:55
  156.6 7.3 %conditional.1 = (f32[1,4,128]{2,1,0:T(4,128)S(1)}, f32[1,4,128,128]{2,3,1,0:T(8,128)S(1)}) conditional(s32[]{:T(128)} %convert_element_type.42, () %tuple.13, (s32[]{:T(128)}, s32[128]{0:T(128)S(1)}, s32[128]{0:T(128)S(1)}, bf16[128,4,128]{0,2,1:T(8,128)(2,1)S(1)}, bf16[4096,128]{0,1:T(8,128)(2,1)}, /*index=5*/bf16[4096,128]{1,0:T(8,128)(2,1)}) %tuple.32), branch_computations={%region_2.3_spmd, %region_3.6_spmd} | conditional | flops 1102577280 | bytes 34224176 | solution.py:81
  156.6 0.1 copy.22
  156.8 0.5 fusion.7
  157.3 2.6 %fusion = (f32[4,128]{1,0:T(4,128)S(1)}, f32[4096,128,4]{1,0,2:T(8,128)S(1)}) fusion(pred[128,4096]{0,1:T(8,128)(4,1)S(1)} %fusion.7, bf16[128,4,128]{2,0,1:T(8,128)(2,1)S(1)} %copy.22, bf16[4096,128]{0,1:T(8,128)(2,1)} %get-tuple-element.47), kind=kOutput, calls=%fused_computation.2 | convolution fusion | flops 543161856 | bytes 10094592 | tf_op jit(solution)/shard_map/cond/branch_1_fun/tkgd,nkd->kgtn/dot_general | solution.py:63
  159.9 2.0 fusion.8
  161.8 2.1 %fusion.2 = f32[4,128]{1,0:T(4,128)S(1)} fusion(f32[4096,128,4]{1,0,2:T(8,128)S(1)} %get-tuple-element.51, f32[4,128]{1,0:T(4,128)S(1)} %broadcast_maximum_fusion, pred[128,4096]{0,1:T(8,128)(4,1)S(1)} %fusion.7), kind=kLoop, calls=%fused_computation.4 | loop fusion | flops 10485248 | bytes 8916992 | tf_op jit(solution)/shard_map/cond/branch_1_fun/reduce_sum | solution.py:71
  163.9 0.7 divide_convert_fusion
  164.6 29.4 %all-gather.7.cloned.1.call-done = bf16[128,4096]{0,1:T(8,128)(2,1)} async-done(((bf16[128,512]{0,1:T(8,128)(2,1)}), bf16[128,4096]{0,1:T(8,128)(2,1)}) %all-gather.7.cloned.1.call-update) | async-done | bytes 1048592 | tf_op jit(solution)/shard_map/all_gather | solution.py:86
  194.1 5.7 %convolution_convert_fusion = bf16[128,1024]{1,0:T(8,128)(2,1)} fusion(bf16[128,4096]{0,1:T(8,128)(2,1)} %all-gather.7.cloned.1.call-done, bf16[4096,1024]{1,0:T(8,128)(2,1)} %param.11), kind=kOutput, calls=%fused_computation.21 | convolution fusion | flops 1073872896 | bytes 9699328 | tf_op jit(solution)/shard_map/dot_general | solution.py:85
  (14 shorter events, 0.1 us)
Async XLA Ops:
  6.5 78.5 %all-gather.5.cloned.1.call-start = ((), (), s32[]{:S(2)}) async-start(), calls=%async_computation | async-start | bytes 1081344 | tf_op jit(solution)/shard_map/all_gather | solution.py:56
  7.3 149.4 %all-gather.9.cloned.1.call-start = ((), (), s32[]{:S(2)}) async-start(), calls=%async_computation.2 | async-start | bytes 1081344 | tf_op jit(solution)/shard_map/all_gather | solution.py:55
  10.7 183.3 %all-gather.7.cloned.1.call-start = ((), (), s32[]{:S(2)}) async-start(), calls=%async_computation.1 | async-start | bytes 1179648 | tf_op jit(solution)/shard_map/all_gather | solution.py:86
  156.6 3.2 %copy-start = (bf16[4096,128]{1,0:T(8,128)(2,1)S(1)}, bf16[4096,128]{1,0:T(8,128)(2,1)}, u32[]{:S(2)}) copy-start(bf16[4096,128]{1,0:T(8,128)(2,1)} %get-tuple-element.26) | copy-start | bytes 3145732 | tf_op jit(solution)/shard_map/cond
Sparse Core Ops, SparseCore 0:
  9.9 75.0 all-gather.4
  87.5 69.0 all-gather.8
  164.8 29.2 all-gather.6
where the time goes:
time: 207 us; the launch traced here: 206 us
  waiting for transfers between devices  175 us (85%)
  between operations  13.2 us (6%)
  matrix products  10.3 us (5%)
  other arithmetic  5.29 us (3%)
  local copies, waits for them, and re-layouts  2.76 us (1%)
    all_gather x1, waiting for transfers between devices, on_device(): value_part = lax.all_gather(value_proj, 'ctx', axis=0, tiled=True)  72.9 us
    all_gather x1, waiting for transfers between devices, on_device(): key_part = lax.all_gather(k_rot, 'ctx', axis=0, tiled=True)  71.6 us
    all_gather x1, waiting for transfers between devices, on_device(): lax.all_gather(attended, 'head', axis=1, tiled=True)  29.4 us
    dot_general x1, matrix products, on_device(): jnp.dot(lax.all_gather(attended, 'head', axis=1, tiled=True), out_weight,...  5.7 us
  transfers between devices with their start and end apart: 3, of which 3 were waited for; matrix products, arithmetic and copies ran while one was open for 2% of the time, Pallas kernels for 0%

commit v1 on v0

v1 whole, which is shorter than its diff:
```python
import jax
import jax.numpy as jnp
from jax import lax
from jax.sharding import PartitionSpec as P

HD = 128
MOST = 2048


rope_theta = 500000.0


def doc_starts(lengths, positions):
    doc_ends = jnp.cumsum(lengths)
    picked = jnp.where(doc_ends[None, :] <= positions[:, None], lengths[None, :], 0)
    return jnp.sum(picked, axis=1)


def rotary(projected, offsets, head_dim):
    token_count = projected.shape[0]
    heads_grid = projected.astype(jnp.float32).reshape(token_count, -1, head_dim)
    half_dim = head_dim // 2
    inverse = rope_theta ** (-2.0 * jnp.arange(half_dim).astype(jnp.float32) / head_dim)
    angles = offsets.astype(jnp.float32)[:, None] * inverse[None, :]
    cosine = jnp.cos(angles)[:, None, :]
    sine_part = jnp.sin(angles)[:, None, :]
    first_half = heads_grid[..., :half_dim]
    second_half = heads_grid[..., half_dim:]
    rotated = jnp.concatenate(
        [
            first_half * cosine - second_half * sine_part,
            second_half * cosine + first_half * sine_part,
        ],
        axis=-1,
    )
    return rotated.reshape(token_count, -1).astype(jnp.bfloat16)


def make_body(n_ctx, n_head, row):
    def on_device(queries, key_proj, value_proj, lengths, out_weight):
        tok_rows = queries.shape[0]
        kv_width = key_proj.shape[1]
        kv_local = kv_width // HD
        query_group = queries.shape[1] // kv_width
        back = -(-(MOST - 1) // tok_rows)
        rows_back = -(-back // row)
        span = rows_back * row
        ctx = lax.axis_index("ctx")
        first_row = ctx * tok_rows
        positions = first_row + jnp.arange(tok_rows, dtype=jnp.int32)
        starts = doc_starts(lengths, positions)
        offsets = positions - starts
        q_rot = rotary(queries, offsets, HD).reshape(tok_rows, kv_local, query_group, HD)
        k_rot = rotary(key_proj, offsets, HD)
        own = jnp.concatenate([k_rot, value_proj], axis=1)

        bundle = [own]
        for m in range(1, rows_back + 1):
            shift = row * m
            bundle.append(lax.ppermute(own, "ctx", [(s, s + shift) for s in range(n_ctx - shift)]))
        bundle = jnp.stack(bundle)
        blocks = {row * m: bundle[m] for m in range(rows_back + 1)}
        z = ctx % row
        for b in range(1, row):
            lo = jnp.where(z + b >= row, 1, 0)
            piece = lax.dynamic_slice_in_dim(bundle, lo, rows_back, 0)
            pairs = [(r * row + s, r * row + (s + b) % row) for r in range(n_ctx // row) for s in range(row)]
            got = lax.ppermute(piece, "ctx", pairs)
            for m in range(rows_back):
                blocks[b + row * m] = got[m]
        window = jnp.concatenate([blocks[span - k] for k in range(span + 1)], axis=0)
        key_count = window.shape[0]
        key_block = window[:, :kv_width].reshape(key_count, kv_local, HD)
        value_block = window[:, kv_width:].reshape(key_count, kv_local, HD)

        scores = jnp.einsum(
            "tkgd,nkd->kgtn", q_rot, key_block, preferred_element_type=jnp.float32
        ) / jnp.sqrt(jnp.float32(HD))
        key_pos = (ctx - span) * tok_rows + jnp.arange(key_count, dtype=jnp.int32)
        allowed = (key_pos[None, :] <= positions[:, None]) & (key_pos[None, :] >= starts[:, None])
        scores = jnp.where(allowed, scores, -1e30)
        row_max = jnp.max(scores, axis=-1)
        weights = jnp.where(allowed, jnp.exp(scores - row_max[..., None]), 0.0)
        row_sum = jnp.sum(weights, axis=-1)
        weighted = jnp.einsum(
            "kgtn,nkd->kgtd",
            weights.astype(jnp.bfloat16),
            value_block,
            preferred_element_type=jnp.float32,
        )
        normed = (weighted / row_sum[..., None]).astype(jnp.bfloat16)
        attended = jnp.transpose(normed, (2, 0, 1, 3)).reshape(tok_rows, kv_local * query_group * HD)

        feat = attended.shape[1]
        head = lax.axis_index("head")
        total = jnp.dot(
            attended,
            lax.dynamic_slice_in_dim(out_weight, head * feat, feat, 0),
            preferred_element_type=jnp.float32,
        )
        for d in range(1, n_head):
            got = lax.ppermute(attended, "head", [(s, (s + d) % n_head) for s in range(n_head)])
            src = (head - d) % n_head
            total = total + jnp.dot(
                got,
                lax.dynamic_slice_in_dim(out_weight, src * feat, feat, 0),
                preferred_element_type=jnp.float32,
            )
        return total.astype(jnp.bfloat16)

    return on_device


def solution(mesh):
    n_ctx, n_head = mesh.shape["ctx"], mesh.shape["head"]
    row = 8 if n_ctx % 8 == 0 else n_ctx
    placed = (P("ctx", "head"), P("ctx", "head"), P("ctx", "head"), P(), P(None, "head"))
    return jax.shard_map(
        make_body(n_ctx, n_head, row), mesh=mesh, in_specs=placed, out_specs=P("ctx", "head"), check_vma=False
    )
```

time: 207 us -> 72.4 us (0.35)
  waiting for transfers between devices: 175 us -> 25.7 us
  starting transfers between devices: 0.08 us -> 33 us
  between operations: 13.2 us -> 0.59 us
  matrix products: 10.3 us -> 5.18 us
    all_gather x3 -> x0, waiting for transfers between devices: 174 us -> none  [the longest x1 72.9 us: on_device(): value_part = lax.all_gather(value_proj, 'ctx', axis=0, tiled=True)]
    ppermute x0 -> x16, starting transfers between devices: none -> 33 us  [the longest x7 15.5 us: on_device(): got = lax.ppermute(piece, 'ctx', pairs)]
    ppermute x0 -> x16, waiting for transfers between devices: none -> 25.7 us  [the longest x7 20.1 us: on_device(): got = lax.ppermute(piece, 'ctx', pairs)]
    dot_general x3 -> x10, matrix products: 10.3 us -> 5.18 us  [the longest x7 3.1 us: on_device(): jnp.dot(got, lax.dynamic_slice_in_dim(out_weight, src * feat, feat, 0), p...]
  transfers between devices with their start and end apart: 3 -> 16, of which waited for: 3 -> 7; matrix products, arithmetic and copies ran while one was open for 2% -> 7% of each run, Pallas kernels for 0% -> 0%
where the time goes in v1:
time: 72.4 us; the launch traced here: 72.1 us
  starting transfers between devices  33 us (46%)
  waiting for transfers between devices  25.7 us (35%)
  matrix products  5.18 us (7%)
  local copies, waits for them, and re-layouts  4.16 us (6%)
  other arithmetic  3.46 us (5%)
    ppermute x7, waiting for transfers between devices, on_device(): got = lax.ppermute(piece, 'ctx', pairs)  20.1 us
    ppermute x7, starting transfers between devices, on_device(): got = lax.ppermute(piece, 'ctx', pairs)  15.5 us
    ppermute x7, starting transfers between devices, on_device(): lax.ppermute(attended, 'head', [(s, (s + d) % n_head) for s in range(n_he...  8.96 us
    ppermute x2, starting transfers between devices, on_device(): lax.ppermute(own, 'ctx', [(s, s + shift) for s in range(n_ctx - shift)])  8.55 us
    ppermute x7, waiting for transfers between devices, on_device(): lax.ppermute(attended, 'head', [(s, (s + d) % n_head) for s in range(n_he...  5.63 us
    unnamed x25, local copies, waits for them, and re-layouts  3.31 us
    dot_general x7, matrix products, on_device(): jnp.dot(got, lax.dynamic_slice_in_dim(out_weight, src * feat, feat, 0), p...  3.1 us
  transfers between devices with their start and end apart: 16, of which 7 were waited for; matrix products, arithmetic and copies ran while one was open for 7% of the time, Pallas kernels for 0%

profile of v1, /device:TPU:1, one launch (start us, length us, event | category | flops | bytes accessed | tf_op | source)
XLA Modules:
  0.0 72.1 jit_solution(12942680019470436881)
XLA Ops:
  1.7 0.9 %copy.22 = bf16[128,128]{0,1:T(8,128)(2,1)S(1)} copy(bf16[128,128]{1,0:T(8,128)(2,1)} %param.6) | data formatting | bytes 65536 | tf_op args[1]
  2.6 0.9 %copy.23 = bf16[128,128]{0,1:T(8,128)(2,1)S(1)} copy(bf16[128,128]{1,0:T(8,128)(2,1)} %param.7) | data formatting | bytes 65536 | tf_op args[2]
  3.7 4.0 %collective-permute-start.1 = (bf16[128,256]{0,1:T(8,128)(2,1)S(1)}, bf16[128,256]{0,1:T(8,128)(2,1)S(1)}, u32[]{:S(2)}, u32[]{:S(2)}) collective-permute-start(bf16[128,256]{0,1:T(8,128)(2,1)S(1)} %get-tuple-element.19), channel_id=1, source_target_pairs={{0,64},{8,72},{16,80},{24,88},{32,96},{40,104},{48,112},{56,120},{... | collective-permute-start | bytes 196616 | tf_op jit(solution)/shard_map/ppermute | solution.py:60
  7.7 4.5 %collective-permute-start = (bf16[128,256]{0,1:T(8,128)(2,1)S(1)}, bf16[128,256]{0,1:T(8,128)(2,1)S(1)}, u32[]{:S(2)}, u32[]{:S(2)}) collective-permute-start(bf16[128,256]{0,1:T(8,128)(2,1)S(1)} %get-tuple-element.19), channel_id=1, source_target_pairs={{0,128},{8,136},{16,144},{24,152},{32,160},{40,168},{48,176},{56,1... | collective-permute-start | bytes 196616 | tf_op jit(solution)/shard_map/ppermute | solution.py:60
  12.3 1.0 %copy.24 = bf16[128,512]{0,1:T(8,128)(2,1)S(1)} copy(bf16[128,512]{1,0:T(8,128)(2,1)} %param.5) | data formatting | bytes 262144 | tf_op args[0]
  13.3 1.0 %compare_and_fusion = pred[128,2176]{0,1:T(8,128)(4,1)S(1)} fusion(s32[128]{0:T(128)S(1)} %select_reduce_fusion, s32[128]{0:T(128)S(1)} %iota_add_fusion.1, s32[2176]{0:T(1024)S(1)} %iota_add_fusion), kind=kLoop, calls=%fused_computation.19 | loop fusion | flops 835584 | bytes 288256 | tf_op jit(solution)/shard_map/and | solution.py:80
  15.2 5.7 %collective-permute-start.2 = (bf16[2,128,256]{1,2,0:T(8,128)(2,1)S(1)}, bf16[2,128,256]{1,2,0:T(8,128)(2,1)S(1)}, u32[]{:S(2)}, u32[]{:S(2)}) collective-permute-start(bf16[2,128,256]{1,2,0:T(8,128)(2,1)S(1)} %get-tuple-element.13), channel_id=1, source_target_pairs={{0,56},{8,0},{16,8},{24,16},{32,24},{40,32},{48,40},{56,48},{64,12... | collective-permute-start | bytes 393224 | tf_op jit(solution)/shard_map/ppermute | solution.py:68
  21.0 1.2 %collective-permute-start.3 = (bf16[2,128,256]{1,2,0:T(8,128)(2,1)S(1)}, bf16[2,128,256]{1,2,0:T(8,128)(2,1)S(1)}, u32[]{:S(2)}, u32[]{:S(2)}) collective-permute-start(bf16[2,128,256]{1,2,0:T(8,128)(2,1)S(1)} %get-tuple-element.12), channel_id=1, source_target_pairs={{0,48},{8,56},{16,0},{24,8},{32,16},{40,24},{48,32},{56,40},{64,11... | collective-permute-start | bytes 393224 | tf_op jit(solution)/shard_map/ppermute | solution.py:68
  22.8 4.4 %collective-permute-start.5 = (bf16[2,128,256]{1,2,0:T(8,128)(2,1)S(1)}, bf16[2,128,256]{1,2,0:T(8,128)(2,1)S(1)}, u32[]{:S(2)}, u32[]{:S(2)}) collective-permute-start(bf16[2,128,256]{1,2,0:T(8,128)(2,1)S(1)} %get-tuple-element.10), channel_id=1, source_target_pairs={{0,32},{8,40},{16,48},{24,56},{32,0},{40,8},{48,16},{56,24},{64,96... | collective-permute-start | bytes 393224 | tf_op jit(solution)/shard_map/ppermute | solution.py:68
  27.2 2.2 %collective-permute-start.7 = (bf16[2,128,256]{1,2,0:T(8,128)(2,1)S(1)}, bf16[2,128,256]{1,2,0:T(8,128)(2,1)S(1)}, u32[]{:S(2)}, u32[]{:S(2)}) collective-permute-start(bf16[2,128,256]{1,2,0:T(8,128)(2,1)S(1)} %get-tuple-element.8), channel_id=1, source_target_pairs={{0,16},{8,24},{16,32},{24,40},{32,48},{40,56},{48,0},{56,8},{64,80... | collective-permute-start | bytes 393224 | tf_op jit(solution)/shard_map/ppermute | solution.py:68
  29.4 1.5 %collective-permute-start.8 = (bf16[2,128,256]{1,2,0:T(8,128)(2,1)S(1)}, bf16[2,128,256]{1,2,0:T(8,128)(2,1)S(1)}, u32[]{:S(2)}, u32[]{:S(2)}) collective-permute-start(bf16[2,128,256]{1,2,0:T(8,128)(2,1)S(1)} %get-tuple-element.7), channel_id=1, source_target_pairs={{0,8},{8,16},{16,24},{24,32},{32,40},{40,48},{48,56},{56,0},{64,72... | collective-permute-start | bytes 393224 | tf_op jit(solution)/shard_map/ppermute | solution.py:68
  31.0 1.5 %collective-permute-done.4 = bf16[2,128,256]{1,2,0:T(8,128)(2,1)S(1)} collective-permute-done((bf16[2,128,256]{1,2,0:T(8,128)(2,1)S(1)}, bf16[2,128,256]{1,2,0:T(8,128)(2,1)S(1)}, u32[]{:S(2)}, u32[]{:S(2)}) %collective-permute-start.4) | collective-permute-done | bytes 131104 | tf_op jit(solution)/shard_map/ppermute | solution.py:68
  32.5 1.6 %collective-permute-done.5 = bf16[2,128,256]{1,2,0:T(8,128)(2,1)S(1)} collective-permute-done((bf16[2,128,256]{1,2,0:T(8,128)(2,1)S(1)}, bf16[2,128,256]{1,2,0:T(8,128)(2,1)S(1)}, u32[]{:S(2)}, u32[]{:S(2)}) %collective-permute-start.5) | collective-permute-done | bytes 131104 | tf_op jit(solution)/shard_map/ppermute | solution.py:68
  34.1 2.0 %collective-permute-done.6 = bf16[2,128,256]{1,2,0:T(8,128)(2,1)S(1)} collective-permute-done((bf16[2,128,256]{1,2,0:T(8,128)(2,1)S(1)}, bf16[2,128,256]{1,2,0:T(8,128)(2,1)S(1)}, u32[]{:S(2)}, u32[]{:S(2)}) %collective-permute-start.6) | collective-permute-done | bytes 131104 | tf_op jit(solution)/shard_map/ppermute | solution.py:68
  36.1 9.9 %collective-permute-done.7 = bf16[2,128,256]{1,2,0:T(8,128)(2,1)S(1)} collective-permute-done((bf16[2,128,256]{1,2,0:T(8,128)(2,1)S(1)}, bf16[2,128,256]{1,2,0:T(8,128)(2,1)S(1)}, u32[]{:S(2)}, u32[]{:S(2)}) %collective-permute-start.7) | collective-permute-done | bytes 131104 | tf_op jit(solution)/shard_map/ppermute | solution.py:68
  46.1 5.1 %collective-permute-done.8 = bf16[2,128,256]{1,2,0:T(8,128)(2,1)S(1)} collective-permute-done((bf16[2,128,256]{1,2,0:T(8,128)(2,1)S(1)}, bf16[2,128,256]{1,2,0:T(8,128)(2,1)S(1)}, u32[]{:S(2)}, u32[]{:S(2)}) %collective-permute-start.8) | collective-permute-done | bytes 131104 | tf_op jit(solution)/shard_map/ppermute | solution.py:68
  51.4 0.8 %fusion.73 = (f32[4,128]{1,0:T(4,128)S(1)}, f32[1,4,128,2176]{2,3,1,0:T(8,128)S(1)}) fusion(bf16[128,4,64]{2,0,1:T(8,128)(2,1)S(1)} %get-tuple-element.6, bf16[128,4,64]{2,0,1:T(8,128)(2,1)S(1)} %get-tuple-element.5, bf16[2176,256]{0,1:T(8,128)(2,1)S(1)} %constant_dynamic-update-slice_fusion, pred[128,2176]{0,1:T(8,128)(4,1)S(1)} %compare_and_fusion), kind=kOutput, calls=%fused_computation.114 | convolution fusion | flops 288816640 | bytes 5556224 | tf_op jit(solution)/shard_map/tkgd,nkd->kgtn/dot_general | solution.py:76
  53.1 0.9 %fusion.19 = bf16[4,128,128]{1,2,0:T(8,128)(2,1)S(1)} fusion(f32[1,4,128,2176]{2,3,1,0:T(8,128)S(1)} %get-tuple-element.23, f32[4,128]{1,0:T(4,128)S(1)} %get-tuple-element.22, pred[128,2176]{0,1:T(8,128)(4,1)S(1)} %compare_and_fusion, bf16[2176,256]{0,1:T(8,128)(2,1)S(1)} %constant_dynamic-update-slice_fusion, f32[4,128]{1,0:T(4,128)S(1)} %fusion.2), kind=kOutput, calls=%fused_computation.21 | convolution fusion | flops 288686080 | bytes 5427200 | tf_op jit(solution)/shard_map/kgtn,nkd->kgtd/dot_general | solution.py:85
  54.0 2.0 %collective-permute-start.9 = (bf16[128,512]{0,1:T(8,128)(2,1)S(1)}, bf16[128,512]{0,1:T(8,128)(2,1)S(1)}, u32[]{:S(2)}, u32[]{:S(2)}) collective-permute-start(bf16[128,512]{0,1:T(8,128)(2,1)S(1)} %bitcast.107), channel_id=1, source_target_pairs={{0,1},{1,2},{2,3},{3,4},{4,5},{5,6},{6,7},{7,0},{8,9},{9,10},{10,1... | collective-permute-start | bytes 393224 | tf_op jit(solution)/shard_map/ppermute | solution.py:102
  56.0 1.5 %collective-permute-start.14 = (bf16[128,512]{0,1:T(8,128)(2,1)S(1)}, bf16[128,512]{0,1:T(8,128)(2,1)S(1)}, u32[]{:S(2)}, u32[]{:S(2)}) collective-permute-start(bf16[128,512]{0,1:T(8,128)(2,1)S(1)} %bitcast.108), channel_id=1, source_target_pairs={{0,6},{1,7},{2,0},{3,1},{4,2},{5,3},{6,4},{7,5},{8,14},{9,15},{10,... | collective-permute-start | bytes 393224 | tf_op jit(solution)/shard_map/ppermute | solution.py:102
  59.0 3.5 %collective-permute-start.11 = (bf16[128,512]{0,1:T(8,128)(2,1)S(1)}, bf16[128,512]{0,1:T(8,128)(2,1)S(1)}, u32[]{:S(2)}, u32[]{:S(2)}) collective-permute-start(bf16[128,512]{0,1:T(8,128)(2,1)S(1)} %bitcast.111), channel_id=1, source_target_pairs={{0,3},{1,4},{2,5},{3,6},{4,7},{5,0},{6,1},{7,2},{8,11},{9,12},{10,... | collective-permute-start | bytes 393224 | tf_op jit(solution)/shard_map/ppermute | solution.py:102
  64.0 4.3 %collective-permute-done.13 = bf16[128,512]{0,1:T(8,128)(2,1)S(1)} collective-permute-done((bf16[128,512]{0,1:T(8,128)(2,1)S(1)}, bf16[128,512]{0,1:T(8,128)(2,1)S(1)}, u32[]{:S(2)}, u32[]{:S(2)}) %collective-permute-start.13) | collective-permute-done | bytes 131104 | tf_op jit(solution)/shard_map/ppermute | solution.py:102
  69.0 1.3 %collective-permute-done.11 = bf16[128,512]{0,1:T(8,128)(2,1)S(1)} collective-permute-done((bf16[128,512]{0,1:T(8,128)(2,1)S(1)}, bf16[128,512]{0,1:T(8,128)(2,1)S(1)}, u32[]{:S(2)}, u32[]{:S(2)}) %collective-permute-start.11) | collective-permute-done | bytes 131104 | tf_op jit(solution)/shard_map/ppermute | solution.py:102
  71.0 1.1 %fusion.15 = bf16[128,1024]{1,0:T(8,128)(2,1)} fusion(f32[128,1024]{1,0:T(8,128)S(1)} %fusion.22, f32[128,1024]{1,0:T(8,128)S(1)} %fusion.24, f32[128,1024]{1,0:T(8,128)S(1)} %fusion.26, f32[128,1024]{1,0:T(8,128)S(1)} %fusion.28, f32[128,1024]{1,0:T(8,128)S(1)} %fusion.30, f32[128,1024]{1,0:T(8,128)S(1)} %convolution_add_fusion.1, ...), kind=kOutput, calls=%fused_computation.18 | convolution fusion | flops 135135232 | bytes 4587524 | tf_op jit(solution)/shard_map/dot_general | solution.py:104
  (64 shorter events, 8.6 us)
Async XLA Ops:
  3.7 11.3 %collective-permute-start.1 = (bf16[128,256]{0,1:T(8,128)(2,1)S(1)}, bf16[128,256]{0,1:T(8,128)(2,1)S(1)}, u32[]{:S(2)}, u32[]{:S(2)}) collective-permute-start(bf16[128,256]{0,1:T(8,128)(2,1)S(1)} %get-tuple-element.19), channel_id=1, source_target_pairs={{0,64},{8,72},{16,80},{24,88},{32,96},{40,104},{48,112},{56,120},{... | collective-permute-start | bytes 196616 | tf_op jit(solution)/shard_map/ppermute | solution.py:60
  7.7 7.3 %collective-permute-start = (bf16[128,256]{0,1:T(8,128)(2,1)S(1)}, bf16[128,256]{0,1:T(8,128)(2,1)S(1)}, u32[]{:S(2)}, u32[]{:S(2)}) collective-permute-start(bf16[128,256]{0,1:T(8,128)(2,1)S(1)} %get-tuple-element.19), channel_id=1, source_target_pairs={{0,128},{8,136},{16,144},{24,152},{32,160},{40,168},{48,176},{56,1... | collective-permute-start | bytes 196616 | tf_op jit(solution)/shard_map/ppermute | solution.py:60
  15.2 12.1 %collective-permute-start.2 = (bf16[2,128,256]{1,2,0:T(8,128)(2,1)S(1)}, bf16[2,128,256]{1,2,0:T(8,128)(2,1)S(1)}, u32[]{:S(2)}, u32[]{:S(2)}) collective-permute-start(bf16[2,128,256]{1,2,0:T(8,128)(2,1)S(1)} %get-tuple-element.13), channel_id=1, source_target_pairs={{0,56},{8,0},{16,8},{24,16},{32,24},{40,32},{48,40},{56,48},{64,12... | collective-permute-start | bytes 393224 | tf_op jit(solution)/shard_map/ppermute | solution.py:68
  21.0 8.4 %collective-permute-start.3 = (bf16[2,128,256]{1,2,0:T(8,128)(2,1)S(1)}, bf16[2,128,256]{1,2,0:T(8,128)(2,1)S(1)}, u32[]{:S(2)}, u32[]{:S(2)}) collective-permute-start(bf16[2,128,256]{1,2,0:T(8,128)(2,1)S(1)} %get-tuple-element.12), channel_id=1, source_target_pairs={{0,48},{8,56},{16,0},{24,8},{32,16},{40,24},{48,32},{56,40},{64,11... | collective-permute-start | bytes 393224 | tf_op jit(solution)/shard_map/ppermute | solution.py:68
  22.3 10.2 %collective-permute-start.4 = (bf16[2,128,256]{1,2,0:T(8,128)(2,1)S(1)}, bf16[2,128,256]{1,2,0:T(8,128)(2,1)S(1)}, u32[]{:S(2)}, u32[]{:S(2)}) collective-permute-start(bf16[2,128,256]{1,2,0:T(8,128)(2,1)S(1)} %get-tuple-element.11), channel_id=1, source_target_pairs={{0,40},{8,48},{16,56},{24,0},{32,8},{40,16},{48,24},{56,32},{64,10... | collective-permute-start | bytes 393224 | tf_op jit(solution)/shard_map/ppermute | solution.py:68
  22.8 11.3 %collective-permute-start.5 = (bf16[2,128,256]{1,2,0:T(8,128)(2,1)S(1)}, bf16[2,128,256]{1,2,0:T(8,128)(2,1)S(1)}, u32[]{:S(2)}, u32[]{:S(2)}) collective-permute-start(bf16[2,128,256]{1,2,0:T(8,128)(2,1)S(1)} %get-tuple-element.10), channel_id=1, source_target_pairs={{0,32},{8,40},{16,48},{24,56},{32,0},{40,8},{48,16},{56,24},{64,96... | collective-permute-start | bytes 393224 | tf_op jit(solution)/shard_map/ppermute | solution.py:68
  27.2 8.9 %collective-permute-start.6 = (bf16[2,128,256]{1,2,0:T(8,128)(2,1)S(1)}, bf16[2,128,256]{1,2,0:T(8,128)(2,1)S(1)}, u32[]{:S(2)}, u32[]{:S(2)}) collective-permute-start(bf16[2,128,256]{1,2,0:T(8,128)(2,1)S(1)} %get-tuple-element.9), channel_id=1, source_target_pairs={{0,24},{8,32},{16,40},{24,48},{32,56},{40,0},{48,8},{56,16},{64,88... | collective-permute-start | bytes 393224 | tf_op jit(solution)/shard_map/ppermute | solution.py:68
  27.2 18.8 %collective-permute-start.7 = (bf16[2,128,256]{1,2,0:T(8,128)(2,1)S(1)}, bf16[2,128,256]{1,2,0:T(8,128)(2,1)S(1)}, u32[]{:S(2)}, u32[]{:S(2)}) collective-permute-start(bf16[2,128,256]{1,2,0:T(8,128)(2,1)S(1)} %get-tuple-element.8), channel_id=1, source_target_pairs={{0,16},{8,24},{16,32},{24,40},{32,48},{40,56},{48,0},{56,8},{64,80... | collective-permute-start | bytes 393224 | tf_op jit(solution)/shard_map/ppermute | solution.py:68
  29.4 21.7 %collective-permute-start.8 = (bf16[2,128,256]{1,2,0:T(8,128)(2,1)S(1)}, bf16[2,128,256]{1,2,0:T(8,128)(2,1)S(1)}, u32[]{:S(2)}, u32[]{:S(2)}) collective-permute-start(bf16[2,128,256]{1,2,0:T(8,128)(2,1)S(1)} %get-tuple-element.7), channel_id=1, source_target_pairs={{0,8},{8,16},{16,24},{24,32},{32,40},{40,48},{48,56},{56,0},{64,72... | collective-permute-start | bytes 393224 | tf_op jit(solution)/shard_map/ppermute | solution.py:68
  51.4 11.2 %slice-start = ((s8[8388608]{0:T(1024)(128)(4,1)}), s8[4194304]{0:T(1024)(128)(4,1)S(1)}, s32[]{:S(2)}) async-start(s8[8388608]{0:T(1024)(128)(4,1)} %bitcast.102), calls=%async_computation | async-start | bytes 8388608
  52.2 10.3 %slice-start.1 = ((s8[8388608]{0:T(1024)(128)(4,1)}), s8[4194304]{0:T(1024)(128)(4,1)S(1)}, s32[]{:S(2)}) async-start(s8[8388608]{0:T(1024)(128)(4,1)} %bitcast.102), calls=%async_computation.1 | async-start | bytes 8388608
  54.0 8.9 %collective-permute-start.9 = (bf16[128,512]{0,1:T(8,128)(2,1)S(1)}, bf16[128,512]{0,1:T(8,128)(2,1)S(1)}, u32[]{:S(2)}, u32[]{:S(2)}) collective-permute-start(bf16[128,512]{0,1:T(8,128)(2,1)S(1)} %bitcast.107), channel_id=1, source_target_pairs={{0,1},{1,2},{2,3},{3,4},{4,5},{5,6},{6,7},{7,0},{8,9},{9,10},{10,1... | collective-permute-start | bytes 393224 | tf_op jit(solution)/shard_map/ppermute | solution.py:102
  56.0 7.3 %collective-permute-start.14 = (bf16[128,512]{0,1:T(8,128)(2,1)S(1)}, bf16[128,512]{0,1:T(8,128)(2,1)S(1)}, u32[]{:S(2)}, u32[]{:S(2)}) collective-permute-start(bf16[128,512]{0,1:T(8,128)(2,1)S(1)} %bitcast.108), channel_id=1, source_target_pairs={{0,6},{1,7},{2,0},{3,1},{4,2},{5,3},{6,4},{7,5},{8,14},{9,15},{10,... | collective-permute-start | bytes 393224 | tf_op jit(solution)/shard_map/ppermute | solution.py:102
  57.5 10.8 %collective-permute-start.13 = (bf16[128,512]{0,1:T(8,128)(2,1)S(1)}, bf16[128,512]{0,1:T(8,128)(2,1)S(1)}, u32[]{:S(2)}, u32[]{:S(2)}) collective-permute-start(bf16[128,512]{0,1:T(8,128)(2,1)S(1)} %bitcast.109), channel_id=1, source_target_pairs={{0,5},{1,6},{2,7},{3,0},{4,1},{5,2},{6,3},{7,4},{8,13},{9,14},{10,... | collective-permute-start | bytes 393224 | tf_op jit(solution)/shard_map/ppermute | solution.py:102
  58.2 10.4 %collective-permute-start.12 = (bf16[128,512]{0,1:T(8,128)(2,1)S(1)}, bf16[128,512]{0,1:T(8,128)(2,1)S(1)}, u32[]{:S(2)}, u32[]{:S(2)}) collective-permute-start(bf16[128,512]{0,1:T(8,128)(2,1)S(1)} %bitcast.110), channel_id=1, source_target_pairs={{0,4},{1,5},{2,6},{3,7},{4,0},{5,1},{6,2},{7,3},{8,12},{9,13},{10,... | collective-permute-start | bytes 393224 | tf_op jit(solution)/shard_map/ppermute | solution.py:102
  59.0 11.3 %collective-permute-start.11 = (bf16[128,512]{0,1:T(8,128)(2,1)S(1)}, bf16[128,512]{0,1:T(8,128)(2,1)S(1)}, u32[]{:S(2)}, u32[]{:S(2)}) collective-permute-start(bf16[128,512]{0,1:T(8,128)(2,1)S(1)} %bitcast.111), channel_id=1, source_target_pairs={{0,3},{1,4},{2,5},{3,6},{4,7},{5,0},{6,1},{7,2},{8,11},{9,12},{10,... | collective-permute-start | bytes 393224 | tf_op jit(solution)/shard_map/ppermute | solution.py:102
  62.9 7.7 %collective-permute-start.15 = (bf16[128,512]{0,1:T(8,128)(2,1)S(1)}, bf16[128,512]{0,1:T(8,128)(2,1)S(1)}, u32[]{:S(2)}, u32[]{:S(2)}) collective-permute-start(bf16[128,512]{0,1:T(8,128)(2,1)S(1)} %bitcast.113), channel_id=1, source_target_pairs={{0,7},{1,0},{2,1},{3,2},{4,3},{5,4},{6,5},{7,6},{8,15},{9,8},{10,9... | collective-permute-start | bytes 393224 | tf_op jit(solution)/shard_map/ppermute | solution.py:102
  63.3 7.7 %collective-permute-start.10 = (bf16[128,512]{0,1:T(8,128)(2,1)S(1)}, bf16[128,512]{0,1:T(8,128)(2,1)S(1)}, u32[]{:S(2)}, u32[]{:S(2)}) collective-permute-start(bf16[128,512]{0,1:T(8,128)(2,1)S(1)} %bitcast.114), channel_id=1, source_target_pairs={{0,2},{1,3},{2,4},{3,5},{4,6},{5,7},{6,0},{7,1},{8,10},{9,11},{10,... | collective-permute-start | bytes 393224 | tf_op jit(solution)/shard_map/ppermute | solution.py:102

commit v2 on v1

--- a/solution.py
+++ b/solution.py
@@ -58,16 +58,26 @@
         for m in range(1, rows_back + 1):
             shift = row * m
             bundle.append(lax.ppermute(own, "ctx", [(s, s + shift) for s in range(n_ctx - shift)]))
+        blocks = {row * m: bundle[m] for m in range(rows_back + 1)}
         bundle = jnp.stack(bundle)
-        blocks = {row * m: bundle[m] for m in range(rows_back + 1)}
         z = ctx % row
-        for b in range(1, row):
-            lo = jnp.where(z + b >= row, 1, 0)
-            piece = lax.dynamic_slice_in_dim(bundle, lo, rows_back, 0)
-            pairs = [(r * row + s, r * row + (s + b) % row) for r in range(n_ctx // row) for s in range(row)]
-            got = lax.ppermute(piece, "ctx", pairs)
+        n_rows = n_ctx // row
+        ahead = [(r * row + s, r * row + (s + 1) % row) for r in range(n_rows) for s in range(row)]
+        behind = [(r * row + s, r * row + (s - 1) % row) for r in range(n_rows) for s in range(row)]
+
+        def take(packet, b):
+            lo = jnp.where(z < b, 1, 0)
+            got = lax.dynamic_slice_in_dim(packet, lo, rows_back, 0)
             for m in range(rows_back):
                 blocks[b + row * m] = got[m]
+
+        forward, backward = bundle, bundle
+        for step in range(1, row // 2 + 1):
+            forward = lax.ppermute(forward, "ctx", ahead)
+            take(forward, step)
+            if step < row - row // 2:
+                backward = lax.ppermute(backward, "ctx", behind)
+                take(backward, row - step)
         window = jnp.concatenate([blocks[span - k] for k in range(span + 1)], axis=0)
         key_count = window.shape[0]
         key_block = window[:, :kv_width].reshape(key_count, kv_local, HD)
@@ -93,19 +103,29 @@
 
         feat = attended.shape[1]
         head = lax.axis_index("head")
-        total = jnp.dot(
-            attended,
-            lax.dynamic_slice_in_dim(out_weight, head * feat, feat, 0),
-            preferred_element_type=jnp.float32,
-        )
-        for d in range(1, n_head):
-            got = lax.ppermute(attended, "head", [(s, (s + d) % n_head) for s in range(n_head)])
-            src = (head - d) % n_head
-            total = total + jnp.dot(
-                got,
-                lax.dynamic_slice_in_dim(out_weight, src * feat, feat, 0),
-                preferred_element_type=jnp.float32,
-            )
+        core = head % 2
+
+        def project(piece, src):
+            rows = lax.dynamic_slice_in_dim(out_weight, src * feat, feat, 0)
+            return jnp.dot(piece, rows, preferred_element_type=jnp.float32)
+
+        up = lax.ppermute(attended, "head", [(s, (s + 2) % n_head) for s in range(n_head)])
+        down = lax.ppermute(attended, "head", [(s, (s - 2) % n_head) for s in range(n_head)])
+        swap = [(s, s ^ 1) for s in range(n_head)]
+        partner = lax.ppermute(attended, "head", swap)
+        relay_pairs = [(s, (s + 2) % n_head) if s % 2 == 0 else (s, (s - 2) % n_head) for s in range(n_head)]
+        far = lax.ppermute(jnp.where(core == 0, up, down), "head", relay_pairs)
+        near_other = lax.ppermute(jnp.stack([up, down]), "head", swap)
+        far_other = lax.ppermute(far, "head", swap)
+        other = head ^ 1
+        total = project(attended, head)
+        total = total + project(up, (head - 2) % n_head)
+        total = total + project(down, (head + 2) % n_head)
+        total = total + project(partner, other)
+        total = total + project(far, (head + 4) % n_head)
+        total = total + project(near_other[0], (other - 2) % n_head)
+        total = total + project(near_other[1], (other + 2) % n_head)
+        total = total + project(far_other, (other + 4) % n_head)
         return total.astype(jnp.bfloat16)
 
     return on_device

time: 72.4 us -> 69.2 us (0.956)
  waiting for transfers between devices: 25.7 us -> 17.2 us
  starting transfers between devices: 33 us -> 37.9 us
    ppermute x14 -> x13, waiting for transfers between devices: 25.7 us -> 17.2 us  [the longest x4 14.4 us: on_device(): forward = lax.ppermute(forward, 'ctx', ahead)]
    ppermute x14 -> x13, starting transfers between devices: 24.5 us -> 29.3 us  [the longest x3 11.8 us: on_device(): backward = lax.ppermute(backward, 'ctx', behind)]
  transfers between devices with their start and end apart: 16 -> 15, of which waited for: 7 -> 4; matrix products, arithmetic and copies ran while one was open for 7% -> 8% of each run, Pallas kernels for 0% -> 0%
where the time goes in v2:
time: 69.2 us; the launch traced here: 68.5 us
  starting transfers between devices  37.9 us (55%)
  waiting for transfers between devices  17.2 us (25%)
  matrix products  5.15 us (7%)
  local copies, waits for them, and re-layouts  4.16 us (6%)
  other arithmetic  3.5 us (5%)
    ppermute x4, waiting for transfers between devices, on_device(): forward = lax.ppermute(forward, 'ctx', ahead)  14.4 us
    ppermute x3, starting transfers between devices, on_device(): backward = lax.ppermute(backward, 'ctx', behind)  11.8 us
    ppermute x2, starting transfers between devices, on_device(): lax.ppermute(own, 'ctx', [(s, s + shift) for s in range(n_ctx - shift)])  8.55 us
    ppermute x1, starting transfers between devices, on_device(): partner = lax.ppermute(attended, 'head', swap)  6.38 us
    ppermute x1, starting transfers between devices, on_device(): near_other = lax.ppermute(jnp.stack([up, down]), 'head', swap)  4.02 us
    unnamed x25, local copies, waits for them, and re-layouts  3.4 us
    dot_general x8, matrix products, project(): return jnp.dot(piece, rows, preferred_element_type=jnp.float32)  3.4 us
    ppermute x1, starting transfers between devices, on_device(): far_other = lax.ppermute(far, 'head', swap)  3.02 us
  transfers between devices with their start and end apart: 15, of which 4 were waited for; matrix products, arithmetic and copies ran while one was open for 8% of the time, Pallas kernels for 0%

profile of v2, /device:TPU:1, one launch (start us, length us, event | category | flops | bytes accessed | tf_op | source)
XLA Modules:
  0.0 68.5 jit_solution(13229845240793895729)
XLA Ops:
  0.9 0.7 %select_reduce_fusion = s32[128]{0:T(128)S(1)} fusion(s32[32]{0:T(128)} %param.8, s32[128]{0:T(128)S(1)} %iota_add_fusion.1, s32[32]{0:T(128)S(1)} %reduce.2), kind=kLoop, calls=%fused_computation.93 | loop fusion | flops 12160 | bytes 1280 | tf_op jit(solution)/shard_map/reduce_sum | solution.py:16
  1.7 0.9 %copy.22 = bf16[128,128]{0,1:T(8,128)(2,1)S(1)} copy(bf16[128,128]{1,0:T(8,128)(2,1)} %param.6) | data formatting | bytes 65536 | tf_op args[1]
  2.6 0.9 %copy.23 = bf16[128,128]{0,1:T(8,128)(2,1)S(1)} copy(bf16[128,128]{1,0:T(8,128)(2,1)} %param.7) | data formatting | bytes 65536 | tf_op args[2]
  3.7 4.0 %collective-permute-start.1 = (bf16[128,256]{0,1:T(8,128)(2,1)S(1)}, bf16[128,256]{0,1:T(8,128)(2,1)S(1)}, u32[]{:S(2)}, u32[]{:S(2)}) collective-permute-start(bf16[128,256]{0,1:T(8,128)(2,1)S(1)} %get-tuple-element.12), channel_id=1, source_target_pairs={{0,64},{8,72},{16,80},{24,88},{32,96},{40,104},{48,112},{56,120},{... | collective-permute-start | bytes 196616 | tf_op jit(solution)/shard_map/ppermute | solution.py:60
  7.7 4.5 %collective-permute-start = (bf16[128,256]{0,1:T(8,128)(2,1)S(1)}, bf16[128,256]{0,1:T(8,128)(2,1)S(1)}, u32[]{:S(2)}, u32[]{:S(2)}) collective-permute-start(bf16[128,256]{0,1:T(8,128)(2,1)S(1)} %get-tuple-element.12), channel_id=1, source_target_pairs={{0,128},{8,136},{16,144},{24,152},{32,160},{40,168},{48,176},{56,1... | collective-permute-start | bytes 196616 | tf_op jit(solution)/shard_map/ppermute | solution.py:60
  12.3 1.0 %copy.24 = bf16[128,512]{0,1:T(8,128)(2,1)S(1)} copy(bf16[128,512]{1,0:T(8,128)(2,1)} %param.5) | data formatting | bytes 262144 | tf_op args[0]
  13.3 1.0 %compare_and_fusion = pred[128,2176]{0,1:T(8,128)(4,1)S(1)} fusion(s32[128]{0:T(128)S(1)} %select_reduce_fusion, s32[128]{0:T(128)S(1)} %iota_add_fusion.1, s32[2176]{0:T(1024)S(1)} %iota_add_fusion), kind=kLoop, calls=%fused_computation.19 | loop fusion | flops 835584 | bytes 288256 | tf_op jit(solution)/shard_map/and | solution.py:90
  14.7 5.7 %collective-permute-start.2 = (bf16[3,128,256]{1,2,0:T(8,128)(2,1)S(1)}, bf16[3,128,256]{1,2,0:T(8,128)(2,1)S(1)}, u32[]{:S(2)}, u32[]{:S(2)}) collective-permute-start(bf16[3,128,256]{1,2,0:T(8,128)(2,1)S(1)} %pad_maximum_fusion.1), channel_id=1, source_target_pairs={{0,56},{8,0},{16,8},{24,16},{32,24},{40,32},{48,40},{56,48},{64,12... | collective-permute-start | bytes 589832 | tf_op jit(solution)/shard_map/ppermute | solution.py:79
  20.7 2.7 %collective-permute-done.2 = bf16[3,128,256]{1,2,0:T(8,128)(2,1)S(1)} collective-permute-done((bf16[3,128,256]{1,2,0:T(8,128)(2,1)S(1)}, bf16[3,128,256]{1,2,0:T(8,128)(2,1)S(1)}, u32[]{:S(2)}, u32[]{:S(2)}) %collective-permute-start.2) | collective-permute-done | bytes 196640 | tf_op jit(solution)/shard_map/ppermute | solution.py:79
  23.4 3.4 %collective-permute-start.3 = (bf16[3,128,256]{1,2,0:T(8,128)(2,1)S(1)}, bf16[3,128,256]{1,2,0:T(8,128)(2,1)S(1)}, u32[]{:S(2)}, u32[]{:S(2)}) collective-permute-start(bf16[3,128,256]{1,2,0:T(8,128)(2,1)S(1)} %collective-permute-done.2), channel_id=1, source_target_pairs={{0,56},{8,0},{16,8},{24,16},{32,24},{40,32},{48,40},{56,48},{64,12... | collective-permute-start | bytes 589832 | tf_op jit(solution)/shard_map/ppermute | solution.py:79
  27.0 5.5 %collective-permute-done.6 = bf16[3,128,256]{1,2,0:T(8,128)(2,1)S(1)} collective-permute-done((bf16[3,128,256]{1,2,0:T(8,128)(2,1)S(1)}, bf16[3,128,256]{1,2,0:T(8,128)(2,1)S(1)}, u32[]{:S(2)}, u32[]{:S(2)}) %collective-permute-start.6) | collective-permute-done | bytes 196640 | tf_op jit(solution)/shard_map/ppermute | solution.py:76
  32.6 2.7 %collective-permute-start.4 = (bf16[3,128,256]{1,2,0:T(8,128)(2,1)S(1)}, bf16[3,128,256]{1,2,0:T(8,128)(2,1)S(1)}, u32[]{:S(2)}, u32[]{:S(2)}) collective-permute-start(bf16[3,128,256]{1,2,0:T(8,128)(2,1)S(1)} %collective-permute-done.3), channel_id=1, source_target_pairs={{0,56},{8,0},{16,8},{24,16},{32,24},{40,32},{48,40},{56,48},{64,12... | collective-permute-start | bytes 589832 | tf_op jit(solution)/shard_map/ppermute | solution.py:79
  35.3 2.9 %collective-permute-done.7 = bf16[3,128,256]{1,2,0:T(8,128)(2,1)S(1)} collective-permute-done((bf16[3,128,256]{1,2,0:T(8,128)(2,1)S(1)}, bf16[3,128,256]{1,2,0:T(8,128)(2,1)S(1)}, u32[]{:S(2)}, u32[]{:S(2)}) %collective-permute-start.7) | collective-permute-done | bytes 196640 | tf_op jit(solution)/shard_map/ppermute | solution.py:76
  38.3 6.0 %collective-permute-done.8 = bf16[3,128,256]{1,2,0:T(8,128)(2,1)S(1)} collective-permute-done((bf16[3,128,256]{1,2,0:T(8,128)(2,1)S(1)}, bf16[3,128,256]{1,2,0:T(8,128)(2,1)S(1)}, u32[]{:S(2)}, u32[]{:S(2)}) %collective-permute-start.8) | collective-permute-done | bytes 196640 | tf_op jit(solution)/shard_map/ppermute | solution.py:76
  44.8 0.8 %fusion.71 = (f32[4,128]{1,0:T(4,128)S(1)}, f32[1,4,128,2176]{2,3,1,0:T(8,128)S(1)}) fusion(bf16[128,4,64]{2,0,1:T(8,128)(2,1)S(1)} %get-tuple-element.6, bf16[128,4,64]{2,0,1:T(8,128)(2,1)S(1)} %get-tuple-element.5, bf16[2176,256]{0,1:T(8,128)(2,1)S(1)} %constant_dynamic-update-slice_fusion, pred[128,2176]{0,1:T(8,128)(4,1)S(1)} %compare_and_fusion), kind=kOutput, calls=%fused_computation.110 | convolution fusion | flops 288816640 | bytes 5556224 | tf_op jit(solution)/shard_map/tkgd,nkd->kgtn/dot_general | solution.py:86
  45.6 0.8 %fusion.2 = f32[4,128]{1,0:T(4,128)S(1)} fusion(f32[1,4,128,2176]{2,3,1,0:T(8,128)S(1)} %get-tuple-element.16, f32[4,128]{1,0:T(4,128)S(1)} %get-tuple-element.15, pred[128,2176]{0,1:T(8,128)(4,1)S(1)} %compare_and_fusion), kind=kLoop, calls=%fused_computation.4 | loop fusion | flops 3341824 | bytes 4739072 | tf_op jit(solution)/shard_map/reduce_sum | solution.py:94
  46.4 0.9 %fusion.18 = bf16[4,128,128]{1,2,0:T(8,128)(2,1)S(1)} fusion(f32[1,4,128,2176]{2,3,1,0:T(8,128)S(1)} %get-tuple-element.16, f32[4,128]{1,0:T(4,128)S(1)} %get-tuple-element.15, pred[128,2176]{0,1:T(8,128)(4,1)S(1)} %compare_and_fusion, bf16[2176,256]{0,1:T(8,128)(2,1)S(1)} %constant_dynamic-update-slice_fusion, f32[4,128]{1,0:T(4,128)S(1)} %fusion.2), kind=kOutput, calls=%fused_computation.21 | convolution fusion | flops 288686080 | bytes 5427200 | tf_op jit(solution)/shard_map/kgtn,nkd->kgtd/dot_general | solution.py:95
  47.4 1.3 %collective-permute-start.9 = (bf16[128,512]{0,1:T(8,128)(2,1)S(1)}, bf16[128,512]{0,1:T(8,128)(2,1)S(1)}, u32[]{:S(2)}, u32[]{:S(2)}) collective-permute-start(bf16[128,512]{0,1:T(8,128)(2,1)S(1)} %bitcast.115), channel_id=1, source_target_pairs={{0,2},{1,3},{2,4},{3,5},{4,6},{5,7},{6,0},{7,1},{8,10},{9,11},{10,... | collective-permute-start | bytes 393224 | tf_op jit(solution)/shard_map/ppermute | solution.py:112
  48.6 1.5 %collective-permute-start.10 = (bf16[128,512]{0,1:T(8,128)(2,1)S(1)}, bf16[128,512]{0,1:T(8,128)(2,1)S(1)}, u32[]{:S(2)}, u32[]{:S(2)}) collective-permute-start(bf16[128,512]{0,1:T(8,128)(2,1)S(1)} %bitcast.116), channel_id=1, source_target_pairs={{0,6},{1,7},{2,0},{3,1},{4,2},{5,3},{6,4},{7,5},{8,14},{9,15},{10,... | collective-permute-start | bytes 393224 | tf_op jit(solution)/shard_map/ppermute | solution.py:113
  50.1 6.4 %collective-permute-start.11 = (bf16[128,512]{0,1:T(8,128)(2,1)S(1)}, bf16[128,512]{0,1:T(8,128)(2,1)S(1)}, u32[]{:S(2)}, u32[]{:S(2)}) collective-permute-start(bf16[128,512]{0,1:T(8,128)(2,1)S(1)} %bitcast.117), channel_id=1, source_target_pairs={{0,1},{1,0},{2,3},{3,2},{4,5},{5,4},{6,7},{7,6},{8,9},{9,8},{10,11... | collective-permute-start | bytes 393224 | tf_op jit(solution)/shard_map/ppermute | solution.py:115
  56.9 1.3 %collective-permute-start.12 = (bf16[128,512]{0,1:T(8,128)(2,1)S(1)}, bf16[128,512]{0,1:T(8,128)(2,1)S(1)}, u32[]{:S(2)}, u32[]{:S(2)}) collective-permute-start(bf16[128,512]{0,1:T(8,128)(2,1)S(1)} %broadcast_select_fusion), channel_id=1, source_target_pairs={{0,2},{1,7},{2,4},{3,1},{4,6},{5,3},{6,0},{7,5},{8,10},{9,15},{10,... | collective-permute-start | bytes 393224 | tf_op jit(solution)/shard_map/ppermute | solution.py:117
  58.3 4.0 %collective-permute-start.13 = (bf16[2,128,512]{1,2,0:T(8,128)(2,1)S(1)}, bf16[2,128,512]{1,2,0:T(8,128)(2,1)S(1)}, u32[]{:S(2)}, u32[]{:S(2)}) collective-permute-start(bf16[2,128,512]{1,2,0:T(8,128)(2,1)S(1)} %pad_maximum_fusion), channel_id=1, source_target_pairs={{0,1},{1,0},{2,3},{3,2},{4,5},{5,4},{6,7},{7,6},{8,9},{9,8},{10,11... | collective-permute-start | bytes 786440 | tf_op jit(solution)/shard_map/ppermute | solution.py:118
  63.0 3.0 %collective-permute-start.14 = (bf16[128,512]{0,1:T(8,128)(2,1)S(1)}, bf16[128,512]{0,1:T(8,128)(2,1)S(1)}, u32[]{:S(2)}, u32[]{:S(2)}) collective-permute-start(bf16[128,512]{0,1:T(8,128)(2,1)S(1)} %collective-permute-done.12), channel_id=1, source_target_pairs={{0,1},{1,0},{2,3},{3,2},{4,5},{5,4},{6,7},{7,6},{8,9},{9,8},{10,11... | collective-permute-start | bytes 393224 | tf_op jit(solution)/shard_map/ppermute | solution.py:119
  67.4 1.0 %fusion.14 = bf16[128,1024]{1,0:T(8,128)(2,1)} fusion(f32[128,1024]{1,0:T(8,128)S(1)} %fusion.13, bf16[128,512]{0,1:T(8,128)(2,1)S(1)} %collective-permute-done.14, bf16[4096,1024]{1,0:T(8,128)(2,1)S(1)} %bitcast.109, s32[]{:T(128)S(6)} %select_n.134), kind=kOutput, calls=%fused_computation.18 | convolution fusion | flops 134479872 | bytes 1966084 | tf_op jit(solution)/shard_map/dot_general | solution.py:110
  (63 shorter events, 4.7 us)
Async XLA Ops:
  3.7 11.0 %collective-permute-start.1 = (bf16[128,256]{0,1:T(8,128)(2,1)S(1)}, bf16[128,256]{0,1:T(8,128)(2,1)S(1)}, u32[]{:S(2)}, u32[]{:S(2)}) collective-permute-start(bf16[128,256]{0,1:T(8,128)(2,1)S(1)} %get-tuple-element.12), channel_id=1, source_target_pairs={{0,64},{8,72},{16,80},{24,88},{32,96},{40,104},{48,112},{56,120},{... | collective-permute-start | bytes 196616 | tf_op jit(solution)/shard_map/ppermute | solution.py:60
  7.7 6.9 %collective-permute-start = (bf16[128,256]{0,1:T(8,128)(2,1)S(1)}, bf16[128,256]{0,1:T(8,128)(2,1)S(1)}, u32[]{:S(2)}, u32[]{:S(2)}) collective-permute-start(bf16[128,256]{0,1:T(8,128)(2,1)S(1)} %get-tuple-element.12), channel_id=1, source_target_pairs={{0,128},{8,136},{16,144},{24,152},{32,160},{40,168},{48,176},{56,1... | collective-permute-start | bytes 196616 | tf_op jit(solution)/shard_map/ppermute | solution.py:60
  14.7 8.7 %collective-permute-start.2 = (bf16[3,128,256]{1,2,0:T(8,128)(2,1)S(1)}, bf16[3,128,256]{1,2,0:T(8,128)(2,1)S(1)}, u32[]{:S(2)}, u32[]{:S(2)}) collective-permute-start(bf16[3,128,256]{1,2,0:T(8,128)(2,1)S(1)} %pad_maximum_fusion.1), channel_id=1, source_target_pairs={{0,56},{8,0},{16,8},{24,16},{32,24},{40,32},{48,40},{56,48},{64,12... | collective-permute-start | bytes 589832 | tf_op jit(solution)/shard_map/ppermute | solution.py:79
  20.4 6.4 %collective-permute-start.5 = (bf16[3,128,256]{1,2,0:T(8,128)(2,1)S(1)}, bf16[3,128,256]{1,2,0:T(8,128)(2,1)S(1)}, u32[]{:S(2)}, u32[]{:S(2)}) collective-permute-start(bf16[3,128,256]{1,2,0:T(8,128)(2,1)S(1)} %pad_maximum_fusion.1), channel_id=1, source_target_pairs={{0,8},{8,16},{16,24},{24,32},{32,40},{40,48},{48,56},{56,0},{64,72... | collective-permute-start | bytes 589832 | tf_op jit(solution)/shard_map/ppermute | solution.py:76
  23.4 9.2 %collective-permute-start.3 = (bf16[3,128,256]{1,2,0:T(8,128)(2,1)S(1)}, bf16[3,128,256]{1,2,0:T(8,128)(2,1)S(1)}, u32[]{:S(2)}, u32[]{:S(2)}) collective-permute-start(bf16[3,128,256]{1,2,0:T(8,128)(2,1)S(1)} %collective-permute-done.2), channel_id=1, source_target_pairs={{0,56},{8,0},{16,8},{24,16},{32,24},{40,32},{48,40},{56,48},{64,12... | collective-permute-start | bytes 589832 | tf_op jit(solution)/shard_map/ppermute | solution.py:79
  26.8 5.7 %collective-permute-start.6 = (bf16[3,128,256]{1,2,0:T(8,128)(2,1)S(1)}, bf16[3,128,256]{1,2,0:T(8,128)(2,1)S(1)}, u32[]{:S(2)}, u32[]{:S(2)}) collective-permute-start(bf16[3,128,256]{1,2,0:T(8,128)(2,1)S(1)} %collective-permute-done.5), channel_id=1, source_target_pairs={{0,8},{8,16},{16,24},{24,32},{32,40},{40,48},{48,56},{56,0},{64,72... | collective-permute-start | bytes 589832 | tf_op jit(solution)/shard_map/ppermute | solution.py:76
  32.5 5.7 %collective-permute-start.7 = (bf16[3,128,256]{1,2,0:T(8,128)(2,1)S(1)}, bf16[3,128,256]{1,2,0:T(8,128)(2,1)S(1)}, u32[]{:S(2)}, u32[]{:S(2)}) collective-permute-start(bf16[3,128,256]{1,2,0:T(8,128)(2,1)S(1)} %collective-permute-done.6), channel_id=1, source_target_pairs={{0,8},{8,16},{16,24},{24,32},{32,40},{40,48},{48,56},{56,0},{64,72... | collective-permute-start | bytes 589832 | tf_op jit(solution)/shard_map/ppermute | solution.py:76
  32.6 5.7 %collective-permute-start.4 = (bf16[3,128,256]{1,2,0:T(8,128)(2,1)S(1)}, bf16[3,128,256]{1,2,0:T(8,128)(2,1)S(1)}, u32[]{:S(2)}, u32[]{:S(2)}) collective-permute-start(bf16[3,128,256]{1,2,0:T(8,128)(2,1)S(1)} %collective-permute-done.3), channel_id=1, source_target_pairs={{0,56},{8,0},{16,8},{24,16},{32,24},{40,32},{48,40},{56,48},{64,12... | collective-permute-start | bytes 589832 | tf_op jit(solution)/shard_map/ppermute | solution.py:79
  38.3 6.1 %collective-permute-start.8 = (bf16[3,128,256]{1,2,0:T(8,128)(2,1)S(1)}, bf16[3,128,256]{1,2,0:T(8,128)(2,1)S(1)}, u32[]{:S(2)}, u32[]{:S(2)}) collective-permute-start(bf16[3,128,256]{1,2,0:T(8,128)(2,1)S(1)} %collective-permute-done.7), channel_id=1, source_target_pairs={{0,8},{8,16},{16,24},{24,32},{32,40},{40,48},{48,56},{56,0},{64,72... | collective-permute-start | bytes 589832 | tf_op jit(solution)/shard_map/ppermute | solution.py:76
  44.8 11.7 %slice-start = ((s8[8388608]{0:T(1024)(128)(4,1)}), s8[4194304]{0:T(1024)(128)(4,1)S(1)}, s32[]{:S(2)}) async-start(s8[8388608]{0:T(1024)(128)(4,1)} %bitcast.108), calls=%async_computation | async-start | bytes 8388608
  45.6 10.9 %slice-start.1 = ((s8[8388608]{0:T(1024)(128)(4,1)}), s8[4194304]{0:T(1024)(128)(4,1)S(1)}, s32[]{:S(2)}) async-start(s8[8388608]{0:T(1024)(128)(4,1)} %bitcast.108), calls=%async_computation.1 | async-start | bytes 8388608
  47.4 9.5 %collective-permute-start.9 = (bf16[128,512]{0,1:T(8,128)(2,1)S(1)}, bf16[128,512]{0,1:T(8,128)(2,1)S(1)}, u32[]{:S(2)}, u32[]{:S(2)}) collective-permute-start(bf16[128,512]{0,1:T(8,128)(2,1)S(1)} %bitcast.115), channel_id=1, source_target_pairs={{0,2},{1,3},{2,4},{3,5},{4,6},{5,7},{6,0},{7,1},{8,10},{9,11},{10,... | collective-permute-start | bytes 393224 | tf_op jit(solution)/shard_map/ppermute | solution.py:112
  48.6 8.2 %collective-permute-start.10 = (bf16[128,512]{0,1:T(8,128)(2,1)S(1)}, bf16[128,512]{0,1:T(8,128)(2,1)S(1)}, u32[]{:S(2)}, u32[]{:S(2)}) collective-permute-start(bf16[128,512]{0,1:T(8,128)(2,1)S(1)} %bitcast.116), channel_id=1, source_target_pairs={{0,6},{1,7},{2,0},{3,1},{4,2},{5,3},{6,4},{7,5},{8,14},{9,15},{10,... | collective-permute-start | bytes 393224 | tf_op jit(solution)/shard_map/ppermute | solution.py:113
  50.1 12.5 %collective-permute-start.11 = (bf16[128,512]{0,1:T(8,128)(2,1)S(1)}, bf16[128,512]{0,1:T(8,128)(2,1)S(1)}, u32[]{:S(2)}, u32[]{:S(2)}) collective-permute-start(bf16[128,512]{0,1:T(8,128)(2,1)S(1)} %bitcast.117), channel_id=1, source_target_pairs={{0,1},{1,0},{2,3},{3,2},{4,5},{5,4},{6,7},{7,6},{8,9},{9,8},{10,11... | collective-permute-start | bytes 393224 | tf_op jit(solution)/shard_map/ppermute | solution.py:115
  56.9 6.1 %collective-permute-start.12 = (bf16[128,512]{0,1:T(8,128)(2,1)S(1)}, bf16[128,512]{0,1:T(8,128)(2,1)S(1)}, u32[]{:S(2)}, u32[]{:S(2)}) collective-permute-start(bf16[128,512]{0,1:T(8,128)(2,1)S(1)} %broadcast_select_fusion), channel_id=1, source_target_pairs={{0,2},{1,7},{2,4},{3,1},{4,6},{5,3},{6,0},{7,5},{8,10},{9,15},{10,... | collective-permute-start | bytes 393224 | tf_op jit(solution)/shard_map/ppermute | solution.py:117
  58.3 8.1 %collective-permute-start.13 = (bf16[2,128,512]{1,2,0:T(8,128)(2,1)S(1)}, bf16[2,128,512]{1,2,0:T(8,128)(2,1)S(1)}, u32[]{:S(2)}, u32[]{:S(2)}) collective-permute-start(bf16[2,128,512]{1,2,0:T(8,128)(2,1)S(1)} %pad_maximum_fusion), channel_id=1, source_target_pairs={{0,1},{1,0},{2,3},{3,2},{4,5},{5,4},{6,7},{7,6},{8,9},{9,8},{10,11... | collective-permute-start | bytes 786440 | tf_op jit(solution)/shard_map/ppermute | solution.py:118
  63.0 4.4 %collective-permute-start.14 = (bf16[128,512]{0,1:T(8,128)(2,1)S(1)}, bf16[128,512]{0,1:T(8,128)(2,1)S(1)}, u32[]{:S(2)}, u32[]{:S(2)}) collective-permute-start(bf16[128,512]{0,1:T(8,128)(2,1)S(1)} %collective-permute-done.12), channel_id=1, source_target_pairs={{0,1},{1,0},{2,3},{3,2},{4,5},{5,4},{6,7},{7,6},{8,9},{9,8},{10,11... | collective-permute-start | bytes 393224 | tf_op jit(solution)/shard_map/ppermute | solution.py:119

commit v3 on v2

--- a/solution.py
+++ b/solution.py
@@ -51,8 +51,12 @@
         starts = doc_starts(lengths, positions)
         offsets = positions - starts
         q_rot = rotary(queries, offsets, HD).reshape(tok_rows, kv_local, query_group, HD)
-        k_rot = rotary(key_proj, offsets, HD)
-        own = jnp.concatenate([k_rot, value_proj], axis=1)
+        own = jnp.concatenate([key_proj, value_proj], axis=1)
+
+        def rotate_keys(block, k):
+            pos = (ctx - k) * tok_rows + jnp.arange(tok_rows, dtype=jnp.int32)
+            k_rot = rotary(block[:, :kv_width], pos - doc_starts(lengths, pos), HD)
+            return jnp.concatenate([k_rot, block[:, kv_width:]], axis=1)
 
         bundle = [own]
         for m in range(1, rows_back + 1):
@@ -78,7 +82,7 @@
             if step < row - row // 2:
                 backward = lax.ppermute(backward, "ctx", behind)
                 take(backward, row - step)
-        window = jnp.concatenate([blocks[span - k] for k in range(span + 1)], axis=0)
+        window = jnp.concatenate([rotate_keys(blocks[span - k], span - k) for k in range(span + 1)], axis=0)
         key_count = window.shape[0]
         key_block = window[:, :kv_width].reshape(key_count, kv_local, HD)
         value_block = window[:, kv_width:].reshape(key_count, kv_local, HD)

time: 69.2 us -> 72.1 us (1.042)
  other arithmetic: 3.5 us -> 5.91 us
    another operation x4 -> x9, other arithmetic: 0.46 us -> 2.82 us
    ppermute x4, starting transfers between devices: 0.01 us -> 2.15 us  [on_device(): forward = lax.ppermute(forward, 'ctx', ahead)]
    ppermute x3, starting transfers between devices: 11.8 us -> 10.2 us  [on_device(): backward = lax.ppermute(backward, 'ctx', behind)]
    unnamed x25 -> x11, local copies, waits for them, and re-layouts: 3.4 us -> 3.04 us
  transfers between devices with their start and end apart: 15 -> 15, of which waited for: 4 -> 4; matrix products, arithmetic and copies ran while one was open for 8% -> 10% of each run, Pallas kernels for 0% -> 0%
where the time goes in v3:
time: 72.1 us; the launch traced here: 71.8 us
  starting transfers between devices  38.4 us (53%)
  waiting for transfers between devices  17.4 us (24%)
  other arithmetic  5.91 us (8%)
  matrix products  5.15 us (7%)
  local copies, waits for them, and re-layouts  3.9 us (5%)
  between operations  1.11 us (2%)
    ppermute x4, waiting for transfers between devices, on_device(): forward = lax.ppermute(forward, 'ctx', ahead)  14.3 us
    ppermute x3, starting transfers between devices, on_device(): backward = lax.ppermute(backward, 'ctx', behind)  10.2 us
    ppermute x2, starting transfers between devices, on_device(): lax.ppermute(own, 'ctx', [(s, s + shift) for s in range(n_ctx - shift)])  8.55 us
    ppermute x1, starting transfers between devices, on_device(): partner = lax.ppermute(attended, 'head', swap)  6.38 us
    ppermute x1, starting transfers between devices, on_device(): near_other = lax.ppermute(jnp.stack([up, down]), 'head', swap)  4.03 us
    dot_general x8, matrix products, project(): return jnp.dot(piece, rows, preferred_element_type=jnp.float32)  3.4 us
    unnamed x11, local copies, waits for them, and re-layouts  3.04 us
    ppermute x1, starting transfers between devices, on_device(): far_other = lax.ppermute(far, 'head', swap)  3 us
  transfers between devices with their start and end apart: 15, of which 4 were waited for; matrix products, arithmetic and copies ran while one was open for 10% of the time, Pallas kernels for 0%

profile of v3, /device:TPU:1, one launch (start us, length us, event | category | flops | bytes accessed | tf_op | source)
XLA Modules:
  0.0 71.8 jit_solution(777956117470627584)
XLA Ops:
  0.0 0.9 %copy.22 = bf16[128,128]{0,1:T(8,128)(2,1)S(1)} copy(bf16[128,128]{1,0:T(8,128)(2,1)} %param.6) | data formatting | bytes 65536 | tf_op args[1]
  0.9 0.9 %copy.23 = bf16[128,128]{0,1:T(8,128)(2,1)S(1)} copy(bf16[128,128]{1,0:T(8,128)(2,1)} %param.7) | data formatting | bytes 65536 | tf_op args[2]
  1.8 4.0 %collective-permute-start.1 = (bf16[128,256]{0,1:T(8,128)(2,1)S(1)}, bf16[128,256]{0,1:T(8,128)(2,1)S(1)}, u32[]{:S(2)}, u32[]{:S(2)}) collective-permute-start(bf16[128,256]{0,1:T(8,128)(2,1)S(1)} %get-tuple-element.105), channel_id=1, source_target_pairs={{0,64},{8,72},{16,80},{24,88},{32,96},{40,104},{48,112},{56,120},{... | collective-permute-start | bytes 196616 | tf_op jit(solution)/shard_map/ppermute | solution.py:64
  5.8 4.5 %collective-permute-start = (bf16[128,256]{0,1:T(8,128)(2,1)S(1)}, bf16[128,256]{0,1:T(8,128)(2,1)S(1)}, u32[]{:S(2)}, u32[]{:S(2)}) collective-permute-start(bf16[128,256]{0,1:T(8,128)(2,1)S(1)} %get-tuple-element.105), channel_id=1, source_target_pairs={{0,128},{8,136},{16,144},{24,152},{32,160},{40,168},{48,176},{56,1... | collective-permute-start | bytes 196616 | tf_op jit(solution)/shard_map/ppermute | solution.py:64
  11.6 1.0 %copy.26 = bf16[128,512]{0,1:T(8,128)(2,1)S(1)} copy(bf16[128,512]{1,0:T(8,128)(2,1)} %param.5) | data formatting | bytes 262144 | tf_op args[0]
  13.1 1.0 %compare_and_fusion = pred[128,2176]{0,1:T(8,128)(4,1)S(1)} fusion(s32[128]{0:T(128)S(1)} %get-tuple-element.21, s32[128]{0:T(128)S(1)} %iota_add_fusion.17, s32[2176]{0:T(1024)S(1)} %iota_add_fusion), kind=kLoop, calls=%fused_computation.19 | loop fusion | flops 835584 | bytes 288256 | tf_op jit(solution)/shard_map/and | solution.py:94
  14.8 1.7 %collective-permute-start.5 = (bf16[3,128,256]{1,2,0:T(8,128)(2,1)S(1)}, bf16[3,128,256]{1,2,0:T(8,128)(2,1)S(1)}, u32[]{:S(2)}, u32[]{:S(2)}) collective-permute-start(bf16[3,128,256]{1,2,0:T(8,128)(2,1)S(1)} %pad_maximum_fusion.1), channel_id=1, source_target_pairs={{0,8},{8,16},{16,24},{24,32},{32,40},{40,48},{48,56},{56,0},{64,72... | collective-permute-start | bytes 589832 | tf_op jit(solution)/shard_map/ppermute | solution.py:80
  16.6 4.0 %collective-permute-start.2 = (bf16[3,128,256]{1,2,0:T(8,128)(2,1)S(1)}, bf16[3,128,256]{1,2,0:T(8,128)(2,1)S(1)}, u32[]{:S(2)}, u32[]{:S(2)}) collective-permute-start(bf16[3,128,256]{1,2,0:T(8,128)(2,1)S(1)} %pad_maximum_fusion.1), channel_id=1, source_target_pairs={{0,56},{8,0},{16,8},{24,16},{32,24},{40,32},{48,40},{56,48},{64,12... | collective-permute-start | bytes 589832 | tf_op jit(solution)/shard_map/ppermute | solution.py:83
  20.6 3.0 %collective-permute-done.2 = bf16[3,128,256]{1,2,0:T(8,128)(2,1)S(1)} collective-permute-done((bf16[3,128,256]{1,2,0:T(8,128)(2,1)S(1)}, bf16[3,128,256]{1,2,0:T(8,128)(2,1)S(1)}, u32[]{:S(2)}, u32[]{:S(2)}) %collective-permute-start.2) | collective-permute-done | bytes 196640 | tf_op jit(solution)/shard_map/ppermute | solution.py:83
  24.0 3.5 %collective-permute-start.3 = (bf16[3,128,256]{1,2,0:T(8,128)(2,1)S(1)}, bf16[3,128,256]{1,2,0:T(8,128)(2,1)S(1)}, u32[]{:S(2)}, u32[]{:S(2)}) collective-permute-start(bf16[3,128,256]{1,2,0:T(8,128)(2,1)S(1)} %collective-permute-done.2), channel_id=1, source_target_pairs={{0,56},{8,0},{16,8},{24,16},{32,24},{40,32},{48,40},{56,48},{64,12... | collective-permute-start | bytes 589832 | tf_op jit(solution)/shard_map/ppermute | solution.py:83
  27.7 5.7 %collective-permute-done.6 = bf16[3,128,256]{1,2,0:T(8,128)(2,1)S(1)} collective-permute-done((bf16[3,128,256]{1,2,0:T(8,128)(2,1)S(1)}, bf16[3,128,256]{1,2,0:T(8,128)(2,1)S(1)}, u32[]{:S(2)}, u32[]{:S(2)}) %collective-permute-start.6) | collective-permute-done | bytes 196640 | tf_op jit(solution)/shard_map/ppermute | solution.py:80
  34.5 2.7 %collective-permute-start.4 = (bf16[3,128,256]{1,2,0:T(8,128)(2,1)S(1)}, bf16[3,128,256]{1,2,0:T(8,128)(2,1)S(1)}, u32[]{:S(2)}, u32[]{:S(2)}) collective-permute-start(bf16[3,128,256]{1,2,0:T(8,128)(2,1)S(1)} %collective-permute-done.3), channel_id=1, source_target_pairs={{0,56},{8,0},{16,8},{24,16},{32,24},{40,32},{48,40},{56,48},{64,12... | collective-permute-start | bytes 589832 | tf_op jit(solution)/shard_map/ppermute | solution.py:83
  37.2 3.0 %collective-permute-done.7 = bf16[3,128,256]{1,2,0:T(8,128)(2,1)S(1)} collective-permute-done((bf16[3,128,256]{1,2,0:T(8,128)(2,1)S(1)}, bf16[3,128,256]{1,2,0:T(8,128)(2,1)S(1)}, u32[]{:S(2)}, u32[]{:S(2)}) %collective-permute-start.7) | collective-permute-done | bytes 196640 | tf_op jit(solution)/shard_map/ppermute | solution.py:80
  41.1 5.6 %collective-permute-done.8 = bf16[3,128,256]{1,2,0:T(8,128)(2,1)S(1)} collective-permute-done((bf16[3,128,256]{1,2,0:T(8,128)(2,1)S(1)}, bf16[3,128,256]{1,2,0:T(8,128)(2,1)S(1)}, u32[]{:S(2)}, u32[]{:S(2)}) %collective-permute-start.8) | collective-permute-done | bytes 196640 | tf_op jit(solution)/shard_map/ppermute | solution.py:80
  48.1 0.8 %fusion.202 = (f32[4,128]{1,0:T(4,128)S(1)}, f32[1,4,128,2176]{2,3,1,0:T(8,128)S(1)}) fusion(bf16[128,4,64]{2,0,1:T(8,128)(2,1)S(1)} %get-tuple-element.23, bf16[128,4,64]{2,0,1:T(8,128)(2,1)S(1)} %get-tuple-element.22, bf16[2176,256]{0,1:T(8,128)(2,1)S(1)} %fusion.37, pred[128,2176]{0,1:T(8,128)(4,1)S(1)} %compare_and_fusion), kind=kOutput, calls=%fused_computation.367 | convolution fusion | flops 288816640 | bytes 5556224 | tf_op jit(solution)/shard_map/tkgd,nkd->kgtn/dot_general | solution.py:90
  49.0 0.8 %fusion.2 = f32[4,128]{1,0:T(4,128)S(1)} fusion(f32[1,4,128,2176]{2,3,1,0:T(8,128)S(1)} %get-tuple-element.133, f32[4,128]{1,0:T(4,128)S(1)} %get-tuple-element.132, pred[128,2176]{0,1:T(8,128)(4,1)S(1)} %compare_and_fusion), kind=kLoop, calls=%fused_computation.4 | loop fusion | flops 3341824 | bytes 4739072 | tf_op jit(solution)/shard_map/reduce_sum | solution.py:98
  49.8 0.9 %fusion.18 = bf16[4,128,128]{1,2,0:T(8,128)(2,1)S(1)} fusion(f32[1,4,128,2176]{2,3,1,0:T(8,128)S(1)} %get-tuple-element.133, f32[4,128]{1,0:T(4,128)S(1)} %get-tuple-element.132, pred[128,2176]{0,1:T(8,128)(4,1)S(1)} %compare_and_fusion, bf16[2176,256]{0,1:T(8,128)(2,1)S(1)} %fusion.37, f32[4,128]{1,0:T(4,128)S(1)} %fusion.2), kind=kOutput, calls=%fused_computation.21 | convolution fusion | flops 288686080 | bytes 5427200 | tf_op jit(solution)/shard_map/kgtn,nkd->kgtd/dot_general | solution.py:99
  50.7 1.3 %collective-permute-start.9 = (bf16[128,512]{0,1:T(8,128)(2,1)S(1)}, bf16[128,512]{0,1:T(8,128)(2,1)S(1)}, u32[]{:S(2)}, u32[]{:S(2)}) collective-permute-start(bf16[128,512]{0,1:T(8,128)(2,1)S(1)} %bitcast.199), channel_id=1, source_target_pairs={{0,2},{1,3},{2,4},{3,5},{4,6},{5,7},{6,0},{7,1},{8,10},{9,11},{10,... | collective-permute-start | bytes 393224 | tf_op jit(solution)/shard_map/ppermute | solution.py:116
  52.0 1.5 %collective-permute-start.10 = (bf16[128,512]{0,1:T(8,128)(2,1)S(1)}, bf16[128,512]{0,1:T(8,128)(2,1)S(1)}, u32[]{:S(2)}, u32[]{:S(2)}) collective-permute-start(bf16[128,512]{0,1:T(8,128)(2,1)S(1)} %bitcast.200), channel_id=1, source_target_pairs={{0,6},{1,7},{2,0},{3,1},{4,2},{5,3},{6,4},{7,5},{8,14},{9,15},{10,... | collective-permute-start | bytes 393224 | tf_op jit(solution)/shard_map/ppermute | solution.py:117
  53.5 6.4 %collective-permute-start.11 = (bf16[128,512]{0,1:T(8,128)(2,1)S(1)}, bf16[128,512]{0,1:T(8,128)(2,1)S(1)}, u32[]{:S(2)}, u32[]{:S(2)}) collective-permute-start(bf16[128,512]{0,1:T(8,128)(2,1)S(1)} %bitcast.201), channel_id=1, source_target_pairs={{0,1},{1,0},{2,3},{3,2},{4,5},{5,4},{6,7},{7,6},{8,9},{9,8},{10,11... | collective-permute-start | bytes 393224 | tf_op jit(solution)/shard_map/ppermute | solution.py:119
  60.2 1.3 %collective-permute-start.12 = (bf16[128,512]{0,1:T(8,128)(2,1)S(1)}, bf16[128,512]{0,1:T(8,128)(2,1)S(1)}, u32[]{:S(2)}, u32[]{:S(2)}) collective-permute-start(bf16[128,512]{0,1:T(8,128)(2,1)S(1)} %broadcast_select_fusion), channel_id=1, source_target_pairs={{0,2},{1,7},{2,4},{3,1},{4,6},{5,3},{6,0},{7,5},{8,10},{9,15},{10,... | collective-permute-start | bytes 393224 | tf_op jit(solution)/shard_map/ppermute | solution.py:121
  61.6 4.0 %collective-permute-start.13 = (bf16[2,128,512]{1,2,0:T(8,128)(2,1)S(1)}, bf16[2,128,512]{1,2,0:T(8,128)(2,1)S(1)}, u32[]{:S(2)}, u32[]{:S(2)}) collective-permute-start(bf16[2,128,512]{1,2,0:T(8,128)(2,1)S(1)} %pad_maximum_fusion), channel_id=1, source_target_pairs={{0,1},{1,0},{2,3},{3,2},{4,5},{5,4},{6,7},{7,6},{8,9},{9,8},{10,11... | collective-permute-start | bytes 786440 | tf_op jit(solution)/shard_map/ppermute | solution.py:122
  66.4 3.0 %collective-permute-start.14 = (bf16[128,512]{0,1:T(8,128)(2,1)S(1)}, bf16[128,512]{0,1:T(8,128)(2,1)S(1)}, u32[]{:S(2)}, u32[]{:S(2)}) collective-permute-start(bf16[128,512]{0,1:T(8,128)(2,1)S(1)} %collective-permute-done.12), channel_id=1, source_target_pairs={{0,1},{1,0},{2,3},{3,2},{4,5},{5,4},{6,7},{7,6},{8,9},{9,8},{10,11... | collective-permute-start | bytes 393224 | tf_op jit(solution)/shard_map/ppermute | solution.py:123
  70.8 1.0 %fusion.14 = bf16[128,1024]{1,0:T(8,128)(2,1)} fusion(f32[128,1024]{1,0:T(8,128)S(1)} %fusion.13, bf16[128,512]{0,1:T(8,128)(2,1)S(1)} %collective-permute-done.14, bf16[4096,1024]{1,0:T(8,128)(2,1)S(1)} %bitcast.193, s32[]{:T(128)S(6)} %select_n.199), kind=kOutput, calls=%fused_computation.18 | convolution fusion | flops 134479872 | bytes 1966084 | tf_op jit(solution)/shard_map/dot_general | solution.py:114
  (126 shorter events, 8.0 us)
Async XLA Ops:
  0.0 12.9 %copy-start = (s32[32]{0:T(128)S(1)}, s32[32]{0:T(128)}, u32[]{:S(2)}) copy-start(s32[32]{0:T(128)} %param.8) | copy-start | bytes 388
  1.8 13.0 %collective-permute-start.1 = (bf16[128,256]{0,1:T(8,128)(2,1)S(1)}, bf16[128,256]{0,1:T(8,128)(2,1)S(1)}, u32[]{:S(2)}, u32[]{:S(2)}) collective-permute-start(bf16[128,256]{0,1:T(8,128)(2,1)S(1)} %get-tuple-element.105), channel_id=1, source_target_pairs={{0,64},{8,72},{16,80},{24,88},{32,96},{40,104},{48,112},{56,120},{... | collective-permute-start | bytes 196616 | tf_op jit(solution)/shard_map/ppermute | solution.py:64
  5.8 9.0 %collective-permute-start = (bf16[128,256]{0,1:T(8,128)(2,1)S(1)}, bf16[128,256]{0,1:T(8,128)(2,1)S(1)}, u32[]{:S(2)}, u32[]{:S(2)}) collective-permute-start(bf16[128,256]{0,1:T(8,128)(2,1)S(1)} %get-tuple-element.105), channel_id=1, source_target_pairs={{0,128},{8,136},{16,144},{24,152},{32,160},{40,168},{48,176},{56,1... | collective-permute-start | bytes 196616 | tf_op jit(solution)/shard_map/ppermute | solution.py:64
  14.8 12.7 %collective-permute-start.5 = (bf16[3,128,256]{1,2,0:T(8,128)(2,1)S(1)}, bf16[3,128,256]{1,2,0:T(8,128)(2,1)S(1)}, u32[]{:S(2)}, u32[]{:S(2)}) collective-permute-start(bf16[3,128,256]{1,2,0:T(8,128)(2,1)S(1)} %pad_maximum_fusion.1), channel_id=1, source_target_pairs={{0,8},{8,16},{16,24},{24,32},{32,40},{40,48},{48,56},{56,0},{64,72... | collective-permute-start | bytes 589832 | tf_op jit(solution)/shard_map/ppermute | solution.py:80
  16.6 7.0 %collective-permute-start.2 = (bf16[3,128,256]{1,2,0:T(8,128)(2,1)S(1)}, bf16[3,128,256]{1,2,0:T(8,128)(2,1)S(1)}, u32[]{:S(2)}, u32[]{:S(2)}) collective-permute-start(bf16[3,128,256]{1,2,0:T(8,128)(2,1)S(1)} %pad_maximum_fusion.1), channel_id=1, source_target_pairs={{0,56},{8,0},{16,8},{24,16},{32,24},{40,32},{48,40},{56,48},{64,12... | collective-permute-start | bytes 589832 | tf_op jit(solution)/shard_map/ppermute | solution.py:83
  24.0 9.4 %collective-permute-start.3 = (bf16[3,128,256]{1,2,0:T(8,128)(2,1)S(1)}, bf16[3,128,256]{1,2,0:T(8,128)(2,1)S(1)}, u32[]{:S(2)}, u32[]{:S(2)}) collective-permute-start(bf16[3,128,256]{1,2,0:T(8,128)(2,1)S(1)} %collective-permute-done.2), channel_id=1, source_target_pairs={{0,56},{8,0},{16,8},{24,16},{32,24},{40,32},{48,40},{56,48},{64,12... | collective-permute-start | bytes 589832 | tf_op jit(solution)/shard_map/ppermute | solution.py:83
  27.5 5.8 %collective-permute-start.6 = (bf16[3,128,256]{1,2,0:T(8,128)(2,1)S(1)}, bf16[3,128,256]{1,2,0:T(8,128)(2,1)S(1)}, u32[]{:S(2)}, u32[]{:S(2)}) collective-permute-start(bf16[3,128,256]{1,2,0:T(8,128)(2,1)S(1)} %collective-permute-done.5), channel_id=1, source_target_pairs={{0,8},{8,16},{16,24},{24,32},{32,40},{40,48},{48,56},{56,0},{64,72... | collective-permute-start | bytes 589832 | tf_op jit(solution)/shard_map/ppermute | solution.py:80
  34.4 5.8 %collective-permute-start.7 = (bf16[3,128,256]{1,2,0:T(8,128)(2,1)S(1)}, bf16[3,128,256]{1,2,0:T(8,128)(2,1)S(1)}, u32[]{:S(2)}, u32[]{:S(2)}) collective-permute-start(bf16[3,128,256]{1,2,0:T(8,128)(2,1)S(1)} %collective-permute-done.6), channel_id=1, source_target_pairs={{0,8},{8,16},{16,24},{24,32},{32,40},{40,48},{48,56},{56,0},{64,72... | collective-permute-start | bytes 589832 | tf_op jit(solution)/shard_map/ppermute | solution.py:80
  34.5 6.5 %collective-permute-start.4 = (bf16[3,128,256]{1,2,0:T(8,128)(2,1)S(1)}, bf16[3,128,256]{1,2,0:T(8,128)(2,1)S(1)}, u32[]{:S(2)}, u32[]{:S(2)}) collective-permute-start(bf16[3,128,256]{1,2,0:T(8,128)(2,1)S(1)} %collective-permute-done.3), channel_id=1, source_target_pairs={{0,56},{8,0},{16,8},{24,16},{32,24},{40,32},{48,40},{56,48},{64,12... | collective-permute-start | bytes 589832 | tf_op jit(solution)/shard_map/ppermute | solution.py:83
  40.7 6.0 %collective-permute-start.8 = (bf16[3,128,256]{1,2,0:T(8,128)(2,1)S(1)}, bf16[3,128,256]{1,2,0:T(8,128)(2,1)S(1)}, u32[]{:S(2)}, u32[]{:S(2)}) collective-permute-start(bf16[3,128,256]{1,2,0:T(8,128)(2,1)S(1)} %collective-permute-done.7), channel_id=1, source_target_pairs={{0,8},{8,16},{16,24},{24,32},{32,40},{40,48},{48,56},{56,0},{64,72... | collective-permute-start | bytes 589832 | tf_op jit(solution)/shard_map/ppermute | solution.py:80
  48.1 11.7 %slice-start = ((s8[8388608]{0:T(1024)(128)(4,1)}), s8[4194304]{0:T(1024)(128)(4,1)S(1)}, s32[]{:S(2)}) async-start(s8[8388608]{0:T(1024)(128)(4,1)} %bitcast.192), calls=%async_computation | async-start | bytes 8388608
  49.0 10.9 %slice-start.1 = ((s8[8388608]{0:T(1024)(128)(4,1)}), s8[4194304]{0:T(1024)(128)(4,1)S(1)}, s32[]{:S(2)}) async-start(s8[8388608]{0:T(1024)(128)(4,1)} %bitcast.192), calls=%async_computation.1 | async-start | bytes 8388608
  50.7 9.5 %collective-permute-start.9 = (bf16[128,512]{0,1:T(8,128)(2,1)S(1)}, bf16[128,512]{0,1:T(8,128)(2,1)S(1)}, u32[]{:S(2)}, u32[]{:S(2)}) collective-permute-start(bf16[128,512]{0,1:T(8,128)(2,1)S(1)} %bitcast.199), channel_id=1, source_target_pairs={{0,2},{1,3},{2,4},{3,5},{4,6},{5,7},{6,0},{7,1},{8,10},{9,11},{10,... | collective-permute-start | bytes 393224 | tf_op jit(solution)/shard_map/ppermute | solution.py:116
  52.0 8.2 %collective-permute-start.10 = (bf16[128,512]{0,1:T(8,128)(2,1)S(1)}, bf16[128,512]{0,1:T(8,128)(2,1)S(1)}, u32[]{:S(2)}, u32[]{:S(2)}) collective-permute-start(bf16[128,512]{0,1:T(8,128)(2,1)S(1)} %bitcast.200), channel_id=1, source_target_pairs={{0,6},{1,7},{2,0},{3,1},{4,2},{5,3},{6,4},{7,5},{8,14},{9,15},{10,... | collective-permute-start | bytes 393224 | tf_op jit(solution)/shard_map/ppermute | solution.py:117
  53.5 12.5 %collective-permute-start.11 = (bf16[128,512]{0,1:T(8,128)(2,1)S(1)}, bf16[128,512]{0,1:T(8,128)(2,1)S(1)}, u32[]{:S(2)}, u32[]{:S(2)}) collective-permute-start(bf16[128,512]{0,1:T(8,128)(2,1)S(1)} %bitcast.201), channel_id=1, source_target_pairs={{0,1},{1,0},{2,3},{3,2},{4,5},{5,4},{6,7},{7,6},{8,9},{9,8},{10,11... | collective-permute-start | bytes 393224 | tf_op jit(solution)/shard_map/ppermute | solution.py:119
  60.2 6.1 %collective-permute-start.12 = (bf16[128,512]{0,1:T(8,128)(2,1)S(1)}, bf16[128,512]{0,1:T(8,128)(2,1)S(1)}, u32[]{:S(2)}, u32[]{:S(2)}) collective-permute-start(bf16[128,512]{0,1:T(8,128)(2,1)S(1)} %broadcast_select_fusion), channel_id=1, source_target_pairs={{0,2},{1,7},{2,4},{3,1},{4,6},{5,3},{6,0},{7,5},{8,10},{9,15},{10,... | collective-permute-start | bytes 393224 | tf_op jit(solution)/shard_map/ppermute | solution.py:121
  61.6 8.1 %collective-permute-start.13 = (bf16[2,128,512]{1,2,0:T(8,128)(2,1)S(1)}, bf16[2,128,512]{1,2,0:T(8,128)(2,1)S(1)}, u32[]{:S(2)}, u32[]{:S(2)}) collective-permute-start(bf16[2,128,512]{1,2,0:T(8,128)(2,1)S(1)} %pad_maximum_fusion), channel_id=1, source_target_pairs={{0,1},{1,0},{2,3},{3,2},{4,5},{5,4},{6,7},{7,6},{8,9},{9,8},{10,11... | collective-permute-start | bytes 786440 | tf_op jit(solution)/shard_map/ppermute | solution.py:122
  66.4 4.4 %collective-permute-start.14 = (bf16[128,512]{0,1:T(8,128)(2,1)S(1)}, bf16[128,512]{0,1:T(8,128)(2,1)S(1)}, u32[]{:S(2)}, u32[]{:S(2)}) collective-permute-start(bf16[128,512]{0,1:T(8,128)(2,1)S(1)} %collective-permute-done.12), channel_id=1, source_target_pairs={{0,1},{1,0},{2,3},{3,2},{4,5},{5,4},{6,7},{7,6},{8,9},{9,8},{10,11... | collective-permute-start | bytes 393224 | tf_op jit(solution)/shard_map/ppermute | solution.py:123

commit v4 on v2

--- a/solution.py
+++ b/solution.py
@@ -62,22 +62,19 @@
         bundle = jnp.stack(bundle)
         z = ctx % row
         n_rows = n_ctx // row
-        ahead = [(r * row + s, r * row + (s + 1) % row) for r in range(n_rows) for s in range(row)]
-        behind = [(r * row + s, r * row + (s - 1) % row) for r in range(n_rows) for s in range(row)]
-
-        def take(packet, b):
-            lo = jnp.where(z < b, 1, 0)
-            got = lax.dynamic_slice_in_dim(packet, lo, rows_back, 0)
-            for m in range(rows_back):
-                blocks[b + row * m] = got[m]
-
-        forward, backward = bundle, bundle
-        for step in range(1, row // 2 + 1):
-            forward = lax.ppermute(forward, "ctx", ahead)
-            take(forward, step)
-            if step < row - row // 2:
-                backward = lax.ppermute(backward, "ctx", behind)
-                take(backward, row - step)
+        for chain in relay_plan(row, rows_back):
+            packet = bundle
+            for step in chain:
+                lo = jnp.asarray(step["send"], jnp.int32)[z]
+                packet = lax.ppermute(
+                    lax.dynamic_slice_in_dim(packet, lo, step["width"], 0),
+                    "ctx",
+                    [(r * row + s, r * row + (s + step["dir"]) % row) for r in range(n_rows) for s in range(row)],
+                )
+                at = jnp.asarray(step["take"], jnp.int32)[z]
+                got = lax.dynamic_slice_in_dim(packet, at, len(step["blocks"]), 0)
+                for i, blk in enumerate(step["blocks"]):
+                    blocks[blk] = got[i]
         window = jnp.concatenate([blocks[span - k] for k in range(span + 1)], axis=0)
         key_count = window.shape[0]
         key_block = window[:, :kv_width].reshape(key_count, kv_local, HD)
@@ -131,6 +128,54 @@
     return on_device
 
 
+def relay_plan(row, rows_back):
+    half = row // 2
+    split = row % 2 == 0
+
+    def part(z, b, direction):
+        lo = 1 if z < b else 0
+        slots = list(range(lo, lo + rows_back))
+        if split and b == half:
+            cut = (rows_back + 1) // 2
+            slots = slots[:cut] if direction == 1 else slots[cut:]
+        return slots
+
+    chains = []
+    for direction in (1, -1):
+        rounds = range(1, half + 1) if direction == 1 else range(1, (half if split else row - 1 - half) + 1)
+        bs = [r if direction == 1 else row - r for r in rounds]
+        steps, held = [], None
+        for i, b in enumerate(bs):
+            need = {}
+            for n in range(row):
+                source = (n - direction * i) % row
+                slots = set()
+                for later in bs[i:]:
+                    receiver = (source + later) % row
+                    slots.update(part(receiver, later, direction))
+                need[n] = slots
+            width = max(max(v) - min(v) + 1 for v in need.values())
+            lo = {n: min(min(v), rows_back + 1 - width) for n, v in need.items()}
+            send = []
+            for z in range(row):
+                offset = lo[z] - (0 if held is None else held[(z - direction) % row])
+                assert 0 <= offset and offset + width <= (rows_back + 1 if held is None else steps[-1]["width"])
+                send.append(offset)
+            take, blocks = [], None
+            for z in range(row):
+                sender = (z - direction) % row
+                slots = part(z, b, direction)
+                take.append(slots[0] - lo[sender])
+                lo_z = 1 if z < b else 0
+                mine = [b + row * (m - lo_z) for m in slots]
+                assert blocks is None or blocks == mine
+                blocks = mine
+            steps.append({"dir": direction, "width": width, "send": send, "take": take, "blocks": blocks})
+            held = lo
+        chains.append(steps)
+    return chains
+
+
 def solution(mesh):
     n_ctx, n_head = mesh.shape["ctx"], mesh.shape["head"]
     row = 8 if n_ctx % 8 == 0 else n_ctx

time: 69.2 us -> 83.5 us (1.21)
  between operations: 0.58 us -> 16 us
  waiting for transfers between devices: 17.2 us -> 8.5 us
  local copies, waits for them, and re-layouts: 4.16 us -> 9.22 us
  starting transfers between devices: 37.9 us -> 40.6 us
    ppermute x7 -> x8, waiting for transfers between devices: 17.2 us -> 8.48 us  [on_device(): lax.ppermute(lax.dynamic_slice_in_dim(packet, lo, step['width'], 0), 'ctx...]
    dynamic_slice x0 -> x12, local copies, waits for them, and re-layouts: none -> 5.02 us  [the longest x4 2.53 us: on_device(): lo = jnp.asarray(step['send'], jnp.int32)[z]]
    ppermute x7 -> x8, starting transfers between devices: 11.8 us -> 14.9 us  [on_device(): lax.ppermute(lax.dynamic_slice_in_dim(packet, lo, step['width'], 0), 'ctx...]
    unnamed x25 -> x41, local copies, waits for them, and re-layouts: 3.4 us -> 3.44 us
  transfers between devices with their start and end apart: 15 -> 16, of which waited for: 4 -> 5; matrix products, arithmetic and copies ran while one was open for 8% -> 13% of each run, Pallas kernels for 0% -> 0%
where the time goes in v4:
time: 83.5 us; the launch traced here: 83 us
  starting transfers between devices  40.6 us (49%)
  between operations  16 us (19%)
  local copies, waits for them, and re-layouts  9.22 us (11%)
  waiting for transfers between devices  8.5 us (10%)
  matrix products  5.15 us (6%)
  other arithmetic  3.5 us (4%)
    ppermute x8, starting transfers between devices, on_device(): lax.ppermute(lax.dynamic_slice_in_dim(packet, lo, step['width'], 0), 'ctx...  14.9 us
    ppermute x2, starting transfers between devices, on_device(): lax.ppermute(own, 'ctx', [(s, s + shift) for s in range(n_ctx - shift)])  8.55 us
    ppermute x8, waiting for transfers between devices, on_device(): lax.ppermute(lax.dynamic_slice_in_dim(packet, lo, step['width'], 0), 'ctx...  8.48 us
    ppermute x1, starting transfers between devices, on_device(): partner = lax.ppermute(attended, 'head', swap)  6.01 us
    ppermute x1, starting transfers between devices, on_device(): near_other = lax.ppermute(jnp.stack([up, down]), 'head', swap)  4.02 us
    unnamed x41, local copies, waits for them, and re-layouts  3.44 us
    dot_general x8, matrix products, project(): return jnp.dot(piece, rows, preferred_element_type=jnp.float32)  3.4 us
    ppermute x1, starting transfers between devices, on_device(): far_other = lax.ppermute(far, 'head', swap)  3.01 us
  transfers between devices with their start and end apart: 16, of which 5 were waited for; matrix products, arithmetic and copies ran while one was open for 13% of the time, Pallas kernels for 0%

profile of v4, /device:TPU:1, one launch (start us, length us, event | category | flops | bytes accessed | tf_op | source)
XLA Modules:
  0.0 83.0 jit_solution(11474815772154813282)
XLA Ops:
  1.7 0.9 %copy.30 = bf16[128,128]{0,1:T(8,128)(2,1)S(1)} copy(bf16[128,128]{1,0:T(8,128)(2,1)} %param.14) | data formatting | bytes 65536 | tf_op args[1]
  2.6 0.9 %copy.31 = bf16[128,128]{0,1:T(8,128)(2,1)S(1)} copy(bf16[128,128]{1,0:T(8,128)(2,1)} %param.15) | data formatting | bytes 65536 | tf_op args[2]
  3.7 4.0 %collective-permute-start.1 = (bf16[128,256]{0,1:T(8,128)(2,1)S(1)}, bf16[128,256]{0,1:T(8,128)(2,1)S(1)}, u32[]{:S(2)}, u32[]{:S(2)}) collective-permute-start(bf16[128,256]{0,1:T(8,128)(2,1)S(1)} %get-tuple-element.12), channel_id=1, source_target_pairs={{0,64},{8,72},{16,80},{24,88},{32,96},{40,104},{48,112},{56,120},{... | collective-permute-start | bytes 196616 | tf_op jit(solution)/shard_map/ppermute | solution.py:60
  7.7 4.5 %collective-permute-start = (bf16[128,256]{0,1:T(8,128)(2,1)S(1)}, bf16[128,256]{0,1:T(8,128)(2,1)S(1)}, u32[]{:S(2)}, u32[]{:S(2)}) collective-permute-start(bf16[128,256]{0,1:T(8,128)(2,1)S(1)} %get-tuple-element.12), channel_id=1, source_target_pairs={{0,128},{8,136},{16,144},{24,152},{32,160},{40,168},{48,176},{56,1... | collective-permute-start | bytes 196616 | tf_op jit(solution)/shard_map/ppermute | solution.py:60
  12.3 1.0 %copy.32 = bf16[128,512]{0,1:T(8,128)(2,1)S(1)} copy(bf16[128,512]{1,0:T(8,128)(2,1)} %param.13) | data formatting | bytes 262144 | tf_op args[0]
  13.3 1.0 %compare_and_fusion = pred[128,2176]{0,1:T(8,128)(4,1)S(1)} fusion(s32[128]{0:T(128)S(1)} %select_reduce_fusion, s32[128]{0:T(128)S(1)} %iota_add_fusion.1, s32[2176]{0:T(1024)S(1)} %iota_add_fusion), kind=kLoop, calls=%fused_computation.19 | loop fusion | flops 835584 | bytes 288256 | tf_op jit(solution)/shard_map/and | solution.py:87
  15.1 5.7 %collective-permute-start.2 = (bf16[3,128,256]{1,2,0:T(8,128)(2,1)S(1)}, bf16[3,128,256]{1,2,0:T(8,128)(2,1)S(1)}, u32[]{:S(2)}, u32[]{:S(2)}) collective-permute-start(bf16[3,128,256]{1,2,0:T(8,128)(2,1)S(1)} %pad_maximum_fusion.1), channel_id=1, source_target_pairs={{0,56},{8,0},{16,8},{24,16},{32,24},{40,32},{48,40},{56,48},{64,12... | collective-permute-start | bytes 589832 | tf_op jit(solution)/shard_map/ppermute | solution.py:69
  41.4 2.7 %collective-permute-start.3 = (bf16[3,128,256]{1,2,0:T(8,128)(2,1)S(1)}, bf16[3,128,256]{1,2,0:T(8,128)(2,1)S(1)}, u32[]{:S(2)}, u32[]{:S(2)}) collective-permute-start(bf16[3,128,256]{1,2,0:T(8,128)(2,1)S(1)} %collective-permute-done.2), channel_id=1, source_target_pairs={{0,56},{8,0},{16,8},{24,16},{32,24},{40,32},{48,40},{56,48},{64,12... | collective-permute-start | bytes 589832 | tf_op jit(solution)/shard_map/ppermute | solution.py:69
  44.3 2.5 %collective-permute-done.3 = bf16[3,128,256]{1,2,0:T(8,128)(2,1)S(1)} collective-permute-done((bf16[3,128,256]{1,2,0:T(8,128)(2,1)S(1)}, bf16[3,128,256]{1,2,0:T(8,128)(2,1)S(1)}, u32[]{:S(2)}, u32[]{:S(2)}) %collective-permute-start.3) | collective-permute-done | bytes 196640 | tf_op jit(solution)/shard_map/ppermute | solution.py:69
  46.8 3.2 %collective-permute-start.4 = (bf16[2,128,256]{1,2,0:T(8,128)(2,1)S(1)}, bf16[2,128,256]{1,2,0:T(8,128)(2,1)S(1)}, u32[]{:S(2)}, u32[]{:S(2)}) collective-permute-start(bf16[2,128,256]{1,2,0:T(8,128)(2,1)S(1)} %constant_dynamic-slice_fusion.3), channel_id=1, source_target_pairs={{0,56},{8,0},{16,8},{24,16},{32,24},{40,32},{48,40},{56,48},{64,12... | collective-permute-start | bytes 393224 | tf_op jit(solution)/shard_map/ppermute | solution.py:69
  50.1 1.8 %collective-permute-done.4 = bf16[2,128,256]{1,2,0:T(8,128)(2,1)S(1)} collective-permute-done((bf16[2,128,256]{1,2,0:T(8,128)(2,1)S(1)}, bf16[2,128,256]{1,2,0:T(8,128)(2,1)S(1)}, u32[]{:S(2)}, u32[]{:S(2)}) %collective-permute-start.4) | collective-permute-done | bytes 131104 | tf_op jit(solution)/shard_map/ppermute | solution.py:69
  51.9 3.1 %collective-permute-start.5 = (bf16[1,128,256]{1,2,0:T(8,128)(2,1)S(1)}, bf16[1,128,256]{1,2,0:T(8,128)(2,1)S(1)}, u32[]{:S(2)}, u32[]{:S(2)}) collective-permute-start(bf16[1,128,256]{1,2,0:T(8,128)(2,1)S(1)} %constant_dynamic-slice_fusion.2), channel_id=1, source_target_pairs={{0,56},{8,0},{16,8},{24,16},{32,24},{40,32},{48,40},{56,48},{64,12... | collective-permute-start | bytes 196616 | tf_op jit(solution)/shard_map/ppermute | solution.py:69
  55.1 1.2 %collective-permute-done.5 = bf16[1,128,256]{1,2,0:T(8,128)(2,1)S(1)} collective-permute-done((bf16[1,128,256]{1,2,0:T(8,128)(2,1)S(1)}, bf16[1,128,256]{1,2,0:T(8,128)(2,1)S(1)}, u32[]{:S(2)}, u32[]{:S(2)}) %collective-permute-start.5) | collective-permute-done | bytes 65568 | tf_op jit(solution)/shard_map/ppermute | solution.py:69
  56.6 2.9 %collective-permute-done.9 = bf16[1,128,256]{1,2,0:T(8,128)(2,1)S(1)} collective-permute-done((bf16[1,128,256]{1,2,0:T(8,128)(2,1)S(1)}, bf16[1,128,256]{1,2,0:T(8,128)(2,1)S(1)}, u32[]{:S(2)}, u32[]{:S(2)}) %collective-permute-start.9) | collective-permute-done | bytes 65568 | tf_op jit(solution)/shard_map/ppermute | solution.py:69
  59.6 0.8 %fusion.69 = (f32[4,128]{1,0:T(4,128)S(1)}, f32[1,4,128,2176]{2,3,1,0:T(8,128)S(1)}) fusion(bf16[128,4,64]{2,0,1:T(8,128)(2,1)S(1)} %get-tuple-element.6, bf16[128,4,64]{2,0,1:T(8,128)(2,1)S(1)} %get-tuple-element.5, bf16[2176,256]{0,1:T(8,128)(2,1)S(1)} %constant_dynamic-update-slice_fusion, pred[128,2176]{0,1:T(8,128)(4,1)S(1)} %compare_and_fusion), kind=kOutput, calls=%fused_computation.112 | convolution fusion | flops 288816640 | bytes 5556224 | tf_op jit(solution)/shard_map/tkgd,nkd->kgtn/dot_general | solution.py:83
  60.5 0.8 fusion.2
  61.3 0.9 %fusion.18 = bf16[4,128,128]{1,2,0:T(8,128)(2,1)S(1)} fusion(f32[1,4,128,2176]{2,3,1,0:T(8,128)S(1)} %get-tuple-element.16, f32[4,128]{1,0:T(4,128)S(1)} %get-tuple-element.15, pred[128,2176]{0,1:T(8,128)(4,1)S(1)} %compare_and_fusion, bf16[2176,256]{0,1:T(8,128)(2,1)S(1)} %constant_dynamic-update-slice_fusion, f32[4,128]{1,0:T(4,128)S(1)} %fusion.2), kind=kOutput, calls=%fused_computation.21 | convolution fusion | flops 288686080 | bytes 5427200 | tf_op jit(solution)/shard_map/kgtn,nkd->kgtd/dot_general | solution.py:92
  62.2 1.3 %collective-permute-start.10 = (bf16[128,512]{0,1:T(8,128)(2,1)S(1)}, bf16[128,512]{0,1:T(8,128)(2,1)S(1)}, u32[]{:S(2)}, u32[]{:S(2)}) collective-permute-start(bf16[128,512]{0,1:T(8,128)(2,1)S(1)} %bitcast.119), channel_id=1, source_target_pairs={{0,2},{1,3},{2,4},{3,5},{4,6},{5,7},{6,0},{7,1},{8,10},{9,11},{10,... | collective-permute-start | bytes 393224 | tf_op jit(solution)/shard_map/ppermute | solution.py:109
  63.5 1.5 %collective-permute-start.11 = (bf16[128,512]{0,1:T(8,128)(2,1)S(1)}, bf16[128,512]{0,1:T(8,128)(2,1)S(1)}, u32[]{:S(2)}, u32[]{:S(2)}) collective-permute-start(bf16[128,512]{0,1:T(8,128)(2,1)S(1)} %bitcast.120), channel_id=1, source_target_pairs={{0,6},{1,7},{2,0},{3,1},{4,2},{5,3},{6,4},{7,5},{8,14},{9,15},{10,... | collective-permute-start | bytes 393224 | tf_op jit(solution)/shard_map/ppermute | solution.py:110
  65.1 6.0 %collective-permute-start.12 = (bf16[128,512]{0,1:T(8,128)(2,1)S(1)}, bf16[128,512]{0,1:T(8,128)(2,1)S(1)}, u32[]{:S(2)}, u32[]{:S(2)}) collective-permute-start(bf16[128,512]{0,1:T(8,128)(2,1)S(1)} %bitcast.121), channel_id=1, source_target_pairs={{0,1},{1,0},{2,3},{3,2},{4,5},{5,4},{6,7},{7,6},{8,9},{9,8},{10,11... | collective-permute-start | bytes 393224 | tf_op jit(solution)/shard_map/ppermute | solution.py:112
  71.4 1.3 %collective-permute-start.13 = (bf16[128,512]{0,1:T(8,128)(2,1)S(1)}, bf16[128,512]{0,1:T(8,128)(2,1)S(1)}, u32[]{:S(2)}, u32[]{:S(2)}) collective-permute-start(bf16[128,512]{0,1:T(8,128)(2,1)S(1)} %broadcast_select_fusion), channel_id=1, source_target_pairs={{0,2},{1,7},{2,4},{3,1},{4,6},{5,3},{6,0},{7,5},{8,10},{9,15},{10,... | collective-permute-start | bytes 393224 | tf_op jit(solution)/shard_map/ppermute | solution.py:114
  72.8 4.0 %collective-permute-start.14 = (bf16[2,128,512]{1,2,0:T(8,128)(2,1)S(1)}, bf16[2,128,512]{1,2,0:T(8,128)(2,1)S(1)}, u32[]{:S(2)}, u32[]{:S(2)}) collective-permute-start(bf16[2,128,512]{1,2,0:T(8,128)(2,1)S(1)} %pad_maximum_fusion), channel_id=1, source_target_pairs={{0,1},{1,0},{2,3},{3,2},{4,5},{5,4},{6,7},{7,6},{8,9},{9,8},{10,11... | collective-permute-start | bytes 786440 | tf_op jit(solution)/shard_map/ppermute | solution.py:115
  77.5 3.0 %collective-permute-start.15 = (bf16[128,512]{0,1:T(8,128)(2,1)S(1)}, bf16[128,512]{0,1:T(8,128)(2,1)S(1)}, u32[]{:S(2)}, u32[]{:S(2)}) collective-permute-start(bf16[128,512]{0,1:T(8,128)(2,1)S(1)} %collective-permute-done.13), channel_id=1, source_target_pairs={{0,1},{1,0},{2,3},{3,2},{4,5},{5,4},{6,7},{7,6},{8,9},{9,8},{10,11... | collective-permute-start | bytes 393224 | tf_op jit(solution)/shard_map/ppermute | solution.py:116
  82.0 1.0 %fusion.14 = bf16[128,1024]{1,0:T(8,128)(2,1)} fusion(f32[128,1024]{1,0:T(8,128)S(1)} %fusion.13, bf16[128,512]{0,1:T(8,128)(2,1)S(1)} %collective-permute-done.15, bf16[4096,1024]{1,0:T(8,128)(2,1)S(1)} %bitcast.113, s32[]{:T(128)S(6)} %select_n.157), kind=kOutput, calls=%fused_computation.18 | convolution fusion | flops 134479872 | bytes 1966084 | tf_op jit(solution)/shard_map/dot_general | solution.py:107
  (93 shorter events, 10.8 us)
Async XLA Ops:
  3.7 11.4 %collective-permute-start.1 = (bf16[128,256]{0,1:T(8,128)(2,1)S(1)}, bf16[128,256]{0,1:T(8,128)(2,1)S(1)}, u32[]{:S(2)}, u32[]{:S(2)}) collective-permute-start(bf16[128,256]{0,1:T(8,128)(2,1)S(1)} %get-tuple-element.12), channel_id=1, source_target_pairs={{0,64},{8,72},{16,80},{24,88},{32,96},{40,104},{48,112},{56,120},{... | collective-permute-start | bytes 196616 | tf_op jit(solution)/shard_map/ppermute | solution.py:60
  7.7 7.4 %collective-permute-start = (bf16[128,256]{0,1:T(8,128)(2,1)S(1)}, bf16[128,256]{0,1:T(8,128)(2,1)S(1)}, u32[]{:S(2)}, u32[]{:S(2)}) collective-permute-start(bf16[128,256]{0,1:T(8,128)(2,1)S(1)} %get-tuple-element.12), channel_id=1, source_target_pairs={{0,128},{8,136},{16,144},{24,152},{32,160},{40,168},{48,176},{56,1... | collective-permute-start | bytes 196616 | tf_op jit(solution)/shard_map/ppermute | solution.py:60
  14.4 10.2 %copy-start.5 = (s32[8]{0:T(128)S(1)}, s32[8]{0:T(128)}, u32[]{:S(2)}) copy-start(s32[8]{0:T(128)} %constant.117.clone) | copy-start | bytes 100
  14.4 11.9 %copy-start.4 = (s32[8]{0:T(128)S(1)}, s32[8]{0:T(128)}, u32[]{:S(2)}) copy-start(s32[8]{0:T(128)} %constant.113.clone) | copy-start | bytes 100
  14.7 13.7 %copy-start.3 = (s32[8]{0:T(128)S(1)}, s32[8]{0:T(128)}, u32[]{:S(2)}) copy-start(s32[8]{0:T(128)} %constant.112.clone) | copy-start | bytes 100
  14.8 15.5 %copy-start.2 = (s32[8]{0:T(128)S(1)}, s32[8]{0:T(128)}, u32[]{:S(2)}) copy-start(s32[8]{0:T(128)} %constant.111.clone) | copy-start | bytes 100
  14.8 17.6 %copy-start.1 = (s32[8]{0:T(128)S(1)}, s32[8]{0:T(128)}, u32[]{:S(2)}) copy-start(s32[8]{0:T(128)} %constant.118.clone) | copy-start | bytes 100
  14.8 19.5 %copy-start = (s32[8]{0:T(128)S(1)}, s32[8]{0:T(128)}, u32[]{:S(2)}) copy-start(s32[8]{0:T(128)} %constant.114.clone) | copy-start | bytes 100
  15.1 26.3 %collective-permute-start.2 = (bf16[3,128,256]{1,2,0:T(8,128)(2,1)S(1)}, bf16[3,128,256]{1,2,0:T(8,128)(2,1)S(1)}, u32[]{:S(2)}, u32[]{:S(2)}) collective-permute-start(bf16[3,128,256]{1,2,0:T(8,128)(2,1)S(1)} %pad_maximum_fusion.1), channel_id=1, source_target_pairs={{0,56},{8,0},{16,8},{24,16},{32,24},{40,32},{48,40},{56,48},{64,12... | collective-permute-start | bytes 589832 | tf_op jit(solution)/shard_map/ppermute | solution.py:69
  20.8 23.4 %collective-permute-start.6 = (bf16[3,128,256]{1,2,0:T(8,128)(2,1)S(1)}, bf16[3,128,256]{1,2,0:T(8,128)(2,1)S(1)}, u32[]{:S(2)}, u32[]{:S(2)}) collective-permute-start(bf16[3,128,256]{1,2,0:T(8,128)(2,1)S(1)} %pad_maximum_fusion.1), channel_id=1, source_target_pairs={{0,8},{8,16},{16,24},{24,32},{32,40},{40,48},{48,56},{56,0},{64,72... | collective-permute-start | bytes 589832 | tf_op jit(solution)/shard_map/ppermute | solution.py:69
  41.4 5.4 %collective-permute-start.3 = (bf16[3,128,256]{1,2,0:T(8,128)(2,1)S(1)}, bf16[3,128,256]{1,2,0:T(8,128)(2,1)S(1)}, u32[]{:S(2)}, u32[]{:S(2)}) collective-permute-start(bf16[3,128,256]{1,2,0:T(8,128)(2,1)S(1)} %collective-permute-done.2), channel_id=1, source_target_pairs={{0,56},{8,0},{16,8},{24,16},{32,24},{40,32},{48,40},{56,48},{64,12... | collective-permute-start | bytes 589832 | tf_op jit(solution)/shard_map/ppermute | solution.py:69
  44.2 5.8 %collective-permute-start.7 = (bf16[3,128,256]{1,2,0:T(8,128)(2,1)S(1)}, bf16[3,128,256]{1,2,0:T(8,128)(2,1)S(1)}, u32[]{:S(2)}, u32[]{:S(2)}) collective-permute-start(bf16[3,128,256]{1,2,0:T(8,128)(2,1)S(1)} %collective-permute-done.6), channel_id=1, source_target_pairs={{0,8},{8,16},{16,24},{24,32},{32,40},{40,48},{48,56},{56,0},{64,72... | collective-permute-start | bytes 589832 | tf_op jit(solution)/shard_map/ppermute | solution.py:69
  46.8 5.1 %collective-permute-start.4 = (bf16[2,128,256]{1,2,0:T(8,128)(2,1)S(1)}, bf16[2,128,256]{1,2,0:T(8,128)(2,1)S(1)}, u32[]{:S(2)}, u32[]{:S(2)}) collective-permute-start(bf16[2,128,256]{1,2,0:T(8,128)(2,1)S(1)} %constant_dynamic-slice_fusion.3), channel_id=1, source_target_pairs={{0,56},{8,0},{16,8},{24,16},{32,24},{40,32},{48,40},{56,48},{64,12... | collective-permute-start | bytes 393224 | tf_op jit(solution)/shard_map/ppermute | solution.py:69
  50.0 5.1 %collective-permute-start.8 = (bf16[2,128,256]{1,2,0:T(8,128)(2,1)S(1)}, bf16[2,128,256]{1,2,0:T(8,128)(2,1)S(1)}, u32[]{:S(2)}, u32[]{:S(2)}) collective-permute-start(bf16[2,128,256]{1,2,0:T(8,128)(2,1)S(1)} %constant_dynamic-slice_fusion.1), channel_id=1, source_target_pairs={{0,8},{8,16},{16,24},{24,32},{32,40},{40,48},{48,56},{56,0},{64,72... | collective-permute-start | bytes 393224 | tf_op jit(solution)/shard_map/ppermute | solution.py:69
  51.9 4.4 %collective-permute-start.5 = (bf16[1,128,256]{1,2,0:T(8,128)(2,1)S(1)}, bf16[1,128,256]{1,2,0:T(8,128)(2,1)S(1)}, u32[]{:S(2)}, u32[]{:S(2)}) collective-permute-start(bf16[1,128,256]{1,2,0:T(8,128)(2,1)S(1)} %constant_dynamic-slice_fusion.2), channel_id=1, source_target_pairs={{0,56},{8,0},{16,8},{24,16},{32,24},{40,32},{48,40},{56,48},{64,12... | collective-permute-start | bytes 196616 | tf_op jit(solution)/shard_map/ppermute | solution.py:69
  55.1 4.4 %collective-permute-start.9 = (bf16[1,128,256]{1,2,0:T(8,128)(2,1)S(1)}, bf16[1,128,256]{1,2,0:T(8,128)(2,1)S(1)}, u32[]{:S(2)}, u32[]{:S(2)}) collective-permute-start(bf16[1,128,256]{1,2,0:T(8,128)(2,1)S(1)} %constant_dynamic-slice_fusion), channel_id=1, source_target_pairs={{0,8},{8,16},{16,24},{24,32},{32,40},{40,48},{48,56},{56,0},{64,72... | collective-permute-start | bytes 196616 | tf_op jit(solution)/shard_map/ppermute | solution.py:69
  59.6 11.4 %slice-start = ((s8[8388608]{0:T(1024)(128)(4,1)}), s8[4194304]{0:T(1024)(128)(4,1)S(1)}, s32[]{:S(2)}) async-start(s8[8388608]{0:T(1024)(128)(4,1)} %bitcast.112), calls=%async_computation | async-start | bytes 8388608
  60.5 10.6 %slice-start.1 = ((s8[8388608]{0:T(1024)(128)(4,1)}), s8[4194304]{0:T(1024)(128)(4,1)S(1)}, s32[]{:S(2)}) async-start(s8[8388608]{0:T(1024)(128)(4,1)} %bitcast.112), calls=%async_computation.1 | async-start | bytes 8388608
  62.2 9.2 %collective-permute-start.10 = (bf16[128,512]{0,1:T(8,128)(2,1)S(1)}, bf16[128,512]{0,1:T(8,128)(2,1)S(1)}, u32[]{:S(2)}, u32[]{:S(2)}) collective-permute-start(bf16[128,512]{0,1:T(8,128)(2,1)S(1)} %bitcast.119), channel_id=1, source_target_pairs={{0,2},{1,3},{2,4},{3,5},{4,6},{5,7},{6,0},{7,1},{8,10},{9,11},{10,... | collective-permute-start | bytes 393224 | tf_op jit(solution)/shard_map/ppermute | solution.py:109
  63.5 7.9 %collective-permute-start.11 = (bf16[128,512]{0,1:T(8,128)(2,1)S(1)}, bf16[128,512]{0,1:T(8,128)(2,1)S(1)}, u32[]{:S(2)}, u32[]{:S(2)}) collective-permute-start(bf16[128,512]{0,1:T(8,128)(2,1)S(1)} %bitcast.120), channel_id=1, source_target_pairs={{0,6},{1,7},{2,0},{3,1},{4,2},{5,3},{6,4},{7,5},{8,14},{9,15},{10,... | collective-permute-start | bytes 393224 | tf_op jit(solution)/shard_map/ppermute | solution.py:110
  65.1 12.1 %collective-permute-start.12 = (bf16[128,512]{0,1:T(8,128)(2,1)S(1)}, bf16[128,512]{0,1:T(8,128)(2,1)S(1)}, u32[]{:S(2)}, u32[]{:S(2)}) collective-permute-start(bf16[128,512]{0,1:T(8,128)(2,1)S(1)} %bitcast.121), channel_id=1, source_target_pairs={{0,1},{1,0},{2,3},{3,2},{4,5},{5,4},{6,7},{7,6},{8,9},{9,8},{10,11... | collective-permute-start | bytes 393224 | tf_op jit(solution)/shard_map/ppermute | solution.py:112
  71.4 6.1 %collective-permute-start.13 = (bf16[128,512]{0,1:T(8,128)(2,1)S(1)}, bf16[128,512]{0,1:T(8,128)(2,1)S(1)}, u32[]{:S(2)}, u32[]{:S(2)}) collective-permute-start(bf16[128,512]{0,1:T(8,128)(2,1)S(1)} %broadcast_select_fusion), channel_id=1, source_target_pairs={{0,2},{1,7},{2,4},{3,1},{4,6},{5,3},{6,0},{7,5},{8,10},{9,15},{10,... | collective-permute-start | bytes 393224 | tf_op jit(solution)/shard_map/ppermute | solution.py:114
  72.8 8.1 %collective-permute-start.14 = (bf16[2,128,512]{1,2,0:T(8,128)(2,1)S(1)}, bf16[2,128,512]{1,2,0:T(8,128)(2,1)S(1)}, u32[]{:S(2)}, u32[]{:S(2)}) collective-permute-start(bf16[2,128,512]{1,2,0:T(8,128)(2,1)S(1)} %pad_maximum_fusion), channel_id=1, source_target_pairs={{0,1},{1,0},{2,3},{3,2},{4,5},{5,4},{6,7},{7,6},{8,9},{9,8},{10,11... | collective-permute-start | bytes 786440 | tf_op jit(solution)/shard_map/ppermute | solution.py:115
  77.5 4.4 %collective-permute-start.15 = (bf16[128,512]{0,1:T(8,128)(2,1)S(1)}, bf16[128,512]{0,1:T(8,128)(2,1)S(1)}, u32[]{:S(2)}, u32[]{:S(2)}) collective-permute-start(bf16[128,512]{0,1:T(8,128)(2,1)S(1)} %collective-permute-done.13), channel_id=1, source_target_pairs={{0,1},{1,0},{2,3},{3,2},{4,5},{5,4},{6,7},{7,6},{8,9},{9,8},{10,11... | collective-permute-start | bytes 393224 | tf_op jit(solution)/shard_map/ppermute | solution.py:116
  (2 other events, 14.9 us)

commit v5 on v4

--- a/solution.py
+++ b/solution.py
@@ -65,13 +65,13 @@
         for chain in relay_plan(row, rows_back):
             packet = bundle
             for step in chain:
-                lo = jnp.asarray(step["send"], jnp.int32)[z]
+                lo = pick(step["send"], z)
                 packet = lax.ppermute(
                     lax.dynamic_slice_in_dim(packet, lo, step["width"], 0),
                     "ctx",
                     [(r * row + s, r * row + (s + step["dir"]) % row) for r in range(n_rows) for s in range(row)],
                 )
-                at = jnp.asarray(step["take"], jnp.int32)[z]
+                at = pick(step["take"], z)
                 got = lax.dynamic_slice_in_dim(packet, at, len(step["blocks"]), 0)
                 for i, blk in enumerate(step["blocks"]):
                     blocks[blk] = got[i]
@@ -126,6 +126,14 @@
         return total.astype(jnp.bfloat16)
 
     return on_device
+
+
+def pick(table, z):
+    out = jnp.int32(0)
+    for i, v in enumerate(table):
+        if v:
+            out = out + jnp.where(z == i, jnp.int32(v), jnp.int32(0))
+    return out
 
 
 def relay_plan(row, rows_back):

time: 83.5 us -> 66.9 us (0.80)
  between operations: 16 us -> 0.62 us
  local copies, waits for them, and re-layouts: 9.22 us -> 4.17 us
  waiting for transfers between devices: 8.5 us -> 11.6 us
  starting transfers between devices: 40.6 us -> 41.6 us
    dynamic_slice x8 -> x0, local copies, waits for them, and re-layouts: 4.99 us -> none  [the longest x4 2.53 us: on_device(): lo = jnp.asarray(step['send'], jnp.int32)[z]]
    ppermute x8, waiting for transfers between devices: 8.48 us -> 11.5 us  [on_device(): lax.ppermute(lax.dynamic_slice_in_dim(packet, lo, step['width'], 0), 'ctx...]
    unnamed x41 -> x25, local copies, waits for them, and re-layouts: 3.44 us -> 3.38 us
  transfers between devices with their start and end apart: 16 -> 16, of which waited for: 5 -> 6; matrix products, arithmetic and copies ran while one was open for 13% -> 8% of each run, Pallas kernels for 0% -> 0%
where the time goes in v5:
time: 66.9 us; the launch traced here: 66.6 us
  starting transfers between devices  41.6 us (62%)
  waiting for transfers between devices  11.6 us (17%)
  matrix products  5.15 us (8%)
  local copies, waits for them, and re-layouts  4.17 us (6%)
  other arithmetic  3.5 us (5%)
    ppermute x8, starting transfers between devices, on_device(): lax.ppermute(lax.dynamic_slice_in_dim(packet, lo, step['width'], 0), 'ctx...  15.5 us
    ppermute x8, waiting for transfers between devices, on_device(): lax.ppermute(lax.dynamic_slice_in_dim(packet, lo, step['width'], 0), 'ctx...  11.5 us
    ppermute x2, starting transfers between devices, on_device(): lax.ppermute(own, 'ctx', [(s, s + shift) for s in range(n_ctx - shift)])  8.55 us
    ppermute x1, starting transfers between devices, on_device(): partner = lax.ppermute(attended, 'head', swap)  6.3 us
    ppermute x1, starting transfers between devices, on_device(): near_other = lax.ppermute(jnp.stack([up, down]), 'head', swap)  4.04 us
    dot_general x8, matrix products, project(): return jnp.dot(piece, rows, preferred_element_type=jnp.float32)  3.4 us
    unnamed x25, local copies, waits for them, and re-layouts  3.38 us
    ppermute x1, starting transfers between devices, on_device(): far_other = lax.ppermute(far, 'head', swap)  3 us
  transfers between devices with their start and end apart: 16, of which 6 were waited for; matrix products, arithmetic and copies ran while one was open for 8% of the time, Pallas kernels for 0%

profile of v5, /device:TPU:1, one launch (start us, length us, event | category | flops | bytes accessed | tf_op | source)
XLA Modules:
  0.0 66.6 jit_solution(6606609734410608684)
XLA Ops:
  1.7 0.9 %copy.22 = bf16[128,128]{0,1:T(8,128)(2,1)S(1)} copy(bf16[128,128]{1,0:T(8,128)(2,1)} %param.6) | data formatting | bytes 65536 | tf_op args[1]
  2.6 0.9 %copy.23 = bf16[128,128]{0,1:T(8,128)(2,1)S(1)} copy(bf16[128,128]{1,0:T(8,128)(2,1)} %param.7) | data formatting | bytes 65536 | tf_op args[2]
  3.7 4.0 %collective-permute-start.1 = (bf16[128,256]{0,1:T(8,128)(2,1)S(1)}, bf16[128,256]{0,1:T(8,128)(2,1)S(1)}, u32[]{:S(2)}, u32[]{:S(2)}) collective-permute-start(bf16[128,256]{0,1:T(8,128)(2,1)S(1)} %get-tuple-element.12), channel_id=1, source_target_pairs={{0,64},{8,72},{16,80},{24,88},{32,96},{40,104},{48,112},{56,120},{... | collective-permute-start | bytes 196616 | tf_op jit(solution)/shard_map/ppermute | solution.py:60
  7.7 4.5 %collective-permute-start = (bf16[128,256]{0,1:T(8,128)(2,1)S(1)}, bf16[128,256]{0,1:T(8,128)(2,1)S(1)}, u32[]{:S(2)}, u32[]{:S(2)}) collective-permute-start(bf16[128,256]{0,1:T(8,128)(2,1)S(1)} %get-tuple-element.12), channel_id=1, source_target_pairs={{0,128},{8,136},{16,144},{24,152},{32,160},{40,168},{48,176},{56,1... | collective-permute-start | bytes 196616 | tf_op jit(solution)/shard_map/ppermute | solution.py:60
  12.3 1.0 %copy.24 = bf16[128,512]{0,1:T(8,128)(2,1)S(1)} copy(bf16[128,512]{1,0:T(8,128)(2,1)} %param.5) | data formatting | bytes 262144 | tf_op args[0]
  13.3 1.0 %compare_and_fusion = pred[128,2176]{0,1:T(8,128)(4,1)S(1)} fusion(s32[128]{0:T(128)S(1)} %select_reduce_fusion, s32[128]{0:T(128)S(1)} %iota_add_fusion.1, s32[2176]{0:T(1024)S(1)} %iota_add_fusion), kind=kLoop, calls=%fused_computation.19 | loop fusion | flops 835584 | bytes 288256 | tf_op jit(solution)/shard_map/and | solution.py:87
  15.0 5.7 %collective-permute-start.2 = (bf16[3,128,256]{1,2,0:T(8,128)(2,1)S(1)}, bf16[3,128,256]{1,2,0:T(8,128)(2,1)S(1)}, u32[]{:S(2)}, u32[]{:S(2)}) collective-permute-start(bf16[3,128,256]{1,2,0:T(8,128)(2,1)S(1)} %pad_maximum_fusion.1), channel_id=1, source_target_pairs={{0,56},{8,0},{16,8},{24,16},{32,24},{40,32},{48,40},{56,48},{64,12... | collective-permute-start | bytes 589832 | tf_op jit(solution)/shard_map/ppermute | solution.py:69
  20.9 2.8 %collective-permute-done.2 = bf16[3,128,256]{1,2,0:T(8,128)(2,1)S(1)} collective-permute-done((bf16[3,128,256]{1,2,0:T(8,128)(2,1)S(1)}, bf16[3,128,256]{1,2,0:T(8,128)(2,1)S(1)}, u32[]{:S(2)}, u32[]{:S(2)}) %collective-permute-start.2) | collective-permute-done | bytes 196640 | tf_op jit(solution)/shard_map/ppermute | solution.py:69
  23.7 3.4 %collective-permute-start.3 = (bf16[3,128,256]{1,2,0:T(8,128)(2,1)S(1)}, bf16[3,128,256]{1,2,0:T(8,128)(2,1)S(1)}, u32[]{:S(2)}, u32[]{:S(2)}) collective-permute-start(bf16[3,128,256]{1,2,0:T(8,128)(2,1)S(1)} %collective-permute-done.2), channel_id=1, source_target_pairs={{0,56},{8,0},{16,8},{24,16},{32,24},{40,32},{48,40},{56,48},{64,12... | collective-permute-start | bytes 589832 | tf_op jit(solution)/shard_map/ppermute | solution.py:69
  27.3 2.5 %collective-permute-done.3 = bf16[3,128,256]{1,2,0:T(8,128)(2,1)S(1)} collective-permute-done((bf16[3,128,256]{1,2,0:T(8,128)(2,1)S(1)}, bf16[3,128,256]{1,2,0:T(8,128)(2,1)S(1)}, u32[]{:S(2)}, u32[]{:S(2)}) %collective-permute-start.3) | collective-permute-done | bytes 196640 | tf_op jit(solution)/shard_map/ppermute | solution.py:69
  29.7 3.2 %collective-permute-start.4 = (bf16[2,128,256]{1,2,0:T(8,128)(2,1)S(1)}, bf16[2,128,256]{1,2,0:T(8,128)(2,1)S(1)}, u32[]{:S(2)}, u32[]{:S(2)}) collective-permute-start(bf16[2,128,256]{1,2,0:T(8,128)(2,1)S(1)} %constant_dynamic-slice_fusion.3), channel_id=1, source_target_pairs={{0,56},{8,0},{16,8},{24,16},{32,24},{40,32},{48,40},{56,48},{64,12... | collective-permute-start | bytes 393224 | tf_op jit(solution)/shard_map/ppermute | solution.py:69
  33.1 1.8 %collective-permute-done.4 = bf16[2,128,256]{1,2,0:T(8,128)(2,1)S(1)} collective-permute-done((bf16[2,128,256]{1,2,0:T(8,128)(2,1)S(1)}, bf16[2,128,256]{1,2,0:T(8,128)(2,1)S(1)}, u32[]{:S(2)}, u32[]{:S(2)}) %collective-permute-start.4) | collective-permute-done | bytes 131104 | tf_op jit(solution)/shard_map/ppermute | solution.py:69
  34.9 3.1 %collective-permute-start.5 = (bf16[1,128,256]{1,2,0:T(8,128)(2,1)S(1)}, bf16[1,128,256]{1,2,0:T(8,128)(2,1)S(1)}, u32[]{:S(2)}, u32[]{:S(2)}) collective-permute-start(bf16[1,128,256]{1,2,0:T(8,128)(2,1)S(1)} %constant_dynamic-slice_fusion.2), channel_id=1, source_target_pairs={{0,56},{8,0},{16,8},{24,16},{32,24},{40,32},{48,40},{56,48},{64,12... | collective-permute-start | bytes 196616 | tf_op jit(solution)/shard_map/ppermute | solution.py:69
  38.1 1.2 %collective-permute-done.5 = bf16[1,128,256]{1,2,0:T(8,128)(2,1)S(1)} collective-permute-done((bf16[1,128,256]{1,2,0:T(8,128)(2,1)S(1)}, bf16[1,128,256]{1,2,0:T(8,128)(2,1)S(1)}, u32[]{:S(2)}, u32[]{:S(2)}) %collective-permute-start.5) | collective-permute-done | bytes 65568 | tf_op jit(solution)/shard_map/ppermute | solution.py:69
  39.5 3.2 %collective-permute-done.9 = bf16[1,128,256]{1,2,0:T(8,128)(2,1)S(1)} collective-permute-done((bf16[1,128,256]{1,2,0:T(8,128)(2,1)S(1)}, bf16[1,128,256]{1,2,0:T(8,128)(2,1)S(1)}, u32[]{:S(2)}, u32[]{:S(2)}) %collective-permute-start.9) | collective-permute-done | bytes 65568 | tf_op jit(solution)/shard_map/ppermute | solution.py:69
  42.9 0.8 %fusion.69 = (f32[4,128]{1,0:T(4,128)S(1)}, f32[1,4,128,2176]{2,3,1,0:T(8,128)S(1)}) fusion(bf16[128,4,64]{2,0,1:T(8,128)(2,1)S(1)} %get-tuple-element.6, bf16[128,4,64]{2,0,1:T(8,128)(2,1)S(1)} %get-tuple-element.5, bf16[2176,256]{0,1:T(8,128)(2,1)S(1)} %constant_dynamic-update-slice_fusion, pred[128,2176]{0,1:T(8,128)(4,1)S(1)} %compare_and_fusion), kind=kOutput, calls=%fused_computation.112 | convolution fusion | flops 288816640 | bytes 5556224 | tf_op jit(solution)/shard_map/tkgd,nkd->kgtn/dot_general | solution.py:83
  44.6 0.9 %fusion.18 = bf16[4,128,128]{1,2,0:T(8,128)(2,1)S(1)} fusion(f32[1,4,128,2176]{2,3,1,0:T(8,128)S(1)} %get-tuple-element.16, f32[4,128]{1,0:T(4,128)S(1)} %get-tuple-element.15, pred[128,2176]{0,1:T(8,128)(4,1)S(1)} %compare_and_fusion, bf16[2176,256]{0,1:T(8,128)(2,1)S(1)} %constant_dynamic-update-slice_fusion, f32[4,128]{1,0:T(4,128)S(1)} %fusion.2), kind=kOutput, calls=%fused_computation.21 | convolution fusion | flops 288686080 | bytes 5427200 | tf_op jit(solution)/shard_map/kgtn,nkd->kgtd/dot_general | solution.py:92
  45.5 1.3 %collective-permute-start.10 = (bf16[128,512]{0,1:T(8,128)(2,1)S(1)}, bf16[128,512]{0,1:T(8,128)(2,1)S(1)}, u32[]{:S(2)}, u32[]{:S(2)}) collective-permute-start(bf16[128,512]{0,1:T(8,128)(2,1)S(1)} %bitcast.111), channel_id=1, source_target_pairs={{0,2},{1,3},{2,4},{3,5},{4,6},{5,7},{6,0},{7,1},{8,10},{9,11},{10,... | collective-permute-start | bytes 393224 | tf_op jit(solution)/shard_map/ppermute | solution.py:109
  46.8 1.5 %collective-permute-start.11 = (bf16[128,512]{0,1:T(8,128)(2,1)S(1)}, bf16[128,512]{0,1:T(8,128)(2,1)S(1)}, u32[]{:S(2)}, u32[]{:S(2)}) collective-permute-start(bf16[128,512]{0,1:T(8,128)(2,1)S(1)} %bitcast.112), channel_id=1, source_target_pairs={{0,6},{1,7},{2,0},{3,1},{4,2},{5,3},{6,4},{7,5},{8,14},{9,15},{10,... | collective-permute-start | bytes 393224 | tf_op jit(solution)/shard_map/ppermute | solution.py:110
  48.3 6.3 %collective-permute-start.12 = (bf16[128,512]{0,1:T(8,128)(2,1)S(1)}, bf16[128,512]{0,1:T(8,128)(2,1)S(1)}, u32[]{:S(2)}, u32[]{:S(2)}) collective-permute-start(bf16[128,512]{0,1:T(8,128)(2,1)S(1)} %bitcast.113), channel_id=1, source_target_pairs={{0,1},{1,0},{2,3},{3,2},{4,5},{5,4},{6,7},{7,6},{8,9},{9,8},{10,11... | collective-permute-start | bytes 393224 | tf_op jit(solution)/shard_map/ppermute | solution.py:112
  55.0 1.3 %collective-permute-start.13 = (bf16[128,512]{0,1:T(8,128)(2,1)S(1)}, bf16[128,512]{0,1:T(8,128)(2,1)S(1)}, u32[]{:S(2)}, u32[]{:S(2)}) collective-permute-start(bf16[128,512]{0,1:T(8,128)(2,1)S(1)} %broadcast_select_fusion), channel_id=1, source_target_pairs={{0,2},{1,7},{2,4},{3,1},{4,6},{5,3},{6,0},{7,5},{8,10},{9,15},{10,... | collective-permute-start | bytes 393224 | tf_op jit(solution)/shard_map/ppermute | solution.py:114
  56.4 4.0 %collective-permute-start.14 = (bf16[2,128,512]{1,2,0:T(8,128)(2,1)S(1)}, bf16[2,128,512]{1,2,0:T(8,128)(2,1)S(1)}, u32[]{:S(2)}, u32[]{:S(2)}) collective-permute-start(bf16[2,128,512]{1,2,0:T(8,128)(2,1)S(1)} %pad_maximum_fusion), channel_id=1, source_target_pairs={{0,1},{1,0},{2,3},{3,2},{4,5},{5,4},{6,7},{7,6},{8,9},{9,8},{10,11... | collective-permute-start | bytes 786440 | tf_op jit(solution)/shard_map/ppermute | solution.py:115
  61.1 3.0 %collective-permute-start.15 = (bf16[128,512]{0,1:T(8,128)(2,1)S(1)}, bf16[128,512]{0,1:T(8,128)(2,1)S(1)}, u32[]{:S(2)}, u32[]{:S(2)}) collective-permute-start(bf16[128,512]{0,1:T(8,128)(2,1)S(1)} %collective-permute-done.13), channel_id=1, source_target_pairs={{0,1},{1,0},{2,3},{3,2},{4,5},{5,4},{6,7},{7,6},{8,9},{9,8},{10,11... | collective-permute-start | bytes 393224 | tf_op jit(solution)/shard_map/ppermute | solution.py:116
  65.5 1.0 %fusion.14 = bf16[128,1024]{1,0:T(8,128)(2,1)} fusion(f32[128,1024]{1,0:T(8,128)S(1)} %fusion.13, bf16[128,512]{0,1:T(8,128)(2,1)S(1)} %collective-permute-done.15, bf16[4096,1024]{1,0:T(8,128)(2,1)S(1)} %bitcast.105, s32[]{:T(128)S(6)} %select_n.180), kind=kOutput, calls=%fused_computation.18 | convolution fusion | flops 134479872 | bytes 1966084 | tf_op jit(solution)/shard_map/dot_general | solution.py:107
  (69 shorter events, 6.6 us)
Async XLA Ops:
  3.7 11.3 %collective-permute-start.1 = (bf16[128,256]{0,1:T(8,128)(2,1)S(1)}, bf16[128,256]{0,1:T(8,128)(2,1)S(1)}, u32[]{:S(2)}, u32[]{:S(2)}) collective-permute-start(bf16[128,256]{0,1:T(8,128)(2,1)S(1)} %get-tuple-element.12), channel_id=1, source_target_pairs={{0,64},{8,72},{16,80},{24,88},{32,96},{40,104},{48,112},{56,120},{... | collective-permute-start | bytes 196616 | tf_op jit(solution)/shard_map/ppermute | solution.py:60
  7.7 7.3 %collective-permute-start = (bf16[128,256]{0,1:T(8,128)(2,1)S(1)}, bf16[128,256]{0,1:T(8,128)(2,1)S(1)}, u32[]{:S(2)}, u32[]{:S(2)}) collective-permute-start(bf16[128,256]{0,1:T(8,128)(2,1)S(1)} %get-tuple-element.12), channel_id=1, source_target_pairs={{0,128},{8,136},{16,144},{24,152},{32,160},{40,168},{48,176},{56,1... | collective-permute-start | bytes 196616 | tf_op jit(solution)/shard_map/ppermute | solution.py:60
  15.0 8.7 %collective-permute-start.2 = (bf16[3,128,256]{1,2,0:T(8,128)(2,1)S(1)}, bf16[3,128,256]{1,2,0:T(8,128)(2,1)S(1)}, u32[]{:S(2)}, u32[]{:S(2)}) collective-permute-start(bf16[3,128,256]{1,2,0:T(8,128)(2,1)S(1)} %pad_maximum_fusion.1), channel_id=1, source_target_pairs={{0,56},{8,0},{16,8},{24,16},{32,24},{40,32},{48,40},{56,48},{64,12... | collective-permute-start | bytes 589832 | tf_op jit(solution)/shard_map/ppermute | solution.py:69
  20.7 6.5 %collective-permute-start.6 = (bf16[3,128,256]{1,2,0:T(8,128)(2,1)S(1)}, bf16[3,128,256]{1,2,0:T(8,128)(2,1)S(1)}, u32[]{:S(2)}, u32[]{:S(2)}) collective-permute-start(bf16[3,128,256]{1,2,0:T(8,128)(2,1)S(1)} %pad_maximum_fusion.1), channel_id=1, source_target_pairs={{0,8},{8,16},{16,24},{24,32},{32,40},{40,48},{48,56},{56,0},{64,72... | collective-permute-start | bytes 589832 | tf_op jit(solution)/shard_map/ppermute | solution.py:69
  23.7 6.0 %collective-permute-start.3 = (bf16[3,128,256]{1,2,0:T(8,128)(2,1)S(1)}, bf16[3,128,256]{1,2,0:T(8,128)(2,1)S(1)}, u32[]{:S(2)}, u32[]{:S(2)}) collective-permute-start(bf16[3,128,256]{1,2,0:T(8,128)(2,1)S(1)} %collective-permute-done.2), channel_id=1, source_target_pairs={{0,56},{8,0},{16,8},{24,16},{32,24},{40,32},{48,40},{56,48},{64,12... | collective-permute-start | bytes 589832 | tf_op jit(solution)/shard_map/ppermute | solution.py:69
  27.1 5.8 %collective-permute-start.7 = (bf16[3,128,256]{1,2,0:T(8,128)(2,1)S(1)}, bf16[3,128,256]{1,2,0:T(8,128)(2,1)S(1)}, u32[]{:S(2)}, u32[]{:S(2)}) collective-permute-start(bf16[3,128,256]{1,2,0:T(8,128)(2,1)S(1)} %collective-permute-done.6), channel_id=1, source_target_pairs={{0,8},{8,16},{16,24},{24,32},{32,40},{40,48},{48,56},{56,0},{64,72... | collective-permute-start | bytes 589832 | tf_op jit(solution)/shard_map/ppermute | solution.py:69
  29.7 5.1 %collective-permute-start.4 = (bf16[2,128,256]{1,2,0:T(8,128)(2,1)S(1)}, bf16[2,128,256]{1,2,0:T(8,128)(2,1)S(1)}, u32[]{:S(2)}, u32[]{:S(2)}) collective-permute-start(bf16[2,128,256]{1,2,0:T(8,128)(2,1)S(1)} %constant_dynamic-slice_fusion.3), channel_id=1, source_target_pairs={{0,56},{8,0},{16,8},{24,16},{32,24},{40,32},{48,40},{56,48},{64,12... | collective-permute-start | bytes 393224 | tf_op jit(solution)/shard_map/ppermute | solution.py:69
  33.0 5.1 %collective-permute-start.8 = (bf16[2,128,256]{1,2,0:T(8,128)(2,1)S(1)}, bf16[2,128,256]{1,2,0:T(8,128)(2,1)S(1)}, u32[]{:S(2)}, u32[]{:S(2)}) collective-permute-start(bf16[2,128,256]{1,2,0:T(8,128)(2,1)S(1)} %constant_dynamic-slice_fusion.1), channel_id=1, source_target_pairs={{0,8},{8,16},{16,24},{24,32},{32,40},{40,48},{48,56},{56,0},{64,72... | collective-permute-start | bytes 393224 | tf_op jit(solution)/shard_map/ppermute | solution.py:69
  34.9 4.4 %collective-permute-start.5 = (bf16[1,128,256]{1,2,0:T(8,128)(2,1)S(1)}, bf16[1,128,256]{1,2,0:T(8,128)(2,1)S(1)}, u32[]{:S(2)}, u32[]{:S(2)}) collective-permute-start(bf16[1,128,256]{1,2,0:T(8,128)(2,1)S(1)} %constant_dynamic-slice_fusion.2), channel_id=1, source_target_pairs={{0,56},{8,0},{16,8},{24,16},{32,24},{40,32},{48,40},{56,48},{64,12... | collective-permute-start | bytes 196616 | tf_op jit(solution)/shard_map/ppermute | solution.py:69
  38.1 4.7 %collective-permute-start.9 = (bf16[1,128,256]{1,2,0:T(8,128)(2,1)S(1)}, bf16[1,128,256]{1,2,0:T(8,128)(2,1)S(1)}, u32[]{:S(2)}, u32[]{:S(2)}) collective-permute-start(bf16[1,128,256]{1,2,0:T(8,128)(2,1)S(1)} %constant_dynamic-slice_fusion), channel_id=1, source_target_pairs={{0,8},{8,16},{16,24},{24,32},{32,40},{40,48},{48,56},{56,0},{64,72... | collective-permute-start | bytes 196616 | tf_op jit(solution)/shard_map/ppermute | solution.py:69
  42.9 11.7 %slice-start = ((s8[8388608]{0:T(1024)(128)(4,1)}), s8[4194304]{0:T(1024)(128)(4,1)S(1)}, s32[]{:S(2)}) async-start(s8[8388608]{0:T(1024)(128)(4,1)} %bitcast.104), calls=%async_computation | async-start | bytes 8388608
  43.7 10.9 %slice-start.1 = ((s8[8388608]{0:T(1024)(128)(4,1)}), s8[4194304]{0:T(1024)(128)(4,1)S(1)}, s32[]{:S(2)}) async-start(s8[8388608]{0:T(1024)(128)(4,1)} %bitcast.104), calls=%async_computation.1 | async-start | bytes 8388608
  45.5 9.5 %collective-permute-start.10 = (bf16[128,512]{0,1:T(8,128)(2,1)S(1)}, bf16[128,512]{0,1:T(8,128)(2,1)S(1)}, u32[]{:S(2)}, u32[]{:S(2)}) collective-permute-start(bf16[128,512]{0,1:T(8,128)(2,1)S(1)} %bitcast.111), channel_id=1, source_target_pairs={{0,2},{1,3},{2,4},{3,5},{4,6},{5,7},{6,0},{7,1},{8,10},{9,11},{10,... | collective-permute-start | bytes 393224 | tf_op jit(solution)/shard_map/ppermute | solution.py:109
  46.8 8.2 %collective-permute-start.11 = (bf16[128,512]{0,1:T(8,128)(2,1)S(1)}, bf16[128,512]{0,1:T(8,128)(2,1)S(1)}, u32[]{:S(2)}, u32[]{:S(2)}) collective-permute-start(bf16[128,512]{0,1:T(8,128)(2,1)S(1)} %bitcast.112), channel_id=1, source_target_pairs={{0,6},{1,7},{2,0},{3,1},{4,2},{5,3},{6,4},{7,5},{8,14},{9,15},{10,... | collective-permute-start | bytes 393224 | tf_op jit(solution)/shard_map/ppermute | solution.py:110
  48.3 12.4 %collective-permute-start.12 = (bf16[128,512]{0,1:T(8,128)(2,1)S(1)}, bf16[128,512]{0,1:T(8,128)(2,1)S(1)}, u32[]{:S(2)}, u32[]{:S(2)}) collective-permute-start(bf16[128,512]{0,1:T(8,128)(2,1)S(1)} %bitcast.113), channel_id=1, source_target_pairs={{0,1},{1,0},{2,3},{3,2},{4,5},{5,4},{6,7},{7,6},{8,9},{9,8},{10,11... | collective-permute-start | bytes 393224 | tf_op jit(solution)/shard_map/ppermute | solution.py:112
  55.0 6.1 %collective-permute-start.13 = (bf16[128,512]{0,1:T(8,128)(2,1)S(1)}, bf16[128,512]{0,1:T(8,128)(2,1)S(1)}, u32[]{:S(2)}, u32[]{:S(2)}) collective-permute-start(bf16[128,512]{0,1:T(8,128)(2,1)S(1)} %broadcast_select_fusion), channel_id=1, source_target_pairs={{0,2},{1,7},{2,4},{3,1},{4,6},{5,3},{6,0},{7,5},{8,10},{9,15},{10,... | collective-permute-start | bytes 393224 | tf_op jit(solution)/shard_map/ppermute | solution.py:114
  56.4 8.1 %collective-permute-start.14 = (bf16[2,128,512]{1,2,0:T(8,128)(2,1)S(1)}, bf16[2,128,512]{1,2,0:T(8,128)(2,1)S(1)}, u32[]{:S(2)}, u32[]{:S(2)}) collective-permute-start(bf16[2,128,512]{1,2,0:T(8,128)(2,1)S(1)} %pad_maximum_fusion), channel_id=1, source_target_pairs={{0,1},{1,0},{2,3},{3,2},{4,5},{5,4},{6,7},{7,6},{8,9},{9,8},{10,11... | collective-permute-start | bytes 786440 | tf_op jit(solution)/shard_map/ppermute | solution.py:115
  61.1 4.4 %collective-permute-start.15 = (bf16[128,512]{0,1:T(8,128)(2,1)S(1)}, bf16[128,512]{0,1:T(8,128)(2,1)S(1)}, u32[]{:S(2)}, u32[]{:S(2)}) collective-permute-start(bf16[128,512]{0,1:T(8,128)(2,1)S(1)} %collective-permute-done.13), channel_id=1, source_target_pairs={{0,1},{1,0},{2,3},{3,2},{4,5},{5,4},{6,7},{7,6},{8,9},{9,8},{10,11... | collective-permute-start | bytes 393224 | tf_op jit(solution)/shard_map/ppermute | solution.py:116

commit v6 on v5

--- a/solution.py
+++ b/solution.py
@@ -62,7 +62,18 @@
         bundle = jnp.stack(bundle)
         z = ctx % row
         n_rows = n_ctx // row
-        for chain in relay_plan(row, rows_back):
+        chains, direct = relay_plan(row, rows_back)
+        if direct:
+            half = row // 2
+            lo = jnp.where((z + half) % row < half, 1, 0)
+            got = lax.ppermute(
+                lax.dynamic_slice_in_dim(bundle, lo, rows_back, 0),
+                "ctx",
+                [(r * row + s, r * row + (s + half) % row) for r in range(n_rows) for s in range(row)],
+            )
+            for m in range(rows_back):
+                blocks[half + row * m] = got[m]
+        for chain in chains:
             packet = bundle
             for step in chain:
                 lo = pick(step["send"], z)
@@ -138,7 +149,8 @@
 
 def relay_plan(row, rows_back):
     half = row // 2
-    split = row % 2 == 0
+    direct = row % 2 == 0 and row > 2
+    split = False
 
     def part(z, b, direction):
         lo = 1 if z < b else 0
@@ -150,7 +162,7 @@
 
     chains = []
     for direction in (1, -1):
-        rounds = range(1, half + 1) if direction == 1 else range(1, (half if split else row - 1 - half) + 1)
+        rounds = range(1, (half - 1 if direct else half) + 1) if direction == 1 else range(1, row - 1 - half + 1)
         bs = [r if direction == 1 else row - r for r in rounds]
         steps, held = [], None
         for i, b in enumerate(bs):
@@ -181,7 +193,7 @@
             steps.append({"dir": direction, "width": width, "send": send, "take": take, "blocks": blocks})
             held = lo
         chains.append(steps)
-    return chains
+    return chains, direct
 
 
 def solution(mesh):

time: 66.9 us -> 64.6 us (0.966)
  starting transfers between devices: 41.6 us -> 38.4 us
  waiting for transfers between devices: 11.6 us -> 12.5 us
    ppermute x8 -> x6, starting transfers between devices: 15.5 us -> 12.5 us  [on_device(): lax.ppermute(lax.dynamic_slice_in_dim(packet, lo, step['width'], 0), 'ctx...]
    ppermute x1, starting transfers between devices: 6.3 us -> 3.33 us  [on_device(): partner = lax.ppermute(attended, 'head', swap)]
    ppermute x0 -> x1, starting transfers between devices: none -> 2.86 us  [on_device(): lax.ppermute(lax.dynamic_slice_in_dim(bundle, lo, rows_back, 0), 'ctx', [...]
    ppermute x8 -> x6, waiting for transfers between devices: 11.5 us -> 12.5 us  [on_device(): lax.ppermute(lax.dynamic_slice_in_dim(packet, lo, step['width'], 0), 'ctx...]
  transfers between devices with their start and end apart: 16 -> 15, of which waited for: 6 -> 4; matrix products, arithmetic and copies ran while one was open for 8% -> 8% of each run, Pallas kernels for 0% -> 0%
where the time goes in v6:
time: 64.6 us; the launch traced here: 64.3 us
  starting transfers between devices  38.4 us (59%)
  waiting for transfers between devices  12.5 us (19%)
  matrix products  5.15 us (8%)
  local copies, waits for them, and re-layouts  4.17 us (6%)
  other arithmetic  3.5 us (5%)
    ppermute x6, waiting for transfers between devices, on_device(): lax.ppermute(lax.dynamic_slice_in_dim(packet, lo, step['width'], 0), 'ctx...  12.5 us
    ppermute x6, starting transfers between devices, on_device(): lax.ppermute(lax.dynamic_slice_in_dim(packet, lo, step['width'], 0), 'ctx...  12.5 us
    ppermute x2, starting transfers between devices, on_device(): lax.ppermute(own, 'ctx', [(s, s + shift) for s in range(n_ctx - shift)])  8.55 us
    ppermute x1, starting transfers between devices, on_device(): near_other = lax.ppermute(jnp.stack([up, down]), 'head', swap)  3.95 us
    dot_general x8, matrix products, project(): return jnp.dot(piece, rows, preferred_element_type=jnp.float32)  3.4 us
    unnamed x25, local copies, waits for them, and re-layouts  3.37 us
    ppermute x1, starting transfers between devices, on_device(): partner = lax.ppermute(attended, 'head', swap)  3.33 us
    ppermute x1, starting transfers between devices, on_device(): far_other = lax.ppermute(far, 'head', swap)  3.02 us
  transfers between devices with their start and end apart: 15, of which 4 were waited for; matrix products, arithmetic and copies ran while one was open for 8% of the time, Pallas kernels for 0%

profile of v6, /device:TPU:1, one launch (start us, length us, event | category | flops | bytes accessed | tf_op | source)
XLA Modules:
  0.0 64.3 jit_solution(11781309611933062229)
XLA Ops:
  1.7 0.9 %copy.22 = bf16[128,128]{0,1:T(8,128)(2,1)S(1)} copy(bf16[128,128]{1,0:T(8,128)(2,1)} %param.6) | data formatting | bytes 65536 | tf_op args[1]
  2.6 0.9 %copy.23 = bf16[128,128]{0,1:T(8,128)(2,1)S(1)} copy(bf16[128,128]{1,0:T(8,128)(2,1)} %param.7) | data formatting | bytes 65536 | tf_op args[2]
  3.7 4.0 %collective-permute-start.1 = (bf16[128,256]{0,1:T(8,128)(2,1)S(1)}, bf16[128,256]{0,1:T(8,128)(2,1)S(1)}, u32[]{:S(2)}, u32[]{:S(2)}) collective-permute-start(bf16[128,256]{0,1:T(8,128)(2,1)S(1)} %get-tuple-element.12), channel_id=1, source_target_pairs={{0,64},{8,72},{16,80},{24,88},{32,96},{40,104},{48,112},{56,120},{... | collective-permute-start | bytes 196616 | tf_op jit(solution)/shard_map/ppermute | solution.py:60
  7.7 4.5 %collective-permute-start = (bf16[128,256]{0,1:T(8,128)(2,1)S(1)}, bf16[128,256]{0,1:T(8,128)(2,1)S(1)}, u32[]{:S(2)}, u32[]{:S(2)}) collective-permute-start(bf16[128,256]{0,1:T(8,128)(2,1)S(1)} %get-tuple-element.12), channel_id=1, source_target_pairs={{0,128},{8,136},{16,144},{24,152},{32,160},{40,168},{48,176},{56,1... | collective-permute-start | bytes 196616 | tf_op jit(solution)/shard_map/ppermute | solution.py:60
  12.3 1.0 %copy.24 = bf16[128,512]{0,1:T(8,128)(2,1)S(1)} copy(bf16[128,512]{1,0:T(8,128)(2,1)} %param.5) | data formatting | bytes 262144 | tf_op args[0]
  13.3 1.0 %compare_and_fusion = pred[128,2176]{0,1:T(8,128)(4,1)S(1)} fusion(s32[128]{0:T(128)S(1)} %select_reduce_fusion, s32[128]{0:T(128)S(1)} %iota_add_fusion.1, s32[2176]{0:T(1024)S(1)} %iota_add_fusion), kind=kLoop, calls=%fused_computation.19 | loop fusion | flops 835584 | bytes 288256 | tf_op jit(solution)/shard_map/and | solution.py:98
  15.0 5.7 %collective-permute-start.2 = (bf16[3,128,256]{1,2,0:T(8,128)(2,1)S(1)}, bf16[3,128,256]{1,2,0:T(8,128)(2,1)S(1)}, u32[]{:S(2)}, u32[]{:S(2)}) collective-permute-start(bf16[3,128,256]{1,2,0:T(8,128)(2,1)S(1)} %pad_maximum_fusion.1), channel_id=1, source_target_pairs={{0,56},{8,0},{16,8},{24,16},{32,24},{40,32},{48,40},{56,48},{64,12... | collective-permute-start | bytes 589832 | tf_op jit(solution)/shard_map/ppermute | solution.py:80
  21.1 2.9 %collective-permute-start.5 = (bf16[2,128,256]{1,2,0:T(8,128)(2,1)S(1)}, bf16[2,128,256]{1,2,0:T(8,128)(2,1)S(1)}, u32[]{:S(2)}, u32[]{:S(2)}) collective-permute-start(bf16[2,128,256]{1,2,0:T(8,128)(2,1)S(1)} %constant_dynamic-slice_fusion.1), channel_id=1, source_target_pairs={{0,32},{8,40},{16,48},{24,56},{32,0},{40,8},{48,16},{56,24},{64,96... | collective-permute-start | bytes 393224 | tf_op jit(solution)/shard_map/ppermute | solution.py:69
  23.9 3.2 %collective-permute-start.3 = (bf16[3,128,256]{1,2,0:T(8,128)(2,1)S(1)}, bf16[3,128,256]{1,2,0:T(8,128)(2,1)S(1)}, u32[]{:S(2)}, u32[]{:S(2)}) collective-permute-start(bf16[3,128,256]{1,2,0:T(8,128)(2,1)S(1)} %collective-permute-done.2), channel_id=1, source_target_pairs={{0,56},{8,0},{16,8},{24,16},{32,24},{40,32},{48,40},{56,48},{64,12... | collective-permute-start | bytes 589832 | tf_op jit(solution)/shard_map/ppermute | solution.py:80
  27.1 2.0 %collective-permute-done.6 = bf16[3,128,256]{1,2,0:T(8,128)(2,1)S(1)} collective-permute-done((bf16[3,128,256]{1,2,0:T(8,128)(2,1)S(1)}, bf16[3,128,256]{1,2,0:T(8,128)(2,1)S(1)}, u32[]{:S(2)}, u32[]{:S(2)}) %collective-permute-start.6) | collective-permute-done | bytes 196640 | tf_op jit(solution)/shard_map/ppermute | solution.py:80
  29.1 5.6 %collective-permute-done.3 = bf16[3,128,256]{1,2,0:T(8,128)(2,1)S(1)} collective-permute-done((bf16[3,128,256]{1,2,0:T(8,128)(2,1)S(1)}, bf16[3,128,256]{1,2,0:T(8,128)(2,1)S(1)}, u32[]{:S(2)}, u32[]{:S(2)}) %collective-permute-start.3) | collective-permute-done | bytes 196640 | tf_op jit(solution)/shard_map/ppermute | solution.py:80
  34.7 3.5 %collective-permute-start.4 = (bf16[2,128,256]{1,2,0:T(8,128)(2,1)S(1)}, bf16[2,128,256]{1,2,0:T(8,128)(2,1)S(1)}, u32[]{:S(2)}, u32[]{:S(2)}) collective-permute-start(bf16[2,128,256]{1,2,0:T(8,128)(2,1)S(1)} %constant_dynamic-slice_fusion.2), channel_id=1, source_target_pairs={{0,56},{8,0},{16,8},{24,16},{32,24},{40,32},{48,40},{56,48},{64,12... | collective-permute-start | bytes 393224 | tf_op jit(solution)/shard_map/ppermute | solution.py:80
  38.4 1.8 %collective-permute-done.4 = bf16[2,128,256]{1,2,0:T(8,128)(2,1)S(1)} collective-permute-done((bf16[2,128,256]{1,2,0:T(8,128)(2,1)S(1)}, bf16[2,128,256]{1,2,0:T(8,128)(2,1)S(1)}, u32[]{:S(2)}, u32[]{:S(2)}) %collective-permute-start.4) | collective-permute-done | bytes 131104 | tf_op jit(solution)/shard_map/ppermute | solution.py:80
  40.2 3.1 %collective-permute-done.8 = bf16[2,128,256]{1,2,0:T(8,128)(2,1)S(1)} collective-permute-done((bf16[2,128,256]{1,2,0:T(8,128)(2,1)S(1)}, bf16[2,128,256]{1,2,0:T(8,128)(2,1)S(1)}, u32[]{:S(2)}, u32[]{:S(2)}) %collective-permute-start.8) | collective-permute-done | bytes 131104 | tf_op jit(solution)/shard_map/ppermute | solution.py:80
  43.7 0.8 %fusion.71 = (f32[4,128]{1,0:T(4,128)S(1)}, f32[1,4,128,2176]{2,3,1,0:T(8,128)S(1)}) fusion(bf16[128,4,64]{2,0,1:T(8,128)(2,1)S(1)} %get-tuple-element.6, bf16[128,4,64]{2,0,1:T(8,128)(2,1)S(1)} %get-tuple-element.5, bf16[2176,256]{0,1:T(8,128)(2,1)S(1)} %constant_dynamic-update-slice_fusion, pred[128,2176]{0,1:T(8,128)(4,1)S(1)} %compare_and_fusion), kind=kOutput, calls=%fused_computation.113 | convolution fusion | flops 288816640 | bytes 5556224 | tf_op jit(solution)/shard_map/tkgd,nkd->kgtn/dot_general | solution.py:94
  44.6 0.8 %fusion.2 = f32[4,128]{1,0:T(4,128)S(1)} fusion(f32[1,4,128,2176]{2,3,1,0:T(8,128)S(1)} %get-tuple-element.16, f32[4,128]{1,0:T(4,128)S(1)} %get-tuple-element.15, pred[128,2176]{0,1:T(8,128)(4,1)S(1)} %compare_and_fusion), kind=kLoop, calls=%fused_computation.4 | loop fusion | flops 3341824 | bytes 4739072 | tf_op jit(solution)/shard_map/reduce_sum | solution.py:102
  45.4 0.9 %fusion.18 = bf16[4,128,128]{1,2,0:T(8,128)(2,1)S(1)} fusion(f32[1,4,128,2176]{2,3,1,0:T(8,128)S(1)} %get-tuple-element.16, f32[4,128]{1,0:T(4,128)S(1)} %get-tuple-element.15, pred[128,2176]{0,1:T(8,128)(4,1)S(1)} %compare_and_fusion, bf16[2176,256]{0,1:T(8,128)(2,1)S(1)} %constant_dynamic-update-slice_fusion, f32[4,128]{1,0:T(4,128)S(1)} %fusion.2), kind=kOutput, calls=%fused_computation.21 | convolution fusion | flops 288686080 | bytes 5427200 | tf_op jit(solution)/shard_map/kgtn,nkd->kgtd/dot_general | solution.py:103
  46.3 1.3 %collective-permute-start.9 = (bf16[128,512]{0,1:T(8,128)(2,1)S(1)}, bf16[128,512]{0,1:T(8,128)(2,1)S(1)}, u32[]{:S(2)}, u32[]{:S(2)}) collective-permute-start(bf16[128,512]{0,1:T(8,128)(2,1)S(1)} %bitcast.115), channel_id=1, source_target_pairs={{0,2},{1,3},{2,4},{3,5},{4,6},{5,7},{6,0},{7,1},{8,10},{9,11},{10,... | collective-permute-start | bytes 393224 | tf_op jit(solution)/shard_map/ppermute | solution.py:120
  47.6 1.5 %collective-permute-start.10 = (bf16[128,512]{0,1:T(8,128)(2,1)S(1)}, bf16[128,512]{0,1:T(8,128)(2,1)S(1)}, u32[]{:S(2)}, u32[]{:S(2)}) collective-permute-start(bf16[128,512]{0,1:T(8,128)(2,1)S(1)} %bitcast.116), channel_id=1, source_target_pairs={{0,6},{1,7},{2,0},{3,1},{4,2},{5,3},{6,4},{7,5},{8,14},{9,15},{10,... | collective-permute-start | bytes 393224 | tf_op jit(solution)/shard_map/ppermute | solution.py:121
  49.1 3.3 %collective-permute-start.11 = (bf16[128,512]{0,1:T(8,128)(2,1)S(1)}, bf16[128,512]{0,1:T(8,128)(2,1)S(1)}, u32[]{:S(2)}, u32[]{:S(2)}) collective-permute-start(bf16[128,512]{0,1:T(8,128)(2,1)S(1)} %bitcast.117), channel_id=1, source_target_pairs={{0,1},{1,0},{2,3},{3,2},{4,5},{5,4},{6,7},{7,6},{8,9},{9,8},{10,11... | collective-permute-start | bytes 393224 | tf_op jit(solution)/shard_map/ppermute | solution.py:123
  52.8 1.4 %collective-permute-start.12 = (bf16[128,512]{0,1:T(8,128)(2,1)S(1)}, bf16[128,512]{0,1:T(8,128)(2,1)S(1)}, u32[]{:S(2)}, u32[]{:S(2)}) collective-permute-start(bf16[128,512]{0,1:T(8,128)(2,1)S(1)} %broadcast_select_fusion), channel_id=1, source_target_pairs={{0,2},{1,7},{2,4},{3,1},{4,6},{5,3},{6,0},{7,5},{8,10},{9,15},{10,... | collective-permute-start | bytes 393224 | tf_op jit(solution)/shard_map/ppermute | solution.py:125
  54.2 4.0 %collective-permute-start.13 = (bf16[2,128,512]{1,2,0:T(8,128)(2,1)S(1)}, bf16[2,128,512]{1,2,0:T(8,128)(2,1)S(1)}, u32[]{:S(2)}, u32[]{:S(2)}) collective-permute-start(bf16[2,128,512]{1,2,0:T(8,128)(2,1)S(1)} %pad_maximum_fusion), channel_id=1, source_target_pairs={{0,1},{1,0},{2,3},{3,2},{4,5},{5,4},{6,7},{7,6},{8,9},{9,8},{10,11... | collective-permute-start | bytes 786440 | tf_op jit(solution)/shard_map/ppermute | solution.py:126
  58.9 3.0 %collective-permute-start.14 = (bf16[128,512]{0,1:T(8,128)(2,1)S(1)}, bf16[128,512]{0,1:T(8,128)(2,1)S(1)}, u32[]{:S(2)}, u32[]{:S(2)}) collective-permute-start(bf16[128,512]{0,1:T(8,128)(2,1)S(1)} %collective-permute-done.12), channel_id=1, source_target_pairs={{0,1},{1,0},{2,3},{3,2},{4,5},{5,4},{6,7},{7,6},{8,9},{9,8},{10,11... | collective-permute-start | bytes 393224 | tf_op jit(solution)/shard_map/ppermute | solution.py:127
  63.3 1.0 %fusion.14 = bf16[128,1024]{1,0:T(8,128)(2,1)} fusion(f32[128,1024]{1,0:T(8,128)S(1)} %fusion.13, bf16[128,512]{0,1:T(8,128)(2,1)S(1)} %collective-permute-done.14, bf16[4096,1024]{1,0:T(8,128)(2,1)S(1)} %bitcast.109, s32[]{:T(128)S(6)} %select_n.178), kind=kOutput, calls=%fused_computation.18 | convolution fusion | flops 134479872 | bytes 1966084 | tf_op jit(solution)/shard_map/dot_general | solution.py:118
  (66 shorter events, 5.6 us)
Async XLA Ops:
  3.7 11.3 %collective-permute-start.1 = (bf16[128,256]{0,1:T(8,128)(2,1)S(1)}, bf16[128,256]{0,1:T(8,128)(2,1)S(1)}, u32[]{:S(2)}, u32[]{:S(2)}) collective-permute-start(bf16[128,256]{0,1:T(8,128)(2,1)S(1)} %get-tuple-element.12), channel_id=1, source_target_pairs={{0,64},{8,72},{16,80},{24,88},{32,96},{40,104},{48,112},{56,120},{... | collective-permute-start | bytes 196616 | tf_op jit(solution)/shard_map/ppermute | solution.py:60
  7.7 7.3 %collective-permute-start = (bf16[128,256]{0,1:T(8,128)(2,1)S(1)}, bf16[128,256]{0,1:T(8,128)(2,1)S(1)}, u32[]{:S(2)}, u32[]{:S(2)}) collective-permute-start(bf16[128,256]{0,1:T(8,128)(2,1)S(1)} %get-tuple-element.12), channel_id=1, source_target_pairs={{0,128},{8,136},{16,144},{24,152},{32,160},{40,168},{48,176},{56,1... | collective-permute-start | bytes 196616 | tf_op jit(solution)/shard_map/ppermute | solution.py:60
  15.0 8.9 %collective-permute-start.2 = (bf16[3,128,256]{1,2,0:T(8,128)(2,1)S(1)}, bf16[3,128,256]{1,2,0:T(8,128)(2,1)S(1)}, u32[]{:S(2)}, u32[]{:S(2)}) collective-permute-start(bf16[3,128,256]{1,2,0:T(8,128)(2,1)S(1)} %pad_maximum_fusion.1), channel_id=1, source_target_pairs={{0,56},{8,0},{16,8},{24,16},{32,24},{40,32},{48,40},{56,48},{64,12... | collective-permute-start | bytes 589832 | tf_op jit(solution)/shard_map/ppermute | solution.py:80
  20.9 8.2 %collective-permute-start.6 = (bf16[3,128,256]{1,2,0:T(8,128)(2,1)S(1)}, bf16[3,128,256]{1,2,0:T(8,128)(2,1)S(1)}, u32[]{:S(2)}, u32[]{:S(2)}) collective-permute-start(bf16[3,128,256]{1,2,0:T(8,128)(2,1)S(1)} %pad_maximum_fusion.1), channel_id=1, source_target_pairs={{0,8},{8,16},{16,24},{24,32},{32,40},{40,48},{48,56},{56,0},{64,72... | collective-permute-start | bytes 589832 | tf_op jit(solution)/shard_map/ppermute | solution.py:80
  21.1 19.1 %collective-permute-start.5 = (bf16[2,128,256]{1,2,0:T(8,128)(2,1)S(1)}, bf16[2,128,256]{1,2,0:T(8,128)(2,1)S(1)}, u32[]{:S(2)}, u32[]{:S(2)}) collective-permute-start(bf16[2,128,256]{1,2,0:T(8,128)(2,1)S(1)} %constant_dynamic-slice_fusion.1), channel_id=1, source_target_pairs={{0,32},{8,40},{16,48},{24,56},{32,0},{40,8},{48,16},{56,24},{64,96... | collective-permute-start | bytes 393224 | tf_op jit(solution)/shard_map/ppermute | solution.py:69
  23.9 10.8 %collective-permute-start.3 = (bf16[3,128,256]{1,2,0:T(8,128)(2,1)S(1)}, bf16[3,128,256]{1,2,0:T(8,128)(2,1)S(1)}, u32[]{:S(2)}, u32[]{:S(2)}) collective-permute-start(bf16[3,128,256]{1,2,0:T(8,128)(2,1)S(1)} %collective-permute-done.2), channel_id=1, source_target_pairs={{0,56},{8,0},{16,8},{24,16},{32,24},{40,32},{48,40},{56,48},{64,12... | collective-permute-start | bytes 589832 | tf_op jit(solution)/shard_map/ppermute | solution.py:80
  29.1 9.1 %collective-permute-start.7 = (bf16[3,128,256]{1,2,0:T(8,128)(2,1)S(1)}, bf16[3,128,256]{1,2,0:T(8,128)(2,1)S(1)}, u32[]{:S(2)}, u32[]{:S(2)}) collective-permute-start(bf16[3,128,256]{1,2,0:T(8,128)(2,1)S(1)} %collective-permute-done.6), channel_id=1, source_target_pairs={{0,8},{8,16},{16,24},{24,32},{32,40},{40,48},{48,56},{56,0},{64,72... | collective-permute-start | bytes 589832 | tf_op jit(solution)/shard_map/ppermute | solution.py:80
  34.7 5.4 %collective-permute-start.4 = (bf16[2,128,256]{1,2,0:T(8,128)(2,1)S(1)}, bf16[2,128,256]{1,2,0:T(8,128)(2,1)S(1)}, u32[]{:S(2)}, u32[]{:S(2)}) collective-permute-start(bf16[2,128,256]{1,2,0:T(8,128)(2,1)S(1)} %constant_dynamic-slice_fusion.2), channel_id=1, source_target_pairs={{0,56},{8,0},{16,8},{24,16},{32,24},{40,32},{48,40},{56,48},{64,12... | collective-permute-start | bytes 393224 | tf_op jit(solution)/shard_map/ppermute | solution.py:80
  38.2 5.1 %collective-permute-start.8 = (bf16[2,128,256]{1,2,0:T(8,128)(2,1)S(1)}, bf16[2,128,256]{1,2,0:T(8,128)(2,1)S(1)}, u32[]{:S(2)}, u32[]{:S(2)}) collective-permute-start(bf16[2,128,256]{1,2,0:T(8,128)(2,1)S(1)} %constant_dynamic-slice_fusion), channel_id=1, source_target_pairs={{0,8},{8,16},{16,24},{24,32},{32,40},{40,48},{48,56},{56,0},{64,72... | collective-permute-start | bytes 393224 | tf_op jit(solution)/shard_map/ppermute | solution.py:80
  43.7 8.7 %slice-start = ((s8[8388608]{0:T(1024)(128)(4,1)}), s8[4194304]{0:T(1024)(128)(4,1)S(1)}, s32[]{:S(2)}) async-start(s8[8388608]{0:T(1024)(128)(4,1)} %bitcast.108), calls=%async_computation | async-start | bytes 8388608
  44.6 7.8 %slice-start.1 = ((s8[8388608]{0:T(1024)(128)(4,1)}), s8[4194304]{0:T(1024)(128)(4,1)S(1)}, s32[]{:S(2)}) async-start(s8[8388608]{0:T(1024)(128)(4,1)} %bitcast.108), calls=%async_computation.1 | async-start | bytes 8388608
  46.3 6.4 %collective-permute-start.9 = (bf16[128,512]{0,1:T(8,128)(2,1)S(1)}, bf16[128,512]{0,1:T(8,128)(2,1)S(1)}, u32[]{:S(2)}, u32[]{:S(2)}) collective-permute-start(bf16[128,512]{0,1:T(8,128)(2,1)S(1)} %bitcast.115), channel_id=1, source_target_pairs={{0,2},{1,3},{2,4},{3,5},{4,6},{5,7},{6,0},{7,1},{8,10},{9,11},{10,... | collective-permute-start | bytes 393224 | tf_op jit(solution)/shard_map/ppermute | solution.py:120
  47.6 5.2 %collective-permute-start.10 = (bf16[128,512]{0,1:T(8,128)(2,1)S(1)}, bf16[128,512]{0,1:T(8,128)(2,1)S(1)}, u32[]{:S(2)}, u32[]{:S(2)}) collective-permute-start(bf16[128,512]{0,1:T(8,128)(2,1)S(1)} %bitcast.116), channel_id=1, source_target_pairs={{0,6},{1,7},{2,0},{3,1},{4,2},{5,3},{6,4},{7,5},{8,14},{9,15},{10,... | collective-permute-start | bytes 393224 | tf_op jit(solution)/shard_map/ppermute | solution.py:121
  49.1 9.5 %collective-permute-start.11 = (bf16[128,512]{0,1:T(8,128)(2,1)S(1)}, bf16[128,512]{0,1:T(8,128)(2,1)S(1)}, u32[]{:S(2)}, u32[]{:S(2)}) collective-permute-start(bf16[128,512]{0,1:T(8,128)(2,1)S(1)} %bitcast.117), channel_id=1, source_target_pairs={{0,1},{1,0},{2,3},{3,2},{4,5},{5,4},{6,7},{7,6},{8,9},{9,8},{10,11... | collective-permute-start | bytes 393224 | tf_op jit(solution)/shard_map/ppermute | solution.py:123
  52.8 6.1 %collective-permute-start.12 = (bf16[128,512]{0,1:T(8,128)(2,1)S(1)}, bf16[128,512]{0,1:T(8,128)(2,1)S(1)}, u32[]{:S(2)}, u32[]{:S(2)}) collective-permute-start(bf16[128,512]{0,1:T(8,128)(2,1)S(1)} %broadcast_select_fusion), channel_id=1, source_target_pairs={{0,2},{1,7},{2,4},{3,1},{4,6},{5,3},{6,0},{7,5},{8,10},{9,15},{10,... | collective-permute-start | bytes 393224 | tf_op jit(solution)/shard_map/ppermute | solution.py:125
  54.2 8.0 %collective-permute-start.13 = (bf16[2,128,512]{1,2,0:T(8,128)(2,1)S(1)}, bf16[2,128,512]{1,2,0:T(8,128)(2,1)S(1)}, u32[]{:S(2)}, u32[]{:S(2)}) collective-permute-start(bf16[2,128,512]{1,2,0:T(8,128)(2,1)S(1)} %pad_maximum_fusion), channel_id=1, source_target_pairs={{0,1},{1,0},{2,3},{3,2},{4,5},{5,4},{6,7},{7,6},{8,9},{9,8},{10,11... | collective-permute-start | bytes 786440 | tf_op jit(solution)/shard_map/ppermute | solution.py:126
  58.9 4.4 %collective-permute-start.14 = (bf16[128,512]{0,1:T(8,128)(2,1)S(1)}, bf16[128,512]{0,1:T(8,128)(2,1)S(1)}, u32[]{:S(2)}, u32[]{:S(2)}) collective-permute-start(bf16[128,512]{0,1:T(8,128)(2,1)S(1)} %collective-permute-done.12), channel_id=1, source_target_pairs={{0,1},{1,0},{2,3},{3,2},{4,5},{5,4},{6,7},{7,6},{8,9},{9,8},{10,11... | collective-permute-start | bytes 393224 | tf_op jit(solution)/shard_map/ppermute | solution.py:127

commit v7 on v6

--- a/solution.py
+++ b/solution.py
@@ -121,19 +121,20 @@
         down = lax.ppermute(attended, "head", [(s, (s - 2) % n_head) for s in range(n_head)])
         swap = [(s, s ^ 1) for s in range(n_head)]
         partner = lax.ppermute(attended, "head", swap)
-        relay_pairs = [(s, (s + 2) % n_head) if s % 2 == 0 else (s, (s - 2) % n_head) for s in range(n_head)]
-        far = lax.ppermute(jnp.where(core == 0, up, down), "head", relay_pairs)
+        same_pairs = [(s, (s + 2) % n_head) if s % 2 == 0 else (s, (s - 2) % n_head) for s in range(n_head)]
+        far = lax.ppermute(jnp.where(core == 0, up, down), "head", same_pairs)
+        cross_pairs = [(s, (s + 1) % n_head) if s % 2 == 1 else (s, (s - 1) % n_head) for s in range(n_head)]
+        far_cross = lax.ppermute(jnp.where(core == 1, up, down), "head", cross_pairs)
         near_other = lax.ppermute(jnp.stack([up, down]), "head", swap)
-        far_other = lax.ppermute(far, "head", swap)
         other = head ^ 1
         total = project(attended, head)
         total = total + project(up, (head - 2) % n_head)
         total = total + project(down, (head + 2) % n_head)
         total = total + project(partner, other)
         total = total + project(far, (head + 4) % n_head)
+        total = total + project(far_cross, jnp.where(core == 0, head - 3, head + 3) % n_head)
         total = total + project(near_other[0], (other - 2) % n_head)
         total = total + project(near_other[1], (other + 2) % n_head)
-        total = total + project(far_other, (other + 4) % n_head)
         return total.astype(jnp.bfloat16)
 
     return on_device

time: 64.6 us -> 64 us (level)
  starting transfers between devices: 38.4 us -> 35.9 us
  waiting for transfers between devices: 12.5 us -> 14.3 us
    ppermute x1, starting transfers between devices: 3.95 us -> 0.09 us  [on_device(): near_other = lax.ppermute(jnp.stack([up, down]), 'head', swap)]
    ppermute x2, waiting for transfers between devices: 0.01 us -> 1.81 us  [the longest x1 1.81 us: on_device(): lax.ppermute(jnp.where(core == 1, up, down), 'head', cross_pairs)]
    ppermute x2, starting transfers between devices: 4.42 us -> 5.78 us  [the longest x1 4.38 us: on_device(): lax.ppermute(jnp.where(core == 1, up, down), 'head', cross_pairs)]
  transfers between devices with their start and end apart: 15 -> 15, of which waited for: 4 -> 5; matrix products, arithmetic and copies ran while one was open for 8% -> 7% of each run, Pallas kernels for 0% -> 0%
where the time goes in v7:
time: 64 us; the launch traced here: 63.7 us
  starting transfers between devices  35.9 us (56%)
  waiting for transfers between devices  14.3 us (22%)
  matrix products  5.18 us (8%)
  local copies, waits for them, and re-layouts  4.17 us (7%)
  other arithmetic  3.51 us (5%)
  between operations  0.64 us (1%)
    ppermute x6, waiting for transfers between devices, on_device(): lax.ppermute(lax.dynamic_slice_in_dim(packet, lo, step['width'], 0), 'ctx...  12.5 us
    ppermute x6, starting transfers between devices, on_device(): lax.ppermute(lax.dynamic_slice_in_dim(packet, lo, step['width'], 0), 'ctx...  12.5 us
    ppermute x2, starting transfers between devices, on_device(): lax.ppermute(own, 'ctx', [(s, s + shift) for s in range(n_ctx - shift)])  8.55 us
    ppermute x1, starting transfers between devices, on_device(): lax.ppermute(jnp.where(core == 1, up, down), 'head', cross_pairs)  4.38 us
    dot_general x8, matrix products, project(): return jnp.dot(piece, rows, preferred_element_type=jnp.float32)  3.44 us
    unnamed x25, local copies, waits for them, and re-layouts  3.37 us
    ppermute x1, starting transfers between devices, on_device(): partner = lax.ppermute(attended, 'head', swap)  3.33 us
    ppermute x1, starting transfers between devices, on_device(): lax.ppermute(lax.dynamic_slice_in_dim(bundle, lo, rows_back, 0), 'ctx', [...  2.86 us
  transfers between devices with their start and end apart: 15, of which 5 were waited for; matrix products, arithmetic and copies ran while one was open for 7% of the time, Pallas kernels for 0%

profile of v7, /device:TPU:1, one launch (start us, length us, event | category | flops | bytes accessed | tf_op | source)
XLA Modules:
  0.0 63.7 jit_solution(7002576480503170734)
XLA Ops:
  1.7 0.9 %copy.22 = bf16[128,128]{0,1:T(8,128)(2,1)S(1)} copy(bf16[128,128]{1,0:T(8,128)(2,1)} %param.6) | data formatting | bytes 65536 | tf_op args[1]
  2.6 0.9 %copy.23 = bf16[128,128]{0,1:T(8,128)(2,1)S(1)} copy(bf16[128,128]{1,0:T(8,128)(2,1)} %param.7) | data formatting | bytes 65536 | tf_op args[2]
  3.7 4.0 %collective-permute-start.1 = (bf16[128,256]{0,1:T(8,128)(2,1)S(1)}, bf16[128,256]{0,1:T(8,128)(2,1)S(1)}, u32[]{:S(2)}, u32[]{:S(2)}) collective-permute-start(bf16[128,256]{0,1:T(8,128)(2,1)S(1)} %get-tuple-element.14), channel_id=1, source_target_pairs={{0,64},{8,72},{16,80},{24,88},{32,96},{40,104},{48,112},{56,120},{... | collective-permute-start | bytes 196616 | tf_op jit(solution)/shard_map/ppermute | solution.py:60
  7.7 4.5 %collective-permute-start = (bf16[128,256]{0,1:T(8,128)(2,1)S(1)}, bf16[128,256]{0,1:T(8,128)(2,1)S(1)}, u32[]{:S(2)}, u32[]{:S(2)}) collective-permute-start(bf16[128,256]{0,1:T(8,128)(2,1)S(1)} %get-tuple-element.14), channel_id=1, source_target_pairs={{0,128},{8,136},{16,144},{24,152},{32,160},{40,168},{48,176},{56,1... | collective-permute-start | bytes 196616 | tf_op jit(solution)/shard_map/ppermute | solution.py:60
  12.3 1.0 %copy.24 = bf16[128,512]{0,1:T(8,128)(2,1)S(1)} copy(bf16[128,512]{1,0:T(8,128)(2,1)} %param.5) | data formatting | bytes 262144 | tf_op args[0]
  13.3 1.0 %compare_and_fusion = pred[128,2176]{0,1:T(8,128)(4,1)S(1)} fusion(s32[128]{0:T(128)S(1)} %select_reduce_fusion, s32[128]{0:T(128)S(1)} %iota_add_fusion.1, s32[2176]{0:T(1024)S(1)} %iota_add_fusion), kind=kLoop, calls=%fused_computation.19 | loop fusion | flops 835584 | bytes 288256 | tf_op jit(solution)/shard_map/and | solution.py:98
  15.0 5.7 %collective-permute-start.2 = (bf16[3,128,256]{1,2,0:T(8,128)(2,1)S(1)}, bf16[3,128,256]{1,2,0:T(8,128)(2,1)S(1)}, u32[]{:S(2)}, u32[]{:S(2)}) collective-permute-start(bf16[3,128,256]{1,2,0:T(8,128)(2,1)S(1)} %pad_maximum_fusion.1), channel_id=1, source_target_pairs={{0,56},{8,0},{16,8},{24,16},{32,24},{40,32},{48,40},{56,48},{64,12... | collective-permute-start | bytes 589832 | tf_op jit(solution)/shard_map/ppermute | solution.py:80
  21.1 2.9 %collective-permute-start.5 = (bf16[2,128,256]{1,2,0:T(8,128)(2,1)S(1)}, bf16[2,128,256]{1,2,0:T(8,128)(2,1)S(1)}, u32[]{:S(2)}, u32[]{:S(2)}) collective-permute-start(bf16[2,128,256]{1,2,0:T(8,128)(2,1)S(1)} %constant_dynamic-slice_fusion.1), channel_id=1, source_target_pairs={{0,32},{8,40},{16,48},{24,56},{32,0},{40,8},{48,16},{56,24},{64,96... | collective-permute-start | bytes 393224 | tf_op jit(solution)/shard_map/ppermute | solution.py:69
  23.9 3.2 %collective-permute-start.3 = (bf16[3,128,256]{1,2,0:T(8,128)(2,1)S(1)}, bf16[3,128,256]{1,2,0:T(8,128)(2,1)S(1)}, u32[]{:S(2)}, u32[]{:S(2)}) collective-permute-start(bf16[3,128,256]{1,2,0:T(8,128)(2,1)S(1)} %collective-permute-done.2), channel_id=1, source_target_pairs={{0,56},{8,0},{16,8},{24,16},{32,24},{40,32},{48,40},{56,48},{64,12... | collective-permute-start | bytes 589832 | tf_op jit(solution)/shard_map/ppermute | solution.py:80
  27.1 2.0 %collective-permute-done.6 = bf16[3,128,256]{1,2,0:T(8,128)(2,1)S(1)} collective-permute-done((bf16[3,128,256]{1,2,0:T(8,128)(2,1)S(1)}, bf16[3,128,256]{1,2,0:T(8,128)(2,1)S(1)}, u32[]{:S(2)}, u32[]{:S(2)}) %collective-permute-start.6) | collective-permute-done | bytes 196640 | tf_op jit(solution)/shard_map/ppermute | solution.py:80
  29.1 5.6 %collective-permute-done.3 = bf16[3,128,256]{1,2,0:T(8,128)(2,1)S(1)} collective-permute-done((bf16[3,128,256]{1,2,0:T(8,128)(2,1)S(1)}, bf16[3,128,256]{1,2,0:T(8,128)(2,1)S(1)}, u32[]{:S(2)}, u32[]{:S(2)}) %collective-permute-start.3) | collective-permute-done | bytes 196640 | tf_op jit(solution)/shard_map/ppermute | solution.py:80
  34.7 3.5 %collective-permute-start.4 = (bf16[2,128,256]{1,2,0:T(8,128)(2,1)S(1)}, bf16[2,128,256]{1,2,0:T(8,128)(2,1)S(1)}, u32[]{:S(2)}, u32[]{:S(2)}) collective-permute-start(bf16[2,128,256]{1,2,0:T(8,128)(2,1)S(1)} %constant_dynamic-slice_fusion.2), channel_id=1, source_target_pairs={{0,56},{8,0},{16,8},{24,16},{32,24},{40,32},{48,40},{56,48},{64,12... | collective-permute-start | bytes 393224 | tf_op jit(solution)/shard_map/ppermute | solution.py:80
  38.4 1.8 %collective-permute-done.4 = bf16[2,128,256]{1,2,0:T(8,128)(2,1)S(1)} collective-permute-done((bf16[2,128,256]{1,2,0:T(8,128)(2,1)S(1)}, bf16[2,128,256]{1,2,0:T(8,128)(2,1)S(1)}, u32[]{:S(2)}, u32[]{:S(2)}) %collective-permute-start.4) | collective-permute-done | bytes 131104 | tf_op jit(solution)/shard_map/ppermute | solution.py:80
  40.2 3.1 %collective-permute-done.8 = bf16[2,128,256]{1,2,0:T(8,128)(2,1)S(1)} collective-permute-done((bf16[2,128,256]{1,2,0:T(8,128)(2,1)S(1)}, bf16[2,128,256]{1,2,0:T(8,128)(2,1)S(1)}, u32[]{:S(2)}, u32[]{:S(2)}) %collective-permute-start.8) | collective-permute-done | bytes 131104 | tf_op jit(solution)/shard_map/ppermute | solution.py:80
  43.7 0.8 %fusion.73 = (f32[4,128]{1,0:T(4,128)S(1)}, f32[1,4,128,2176]{2,3,1,0:T(8,128)S(1)}) fusion(bf16[128,4,64]{2,0,1:T(8,128)(2,1)S(1)} %get-tuple-element.6, bf16[128,4,64]{2,0,1:T(8,128)(2,1)S(1)} %get-tuple-element.5, bf16[2176,256]{0,1:T(8,128)(2,1)S(1)} %constant_dynamic-update-slice_fusion, pred[128,2176]{0,1:T(8,128)(4,1)S(1)} %compare_and_fusion), kind=kOutput, calls=%fused_computation.115 | convolution fusion | flops 288816640 | bytes 5556224 | tf_op jit(solution)/shard_map/tkgd,nkd->kgtn/dot_general | solution.py:94
  44.6 0.8 %fusion.2 = f32[4,128]{1,0:T(4,128)S(1)} fusion(f32[1,4,128,2176]{2,3,1,0:T(8,128)S(1)} %get-tuple-element.18, f32[4,128]{1,0:T(4,128)S(1)} %get-tuple-element.17, pred[128,2176]{0,1:T(8,128)(4,1)S(1)} %compare_and_fusion), kind=kLoop, calls=%fused_computation.4 | loop fusion | flops 3341824 | bytes 4739072 | tf_op jit(solution)/shard_map/reduce_sum | solution.py:102
  45.4 0.9 %fusion.19 = bf16[4,128,128]{1,2,0:T(8,128)(2,1)S(1)} fusion(f32[1,4,128,2176]{2,3,1,0:T(8,128)S(1)} %get-tuple-element.18, f32[4,128]{1,0:T(4,128)S(1)} %get-tuple-element.17, pred[128,2176]{0,1:T(8,128)(4,1)S(1)} %compare_and_fusion, bf16[2176,256]{0,1:T(8,128)(2,1)S(1)} %constant_dynamic-update-slice_fusion, f32[4,128]{1,0:T(4,128)S(1)} %fusion.2), kind=kOutput, calls=%fused_computation.21 | convolution fusion | flops 288686080 | bytes 5427200 | tf_op jit(solution)/shard_map/kgtn,nkd->kgtd/dot_general | solution.py:103
  46.3 1.3 %collective-permute-start.9 = (bf16[128,512]{0,1:T(8,128)(2,1)S(1)}, bf16[128,512]{0,1:T(8,128)(2,1)S(1)}, u32[]{:S(2)}, u32[]{:S(2)}) collective-permute-start(bf16[128,512]{0,1:T(8,128)(2,1)S(1)} %bitcast.115), channel_id=1, source_target_pairs={{0,2},{1,3},{2,4},{3,5},{4,6},{5,7},{6,0},{7,1},{8,10},{9,11},{10,... | collective-permute-start | bytes 393224 | tf_op jit(solution)/shard_map/ppermute | solution.py:120
  47.6 1.5 %collective-permute-start.10 = (bf16[128,512]{0,1:T(8,128)(2,1)S(1)}, bf16[128,512]{0,1:T(8,128)(2,1)S(1)}, u32[]{:S(2)}, u32[]{:S(2)}) collective-permute-start(bf16[128,512]{0,1:T(8,128)(2,1)S(1)} %bitcast.116), channel_id=1, source_target_pairs={{0,6},{1,7},{2,0},{3,1},{4,2},{5,3},{6,4},{7,5},{8,14},{9,15},{10,... | collective-permute-start | bytes 393224 | tf_op jit(solution)/shard_map/ppermute | solution.py:121
  49.1 3.3 %collective-permute-start.11 = (bf16[128,512]{0,1:T(8,128)(2,1)S(1)}, bf16[128,512]{0,1:T(8,128)(2,1)S(1)}, u32[]{:S(2)}, u32[]{:S(2)}) collective-permute-start(bf16[128,512]{0,1:T(8,128)(2,1)S(1)} %bitcast.117), channel_id=1, source_target_pairs={{0,1},{1,0},{2,3},{3,2},{4,5},{5,4},{6,7},{7,6},{8,9},{9,8},{10,11... | collective-permute-start | bytes 393224 | tf_op jit(solution)/shard_map/ppermute | solution.py:123
  52.8 1.4 %collective-permute-start.12 = (bf16[128,512]{0,1:T(8,128)(2,1)S(1)}, bf16[128,512]{0,1:T(8,128)(2,1)S(1)}, u32[]{:S(2)}, u32[]{:S(2)}) collective-permute-start(bf16[128,512]{0,1:T(8,128)(2,1)S(1)} %get-tuple-element.7), channel_id=1, source_target_pairs={{0,2},{1,7},{2,4},{3,1},{4,6},{5,3},{6,0},{7,5},{8,10},{9,15},{10,... | collective-permute-start | bytes 393224 | tf_op jit(solution)/shard_map/ppermute | solution.py:125
  54.2 4.4 %collective-permute-start.13 = (bf16[128,512]{0,1:T(8,128)(2,1)S(1)}, bf16[128,512]{0,1:T(8,128)(2,1)S(1)}, u32[]{:S(2)}, u32[]{:S(2)}) collective-permute-start(bf16[128,512]{0,1:T(8,128)(2,1)S(1)} %get-tuple-element.8), channel_id=1, source_target_pairs={{0,7},{1,2},{2,1},{3,4},{4,3},{5,6},{6,5},{7,0},{8,15},{9,10},{10,... | collective-permute-start | bytes 393224 | tf_op jit(solution)/shard_map/ppermute | solution.py:127
  59.7 1.8 %collective-permute-done.13 = bf16[128,512]{0,1:T(8,128)(2,1)S(1)} collective-permute-done((bf16[128,512]{0,1:T(8,128)(2,1)S(1)}, bf16[128,512]{0,1:T(8,128)(2,1)S(1)}, u32[]{:S(2)}, u32[]{:S(2)}) %collective-permute-start.13) | collective-permute-done | bytes 131104 | tf_op jit(solution)/shard_map/ppermute | solution.py:127
  62.6 1.1 %fusion.15 = bf16[128,1024]{1,0:T(8,128)(2,1)} fusion(f32[128,1024]{1,0:T(8,128)S(1)} %fusion.22, f32[128,1024]{1,0:T(8,128)S(1)} %fusion.24, f32[128,1024]{1,0:T(8,128)S(1)} %fusion.26, f32[128,1024]{1,0:T(8,128)S(1)} %fusion.28, f32[128,1024]{1,0:T(8,128)S(1)} %fusion.30, f32[128,1024]{1,0:T(8,128)S(1)} %convolution_add_fusion.1, ...), kind=kOutput, calls=%fused_computation.18 | convolution fusion | flops 135135232 | bytes 4587524 | tf_op jit(solution)/shard_map/dot_general | solution.py:118
  (66 shorter events, 5.7 us)
Async XLA Ops:
  3.7 11.3 %collective-permute-start.1 = (bf16[128,256]{0,1:T(8,128)(2,1)S(1)}, bf16[128,256]{0,1:T(8,128)(2,1)S(1)}, u32[]{:S(2)}, u32[]{:S(2)}) collective-permute-start(bf16[128,256]{0,1:T(8,128)(2,1)S(1)} %get-tuple-element.14), channel_id=1, source_target_pairs={{0,64},{8,72},{16,80},{24,88},{32,96},{40,104},{48,112},{56,120},{... | collective-permute-start | bytes 196616 | tf_op jit(solution)/shard_map/ppermute | solution.py:60
  7.7 7.3 %collective-permute-start = (bf16[128,256]{0,1:T(8,128)(2,1)S(1)}, bf16[128,256]{0,1:T(8,128)(2,1)S(1)}, u32[]{:S(2)}, u32[]{:S(2)}) collective-permute-start(bf16[128,256]{0,1:T(8,128)(2,1)S(1)} %get-tuple-element.14), channel_id=1, source_target_pairs={{0,128},{8,136},{16,144},{24,152},{32,160},{40,168},{48,176},{56,1... | collective-permute-start | bytes 196616 | tf_op jit(solution)/shard_map/ppermute | solution.py:60
  15.0 8.9 %collective-permute-start.2 = (bf16[3,128,256]{1,2,0:T(8,128)(2,1)S(1)}, bf16[3,128,256]{1,2,0:T(8,128)(2,1)S(1)}, u32[]{:S(2)}, u32[]{:S(2)}) collective-permute-start(bf16[3,128,256]{1,2,0:T(8,128)(2,1)S(1)} %pad_maximum_fusion.1), channel_id=1, source_target_pairs={{0,56},{8,0},{16,8},{24,16},{32,24},{40,32},{48,40},{56,48},{64,12... | collective-permute-start | bytes 589832 | tf_op jit(solution)/shard_map/ppermute | solution.py:80
  21.0 8.2 %collective-permute-start.6 = (bf16[3,128,256]{1,2,0:T(8,128)(2,1)S(1)}, bf16[3,128,256]{1,2,0:T(8,128)(2,1)S(1)}, u32[]{:S(2)}, u32[]{:S(2)}) collective-permute-start(bf16[3,128,256]{1,2,0:T(8,128)(2,1)S(1)} %pad_maximum_fusion.1), channel_id=1, source_target_pairs={{0,8},{8,16},{16,24},{24,32},{32,40},{40,48},{48,56},{56,0},{64,72... | collective-permute-start | bytes 589832 | tf_op jit(solution)/shard_map/ppermute | solution.py:80
  21.1 19.1 %collective-permute-start.5 = (bf16[2,128,256]{1,2,0:T(8,128)(2,1)S(1)}, bf16[2,128,256]{1,2,0:T(8,128)(2,1)S(1)}, u32[]{:S(2)}, u32[]{:S(2)}) collective-permute-start(bf16[2,128,256]{1,2,0:T(8,128)(2,1)S(1)} %constant_dynamic-slice_fusion.1), channel_id=1, source_target_pairs={{0,32},{8,40},{16,48},{24,56},{32,0},{40,8},{48,16},{56,24},{64,96... | collective-permute-start | bytes 393224 | tf_op jit(solution)/shard_map/ppermute | solution.py:69
  23.9 10.8 %collective-permute-start.3 = (bf16[3,128,256]{1,2,0:T(8,128)(2,1)S(1)}, bf16[3,128,256]{1,2,0:T(8,128)(2,1)S(1)}, u32[]{:S(2)}, u32[]{:S(2)}) collective-permute-start(bf16[3,128,256]{1,2,0:T(8,128)(2,1)S(1)} %collective-permute-done.2), channel_id=1, source_target_pairs={{0,56},{8,0},{16,8},{24,16},{32,24},{40,32},{48,40},{56,48},{64,12... | collective-permute-start | bytes 589832 | tf_op jit(solution)/shard_map/ppermute | solution.py:80
  29.1 9.1 %collective-permute-start.7 = (bf16[3,128,256]{1,2,0:T(8,128)(2,1)S(1)}, bf16[3,128,256]{1,2,0:T(8,128)(2,1)S(1)}, u32[]{:S(2)}, u32[]{:S(2)}) collective-permute-start(bf16[3,128,256]{1,2,0:T(8,128)(2,1)S(1)} %collective-permute-done.6), channel_id=1, source_target_pairs={{0,8},{8,16},{16,24},{24,32},{32,40},{40,48},{48,56},{56,0},{64,72... | collective-permute-start | bytes 589832 | tf_op jit(solution)/shard_map/ppermute | solution.py:80
  34.7 5.4 %collective-permute-start.4 = (bf16[2,128,256]{1,2,0:T(8,128)(2,1)S(1)}, bf16[2,128,256]{1,2,0:T(8,128)(2,1)S(1)}, u32[]{:S(2)}, u32[]{:S(2)}) collective-permute-start(bf16[2,128,256]{1,2,0:T(8,128)(2,1)S(1)} %constant_dynamic-slice_fusion.2), channel_id=1, source_target_pairs={{0,56},{8,0},{16,8},{24,16},{32,24},{40,32},{48,40},{56,48},{64,12... | collective-permute-start | bytes 393224 | tf_op jit(solution)/shard_map/ppermute | solution.py:80
  38.2 5.1 %collective-permute-start.8 = (bf16[2,128,256]{1,2,0:T(8,128)(2,1)S(1)}, bf16[2,128,256]{1,2,0:T(8,128)(2,1)S(1)}, u32[]{:S(2)}, u32[]{:S(2)}) collective-permute-start(bf16[2,128,256]{1,2,0:T(8,128)(2,1)S(1)} %constant_dynamic-slice_fusion), channel_id=1, source_target_pairs={{0,8},{8,16},{16,24},{24,32},{32,40},{40,48},{48,56},{56,0},{64,72... | collective-permute-start | bytes 393224 | tf_op jit(solution)/shard_map/ppermute | solution.py:80
  43.7 8.7 %slice-start = ((s8[8388608]{0:T(1024)(128)(4,1)}), s8[4194304]{0:T(1024)(128)(4,1)S(1)}, s32[]{:S(2)}) async-start(s8[8388608]{0:T(1024)(128)(4,1)} %bitcast.108), calls=%async_computation | async-start | bytes 8388608
  44.6 7.8 %slice-start.1 = ((s8[8388608]{0:T(1024)(128)(4,1)}), s8[4194304]{0:T(1024)(128)(4,1)S(1)}, s32[]{:S(2)}) async-start(s8[8388608]{0:T(1024)(128)(4,1)} %bitcast.108), calls=%async_computation.1 | async-start | bytes 8388608
  46.3 6.4 %collective-permute-start.9 = (bf16[128,512]{0,1:T(8,128)(2,1)S(1)}, bf16[128,512]{0,1:T(8,128)(2,1)S(1)}, u32[]{:S(2)}, u32[]{:S(2)}) collective-permute-start(bf16[128,512]{0,1:T(8,128)(2,1)S(1)} %bitcast.115), channel_id=1, source_target_pairs={{0,2},{1,3},{2,4},{3,5},{4,6},{5,7},{6,0},{7,1},{8,10},{9,11},{10,... | collective-permute-start | bytes 393224 | tf_op jit(solution)/shard_map/ppermute | solution.py:120
  47.6 5.2 %collective-permute-start.10 = (bf16[128,512]{0,1:T(8,128)(2,1)S(1)}, bf16[128,512]{0,1:T(8,128)(2,1)S(1)}, u32[]{:S(2)}, u32[]{:S(2)}) collective-permute-start(bf16[128,512]{0,1:T(8,128)(2,1)S(1)} %bitcast.116), channel_id=1, source_target_pairs={{0,6},{1,7},{2,0},{3,1},{4,2},{5,3},{6,4},{7,5},{8,14},{9,15},{10,... | collective-permute-start | bytes 393224 | tf_op jit(solution)/shard_map/ppermute | solution.py:121
  49.1 10.0 %collective-permute-start.11 = (bf16[128,512]{0,1:T(8,128)(2,1)S(1)}, bf16[128,512]{0,1:T(8,128)(2,1)S(1)}, u32[]{:S(2)}, u32[]{:S(2)}) collective-permute-start(bf16[128,512]{0,1:T(8,128)(2,1)S(1)} %bitcast.117), channel_id=1, source_target_pairs={{0,1},{1,0},{2,3},{3,2},{4,5},{5,4},{6,7},{7,6},{8,9},{9,8},{10,11... | collective-permute-start | bytes 393224 | tf_op jit(solution)/shard_map/ppermute | solution.py:123
  52.8 6.6 %collective-permute-start.12 = (bf16[128,512]{0,1:T(8,128)(2,1)S(1)}, bf16[128,512]{0,1:T(8,128)(2,1)S(1)}, u32[]{:S(2)}, u32[]{:S(2)}) collective-permute-start(bf16[128,512]{0,1:T(8,128)(2,1)S(1)} %get-tuple-element.7), channel_id=1, source_target_pairs={{0,2},{1,7},{2,4},{3,1},{4,6},{5,3},{6,0},{7,5},{8,10},{9,15},{10,... | collective-permute-start | bytes 393224 | tf_op jit(solution)/shard_map/ppermute | solution.py:125
  54.2 7.4 %collective-permute-start.13 = (bf16[128,512]{0,1:T(8,128)(2,1)S(1)}, bf16[128,512]{0,1:T(8,128)(2,1)S(1)}, u32[]{:S(2)}, u32[]{:S(2)}) collective-permute-start(bf16[128,512]{0,1:T(8,128)(2,1)S(1)} %get-tuple-element.8), channel_id=1, source_target_pairs={{0,7},{1,2},{2,1},{3,4},{4,3},{5,6},{6,5},{7,0},{8,15},{9,10},{10,... | collective-permute-start | bytes 393224 | tf_op jit(solution)/shard_map/ppermute | solution.py:127
  58.6 3.3 %collective-permute-start.14 = (bf16[2,128,512]{1,2,0:T(8,128)(2,1)S(1)}, bf16[2,128,512]{1,2,0:T(8,128)(2,1)S(1)}, u32[]{:S(2)}, u32[]{:S(2)}) collective-permute-start(bf16[2,128,512]{1,2,0:T(8,128)(2,1)S(1)} %pad_maximum_fusion), channel_id=1, source_target_pairs={{0,1},{1,0},{2,3},{3,2},{4,5},{5,4},{6,7},{7,6},{8,9},{9,8},{10,11... | collective-permute-start | bytes 786440 | tf_op jit(solution)/shard_map/ppermute | solution.py:128

commit v8 on v7

--- a/solution.py
+++ b/solution.py
@@ -11,7 +11,8 @@
 
 
 def doc_starts(lengths, positions):
-    doc_ends = jnp.cumsum(lengths)
+    idx = jnp.arange(lengths.shape[0])
+    doc_ends = jnp.sum(jnp.where(idx[None, :] <= idx[:, None], lengths[None, :], 0), axis=1)
     picked = jnp.where(doc_ends[None, :] <= positions[:, None], lengths[None, :], 0)
     return jnp.sum(picked, axis=1)
 

time: 64 us -> 63.9 us (level)
  local copies, waits for them, and re-layouts: 4.17 us -> 3.43 us
    reduce_sum x0 -> x1, other arithmetic: none -> 0.77 us  [doc_starts(): jnp.sum(jnp.where(idx[None, :] <= idx[:, None], lengths[None, :], 0), axi...]
    another operation x1 -> x0, local copies, waits for them, and re-layouts: 0.74 us -> none
where the time goes in v8:
time: 63.9 us; the launch traced here: 63.5 us
  starting transfers between devices  35.9 us (56%)
  waiting for transfers between devices  14.3 us (22%)
  matrix products  5.18 us (8%)
  other arithmetic  4.11 us (6%)
  local copies, waits for them, and re-layouts  3.43 us (5%)
    ppermute x6, waiting for transfers between devices, on_device(): lax.ppermute(lax.dynamic_slice_in_dim(packet, lo, step['width'], 0), 'ctx...  12.5 us
    ppermute x6, starting transfers between devices, on_device(): lax.ppermute(lax.dynamic_slice_in_dim(packet, lo, step['width'], 0), 'ctx...  12.5 us
    ppermute x2, starting transfers between devices, on_device(): lax.ppermute(own, 'ctx', [(s, s + shift) for s in range(n_ctx - shift)])  8.55 us
    ppermute x1, starting transfers between devices, on_device(): lax.ppermute(jnp.where(core == 1, up, down), 'head', cross_pairs)  4.19 us
    dot_general x8, matrix products, project(): return jnp.dot(piece, rows, preferred_element_type=jnp.float32)  3.43 us
    unnamed x25, local copies, waits for them, and re-layouts  3.37 us
    ppermute x1, starting transfers between devices, on_device(): partner = lax.ppermute(attended, 'head', swap)  3.32 us
    ppermute x1, starting transfers between devices, on_device(): lax.ppermute(lax.dynamic_slice_in_dim(bundle, lo, rows_back, 0), 'ctx', [...  2.86 us
  transfers between devices with their start and end apart: 15, of which 5 were waited for; matrix products, arithmetic and copies ran while one was open for 7% of the time, Pallas kernels for 0%

profile of v8, /device:TPU:1, one launch (start us, length us, event | category | flops | bytes accessed | tf_op | source)
XLA Modules:
  0.0 63.5 jit_solution(10329075258800600972)
XLA Ops:
  1.5 0.9 %copy.18 = bf16[128,128]{0,1:T(8,128)(2,1)S(1)} copy(bf16[128,128]{1,0:T(8,128)(2,1)} %param.6) | data formatting | bytes 65536 | tf_op args[1]
  2.4 0.9 %copy.19 = bf16[128,128]{0,1:T(8,128)(2,1)S(1)} copy(bf16[128,128]{1,0:T(8,128)(2,1)} %param.7) | data formatting | bytes 65536 | tf_op args[2]
  3.6 4.0 %collective-permute-start.1 = (bf16[128,256]{0,1:T(8,128)(2,1)S(1)}, bf16[128,256]{0,1:T(8,128)(2,1)S(1)}, u32[]{:S(2)}, u32[]{:S(2)}) collective-permute-start(bf16[128,256]{0,1:T(8,128)(2,1)S(1)} %get-tuple-element.14), channel_id=1, source_target_pairs={{0,64},{8,72},{16,80},{24,88},{32,96},{40,104},{48,112},{56,120},{... | collective-permute-start | bytes 196616 | tf_op jit(solution)/shard_map/ppermute | solution.py:61
  7.6 4.5 %collective-permute-start = (bf16[128,256]{0,1:T(8,128)(2,1)S(1)}, bf16[128,256]{0,1:T(8,128)(2,1)S(1)}, u32[]{:S(2)}, u32[]{:S(2)}) collective-permute-start(bf16[128,256]{0,1:T(8,128)(2,1)S(1)} %get-tuple-element.14), channel_id=1, source_target_pairs={{0,128},{8,136},{16,144},{24,152},{32,160},{40,168},{48,176},{56,1... | collective-permute-start | bytes 196616 | tf_op jit(solution)/shard_map/ppermute | solution.py:61
  12.1 1.0 %copy.20 = bf16[128,512]{0,1:T(8,128)(2,1)S(1)} copy(bf16[128,512]{1,0:T(8,128)(2,1)} %param.5) | data formatting | bytes 262144 | tf_op args[0]
  13.2 1.0 %compare_and_fusion = pred[128,2176]{0,1:T(8,128)(4,1)S(1)} fusion(s32[128]{0:T(128)S(1)} %select_reduce_fusion, s32[128]{0:T(128)S(1)} %iota_add_fusion.1, s32[2176]{0:T(1024)S(1)} %iota_add_fusion), kind=kLoop, calls=%fused_computation.19 | loop fusion | flops 835584 | bytes 288256 | tf_op jit(solution)/shard_map/and | solution.py:99
  14.9 5.7 %collective-permute-start.2 = (bf16[3,128,256]{1,2,0:T(8,128)(2,1)S(1)}, bf16[3,128,256]{1,2,0:T(8,128)(2,1)S(1)}, u32[]{:S(2)}, u32[]{:S(2)}) collective-permute-start(bf16[3,128,256]{1,2,0:T(8,128)(2,1)S(1)} %pad_maximum_fusion.1), channel_id=1, source_target_pairs={{0,56},{8,0},{16,8},{24,16},{32,24},{40,32},{48,40},{56,48},{64,12... | collective-permute-start | bytes 589832 | tf_op jit(solution)/shard_map/ppermute | solution.py:81
  20.9 2.9 %collective-permute-start.5 = (bf16[2,128,256]{1,2,0:T(8,128)(2,1)S(1)}, bf16[2,128,256]{1,2,0:T(8,128)(2,1)S(1)}, u32[]{:S(2)}, u32[]{:S(2)}) collective-permute-start(bf16[2,128,256]{1,2,0:T(8,128)(2,1)S(1)} %constant_dynamic-slice_fusion.1), channel_id=1, source_target_pairs={{0,32},{8,40},{16,48},{24,56},{32,0},{40,8},{48,16},{56,24},{64,96... | collective-permute-start | bytes 393224 | tf_op jit(solution)/shard_map/ppermute | solution.py:70
  23.8 3.2 %collective-permute-start.3 = (bf16[3,128,256]{1,2,0:T(8,128)(2,1)S(1)}, bf16[3,128,256]{1,2,0:T(8,128)(2,1)S(1)}, u32[]{:S(2)}, u32[]{:S(2)}) collective-permute-start(bf16[3,128,256]{1,2,0:T(8,128)(2,1)S(1)} %collective-permute-done.2), channel_id=1, source_target_pairs={{0,56},{8,0},{16,8},{24,16},{32,24},{40,32},{48,40},{56,48},{64,12... | collective-permute-start | bytes 589832 | tf_op jit(solution)/shard_map/ppermute | solution.py:81
  27.0 2.0 %collective-permute-done.6 = bf16[3,128,256]{1,2,0:T(8,128)(2,1)S(1)} collective-permute-done((bf16[3,128,256]{1,2,0:T(8,128)(2,1)S(1)}, bf16[3,128,256]{1,2,0:T(8,128)(2,1)S(1)}, u32[]{:S(2)}, u32[]{:S(2)}) %collective-permute-start.6) | collective-permute-done | bytes 196640 | tf_op jit(solution)/shard_map/ppermute | solution.py:81
  29.0 5.6 %collective-permute-done.3 = bf16[3,128,256]{1,2,0:T(8,128)(2,1)S(1)} collective-permute-done((bf16[3,128,256]{1,2,0:T(8,128)(2,1)S(1)}, bf16[3,128,256]{1,2,0:T(8,128)(2,1)S(1)}, u32[]{:S(2)}, u32[]{:S(2)}) %collective-permute-start.3) | collective-permute-done | bytes 196640 | tf_op jit(solution)/shard_map/ppermute | solution.py:81
  34.6 3.5 %collective-permute-start.4 = (bf16[2,128,256]{1,2,0:T(8,128)(2,1)S(1)}, bf16[2,128,256]{1,2,0:T(8,128)(2,1)S(1)}, u32[]{:S(2)}, u32[]{:S(2)}) collective-permute-start(bf16[2,128,256]{1,2,0:T(8,128)(2,1)S(1)} %constant_dynamic-slice_fusion.2), channel_id=1, source_target_pairs={{0,56},{8,0},{16,8},{24,16},{32,24},{40,32},{48,40},{56,48},{64,12... | collective-permute-start | bytes 393224 | tf_op jit(solution)/shard_map/ppermute | solution.py:81
  38.2 1.8 %collective-permute-done.4 = bf16[2,128,256]{1,2,0:T(8,128)(2,1)S(1)} collective-permute-done((bf16[2,128,256]{1,2,0:T(8,128)(2,1)S(1)}, bf16[2,128,256]{1,2,0:T(8,128)(2,1)S(1)}, u32[]{:S(2)}, u32[]{:S(2)}) %collective-permute-start.4) | collective-permute-done | bytes 131104 | tf_op jit(solution)/shard_map/ppermute | solution.py:81
  40.1 3.1 %collective-permute-done.8 = bf16[2,128,256]{1,2,0:T(8,128)(2,1)S(1)} collective-permute-done((bf16[2,128,256]{1,2,0:T(8,128)(2,1)S(1)}, bf16[2,128,256]{1,2,0:T(8,128)(2,1)S(1)}, u32[]{:S(2)}, u32[]{:S(2)}) %collective-permute-start.8) | collective-permute-done | bytes 131104 | tf_op jit(solution)/shard_map/ppermute | solution.py:81
  43.6 0.8 %fusion.73 = (f32[4,128]{1,0:T(4,128)S(1)}, f32[1,4,128,2176]{2,3,1,0:T(8,128)S(1)}) fusion(bf16[128,4,64]{2,0,1:T(8,128)(2,1)S(1)} %get-tuple-element.6, bf16[128,4,64]{2,0,1:T(8,128)(2,1)S(1)} %get-tuple-element.5, bf16[2176,256]{0,1:T(8,128)(2,1)S(1)} %constant_dynamic-update-slice_fusion, pred[128,2176]{0,1:T(8,128)(4,1)S(1)} %compare_and_fusion), kind=kOutput, calls=%fused_computation.117 | convolution fusion | flops 288816640 | bytes 5556224 | tf_op jit(solution)/shard_map/tkgd,nkd->kgtn/dot_general | solution.py:95
  44.4 0.8 %fusion.2 = f32[4,128]{1,0:T(4,128)S(1)} fusion(f32[1,4,128,2176]{2,3,1,0:T(8,128)S(1)} %get-tuple-element.18, f32[4,128]{1,0:T(4,128)S(1)} %get-tuple-element.17, pred[128,2176]{0,1:T(8,128)(4,1)S(1)} %compare_and_fusion), kind=kLoop, calls=%fused_computation.4 | loop fusion | flops 3341824 | bytes 4739072 | tf_op jit(solution)/shard_map/reduce_sum | solution.py:103
  45.2 0.9 %fusion.19 = bf16[4,128,128]{1,2,0:T(8,128)(2,1)S(1)} fusion(f32[1,4,128,2176]{2,3,1,0:T(8,128)S(1)} %get-tuple-element.18, f32[4,128]{1,0:T(4,128)S(1)} %get-tuple-element.17, pred[128,2176]{0,1:T(8,128)(4,1)S(1)} %compare_and_fusion, bf16[2176,256]{0,1:T(8,128)(2,1)S(1)} %constant_dynamic-update-slice_fusion, f32[4,128]{1,0:T(4,128)S(1)} %fusion.2), kind=kOutput, calls=%fused_computation.21 | convolution fusion | flops 288686080 | bytes 5427200 | tf_op jit(solution)/shard_map/kgtn,nkd->kgtd/dot_general | solution.py:104
  46.2 1.3 %collective-permute-start.9 = (bf16[128,512]{0,1:T(8,128)(2,1)S(1)}, bf16[128,512]{0,1:T(8,128)(2,1)S(1)}, u32[]{:S(2)}, u32[]{:S(2)}) collective-permute-start(bf16[128,512]{0,1:T(8,128)(2,1)S(1)} %bitcast.114), channel_id=1, source_target_pairs={{0,2},{1,3},{2,4},{3,5},{4,6},{5,7},{6,0},{7,1},{8,10},{9,11},{10,... | collective-permute-start | bytes 393224 | tf_op jit(solution)/shard_map/ppermute | solution.py:121
  47.4 1.5 %collective-permute-start.10 = (bf16[128,512]{0,1:T(8,128)(2,1)S(1)}, bf16[128,512]{0,1:T(8,128)(2,1)S(1)}, u32[]{:S(2)}, u32[]{:S(2)}) collective-permute-start(bf16[128,512]{0,1:T(8,128)(2,1)S(1)} %bitcast.115), channel_id=1, source_target_pairs={{0,6},{1,7},{2,0},{3,1},{4,2},{5,3},{6,4},{7,5},{8,14},{9,15},{10,... | collective-permute-start | bytes 393224 | tf_op jit(solution)/shard_map/ppermute | solution.py:122
  48.9 3.3 %collective-permute-start.11 = (bf16[128,512]{0,1:T(8,128)(2,1)S(1)}, bf16[128,512]{0,1:T(8,128)(2,1)S(1)}, u32[]{:S(2)}, u32[]{:S(2)}) collective-permute-start(bf16[128,512]{0,1:T(8,128)(2,1)S(1)} %bitcast.116), channel_id=1, source_target_pairs={{0,1},{1,0},{2,3},{3,2},{4,5},{5,4},{6,7},{7,6},{8,9},{9,8},{10,11... | collective-permute-start | bytes 393224 | tf_op jit(solution)/shard_map/ppermute | solution.py:124
  52.6 1.6 %collective-permute-start.12 = (bf16[128,512]{0,1:T(8,128)(2,1)S(1)}, bf16[128,512]{0,1:T(8,128)(2,1)S(1)}, u32[]{:S(2)}, u32[]{:S(2)}) collective-permute-start(bf16[128,512]{0,1:T(8,128)(2,1)S(1)} %get-tuple-element.7), channel_id=1, source_target_pairs={{0,2},{1,7},{2,4},{3,1},{4,6},{5,3},{6,0},{7,5},{8,10},{9,15},{10,... | collective-permute-start | bytes 393224 | tf_op jit(solution)/shard_map/ppermute | solution.py:126
  54.2 4.2 %collective-permute-start.13 = (bf16[128,512]{0,1:T(8,128)(2,1)S(1)}, bf16[128,512]{0,1:T(8,128)(2,1)S(1)}, u32[]{:S(2)}, u32[]{:S(2)}) collective-permute-start(bf16[128,512]{0,1:T(8,128)(2,1)S(1)} %get-tuple-element.8), channel_id=1, source_target_pairs={{0,7},{1,2},{2,1},{3,4},{4,3},{5,6},{6,5},{7,0},{8,15},{9,10},{10,... | collective-permute-start | bytes 393224 | tf_op jit(solution)/shard_map/ppermute | solution.py:128
  59.6 1.8 %collective-permute-done.13 = bf16[128,512]{0,1:T(8,128)(2,1)S(1)} collective-permute-done((bf16[128,512]{0,1:T(8,128)(2,1)S(1)}, bf16[128,512]{0,1:T(8,128)(2,1)S(1)}, u32[]{:S(2)}, u32[]{:S(2)}) %collective-permute-start.13) | collective-permute-done | bytes 131104 | tf_op jit(solution)/shard_map/ppermute | solution.py:128
  62.4 1.1 %fusion.15 = bf16[128,1024]{1,0:T(8,128)(2,1)} fusion(f32[128,1024]{1,0:T(8,128)S(1)} %fusion.22, f32[128,1024]{1,0:T(8,128)S(1)} %fusion.24, f32[128,1024]{1,0:T(8,128)S(1)} %fusion.26, f32[128,1024]{1,0:T(8,128)S(1)} %fusion.28, f32[128,1024]{1,0:T(8,128)S(1)} %fusion.30, f32[128,1024]{1,0:T(8,128)S(1)} %convolution_add_fusion.1, ...), kind=kOutput, calls=%fused_computation.18 | convolution fusion | flops 135135232 | bytes 4587524 | tf_op jit(solution)/shard_map/dot_general | solution.py:119
  (64 shorter events, 5.5 us)
Async XLA Ops:
  3.6 11.3 %collective-permute-start.1 = (bf16[128,256]{0,1:T(8,128)(2,1)S(1)}, bf16[128,256]{0,1:T(8,128)(2,1)S(1)}, u32[]{:S(2)}, u32[]{:S(2)}) collective-permute-start(bf16[128,256]{0,1:T(8,128)(2,1)S(1)} %get-tuple-element.14), channel_id=1, source_target_pairs={{0,64},{8,72},{16,80},{24,88},{32,96},{40,104},{48,112},{56,120},{... | collective-permute-start | bytes 196616 | tf_op jit(solution)/shard_map/ppermute | solution.py:61
  7.6 7.3 %collective-permute-start = (bf16[128,256]{0,1:T(8,128)(2,1)S(1)}, bf16[128,256]{0,1:T(8,128)(2,1)S(1)}, u32[]{:S(2)}, u32[]{:S(2)}) collective-permute-start(bf16[128,256]{0,1:T(8,128)(2,1)S(1)} %get-tuple-element.14), channel_id=1, source_target_pairs={{0,128},{8,136},{16,144},{24,152},{32,160},{40,168},{48,176},{56,1... | collective-permute-start | bytes 196616 | tf_op jit(solution)/shard_map/ppermute | solution.py:61
  14.9 8.9 %collective-permute-start.2 = (bf16[3,128,256]{1,2,0:T(8,128)(2,1)S(1)}, bf16[3,128,256]{1,2,0:T(8,128)(2,1)S(1)}, u32[]{:S(2)}, u32[]{:S(2)}) collective-permute-start(bf16[3,128,256]{1,2,0:T(8,128)(2,1)S(1)} %pad_maximum_fusion.1), channel_id=1, source_target_pairs={{0,56},{8,0},{16,8},{24,16},{32,24},{40,32},{48,40},{56,48},{64,12... | collective-permute-start | bytes 589832 | tf_op jit(solution)/shard_map/ppermute | solution.py:81
  20.8 8.2 %collective-permute-start.6 = (bf16[3,128,256]{1,2,0:T(8,128)(2,1)S(1)}, bf16[3,128,256]{1,2,0:T(8,128)(2,1)S(1)}, u32[]{:S(2)}, u32[]{:S(2)}) collective-permute-start(bf16[3,128,256]{1,2,0:T(8,128)(2,1)S(1)} %pad_maximum_fusion.1), channel_id=1, source_target_pairs={{0,8},{8,16},{16,24},{24,32},{32,40},{40,48},{48,56},{56,0},{64,72... | collective-permute-start | bytes 589832 | tf_op jit(solution)/shard_map/ppermute | solution.py:81
  20.9 19.1 %collective-permute-start.5 = (bf16[2,128,256]{1,2,0:T(8,128)(2,1)S(1)}, bf16[2,128,256]{1,2,0:T(8,128)(2,1)S(1)}, u32[]{:S(2)}, u32[]{:S(2)}) collective-permute-start(bf16[2,128,256]{1,2,0:T(8,128)(2,1)S(1)} %constant_dynamic-slice_fusion.1), channel_id=1, source_target_pairs={{0,32},{8,40},{16,48},{24,56},{32,0},{40,8},{48,16},{56,24},{64,96... | collective-permute-start | bytes 393224 | tf_op jit(solution)/shard_map/ppermute | solution.py:70
  23.8 10.8 %collective-permute-start.3 = (bf16[3,128,256]{1,2,0:T(8,128)(2,1)S(1)}, bf16[3,128,256]{1,2,0:T(8,128)(2,1)S(1)}, u32[]{:S(2)}, u32[]{:S(2)}) collective-permute-start(bf16[3,128,256]{1,2,0:T(8,128)(2,1)S(1)} %collective-permute-done.2), channel_id=1, source_target_pairs={{0,56},{8,0},{16,8},{24,16},{32,24},{40,32},{48,40},{56,48},{64,12... | collective-permute-start | bytes 589832 | tf_op jit(solution)/shard_map/ppermute | solution.py:81
  29.0 9.1 %collective-permute-start.7 = (bf16[3,128,256]{1,2,0:T(8,128)(2,1)S(1)}, bf16[3,128,256]{1,2,0:T(8,128)(2,1)S(1)}, u32[]{:S(2)}, u32[]{:S(2)}) collective-permute-start(bf16[3,128,256]{1,2,0:T(8,128)(2,1)S(1)} %collective-permute-done.6), channel_id=1, source_target_pairs={{0,8},{8,16},{16,24},{24,32},{32,40},{40,48},{48,56},{56,0},{64,72... | collective-permute-start | bytes 589832 | tf_op jit(solution)/shard_map/ppermute | solution.py:81
  34.6 5.4 %collective-permute-start.4 = (bf16[2,128,256]{1,2,0:T(8,128)(2,1)S(1)}, bf16[2,128,256]{1,2,0:T(8,128)(2,1)S(1)}, u32[]{:S(2)}, u32[]{:S(2)}) collective-permute-start(bf16[2,128,256]{1,2,0:T(8,128)(2,1)S(1)} %constant_dynamic-slice_fusion.2), channel_id=1, source_target_pairs={{0,56},{8,0},{16,8},{24,16},{32,24},{40,32},{48,40},{56,48},{64,12... | collective-permute-start | bytes 393224 | tf_op jit(solution)/shard_map/ppermute | solution.py:81
  38.1 5.1 %collective-permute-start.8 = (bf16[2,128,256]{1,2,0:T(8,128)(2,1)S(1)}, bf16[2,128,256]{1,2,0:T(8,128)(2,1)S(1)}, u32[]{:S(2)}, u32[]{:S(2)}) collective-permute-start(bf16[2,128,256]{1,2,0:T(8,128)(2,1)S(1)} %constant_dynamic-slice_fusion), channel_id=1, source_target_pairs={{0,8},{8,16},{16,24},{24,32},{32,40},{40,48},{48,56},{56,0},{64,72... | collective-permute-start | bytes 393224 | tf_op jit(solution)/shard_map/ppermute | solution.py:81
  43.6 8.7 %slice-start = ((s8[8388608]{0:T(1024)(128)(4,1)}), s8[4194304]{0:T(1024)(128)(4,1)S(1)}, s32[]{:S(2)}) async-start(s8[8388608]{0:T(1024)(128)(4,1)} %bitcast.107), calls=%async_computation | async-start | bytes 8388608
  44.4 7.8 %slice-start.1 = ((s8[8388608]{0:T(1024)(128)(4,1)}), s8[4194304]{0:T(1024)(128)(4,1)S(1)}, s32[]{:S(2)}) async-start(s8[8388608]{0:T(1024)(128)(4,1)} %bitcast.107), calls=%async_computation.1 | async-start | bytes 8388608
  46.2 6.4 %collective-permute-start.9 = (bf16[128,512]{0,1:T(8,128)(2,1)S(1)}, bf16[128,512]{0,1:T(8,128)(2,1)S(1)}, u32[]{:S(2)}, u32[]{:S(2)}) collective-permute-start(bf16[128,512]{0,1:T(8,128)(2,1)S(1)} %bitcast.114), channel_id=1, source_target_pairs={{0,2},{1,3},{2,4},{3,5},{4,6},{5,7},{6,0},{7,1},{8,10},{9,11},{10,... | collective-permute-start | bytes 393224 | tf_op jit(solution)/shard_map/ppermute | solution.py:121
  47.4 5.1 %collective-permute-start.10 = (bf16[128,512]{0,1:T(8,128)(2,1)S(1)}, bf16[128,512]{0,1:T(8,128)(2,1)S(1)}, u32[]{:S(2)}, u32[]{:S(2)}) collective-permute-start(bf16[128,512]{0,1:T(8,128)(2,1)S(1)} %bitcast.115), channel_id=1, source_target_pairs={{0,6},{1,7},{2,0},{3,1},{4,2},{5,3},{6,4},{7,5},{8,14},{9,15},{10,... | collective-permute-start | bytes 393224 | tf_op jit(solution)/shard_map/ppermute | solution.py:122
  48.9 10.0 %collective-permute-start.11 = (bf16[128,512]{0,1:T(8,128)(2,1)S(1)}, bf16[128,512]{0,1:T(8,128)(2,1)S(1)}, u32[]{:S(2)}, u32[]{:S(2)}) collective-permute-start(bf16[128,512]{0,1:T(8,128)(2,1)S(1)} %bitcast.116), channel_id=1, source_target_pairs={{0,1},{1,0},{2,3},{3,2},{4,5},{5,4},{6,7},{7,6},{8,9},{9,8},{10,11... | collective-permute-start | bytes 393224 | tf_op jit(solution)/shard_map/ppermute | solution.py:124
  52.6 6.6 %collective-permute-start.12 = (bf16[128,512]{0,1:T(8,128)(2,1)S(1)}, bf16[128,512]{0,1:T(8,128)(2,1)S(1)}, u32[]{:S(2)}, u32[]{:S(2)}) collective-permute-start(bf16[128,512]{0,1:T(8,128)(2,1)S(1)} %get-tuple-element.7), channel_id=1, source_target_pairs={{0,2},{1,7},{2,4},{3,1},{4,6},{5,3},{6,0},{7,5},{8,10},{9,15},{10,... | collective-permute-start | bytes 393224 | tf_op jit(solution)/shard_map/ppermute | solution.py:126
  54.2 7.2 %collective-permute-start.13 = (bf16[128,512]{0,1:T(8,128)(2,1)S(1)}, bf16[128,512]{0,1:T(8,128)(2,1)S(1)}, u32[]{:S(2)}, u32[]{:S(2)}) collective-permute-start(bf16[128,512]{0,1:T(8,128)(2,1)S(1)} %get-tuple-element.8), channel_id=1, source_target_pairs={{0,7},{1,2},{2,1},{3,4},{4,3},{5,6},{6,5},{7,0},{8,15},{9,10},{10,... | collective-permute-start | bytes 393224 | tf_op jit(solution)/shard_map/ppermute | solution.py:128
  58.4 3.3 %collective-permute-start.14 = (bf16[2,128,512]{1,2,0:T(8,128)(2,1)S(1)}, bf16[2,128,512]{1,2,0:T(8,128)(2,1)S(1)}, u32[]{:S(2)}, u32[]{:S(2)}) collective-permute-start(bf16[2,128,512]{1,2,0:T(8,128)(2,1)S(1)} %pad_maximum_fusion), channel_id=1, source_target_pairs={{0,1},{1,0},{2,3},{3,2},{4,5},{5,4},{6,7},{7,6},{8,9},{9,8},{10,11... | collective-permute-start | bytes 786440 | tf_op jit(solution)/shard_map/ppermute | solution.py:129

commit v9 on v8

--- a/solution.py
+++ b/solution.py
@@ -53,7 +53,7 @@
         offsets = positions - starts
         q_rot = rotary(queries, offsets, HD).reshape(tok_rows, kv_local, query_group, HD)
         k_rot = rotary(key_proj, offsets, HD)
-        own = jnp.concatenate([k_rot, value_proj], axis=1)
+        own = jnp.stack([k_rot.T, value_proj], axis=0)
 
         bundle = [own]
         for m in range(1, rows_back + 1):
@@ -87,10 +87,9 @@
                 got = lax.dynamic_slice_in_dim(packet, at, len(step["blocks"]), 0)
                 for i, blk in enumerate(step["blocks"]):
                     blocks[blk] = got[i]
-        window = jnp.concatenate([blocks[span - k] for k in range(span + 1)], axis=0)
-        key_count = window.shape[0]
-        key_block = window[:, :kv_width].reshape(key_count, kv_local, HD)
-        value_block = window[:, kv_width:].reshape(key_count, kv_local, HD)
+        key_count = (span + 1) * tok_rows
+        key_block = jnp.concatenate([blocks[span - k][0] for k in range(span + 1)], axis=1).T.reshape(key_count, kv_local, HD)
+        value_block = jnp.concatenate([blocks[span - k][1] for k in range(span + 1)], axis=0).reshape(key_count, kv_local, HD)
 
         scores = jnp.einsum(
             "tkgd,nkd->kgtn", q_rot, key_block, preferred_element_type=jnp.float32

time: 63.9 us -> 63.7 us (level)
  local copies, waits for them, and re-layouts: 3.43 us -> 2.53 us
  other arithmetic: 4.11 us -> 4.86 us
    unnamed x25 -> x26, local copies, waits for them, and re-layouts: 3.37 us -> 2.47 us
    another operation x2, other arithmetic: 0.04 us -> 0.8 us  [on_device(): bundle = jnp.stack(bundle)]
where the time goes in v9:
time: 63.7 us; the launch traced here: 63.4 us
  starting transfers between devices  35.9 us (56%)
  waiting for transfers between devices  14.4 us (23%)
  matrix products  5.12 us (8%)
  other arithmetic  4.86 us (8%)
  local copies, waits for them, and re-layouts  2.53 us (4%)
  between operations  0.64 us (1%)
    ppermute x6, waiting for transfers between devices, on_device(): lax.ppermute(lax.dynamic_slice_in_dim(packet, lo, step['width'], 0), 'ctx...  12.5 us
    ppermute x6, starting transfers between devices, on_device(): lax.ppermute(lax.dynamic_slice_in_dim(packet, lo, step['width'], 0), 'ctx...  12.5 us
    ppermute x2, starting transfers between devices, on_device(): lax.ppermute(own, 'ctx', [(s, s + shift) for s in range(n_ctx - shift)])  8.55 us
    ppermute x1, starting transfers between devices, on_device(): lax.ppermute(jnp.where(core == 1, up, down), 'head', cross_pairs)  4.38 us
    dot_general x8, matrix products, project(): return jnp.dot(piece, rows, preferred_element_type=jnp.float32)  3.43 us
    ppermute x1, starting transfers between devices, on_device(): partner = lax.ppermute(attended, 'head', swap)  3.32 us
    ppermute x1, starting transfers between devices, on_device(): lax.ppermute(lax.dynamic_slice_in_dim(bundle, lo, rows_back, 0), 'ctx', [...  2.86 us
    unnamed x26, local copies, waits for them, and re-layouts  2.47 us
  transfers between devices with their start and end apart: 15, of which 5 were waited for; matrix products, arithmetic and copies ran while one was open for 7% of the time, Pallas kernels for 0%

profile of v9, /device:TPU:1, one launch (start us, length us, event | category | flops | bytes accessed | tf_op | source)
XLA Modules:
  0.0 63.4 jit_solution(338032384713450606)
XLA Ops:
  1.6 0.9 %copy.21 = bf16[128,128]{0,1:T(8,128)(2,1)S(1)} copy(bf16[128,128]{1,0:T(8,128)(2,1)} %param.6) | data formatting | bytes 65536 | tf_op args[1]
  2.7 0.8 %fusion.60 = (bf16[1,2,128,128]{3,2,1,0:T(8,128)(2,1)S(1)}, bf16[2,128,128]{2,1,0:T(8,128)(2,1)S(1)}) fusion(bf16[1,128,128]{2,1,0:T(8,128)(2,1)} %bitcast.196, bf16[1,128,128]{2,1,0:T(8,128)(2,1)S(1)} %fusion.49), kind=kLoop, calls=%fused_computation.151 | loop fusion | flops 32768 | bytes 196608 | tf_op jit(solution)/shard_map/stack | solution.py:63
  3.4 4.0 %collective-permute-start.1 = (bf16[2,128,128]{2,1,0:T(8,128)(2,1)S(1)}, bf16[2,128,128]{2,1,0:T(8,128)(2,1)S(1)}, u32[]{:S(2)}, u32[]{:S(2)}) collective-permute-start(bf16[2,128,128]{2,1,0:T(8,128)(2,1)S(1)} %get-tuple-element.46), channel_id=1, source_target_pairs={{0,64},{8,72},{16,80},{24,88},{32,96},{40,104},{48,112},{56,120},{... | collective-permute-start | bytes 196616 | tf_op jit(solution)/shard_map/ppermute | solution.py:61
  7.5 4.5 %collective-permute-start = (bf16[2,128,128]{2,1,0:T(8,128)(2,1)S(1)}, bf16[2,128,128]{2,1,0:T(8,128)(2,1)S(1)}, u32[]{:S(2)}, u32[]{:S(2)}) collective-permute-start(bf16[2,128,128]{2,1,0:T(8,128)(2,1)S(1)} %get-tuple-element.46), channel_id=1, source_target_pairs={{0,128},{8,136},{16,144},{24,152},{32,160},{40,168},{48,176},{56,1... | collective-permute-start | bytes 196616 | tf_op jit(solution)/shard_map/ppermute | solution.py:61
  12.0 1.0 %copy.22 = bf16[128,512]{0,1:T(8,128)(2,1)S(1)} copy(bf16[128,512]{1,0:T(8,128)(2,1)} %param.5) | data formatting | bytes 262144 | tf_op args[0]
  13.1 1.0 %compare_and_fusion = pred[128,2176]{0,1:T(8,128)(4,1)S(1)} fusion(s32[128]{0:T(128)S(1)} %select_reduce_fusion, s32[128]{0:T(128)S(1)} %iota_add_fusion.1, s32[2176]{0:T(1024)S(1)} %iota_add_fusion), kind=kLoop, calls=%fused_computation.19 | loop fusion | flops 835584 | bytes 288256 | tf_op jit(solution)/shard_map/and | solution.py:98
  14.8 5.7 %collective-permute-start.2 = (bf16[3,2,128,128]{3,2,1,0:T(8,128)(2,1)S(1)}, bf16[3,2,128,128]{3,2,1,0:T(8,128)(2,1)S(1)}, u32[]{:S(2)}, u32[]{:S(2)}) collective-permute-start(bf16[3,2,128,128]{3,2,1,0:T(8,128)(2,1)S(1)} %pad_maximum_fusion.1), channel_id=1, source_target_pairs={{0,56},{8,0},{16,8},{24,16},{32,24},{40,32},{48,40},{56,48},{64,12... | collective-permute-start | bytes 589832 | tf_op jit(solution)/shard_map/ppermute | solution.py:81
  20.8 2.9 %collective-permute-start.5 = (bf16[2,2,128,128]{3,2,1,0:T(8,128)(2,1)S(1)}, bf16[2,2,128,128]{3,2,1,0:T(8,128)(2,1)S(1)}, u32[]{:S(2)}, u32[]{:S(2)}) collective-permute-start(bf16[2,2,128,128]{3,2,1,0:T(8,128)(2,1)S(1)} %constant_dynamic-slice_fusion.1), channel_id=1, source_target_pairs={{0,32},{8,40},{16,48},{24,56},{32,0},{40,8},{48,16},{56,24},{64,96... | collective-permute-start | bytes 393224 | tf_op jit(solution)/shard_map/ppermute | solution.py:70
  23.7 3.2 %collective-permute-start.3 = (bf16[3,2,128,128]{3,2,1,0:T(8,128)(2,1)S(1)}, bf16[3,2,128,128]{3,2,1,0:T(8,128)(2,1)S(1)}, u32[]{:S(2)}, u32[]{:S(2)}) collective-permute-start(bf16[3,2,128,128]{3,2,1,0:T(8,128)(2,1)S(1)} %collective-permute-done.2), channel_id=1, source_target_pairs={{0,56},{8,0},{16,8},{24,16},{32,24},{40,32},{48,40},{56,48},{64,12... | collective-permute-start | bytes 589832 | tf_op jit(solution)/shard_map/ppermute | solution.py:81
  26.9 2.0 %collective-permute-done.6 = bf16[3,2,128,128]{3,2,1,0:T(8,128)(2,1)S(1)} collective-permute-done((bf16[3,2,128,128]{3,2,1,0:T(8,128)(2,1)S(1)}, bf16[3,2,128,128]{3,2,1,0:T(8,128)(2,1)S(1)}, u32[]{:S(2)}, u32[]{:S(2)}) %collective-permute-start.6) | collective-permute-done | bytes 196640 | tf_op jit(solution)/shard_map/ppermute | solution.py:81
  28.9 5.6 %collective-permute-done.3 = bf16[3,2,128,128]{3,2,1,0:T(8,128)(2,1)S(1)} collective-permute-done((bf16[3,2,128,128]{3,2,1,0:T(8,128)(2,1)S(1)}, bf16[3,2,128,128]{3,2,1,0:T(8,128)(2,1)S(1)}, u32[]{:S(2)}, u32[]{:S(2)}) %collective-permute-start.3) | collective-permute-done | bytes 196640 | tf_op jit(solution)/shard_map/ppermute | solution.py:81
  34.5 3.5 %collective-permute-start.4 = (bf16[2,2,128,128]{3,2,1,0:T(8,128)(2,1)S(1)}, bf16[2,2,128,128]{3,2,1,0:T(8,128)(2,1)S(1)}, u32[]{:S(2)}, u32[]{:S(2)}) collective-permute-start(bf16[2,2,128,128]{3,2,1,0:T(8,128)(2,1)S(1)} %constant_dynamic-slice_fusion.2), channel_id=1, source_target_pairs={{0,56},{8,0},{16,8},{24,16},{32,24},{40,32},{48,40},{56,48},{64,12... | collective-permute-start | bytes 393224 | tf_op jit(solution)/shard_map/ppermute | solution.py:81
  38.1 1.8 %collective-permute-done.4 = bf16[2,2,128,128]{3,2,1,0:T(8,128)(2,1)S(1)} collective-permute-done((bf16[2,2,128,128]{3,2,1,0:T(8,128)(2,1)S(1)}, bf16[2,2,128,128]{3,2,1,0:T(8,128)(2,1)S(1)}, u32[]{:S(2)}, u32[]{:S(2)}) %collective-permute-start.4) | collective-permute-done | bytes 131104 | tf_op jit(solution)/shard_map/ppermute | solution.py:81
  40.0 3.1 %collective-permute-done.8 = bf16[2,2,128,128]{3,2,1,0:T(8,128)(2,1)S(1)} collective-permute-done((bf16[2,2,128,128]{3,2,1,0:T(8,128)(2,1)S(1)}, bf16[2,2,128,128]{3,2,1,0:T(8,128)(2,1)S(1)}, u32[]{:S(2)}, u32[]{:S(2)}) %collective-permute-start.8) | collective-permute-done | bytes 131104 | tf_op jit(solution)/shard_map/ppermute | solution.py:81
  43.5 0.8 %fusion.62 = (f32[4,128]{1,0:T(4,128)S(1)}, f32[1,4,128,2176]{2,3,1,0:T(8,128)S(1)}) fusion(bf16[128,4,64]{2,0,1:T(8,128)(2,1)S(1)} %get-tuple-element.6, bf16[128,4,64]{2,0,1:T(8,128)(2,1)S(1)} %get-tuple-element.5, bf16[128,2176]{1,0:T(8,128)(2,1)S(1)} %get-tuple-element.51, pred[128,2176]{0,1:T(8,128)(4,1)S(1)} %compare_and_fusion), kind=kOutput, calls=%fused_computation.153 | convolution fusion | flops 288816640 | bytes 5425152 | tf_op jit(solution)/shard_map/tkgd,nkd->kgtn/dot_general | solution.py:94
  44.3 0.8 %fusion.2 = f32[4,128]{1,0:T(4,128)S(1)} fusion(f32[1,4,128,2176]{2,3,1,0:T(8,128)S(1)} %get-tuple-element.50, f32[4,128]{1,0:T(4,128)S(1)} %get-tuple-element.49, pred[128,2176]{0,1:T(8,128)(4,1)S(1)} %compare_and_fusion), kind=kLoop, calls=%fused_computation.4 | loop fusion | flops 3341824 | bytes 4739072 | tf_op jit(solution)/shard_map/reduce_sum | solution.py:102
  45.1 0.8 %fusion.19 = bf16[4,128,128]{1,2,0:T(8,128)(2,1)S(1)} fusion(f32[1,4,128,2176]{2,3,1,0:T(8,128)S(1)} %get-tuple-element.50, f32[4,128]{1,0:T(4,128)S(1)} %get-tuple-element.49, pred[128,2176]{0,1:T(8,128)(4,1)S(1)} %compare_and_fusion, bf16[2176,128]{1,0:T(8,128)(2,1)S(1)} %get-tuple-element.52, f32[4,128]{1,0:T(4,128)S(1)} %fusion.2), kind=kOutput, calls=%fused_computation.21 | convolution fusion | flops 288686080 | bytes 5427200 | tf_op jit(solution)/shard_map/kgtn,nkd->kgtd/dot_general | solution.py:103
  46.0 1.3 %collective-permute-start.9 = (bf16[128,512]{0,1:T(8,128)(2,1)S(1)}, bf16[128,512]{0,1:T(8,128)(2,1)S(1)}, u32[]{:S(2)}, u32[]{:S(2)}) collective-permute-start(bf16[128,512]{0,1:T(8,128)(2,1)S(1)} %bitcast.192), channel_id=1, source_target_pairs={{0,2},{1,3},{2,4},{3,5},{4,6},{5,7},{6,0},{7,1},{8,10},{9,11},{10,... | collective-permute-start | bytes 393224 | tf_op jit(solution)/shard_map/ppermute | solution.py:120
  47.3 1.5 %collective-permute-start.10 = (bf16[128,512]{0,1:T(8,128)(2,1)S(1)}, bf16[128,512]{0,1:T(8,128)(2,1)S(1)}, u32[]{:S(2)}, u32[]{:S(2)}) collective-permute-start(bf16[128,512]{0,1:T(8,128)(2,1)S(1)} %bitcast.193), channel_id=1, source_target_pairs={{0,6},{1,7},{2,0},{3,1},{4,2},{5,3},{6,4},{7,5},{8,14},{9,15},{10,... | collective-permute-start | bytes 393224 | tf_op jit(solution)/shard_map/ppermute | solution.py:121
  48.7 3.3 %collective-permute-start.11 = (bf16[128,512]{0,1:T(8,128)(2,1)S(1)}, bf16[128,512]{0,1:T(8,128)(2,1)S(1)}, u32[]{:S(2)}, u32[]{:S(2)}) collective-permute-start(bf16[128,512]{0,1:T(8,128)(2,1)S(1)} %bitcast.194), channel_id=1, source_target_pairs={{0,1},{1,0},{2,3},{3,2},{4,5},{5,4},{6,7},{7,6},{8,9},{9,8},{10,11... | collective-permute-start | bytes 393224 | tf_op jit(solution)/shard_map/ppermute | solution.py:123
  52.5 1.4 %collective-permute-start.12 = (bf16[128,512]{0,1:T(8,128)(2,1)S(1)}, bf16[128,512]{0,1:T(8,128)(2,1)S(1)}, u32[]{:S(2)}, u32[]{:S(2)}) collective-permute-start(bf16[128,512]{0,1:T(8,128)(2,1)S(1)} %get-tuple-element.7), channel_id=1, source_target_pairs={{0,2},{1,7},{2,4},{3,1},{4,6},{5,3},{6,0},{7,5},{8,10},{9,15},{10,... | collective-permute-start | bytes 393224 | tf_op jit(solution)/shard_map/ppermute | solution.py:125
  53.9 4.4 %collective-permute-start.13 = (bf16[128,512]{0,1:T(8,128)(2,1)S(1)}, bf16[128,512]{0,1:T(8,128)(2,1)S(1)}, u32[]{:S(2)}, u32[]{:S(2)}) collective-permute-start(bf16[128,512]{0,1:T(8,128)(2,1)S(1)} %get-tuple-element.8), channel_id=1, source_target_pairs={{0,7},{1,2},{2,1},{3,4},{4,3},{5,6},{6,5},{7,0},{8,15},{9,10},{10,... | collective-permute-start | bytes 393224 | tf_op jit(solution)/shard_map/ppermute | solution.py:127
  59.4 1.8 %collective-permute-done.13 = bf16[128,512]{0,1:T(8,128)(2,1)S(1)} collective-permute-done((bf16[128,512]{0,1:T(8,128)(2,1)S(1)}, bf16[128,512]{0,1:T(8,128)(2,1)S(1)}, u32[]{:S(2)}, u32[]{:S(2)}) %collective-permute-start.13) | collective-permute-done | bytes 131104 | tf_op jit(solution)/shard_map/ppermute | solution.py:127
  62.3 1.1 %fusion.15 = bf16[128,1024]{1,0:T(8,128)(2,1)} fusion(f32[128,1024]{1,0:T(8,128)S(1)} %fusion.22, f32[128,1024]{1,0:T(8,128)S(1)} %fusion.24, f32[128,1024]{1,0:T(8,128)S(1)} %fusion.26, f32[128,1024]{1,0:T(8,128)S(1)} %fusion.28, f32[128,1024]{1,0:T(8,128)S(1)} %fusion.30, f32[128,1024]{1,0:T(8,128)S(1)} %convolution_add_fusion.1, ...), kind=kOutput, calls=%fused_computation.18 | convolution fusion | flops 135135232 | bytes 4587524 | tf_op jit(solution)/shard_map/dot_general | solution.py:118
  (65 shorter events, 5.5 us)
Async XLA Ops:
  0.0 43.4 %copy-start = (bf16[128,128]{1,0:T(8,128)(2,1)S(1)}, bf16[128,128]{1,0:T(8,128)(2,1)}, u32[]{:S(2)}) copy-start(bf16[128,128]{1,0:T(8,128)(2,1)} %param.7) | copy-start | bytes 98308
  3.4 11.3 %collective-permute-start.1 = (bf16[2,128,128]{2,1,0:T(8,128)(2,1)S(1)}, bf16[2,128,128]{2,1,0:T(8,128)(2,1)S(1)}, u32[]{:S(2)}, u32[]{:S(2)}) collective-permute-start(bf16[2,128,128]{2,1,0:T(8,128)(2,1)S(1)} %get-tuple-element.46), channel_id=1, source_target_pairs={{0,64},{8,72},{16,80},{24,88},{32,96},{40,104},{48,112},{56,120},{... | collective-permute-start | bytes 196616 | tf_op jit(solution)/shard_map/ppermute | solution.py:61
  7.5 7.3 %collective-permute-start = (bf16[2,128,128]{2,1,0:T(8,128)(2,1)S(1)}, bf16[2,128,128]{2,1,0:T(8,128)(2,1)S(1)}, u32[]{:S(2)}, u32[]{:S(2)}) collective-permute-start(bf16[2,128,128]{2,1,0:T(8,128)(2,1)S(1)} %get-tuple-element.46), channel_id=1, source_target_pairs={{0,128},{8,136},{16,144},{24,152},{32,160},{40,168},{48,176},{56,1... | collective-permute-start | bytes 196616 | tf_op jit(solution)/shard_map/ppermute | solution.py:61
  14.8 8.9 %collective-permute-start.2 = (bf16[3,2,128,128]{3,2,1,0:T(8,128)(2,1)S(1)}, bf16[3,2,128,128]{3,2,1,0:T(8,128)(2,1)S(1)}, u32[]{:S(2)}, u32[]{:S(2)}) collective-permute-start(bf16[3,2,128,128]{3,2,1,0:T(8,128)(2,1)S(1)} %pad_maximum_fusion.1), channel_id=1, source_target_pairs={{0,56},{8,0},{16,8},{24,16},{32,24},{40,32},{48,40},{56,48},{64,12... | collective-permute-start | bytes 589832 | tf_op jit(solution)/shard_map/ppermute | solution.py:81
  20.7 8.2 %collective-permute-start.6 = (bf16[3,2,128,128]{3,2,1,0:T(8,128)(2,1)S(1)}, bf16[3,2,128,128]{3,2,1,0:T(8,128)(2,1)S(1)}, u32[]{:S(2)}, u32[]{:S(2)}) collective-permute-start(bf16[3,2,128,128]{3,2,1,0:T(8,128)(2,1)S(1)} %pad_maximum_fusion.1), channel_id=1, source_target_pairs={{0,8},{8,16},{16,24},{24,32},{32,40},{40,48},{48,56},{56,0},{64,72... | collective-permute-start | bytes 589832 | tf_op jit(solution)/shard_map/ppermute | solution.py:81
  20.8 19.1 %collective-permute-start.5 = (bf16[2,2,128,128]{3,2,1,0:T(8,128)(2,1)S(1)}, bf16[2,2,128,128]{3,2,1,0:T(8,128)(2,1)S(1)}, u32[]{:S(2)}, u32[]{:S(2)}) collective-permute-start(bf16[2,2,128,128]{3,2,1,0:T(8,128)(2,1)S(1)} %constant_dynamic-slice_fusion.1), channel_id=1, source_target_pairs={{0,32},{8,40},{16,48},{24,56},{32,0},{40,8},{48,16},{56,24},{64,96... | collective-permute-start | bytes 393224 | tf_op jit(solution)/shard_map/ppermute | solution.py:70
  23.7 10.8 %collective-permute-start.3 = (bf16[3,2,128,128]{3,2,1,0:T(8,128)(2,1)S(1)}, bf16[3,2,128,128]{3,2,1,0:T(8,128)(2,1)S(1)}, u32[]{:S(2)}, u32[]{:S(2)}) collective-permute-start(bf16[3,2,128,128]{3,2,1,0:T(8,128)(2,1)S(1)} %collective-permute-done.2), channel_id=1, source_target_pairs={{0,56},{8,0},{16,8},{24,16},{32,24},{40,32},{48,40},{56,48},{64,12... | collective-permute-start | bytes 589832 | tf_op jit(solution)/shard_map/ppermute | solution.py:81
  28.9 9.1 %collective-permute-start.7 = (bf16[3,2,128,128]{3,2,1,0:T(8,128)(2,1)S(1)}, bf16[3,2,128,128]{3,2,1,0:T(8,128)(2,1)S(1)}, u32[]{:S(2)}, u32[]{:S(2)}) collective-permute-start(bf16[3,2,128,128]{3,2,1,0:T(8,128)(2,1)S(1)} %collective-permute-done.6), channel_id=1, source_target_pairs={{0,8},{8,16},{16,24},{24,32},{32,40},{40,48},{48,56},{56,0},{64,72... | collective-permute-start | bytes 589832 | tf_op jit(solution)/shard_map/ppermute | solution.py:81
  34.5 5.4 %collective-permute-start.4 = (bf16[2,2,128,128]{3,2,1,0:T(8,128)(2,1)S(1)}, bf16[2,2,128,128]{3,2,1,0:T(8,128)(2,1)S(1)}, u32[]{:S(2)}, u32[]{:S(2)}) collective-permute-start(bf16[2,2,128,128]{3,2,1,0:T(8,128)(2,1)S(1)} %constant_dynamic-slice_fusion.2), channel_id=1, source_target_pairs={{0,56},{8,0},{16,8},{24,16},{32,24},{40,32},{48,40},{56,48},{64,12... | collective-permute-start | bytes 393224 | tf_op jit(solution)/shard_map/ppermute | solution.py:81
  38.0 5.1 %collective-permute-start.8 = (bf16[2,2,128,128]{3,2,1,0:T(8,128)(2,1)S(1)}, bf16[2,2,128,128]{3,2,1,0:T(8,128)(2,1)S(1)}, u32[]{:S(2)}, u32[]{:S(2)}) collective-permute-start(bf16[2,2,128,128]{3,2,1,0:T(8,128)(2,1)S(1)} %constant_dynamic-slice_fusion), channel_id=1, source_target_pairs={{0,8},{8,16},{16,24},{24,32},{32,40},{40,48},{48,56},{56,0},{64,72... | collective-permute-start | bytes 393224 | tf_op jit(solution)/shard_map/ppermute | solution.py:81
  43.4 8.6 %slice-start = ((s8[8388608]{0:T(1024)(128)(4,1)}), s8[4194304]{0:T(1024)(128)(4,1)S(1)}, s32[]{:S(2)}) async-start(s8[8388608]{0:T(1024)(128)(4,1)} %bitcast.185), calls=%async_computation | async-start | bytes 8388608
  44.3 7.8 %slice-start.1 = ((s8[8388608]{0:T(1024)(128)(4,1)}), s8[4194304]{0:T(1024)(128)(4,1)S(1)}, s32[]{:S(2)}) async-start(s8[8388608]{0:T(1024)(128)(4,1)} %bitcast.185), calls=%async_computation.1 | async-start | bytes 8388608
  46.0 6.4 %collective-permute-start.9 = (bf16[128,512]{0,1:T(8,128)(2,1)S(1)}, bf16[128,512]{0,1:T(8,128)(2,1)S(1)}, u32[]{:S(2)}, u32[]{:S(2)}) collective-permute-start(bf16[128,512]{0,1:T(8,128)(2,1)S(1)} %bitcast.192), channel_id=1, source_target_pairs={{0,2},{1,3},{2,4},{3,5},{4,6},{5,7},{6,0},{7,1},{8,10},{9,11},{10,... | collective-permute-start | bytes 393224 | tf_op jit(solution)/shard_map/ppermute | solution.py:120
  47.3 5.1 %collective-permute-start.10 = (bf16[128,512]{0,1:T(8,128)(2,1)S(1)}, bf16[128,512]{0,1:T(8,128)(2,1)S(1)}, u32[]{:S(2)}, u32[]{:S(2)}) collective-permute-start(bf16[128,512]{0,1:T(8,128)(2,1)S(1)} %bitcast.193), channel_id=1, source_target_pairs={{0,6},{1,7},{2,0},{3,1},{4,2},{5,3},{6,4},{7,5},{8,14},{9,15},{10,... | collective-permute-start | bytes 393224 | tf_op jit(solution)/shard_map/ppermute | solution.py:121
  48.7 10.0 %collective-permute-start.11 = (bf16[128,512]{0,1:T(8,128)(2,1)S(1)}, bf16[128,512]{0,1:T(8,128)(2,1)S(1)}, u32[]{:S(2)}, u32[]{:S(2)}) collective-permute-start(bf16[128,512]{0,1:T(8,128)(2,1)S(1)} %bitcast.194), channel_id=1, source_target_pairs={{0,1},{1,0},{2,3},{3,2},{4,5},{5,4},{6,7},{7,6},{8,9},{9,8},{10,11... | collective-permute-start | bytes 393224 | tf_op jit(solution)/shard_map/ppermute | solution.py:123
  52.5 6.6 %collective-permute-start.12 = (bf16[128,512]{0,1:T(8,128)(2,1)S(1)}, bf16[128,512]{0,1:T(8,128)(2,1)S(1)}, u32[]{:S(2)}, u32[]{:S(2)}) collective-permute-start(bf16[128,512]{0,1:T(8,128)(2,1)S(1)} %get-tuple-element.7), channel_id=1, source_target_pairs={{0,2},{1,7},{2,4},{3,1},{4,6},{5,3},{6,0},{7,5},{8,10},{9,15},{10,... | collective-permute-start | bytes 393224 | tf_op jit(solution)/shard_map/ppermute | solution.py:125
  53.9 7.4 %collective-permute-start.13 = (bf16[128,512]{0,1:T(8,128)(2,1)S(1)}, bf16[128,512]{0,1:T(8,128)(2,1)S(1)}, u32[]{:S(2)}, u32[]{:S(2)}) collective-permute-start(bf16[128,512]{0,1:T(8,128)(2,1)S(1)} %get-tuple-element.8), channel_id=1, source_target_pairs={{0,7},{1,2},{2,1},{3,4},{4,3},{5,6},{6,5},{7,0},{8,15},{9,10},{10,... | collective-permute-start | bytes 393224 | tf_op jit(solution)/shard_map/ppermute | solution.py:127
  58.3 3.3 %collective-permute-start.14 = (bf16[2,128,512]{1,2,0:T(8,128)(2,1)S(1)}, bf16[2,128,512]{1,2,0:T(8,128)(2,1)S(1)}, u32[]{:S(2)}, u32[]{:S(2)}) collective-permute-start(bf16[2,128,512]{1,2,0:T(8,128)(2,1)S(1)} %pad_maximum_fusion), channel_id=1, source_target_pairs={{0,1},{1,0},{2,3},{3,2},{4,5},{5,4},{6,7},{7,6},{8,9},{9,8},{10,11... | collective-permute-start | bytes 786440 | tf_op jit(solution)/shard_map/ppermute | solution.py:128

commit v10 on v8

--- a/solution.py
+++ b/solution.py
@@ -118,24 +118,15 @@
             rows = lax.dynamic_slice_in_dim(out_weight, src * feat, feat, 0)
             return jnp.dot(piece, rows, preferred_element_type=jnp.float32)
 
-        up = lax.ppermute(attended, "head", [(s, (s + 2) % n_head) for s in range(n_head)])
-        down = lax.ppermute(attended, "head", [(s, (s - 2) % n_head) for s in range(n_head)])
-        swap = [(s, s ^ 1) for s in range(n_head)]
-        partner = lax.ppermute(attended, "head", swap)
-        same_pairs = [(s, (s + 2) % n_head) if s % 2 == 0 else (s, (s - 2) % n_head) for s in range(n_head)]
-        far = lax.ppermute(jnp.where(core == 0, up, down), "head", same_pairs)
-        cross_pairs = [(s, (s + 1) % n_head) if s % 2 == 1 else (s, (s - 1) % n_head) for s in range(n_head)]
-        far_cross = lax.ppermute(jnp.where(core == 1, up, down), "head", cross_pairs)
-        near_other = lax.ppermute(jnp.stack([up, down]), "head", swap)
-        other = head ^ 1
+        def gather(odd, even):
+            pairs = [(s, (s + (odd if s % 2 else even)) % n_head) for s in range(n_head)]
+            return lax.ppermute(attended, "head", pairs)
+
         total = project(attended, head)
-        total = total + project(up, (head - 2) % n_head)
-        total = total + project(down, (head + 2) % n_head)
-        total = total + project(partner, other)
-        total = total + project(far, (head + 4) % n_head)
-        total = total + project(far_cross, jnp.where(core == 0, head - 3, head + 3) % n_head)
-        total = total + project(near_other[0], (other - 2) % n_head)
-        total = total + project(near_other[1], (other + 2) % n_head)
+        for odd, even in ((-1, 1), (2, 2), (-2, -2), (1, 3), (-3, -1), (4, 4), (3, 5)):
+            got = gather(odd, even)
+            shift = jnp.where(core == (1 if odd % 2 else 0), even, odd) if odd % 2 else jnp.int32(odd)
+            total = total + project(got, (head - shift) % n_head)
         return total.astype(jnp.bfloat16)
 
     return on_device

time: 63.9 us -> 66.6 us (1.042)
  waiting for transfers between devices: 14.3 us -> 18.8 us
  starting transfers between devices: 35.9 us -> 34.2 us
    ppermute x6 -> x7, waiting for transfers between devices: 1.83 us -> 6.27 us  [gather(): return lax.ppermute(attended, 'head', pairs)]
    ppermute x6 -> x7, starting transfers between devices: 12 us -> 10.3 us  [gather(): return lax.ppermute(attended, 'head', pairs)]
  transfers between devices with their start and end apart: 15 -> 16, of which waited for: 5 -> 8; matrix products, arithmetic and copies ran while one was open for 7% -> 8% of each run, Pallas kernels for 0% -> 0%
where the time goes in v10:
time: 66.6 us; the launch traced here: 66.3 us
  starting transfers between devices  34.2 us (51%)
  waiting for transfers between devices  18.8 us (28%)
  matrix products  5.15 us (8%)
  other arithmetic  4.06 us (6%)
  local copies, waits for them, and re-layouts  3.43 us (5%)
    ppermute x6, waiting for transfers between devices, on_device(): lax.ppermute(lax.dynamic_slice_in_dim(packet, lo, step['width'], 0), 'ctx...  12.5 us
    ppermute x6, starting transfers between devices, on_device(): lax.ppermute(lax.dynamic_slice_in_dim(packet, lo, step['width'], 0), 'ctx...  12.5 us
    ppermute x7, starting transfers between devices, gather(): return lax.ppermute(attended, 'head', pairs)  10.3 us
    ppermute x2, starting transfers between devices, on_device(): lax.ppermute(own, 'ctx', [(s, s + shift) for s in range(n_ctx - shift)])  8.55 us
    ppermute x7, waiting for transfers between devices, gather(): return lax.ppermute(attended, 'head', pairs)  6.27 us
    dot_general x8, matrix products, project(): return jnp.dot(piece, rows, preferred_element_type=jnp.float32)  3.4 us
    unnamed x25, local copies, waits for them, and re-layouts  3.37 us
    ppermute x1, starting transfers between devices, on_device(): lax.ppermute(lax.dynamic_slice_in_dim(bundle, lo, rows_back, 0), 'ctx', [...  2.86 us
  transfers between devices with their start and end apart: 16, of which 8 were waited for; matrix products, arithmetic and copies ran while one was open for 8% of the time, Pallas kernels for 0%

profile of v10, /device:TPU:1, one launch (start us, length us, event | category | flops | bytes accessed | tf_op | source)
XLA Modules:
  0.0 66.3 jit_solution(18387149963247761456)
XLA Ops:
  1.5 0.9 %copy.18 = bf16[128,128]{0,1:T(8,128)(2,1)S(1)} copy(bf16[128,128]{1,0:T(8,128)(2,1)} %param.6) | data formatting | bytes 65536 | tf_op args[1]
  2.4 0.9 %copy.19 = bf16[128,128]{0,1:T(8,128)(2,1)S(1)} copy(bf16[128,128]{1,0:T(8,128)(2,1)} %param.7) | data formatting | bytes 65536 | tf_op args[2]
  3.6 4.0 %collective-permute-start.1 = (bf16[128,256]{0,1:T(8,128)(2,1)S(1)}, bf16[128,256]{0,1:T(8,128)(2,1)S(1)}, u32[]{:S(2)}, u32[]{:S(2)}) collective-permute-start(bf16[128,256]{0,1:T(8,128)(2,1)S(1)} %get-tuple-element.12), channel_id=1, source_target_pairs={{0,64},{8,72},{16,80},{24,88},{32,96},{40,104},{48,112},{56,120},{... | collective-permute-start | bytes 196616 | tf_op jit(solution)/shard_map/ppermute | solution.py:61
  7.6 4.5 %collective-permute-start = (bf16[128,256]{0,1:T(8,128)(2,1)S(1)}, bf16[128,256]{0,1:T(8,128)(2,1)S(1)}, u32[]{:S(2)}, u32[]{:S(2)}) collective-permute-start(bf16[128,256]{0,1:T(8,128)(2,1)S(1)} %get-tuple-element.12), channel_id=1, source_target_pairs={{0,128},{8,136},{16,144},{24,152},{32,160},{40,168},{48,176},{56,1... | collective-permute-start | bytes 196616 | tf_op jit(solution)/shard_map/ppermute | solution.py:61
  12.1 1.0 %copy.20 = bf16[128,512]{0,1:T(8,128)(2,1)S(1)} copy(bf16[128,512]{1,0:T(8,128)(2,1)} %param.5) | data formatting | bytes 262144 | tf_op args[0]
  13.2 1.0 %compare_and_fusion = pred[128,2176]{0,1:T(8,128)(4,1)S(1)} fusion(s32[128]{0:T(128)S(1)} %select_reduce_fusion, s32[128]{0:T(128)S(1)} %iota_add_fusion.1, s32[2176]{0:T(1024)S(1)} %iota_add_fusion), kind=kLoop, calls=%fused_computation.19 | loop fusion | flops 835584 | bytes 288256 | tf_op jit(solution)/shard_map/and | solution.py:99
  14.9 5.7 %collective-permute-start.2 = (bf16[3,128,256]{1,2,0:T(8,128)(2,1)S(1)}, bf16[3,128,256]{1,2,0:T(8,128)(2,1)S(1)}, u32[]{:S(2)}, u32[]{:S(2)}) collective-permute-start(bf16[3,128,256]{1,2,0:T(8,128)(2,1)S(1)} %pad_maximum_fusion), channel_id=1, source_target_pairs={{0,56},{8,0},{16,8},{24,16},{32,24},{40,32},{48,40},{56,48},{64,12... | collective-permute-start | bytes 589832 | tf_op jit(solution)/shard_map/ppermute | solution.py:81
  20.9 2.9 %collective-permute-start.5 = (bf16[2,128,256]{1,2,0:T(8,128)(2,1)S(1)}, bf16[2,128,256]{1,2,0:T(8,128)(2,1)S(1)}, u32[]{:S(2)}, u32[]{:S(2)}) collective-permute-start(bf16[2,128,256]{1,2,0:T(8,128)(2,1)S(1)} %constant_dynamic-slice_fusion.1), channel_id=1, source_target_pairs={{0,32},{8,40},{16,48},{24,56},{32,0},{40,8},{48,16},{56,24},{64,96... | collective-permute-start | bytes 393224 | tf_op jit(solution)/shard_map/ppermute | solution.py:70
  23.8 3.2 %collective-permute-start.3 = (bf16[3,128,256]{1,2,0:T(8,128)(2,1)S(1)}, bf16[3,128,256]{1,2,0:T(8,128)(2,1)S(1)}, u32[]{:S(2)}, u32[]{:S(2)}) collective-permute-start(bf16[3,128,256]{1,2,0:T(8,128)(2,1)S(1)} %collective-permute-done.2), channel_id=1, source_target_pairs={{0,56},{8,0},{16,8},{24,16},{32,24},{40,32},{48,40},{56,48},{64,12... | collective-permute-start | bytes 589832 | tf_op jit(solution)/shard_map/ppermute | solution.py:81
  27.0 2.0 %collective-permute-done.6 = bf16[3,128,256]{1,2,0:T(8,128)(2,1)S(1)} collective-permute-done((bf16[3,128,256]{1,2,0:T(8,128)(2,1)S(1)}, bf16[3,128,256]{1,2,0:T(8,128)(2,1)S(1)}, u32[]{:S(2)}, u32[]{:S(2)}) %collective-permute-start.6) | collective-permute-done | bytes 196640 | tf_op jit(solution)/shard_map/ppermute | solution.py:81
  29.0 5.6 %collective-permute-done.3 = bf16[3,128,256]{1,2,0:T(8,128)(2,1)S(1)} collective-permute-done((bf16[3,128,256]{1,2,0:T(8,128)(2,1)S(1)}, bf16[3,128,256]{1,2,0:T(8,128)(2,1)S(1)}, u32[]{:S(2)}, u32[]{:S(2)}) %collective-permute-start.3) | collective-permute-done | bytes 196640 | tf_op jit(solution)/shard_map/ppermute | solution.py:81
  34.6 3.5 %collective-permute-start.4 = (bf16[2,128,256]{1,2,0:T(8,128)(2,1)S(1)}, bf16[2,128,256]{1,2,0:T(8,128)(2,1)S(1)}, u32[]{:S(2)}, u32[]{:S(2)}) collective-permute-start(bf16[2,128,256]{1,2,0:T(8,128)(2,1)S(1)} %constant_dynamic-slice_fusion.2), channel_id=1, source_target_pairs={{0,56},{8,0},{16,8},{24,16},{32,24},{40,32},{48,40},{56,48},{64,12... | collective-permute-start | bytes 393224 | tf_op jit(solution)/shard_map/ppermute | solution.py:81
  38.2 1.8 %collective-permute-done.4 = bf16[2,128,256]{1,2,0:T(8,128)(2,1)S(1)} collective-permute-done((bf16[2,128,256]{1,2,0:T(8,128)(2,1)S(1)}, bf16[2,128,256]{1,2,0:T(8,128)(2,1)S(1)}, u32[]{:S(2)}, u32[]{:S(2)}) %collective-permute-start.4) | collective-permute-done | bytes 131104 | tf_op jit(solution)/shard_map/ppermute | solution.py:81
  40.1 3.1 %collective-permute-done.8 = bf16[2,128,256]{1,2,0:T(8,128)(2,1)S(1)} collective-permute-done((bf16[2,128,256]{1,2,0:T(8,128)(2,1)S(1)}, bf16[2,128,256]{1,2,0:T(8,128)(2,1)S(1)}, u32[]{:S(2)}, u32[]{:S(2)}) %collective-permute-start.8) | collective-permute-done | bytes 131104 | tf_op jit(solution)/shard_map/ppermute | solution.py:81
  45.3 0.9 %fusion.19 = bf16[4,128,128]{1,2,0:T(8,128)(2,1)S(1)} fusion(f32[1,4,128,2176]{2,3,1,0:T(8,128)S(1)} %get-tuple-element.16, f32[4,128]{1,0:T(4,128)S(1)} %get-tuple-element.15, pred[128,2176]{0,1:T(8,128)(4,1)S(1)} %compare_and_fusion, bf16[2176,256]{0,1:T(8,128)(2,1)S(1)} %constant_dynamic-update-slice_fusion, f32[4,128]{1,0:T(4,128)S(1)} %fusion.2), kind=kOutput, calls=%fused_computation.21 | convolution fusion | flops 288686080 | bytes 5427200 | tf_op jit(solution)/shard_map/kgtn,nkd->kgtd/dot_general | solution.py:104
  46.2 2.9 %collective-permute-start.9 = (bf16[128,512]{0,1:T(8,128)(2,1)S(1)}, bf16[128,512]{0,1:T(8,128)(2,1)S(1)}, u32[]{:S(2)}, u32[]{:S(2)}) collective-permute-start(bf16[128,512]{0,1:T(8,128)(2,1)S(1)} %bitcast.106), channel_id=1, source_target_pairs={{0,1},{1,0},{2,3},{3,2},{4,5},{5,4},{6,7},{7,6},{8,9},{9,8},{10,11... | collective-permute-start | bytes 393224 | tf_op jit(solution)/shard_map/ppermute | solution.py:123
  49.0 1.2 %collective-permute-start.12 = (bf16[128,512]{0,1:T(8,128)(2,1)S(1)}, bf16[128,512]{0,1:T(8,128)(2,1)S(1)}, u32[]{:S(2)}, u32[]{:S(2)}) collective-permute-start(bf16[128,512]{0,1:T(8,128)(2,1)S(1)} %bitcast.107), channel_id=1, source_target_pairs={{0,3},{1,2},{2,5},{3,4},{4,7},{5,6},{6,1},{7,0},{8,11},{9,10},{10,... | collective-permute-start | bytes 393224 | tf_op jit(solution)/shard_map/ppermute | solution.py:123
  50.2 1.8 %collective-permute-start.13 = (bf16[128,512]{0,1:T(8,128)(2,1)S(1)}, bf16[128,512]{0,1:T(8,128)(2,1)S(1)}, u32[]{:S(2)}, u32[]{:S(2)}) collective-permute-start(bf16[128,512]{0,1:T(8,128)(2,1)S(1)} %bitcast.108), channel_id=1, source_target_pairs={{0,7},{1,6},{2,1},{3,0},{4,3},{5,2},{6,5},{7,4},{8,15},{9,14},{10,... | collective-permute-start | bytes 393224 | tf_op jit(solution)/shard_map/ppermute | solution.py:123
  52.0 1.5 %collective-permute-start.14 = (bf16[128,512]{0,1:T(8,128)(2,1)S(1)}, bf16[128,512]{0,1:T(8,128)(2,1)S(1)}, u32[]{:S(2)}, u32[]{:S(2)}) collective-permute-start(bf16[128,512]{0,1:T(8,128)(2,1)S(1)} %bitcast.109), channel_id=1, source_target_pairs={{0,4},{1,5},{2,6},{3,7},{4,0},{5,1},{6,2},{7,3},{8,12},{9,13},{10,... | collective-permute-start | bytes 393224 | tf_op jit(solution)/shard_map/ppermute | solution.py:123
  54.7 1.9 %collective-permute-start.15 = (bf16[128,512]{0,1:T(8,128)(2,1)S(1)}, bf16[128,512]{0,1:T(8,128)(2,1)S(1)}, u32[]{:S(2)}, u32[]{:S(2)}) collective-permute-start(bf16[128,512]{0,1:T(8,128)(2,1)S(1)} %bitcast.112), channel_id=1, source_target_pairs={{0,5},{1,4},{2,7},{3,6},{4,1},{5,0},{6,3},{7,2},{8,13},{9,12},{10,... | collective-permute-start | bytes 393224 | tf_op jit(solution)/shard_map/ppermute | solution.py:123
  57.9 1.1 %collective-permute-done.14 = bf16[128,512]{0,1:T(8,128)(2,1)S(1)} collective-permute-done((bf16[128,512]{0,1:T(8,128)(2,1)S(1)}, bf16[128,512]{0,1:T(8,128)(2,1)S(1)}, u32[]{:S(2)}, u32[]{:S(2)}) %collective-permute-start.14) | collective-permute-done | bytes 131104 | tf_op jit(solution)/shard_map/ppermute | solution.py:123
  59.3 2.1 %collective-permute-done.11 = bf16[128,512]{0,1:T(8,128)(2,1)S(1)} collective-permute-done((bf16[128,512]{0,1:T(8,128)(2,1)S(1)}, bf16[128,512]{0,1:T(8,128)(2,1)S(1)}, u32[]{:S(2)}, u32[]{:S(2)}) %collective-permute-start.11) | collective-permute-done | bytes 131104 | tf_op jit(solution)/shard_map/ppermute | solution.py:123
  62.7 2.5 %collective-permute-done.10 = bf16[128,512]{0,1:T(8,128)(2,1)S(1)} collective-permute-done((bf16[128,512]{0,1:T(8,128)(2,1)S(1)}, bf16[128,512]{0,1:T(8,128)(2,1)S(1)}, u32[]{:S(2)}, u32[]{:S(2)}) %collective-permute-start.10) | collective-permute-done | bytes 131104 | tf_op jit(solution)/shard_map/ppermute | solution.py:123
  65.2 1.1 %fusion.15 = bf16[128,1024]{1,0:T(8,128)(2,1)} fusion(f32[128,1024]{1,0:T(8,128)S(1)} %fusion.22, f32[128,1024]{1,0:T(8,128)S(1)} %fusion.24, f32[128,1024]{1,0:T(8,128)S(1)} %fusion.26, f32[128,1024]{1,0:T(8,128)S(1)} %fusion.28, f32[128,1024]{1,0:T(8,128)S(1)} %fusion.30, f32[128,1024]{1,0:T(8,128)S(1)} %convolution_add_fusion.1, ...), kind=kOutput, calls=%fused_computation.18 | convolution fusion | flops 135135232 | bytes 4587524 | tf_op jit(solution)/shard_map/dot_general | solution.py:119
  (64 shorter events, 8.7 us)
Async XLA Ops:
  3.6 11.3 %collective-permute-start.1 = (bf16[128,256]{0,1:T(8,128)(2,1)S(1)}, bf16[128,256]{0,1:T(8,128)(2,1)S(1)}, u32[]{:S(2)}, u32[]{:S(2)}) collective-permute-start(bf16[128,256]{0,1:T(8,128)(2,1)S(1)} %get-tuple-element.12), channel_id=1, source_target_pairs={{0,64},{8,72},{16,80},{24,88},{32,96},{40,104},{48,112},{56,120},{... | collective-permute-start | bytes 196616 | tf_op jit(solution)/shard_map/ppermute | solution.py:61
  7.6 7.3 %collective-permute-start = (bf16[128,256]{0,1:T(8,128)(2,1)S(1)}, bf16[128,256]{0,1:T(8,128)(2,1)S(1)}, u32[]{:S(2)}, u32[]{:S(2)}) collective-permute-start(bf16[128,256]{0,1:T(8,128)(2,1)S(1)} %get-tuple-element.12), channel_id=1, source_target_pairs={{0,128},{8,136},{16,144},{24,152},{32,160},{40,168},{48,176},{56,1... | collective-permute-start | bytes 196616 | tf_op jit(solution)/shard_map/ppermute | solution.py:61
  14.9 8.9 %collective-permute-start.2 = (bf16[3,128,256]{1,2,0:T(8,128)(2,1)S(1)}, bf16[3,128,256]{1,2,0:T(8,128)(2,1)S(1)}, u32[]{:S(2)}, u32[]{:S(2)}) collective-permute-start(bf16[3,128,256]{1,2,0:T(8,128)(2,1)S(1)} %pad_maximum_fusion), channel_id=1, source_target_pairs={{0,56},{8,0},{16,8},{24,16},{32,24},{40,32},{48,40},{56,48},{64,12... | collective-permute-start | bytes 589832 | tf_op jit(solution)/shard_map/ppermute | solution.py:81
  20.8 8.2 %collective-permute-start.6 = (bf16[3,128,256]{1,2,0:T(8,128)(2,1)S(1)}, bf16[3,128,256]{1,2,0:T(8,128)(2,1)S(1)}, u32[]{:S(2)}, u32[]{:S(2)}) collective-permute-start(bf16[3,128,256]{1,2,0:T(8,128)(2,1)S(1)} %pad_maximum_fusion), channel_id=1, source_target_pairs={{0,8},{8,16},{16,24},{24,32},{32,40},{40,48},{48,56},{56,0},{64,72... | collective-permute-start | bytes 589832 | tf_op jit(solution)/shard_map/ppermute | solution.py:81
  20.9 19.1 %collective-permute-start.5 = (bf16[2,128,256]{1,2,0:T(8,128)(2,1)S(1)}, bf16[2,128,256]{1,2,0:T(8,128)(2,1)S(1)}, u32[]{:S(2)}, u32[]{:S(2)}) collective-permute-start(bf16[2,128,256]{1,2,0:T(8,128)(2,1)S(1)} %constant_dynamic-slice_fusion.1), channel_id=1, source_target_pairs={{0,32},{8,40},{16,48},{24,56},{32,0},{40,8},{48,16},{56,24},{64,96... | collective-permute-start | bytes 393224 | tf_op jit(solution)/shard_map/ppermute | solution.py:70
  23.8 10.8 %collective-permute-start.3 = (bf16[3,128,256]{1,2,0:T(8,128)(2,1)S(1)}, bf16[3,128,256]{1,2,0:T(8,128)(2,1)S(1)}, u32[]{:S(2)}, u32[]{:S(2)}) collective-permute-start(bf16[3,128,256]{1,2,0:T(8,128)(2,1)S(1)} %collective-permute-done.2), channel_id=1, source_target_pairs={{0,56},{8,0},{16,8},{24,16},{32,24},{40,32},{48,40},{56,48},{64,12... | collective-permute-start | bytes 589832 | tf_op jit(solution)/shard_map/ppermute | solution.py:81
  29.0 9.1 %collective-permute-start.7 = (bf16[3,128,256]{1,2,0:T(8,128)(2,1)S(1)}, bf16[3,128,256]{1,2,0:T(8,128)(2,1)S(1)}, u32[]{:S(2)}, u32[]{:S(2)}) collective-permute-start(bf16[3,128,256]{1,2,0:T(8,128)(2,1)S(1)} %collective-permute-done.6), channel_id=1, source_target_pairs={{0,8},{8,16},{16,24},{24,32},{32,40},{40,48},{48,56},{56,0},{64,72... | collective-permute-start | bytes 589832 | tf_op jit(solution)/shard_map/ppermute | solution.py:81
  34.6 5.4 %collective-permute-start.4 = (bf16[2,128,256]{1,2,0:T(8,128)(2,1)S(1)}, bf16[2,128,256]{1,2,0:T(8,128)(2,1)S(1)}, u32[]{:S(2)}, u32[]{:S(2)}) collective-permute-start(bf16[2,128,256]{1,2,0:T(8,128)(2,1)S(1)} %constant_dynamic-slice_fusion.2), channel_id=1, source_target_pairs={{0,56},{8,0},{16,8},{24,16},{32,24},{40,32},{48,40},{56,48},{64,12... | collective-permute-start | bytes 393224 | tf_op jit(solution)/shard_map/ppermute | solution.py:81
  38.1 5.1 %collective-permute-start.8 = (bf16[2,128,256]{1,2,0:T(8,128)(2,1)S(1)}, bf16[2,128,256]{1,2,0:T(8,128)(2,1)S(1)}, u32[]{:S(2)}, u32[]{:S(2)}) collective-permute-start(bf16[2,128,256]{1,2,0:T(8,128)(2,1)S(1)} %constant_dynamic-slice_fusion), channel_id=1, source_target_pairs={{0,8},{8,16},{16,24},{24,32},{32,40},{40,48},{48,56},{56,0},{64,72... | collective-permute-start | bytes 393224 | tf_op jit(solution)/shard_map/ppermute | solution.py:81
  43.6 10.8 %slice-start = ((s8[8388608]{0:T(1024)(128)(4,1)}), s8[4194304]{0:T(1024)(128)(4,1)S(1)}, s32[]{:S(2)}) async-start(s8[8388608]{0:T(1024)(128)(4,1)} %bitcast.101), calls=%async_computation | async-start | bytes 8388608
  44.4 10.0 %slice-start.1 = ((s8[8388608]{0:T(1024)(128)(4,1)}), s8[4194304]{0:T(1024)(128)(4,1)S(1)}, s32[]{:S(2)}) async-start(s8[8388608]{0:T(1024)(128)(4,1)} %bitcast.101), calls=%async_computation.1 | async-start | bytes 8388608
  46.2 8.6 %collective-permute-start.9 = (bf16[128,512]{0,1:T(8,128)(2,1)S(1)}, bf16[128,512]{0,1:T(8,128)(2,1)S(1)}, u32[]{:S(2)}, u32[]{:S(2)}) collective-permute-start(bf16[128,512]{0,1:T(8,128)(2,1)S(1)} %bitcast.106), channel_id=1, source_target_pairs={{0,1},{1,0},{2,3},{3,2},{4,5},{5,4},{6,7},{7,6},{8,9},{9,8},{10,11... | collective-permute-start | bytes 393224 | tf_op jit(solution)/shard_map/ppermute | solution.py:123
  49.0 7.9 %collective-permute-start.12 = (bf16[128,512]{0,1:T(8,128)(2,1)S(1)}, bf16[128,512]{0,1:T(8,128)(2,1)S(1)}, u32[]{:S(2)}, u32[]{:S(2)}) collective-permute-start(bf16[128,512]{0,1:T(8,128)(2,1)S(1)} %bitcast.107), channel_id=1, source_target_pairs={{0,3},{1,2},{2,5},{3,4},{4,7},{5,6},{6,1},{7,0},{8,11},{9,10},{10,... | collective-permute-start | bytes 393224 | tf_op jit(solution)/shard_map/ppermute | solution.py:123
  50.2 7.3 %collective-permute-start.13 = (bf16[128,512]{0,1:T(8,128)(2,1)S(1)}, bf16[128,512]{0,1:T(8,128)(2,1)S(1)}, u32[]{:S(2)}, u32[]{:S(2)}) collective-permute-start(bf16[128,512]{0,1:T(8,128)(2,1)S(1)} %bitcast.108), channel_id=1, source_target_pairs={{0,7},{1,6},{2,1},{3,0},{4,3},{5,2},{6,5},{7,4},{8,15},{9,14},{10,... | collective-permute-start | bytes 393224 | tf_op jit(solution)/shard_map/ppermute | solution.py:123
  52.0 7.0 %collective-permute-start.14 = (bf16[128,512]{0,1:T(8,128)(2,1)S(1)}, bf16[128,512]{0,1:T(8,128)(2,1)S(1)}, u32[]{:S(2)}, u32[]{:S(2)}) collective-permute-start(bf16[128,512]{0,1:T(8,128)(2,1)S(1)} %bitcast.109), channel_id=1, source_target_pairs={{0,4},{1,5},{2,6},{3,7},{4,0},{5,1},{6,2},{7,3},{8,12},{9,13},{10,... | collective-permute-start | bytes 393224 | tf_op jit(solution)/shard_map/ppermute | solution.py:123
  53.5 7.9 %collective-permute-start.11 = (bf16[128,512]{0,1:T(8,128)(2,1)S(1)}, bf16[128,512]{0,1:T(8,128)(2,1)S(1)}, u32[]{:S(2)}, u32[]{:S(2)}) collective-permute-start(bf16[128,512]{0,1:T(8,128)(2,1)S(1)} %bitcast.110), channel_id=1, source_target_pairs={{0,6},{1,7},{2,0},{3,1},{4,2},{5,3},{6,4},{7,5},{8,14},{9,15},{10,... | collective-permute-start | bytes 393224 | tf_op jit(solution)/shard_map/ppermute | solution.py:123
  54.7 7.6 %collective-permute-start.15 = (bf16[128,512]{0,1:T(8,128)(2,1)S(1)}, bf16[128,512]{0,1:T(8,128)(2,1)S(1)}, u32[]{:S(2)}, u32[]{:S(2)}) collective-permute-start(bf16[128,512]{0,1:T(8,128)(2,1)S(1)} %bitcast.112), channel_id=1, source_target_pairs={{0,5},{1,4},{2,7},{3,6},{4,1},{5,0},{6,3},{7,2},{8,13},{9,12},{10,... | collective-permute-start | bytes 393224 | tf_op jit(solution)/shard_map/ppermute | solution.py:123
  57.0 8.2 %collective-permute-start.10 = (bf16[128,512]{0,1:T(8,128)(2,1)S(1)}, bf16[128,512]{0,1:T(8,128)(2,1)S(1)}, u32[]{:S(2)}, u32[]{:S(2)}) collective-permute-start(bf16[128,512]{0,1:T(8,128)(2,1)S(1)} %bitcast.113), channel_id=1, source_target_pairs={{0,2},{1,3},{2,4},{3,5},{4,6},{5,7},{6,0},{7,1},{8,10},{9,11},{10,... | collective-permute-start | bytes 393224 | tf_op jit(solution)/shard_map/ppermute | solution.py:123

commit v11 on v10

--- a/solution.py
+++ b/solution.py
@@ -113,20 +113,27 @@
         feat = attended.shape[1]
         head = lax.axis_index("head")
         core = head % 2
-
-        def project(piece, src):
-            rows = lax.dynamic_slice_in_dim(out_weight, src * feat, feat, 0)
-            return jnp.dot(piece, rows, preferred_element_type=jnp.float32)
-
-        def gather(odd, even):
-            pairs = [(s, (s + (odd if s % 2 else even)) % n_head) for s in range(n_head)]
-            return lax.ppermute(attended, "head", pairs)
-
-        total = project(attended, head)
-        for odd, even in ((-1, 1), (2, 2), (-2, -2), (1, 3), (-3, -1), (4, 4), (3, 5)):
-            got = gather(odd, even)
-            shift = jnp.where(core == (1 if odd % 2 else 0), even, odd) if odd % 2 else jnp.int32(odd)
-            total = total + project(got, (head - shift) % n_head)
+        chip = head // 2
+        n_chip = n_head // 2
+
+        def project(pair, at):
+            rows = lax.dynamic_slice_in_dim(out_weight, (at % n_chip) * 2 * feat, 2 * feat, 0)
+            return jnp.dot(pair, rows, preferred_element_type=jnp.float32)
+
+        partner = lax.ppermute(attended, "head", [(s, s ^ 1) for s in range(n_head)])
+        pair = jnp.where(
+            core == 0,
+            jnp.concatenate([attended, partner], axis=1),
+            jnp.concatenate([partner, attended], axis=1),
+        )
+        up = lax.ppermute(pair, "head", [(s, (s + 2) % n_head) for s in range(n_head)])
+        down = lax.ppermute(pair, "head", [(s, (s - 2) % n_head) for s in range(n_head)])
+        same_pairs = [(s, (s + 2) % n_head) if s % 2 == 0 else (s, (s - 2) % n_head) for s in range(n_head)]
+        far = lax.ppermute(jnp.where(core == 0, up, down), "head", same_pairs)
+        total = project(pair, chip)
+        total = total + project(up, chip - 1)
+        total = total + project(down, chip + 1)
+        total = total + project(far, chip + 2)
         return total.astype(jnp.bfloat16)
 
     return on_device

time: 66.6 us -> 71 us (1.066)
  matrix products: 5.15 us -> 10.7 us
  starting transfers between devices: 34.2 us -> 32.1 us
    dot_general x8 -> x4, matrix products: 3.4 us -> 8.97 us  [project(): return jnp.dot(pair, rows, preferred_element_type=jnp.float32)]
    ppermute x7 -> x4, starting transfers between devices: 10.3 us -> 8.09 us  [the longest x1 2.87 us: on_device(): lax.ppermute(attended, 'head', [(s, s ^ 1) for s in range(n_head)])]
    ppermute x7 -> x4, waiting for transfers between devices: 6.27 us -> 7.03 us  [the longest x1 6.04 us: on_device(): lax.ppermute(pair, 'head', [(s, (s + 2) % n_head) for s in range(n_head)])]
    unnamed x25 -> x21, local copies, waits for them, and re-layouts: 3.37 us -> 3.36 us
  transfers between devices with their start and end apart: 16 -> 13, of which waited for: 8 -> 6; matrix products, arithmetic and copies ran while one was open for 8% -> 10% of each run, Pallas kernels for 0% -> 0%
where the time goes in v11:
time: 71 us; the launch traced here: 70.3 us
  starting transfers between devices  32.1 us (45%)
  waiting for transfers between devices  19.4 us (27%)
  matrix products  10.7 us (15%)
  other arithmetic  4.17 us (6%)
  local copies, waits for them, and re-layouts  3.41 us (5%)
    ppermute x6, starting transfers between devices, on_device(): lax.ppermute(lax.dynamic_slice_in_dim(packet, lo, step['width'], 0), 'ctx...  12.6 us
    ppermute x6, waiting for transfers between devices, on_device(): lax.ppermute(lax.dynamic_slice_in_dim(packet, lo, step['width'], 0), 'ctx...  12.4 us
    dot_general x4, matrix products, project(): return jnp.dot(pair, rows, preferred_element_type=jnp.float32)  8.97 us
    ppermute x2, starting transfers between devices, on_device(): lax.ppermute(own, 'ctx', [(s, s + shift) for s in range(n_ctx - shift)])  8.55 us
    ppermute x1, waiting for transfers between devices, on_device(): lax.ppermute(pair, 'head', [(s, (s + 2) % n_head) for s in range(n_head)])  6.04 us
    unnamed x21, local copies, waits for them, and re-layouts  3.36 us
    ppermute x1, starting transfers between devices, on_device(): lax.ppermute(attended, 'head', [(s, s ^ 1) for s in range(n_head)])  2.87 us
    ppermute x1, starting transfers between devices, on_device(): lax.ppermute(lax.dynamic_slice_in_dim(bundle, lo, rows_back, 0), 'ctx', [...  2.86 us
  transfers between devices with their start and end apart: 13, of which 6 were waited for; matrix products, arithmetic and copies ran while one was open for 10% of the time, Pallas kernels for 0%

profile of v11, /device:TPU:1, one launch (start us, length us, event | category | flops | bytes accessed | tf_op | source)
XLA Modules:
  0.0 70.3 jit_solution(6639762921552791063)
XLA Ops:
  2.4 0.9 %copy.19 = bf16[128,128]{0,1:T(8,128)(2,1)S(1)} copy(bf16[128,128]{1,0:T(8,128)(2,1)} %param.7) | data formatting | bytes 65536 | tf_op args[2]
  3.6 4.0 %collective-permute-start.1 = (bf16[128,256]{0,1:T(8,128)(2,1)S(1)}, bf16[128,256]{0,1:T(8,128)(2,1)S(1)}, u32[]{:S(2)}, u32[]{:S(2)}) collective-permute-start(bf16[128,256]{0,1:T(8,128)(2,1)S(1)} %get-tuple-element.12), channel_id=1, source_target_pairs={{0,64},{8,72},{16,80},{24,88},{32,96},{40,104},{48,112},{56,120},{... | collective-permute-start | bytes 196616 | tf_op jit(solution)/shard_map/ppermute | solution.py:61
  7.6 4.5 %collective-permute-start = (bf16[128,256]{0,1:T(8,128)(2,1)S(1)}, bf16[128,256]{0,1:T(8,128)(2,1)S(1)}, u32[]{:S(2)}, u32[]{:S(2)}) collective-permute-start(bf16[128,256]{0,1:T(8,128)(2,1)S(1)} %get-tuple-element.12), channel_id=1, source_target_pairs={{0,128},{8,136},{16,144},{24,152},{32,160},{40,168},{48,176},{56,1... | collective-permute-start | bytes 196616 | tf_op jit(solution)/shard_map/ppermute | solution.py:61
  12.1 1.0 %copy.20 = bf16[128,512]{0,1:T(8,128)(2,1)S(1)} copy(bf16[128,512]{1,0:T(8,128)(2,1)} %param.5) | data formatting | bytes 262144 | tf_op args[0]
  13.2 1.0 %compare_and_fusion = pred[128,2176]{0,1:T(8,128)(4,1)S(1)} fusion(s32[128]{0:T(128)S(1)} %select_reduce_fusion, s32[128]{0:T(128)S(1)} %iota_add_fusion.1, s32[2176]{0:T(1024)S(1)} %iota_add_fusion), kind=kLoop, calls=%fused_computation.23 | loop fusion | flops 835584 | bytes 288256 | tf_op jit(solution)/shard_map/and | solution.py:99
  14.9 5.7 %collective-permute-start.2 = (bf16[3,128,256]{1,2,0:T(8,128)(2,1)S(1)}, bf16[3,128,256]{1,2,0:T(8,128)(2,1)S(1)}, u32[]{:S(2)}, u32[]{:S(2)}) collective-permute-start(bf16[3,128,256]{1,2,0:T(8,128)(2,1)S(1)} %pad_maximum_fusion), channel_id=1, source_target_pairs={{0,56},{8,0},{16,8},{24,16},{32,24},{40,32},{48,40},{56,48},{64,12... | collective-permute-start | bytes 589832 | tf_op jit(solution)/shard_map/ppermute | solution.py:81
  20.8 2.9 %collective-permute-start.5 = (bf16[2,128,256]{1,2,0:T(8,128)(2,1)S(1)}, bf16[2,128,256]{1,2,0:T(8,128)(2,1)S(1)}, u32[]{:S(2)}, u32[]{:S(2)}) collective-permute-start(bf16[2,128,256]{1,2,0:T(8,128)(2,1)S(1)} %constant_dynamic-slice_fusion.1), channel_id=1, source_target_pairs={{0,32},{8,40},{16,48},{24,56},{32,0},{40,8},{48,16},{56,24},{64,96... | collective-permute-start | bytes 393224 | tf_op jit(solution)/shard_map/ppermute | solution.py:70
  23.7 3.3 %collective-permute-start.3 = (bf16[3,128,256]{1,2,0:T(8,128)(2,1)S(1)}, bf16[3,128,256]{1,2,0:T(8,128)(2,1)S(1)}, u32[]{:S(2)}, u32[]{:S(2)}) collective-permute-start(bf16[3,128,256]{1,2,0:T(8,128)(2,1)S(1)} %collective-permute-done.2), channel_id=1, source_target_pairs={{0,56},{8,0},{16,8},{24,16},{32,24},{40,32},{48,40},{56,48},{64,12... | collective-permute-start | bytes 589832 | tf_op jit(solution)/shard_map/ppermute | solution.py:81
  27.0 1.9 %collective-permute-done.6 = bf16[3,128,256]{1,2,0:T(8,128)(2,1)S(1)} collective-permute-done((bf16[3,128,256]{1,2,0:T(8,128)(2,1)S(1)}, bf16[3,128,256]{1,2,0:T(8,128)(2,1)S(1)}, u32[]{:S(2)}, u32[]{:S(2)}) %collective-permute-start.6) | collective-permute-done | bytes 196640 | tf_op jit(solution)/shard_map/ppermute | solution.py:81
  28.9 5.6 %collective-permute-done.3 = bf16[3,128,256]{1,2,0:T(8,128)(2,1)S(1)} collective-permute-done((bf16[3,128,256]{1,2,0:T(8,128)(2,1)S(1)}, bf16[3,128,256]{1,2,0:T(8,128)(2,1)S(1)}, u32[]{:S(2)}, u32[]{:S(2)}) %collective-permute-start.3) | collective-permute-done | bytes 196640 | tf_op jit(solution)/shard_map/ppermute | solution.py:81
  34.5 3.5 %collective-permute-start.4 = (bf16[2,128,256]{1,2,0:T(8,128)(2,1)S(1)}, bf16[2,128,256]{1,2,0:T(8,128)(2,1)S(1)}, u32[]{:S(2)}, u32[]{:S(2)}) collective-permute-start(bf16[2,128,256]{1,2,0:T(8,128)(2,1)S(1)} %constant_dynamic-slice_fusion.2), channel_id=1, source_target_pairs={{0,56},{8,0},{16,8},{24,16},{32,24},{40,32},{48,40},{56,48},{64,12... | collective-permute-start | bytes 393224 | tf_op jit(solution)/shard_map/ppermute | solution.py:81
  38.1 1.8 %collective-permute-done.4 = bf16[2,128,256]{1,2,0:T(8,128)(2,1)S(1)} collective-permute-done((bf16[2,128,256]{1,2,0:T(8,128)(2,1)S(1)}, bf16[2,128,256]{1,2,0:T(8,128)(2,1)S(1)}, u32[]{:S(2)}, u32[]{:S(2)}) %collective-permute-start.4) | collective-permute-done | bytes 131104 | tf_op jit(solution)/shard_map/ppermute | solution.py:81
  40.0 3.1 %collective-permute-done.8 = bf16[2,128,256]{1,2,0:T(8,128)(2,1)S(1)} collective-permute-done((bf16[2,128,256]{1,2,0:T(8,128)(2,1)S(1)}, bf16[2,128,256]{1,2,0:T(8,128)(2,1)S(1)}, u32[]{:S(2)}, u32[]{:S(2)}) %collective-permute-start.8) | collective-permute-done | bytes 131104 | tf_op jit(solution)/shard_map/ppermute | solution.py:81
  45.1 0.9 %fusion.33 = bf16[4,128,128]{1,2,0:T(8,128)(2,1)S(1)} fusion(f32[1,4,128,2176]{2,3,1,0:T(8,128)S(1)} %get-tuple-element.16, f32[4,128]{1,0:T(4,128)S(1)} %get-tuple-element.15, pred[128,2176]{0,1:T(8,128)(4,1)S(1)} %compare_and_fusion, bf16[2176,256]{0,1:T(8,128)(2,1)S(1)} %constant_dynamic-update-slice_fusion, f32[4,128]{1,0:T(4,128)S(1)} %fusion.2), kind=kOutput, calls=%fused_computation.25 | convolution fusion | flops 288686080 | bytes 5427200 | tf_op jit(solution)/shard_map/kgtn,nkd->kgtd/dot_general | solution.py:104
  46.0 2.9 %collective-permute-start.9 = (bf16[128,512]{0,1:T(8,128)(2,1)S(1)}, bf16[128,512]{0,1:T(8,128)(2,1)S(1)}, u32[]{:S(2)}, u32[]{:S(2)}) collective-permute-start(bf16[128,512]{0,1:T(8,128)(2,1)S(1)} %bitcast.100), channel_id=1, source_target_pairs={{0,1},{1,0},{2,3},{3,2},{4,5},{5,4},{6,7},{7,6},{8,9},{9,8},{10,11... | collective-permute-start | bytes 393224 | tf_op jit(solution)/shard_map/ppermute | solution.py:123
  48.9 1.0 %collective-permute-done.9 = bf16[128,512]{0,1:T(8,128)(2,1)S(1)} collective-permute-done((bf16[128,512]{0,1:T(8,128)(2,1)S(1)}, bf16[128,512]{0,1:T(8,128)(2,1)S(1)}, u32[]{:S(2)}, u32[]{:S(2)}) %collective-permute-start.9) | collective-permute-done | bytes 131104 | tf_op jit(solution)/shard_map/ppermute | solution.py:123
  50.0 1.3 %collective-permute-start.10 = (bf16[128,1024]{0,1:T(8,128)(2,1)S(1)}, bf16[128,1024]{0,1:T(8,128)(2,1)S(1)}, u32[]{:S(2)}, u32[]{:S(2)}) collective-permute-start(bf16[128,1024]{0,1:T(8,128)(2,1)S(1)} %maximum_select_fusion), channel_id=1, source_target_pairs={{0,2},{1,3},{2,4},{3,5},{4,6},{5,7},{6,0},{7,1},{8,10},{9,11},{10,... | collective-permute-start | bytes 786440 | tf_op jit(solution)/shard_map/ppermute | solution.py:129
  51.3 1.5 %collective-permute-start.11 = (bf16[128,1024]{0,1:T(8,128)(2,1)S(1)}, bf16[128,1024]{0,1:T(8,128)(2,1)S(1)}, u32[]{:S(2)}, u32[]{:S(2)}) collective-permute-start(bf16[128,1024]{0,1:T(8,128)(2,1)S(1)} %maximum_select_fusion), channel_id=1, source_target_pairs={{0,6},{1,7},{2,0},{3,1},{4,2},{5,3},{6,4},{7,5},{8,14},{9,15},{10,... | collective-permute-start | bytes 786440 | tf_op jit(solution)/shard_map/ppermute | solution.py:130
  52.7 6.0 %collective-permute-done.10 = bf16[128,1024]{0,1:T(8,128)(2,1)S(1)} collective-permute-done((bf16[128,1024]{0,1:T(8,128)(2,1)S(1)}, bf16[128,1024]{0,1:T(8,128)(2,1)S(1)}, u32[]{:S(2)}, u32[]{:S(2)}) %collective-permute-start.10) | collective-permute-done | bytes 262176 | tf_op jit(solution)/shard_map/ppermute | solution.py:129
  58.8 2.5 %collective-permute-start.12 = (bf16[128,1024]{0,1:T(8,128)(2,1)S(1)}, bf16[128,1024]{0,1:T(8,128)(2,1)S(1)}, u32[]{:S(2)}, u32[]{:S(2)}) collective-permute-start(bf16[128,1024]{0,1:T(8,128)(2,1)S(1)} %broadcast_select_fusion), channel_id=1, source_target_pairs={{0,2},{1,7},{2,4},{3,1},{4,6},{5,3},{6,0},{7,5},{8,10},{9,15},{10,... | collective-permute-start | bytes 786440 | tf_op jit(solution)/shard_map/ppermute | solution.py:132
  61.3 2.1 %fusion.14 = f32[128,1024]{1,0:T(8,128)S(1)} fusion(bf16[128,1024]{0,1:T(8,128)(2,1)S(1)} %collective-permute-done.10, bf16[4096,1024]{1,0:T(8,128)(2,1)} %param.9, s32[]{:T(128)S(6)} %select_n.162), kind=kOutput, calls=%fused_computation.15 | convolution fusion | flops 268435456 | bytes 2883588 | tf_op jit(solution)/shard_map/dot_general | solution.py:121
  63.3 2.1 %fusion.12 = f32[128,1024]{1,0:T(8,128)S(1)} fusion(bf16[128,1024]{0,1:T(8,128)(2,1)S(1)} %collective-permute-done.11, bf16[4096,1024]{1,0:T(8,128)(2,1)} %param.9, s32[]{:T(128)S(6)} %select_n.164), kind=kOutput, calls=%fused_computation.13 | convolution fusion | flops 268435456 | bytes 2883588 | tf_op jit(solution)/shard_map/dot_general | solution.py:121
  65.4 2.1 %fusion.10 = f32[128,1024]{1,0:T(8,128)S(1)} fusion(bf16[128,1024]{0,1:T(8,128)(2,1)S(1)} %collective-permute-done.12, bf16[4096,1024]{1,0:T(8,128)(2,1)} %param.9, s32[]{:T(128)S(6)} %select_n.167), kind=kOutput, calls=%fused_computation.11 | convolution fusion | flops 268435456 | bytes 2883588 | tf_op jit(solution)/shard_map/dot_general | solution.py:121
  67.5 2.8 %fusion.27 = bf16[128,1024]{1,0:T(8,128)(2,1)} fusion(f32[128,1024]{1,0:T(8,128)S(1)} %fusion.10, f32[128,1024]{1,0:T(8,128)S(1)} %fusion.12, f32[128,1024]{1,0:T(8,128)S(1)} %fusion.14, bf16[128,1024]{0,1:T(8,128)(2,1)S(1)} %maximum_select_fusion, bf16[4096,1024]{1,0:T(8,128)(2,1)} %param.9, s32[]{:T(128)S(6)} %select_n.160), kind=kOutput, calls=%fused_computation.22 | convolution fusion | flops 268959744 | bytes 4194308 | tf_op jit(solution)/shard_map/dot_general | solution.py:121
  (51 shorter events, 5.7 us)
Async XLA Ops:
  3.6 11.3 %collective-permute-start.1 = (bf16[128,256]{0,1:T(8,128)(2,1)S(1)}, bf16[128,256]{0,1:T(8,128)(2,1)S(1)}, u32[]{:S(2)}, u32[]{:S(2)}) collective-permute-start(bf16[128,256]{0,1:T(8,128)(2,1)S(1)} %get-tuple-element.12), channel_id=1, source_target_pairs={{0,64},{8,72},{16,80},{24,88},{32,96},{40,104},{48,112},{56,120},{... | collective-permute-start | bytes 196616 | tf_op jit(solution)/shard_map/ppermute | solution.py:61
  7.6 7.3 %collective-permute-start = (bf16[128,256]{0,1:T(8,128)(2,1)S(1)}, bf16[128,256]{0,1:T(8,128)(2,1)S(1)}, u32[]{:S(2)}, u32[]{:S(2)}) collective-permute-start(bf16[128,256]{0,1:T(8,128)(2,1)S(1)} %get-tuple-element.12), channel_id=1, source_target_pairs={{0,128},{8,136},{16,144},{24,152},{32,160},{40,168},{48,176},{56,1... | collective-permute-start | bytes 196616 | tf_op jit(solution)/shard_map/ppermute | solution.py:61
  14.9 8.8 %collective-permute-start.2 = (bf16[3,128,256]{1,2,0:T(8,128)(2,1)S(1)}, bf16[3,128,256]{1,2,0:T(8,128)(2,1)S(1)}, u32[]{:S(2)}, u32[]{:S(2)}) collective-permute-start(bf16[3,128,256]{1,2,0:T(8,128)(2,1)S(1)} %pad_maximum_fusion), channel_id=1, source_target_pairs={{0,56},{8,0},{16,8},{24,16},{32,24},{40,32},{48,40},{56,48},{64,12... | collective-permute-start | bytes 589832 | tf_op jit(solution)/shard_map/ppermute | solution.py:81
  20.7 8.2 %collective-permute-start.6 = (bf16[3,128,256]{1,2,0:T(8,128)(2,1)S(1)}, bf16[3,128,256]{1,2,0:T(8,128)(2,1)S(1)}, u32[]{:S(2)}, u32[]{:S(2)}) collective-permute-start(bf16[3,128,256]{1,2,0:T(8,128)(2,1)S(1)} %pad_maximum_fusion), channel_id=1, source_target_pairs={{0,8},{8,16},{16,24},{24,32},{32,40},{40,48},{48,56},{56,0},{64,72... | collective-permute-start | bytes 589832 | tf_op jit(solution)/shard_map/ppermute | solution.py:81
  20.8 19.2 %collective-permute-start.5 = (bf16[2,128,256]{1,2,0:T(8,128)(2,1)S(1)}, bf16[2,128,256]{1,2,0:T(8,128)(2,1)S(1)}, u32[]{:S(2)}, u32[]{:S(2)}) collective-permute-start(bf16[2,128,256]{1,2,0:T(8,128)(2,1)S(1)} %constant_dynamic-slice_fusion.1), channel_id=1, source_target_pairs={{0,32},{8,40},{16,48},{24,56},{32,0},{40,8},{48,16},{56,24},{64,96... | collective-permute-start | bytes 393224 | tf_op jit(solution)/shard_map/ppermute | solution.py:70
  23.7 10.8 %collective-permute-start.3 = (bf16[3,128,256]{1,2,0:T(8,128)(2,1)S(1)}, bf16[3,128,256]{1,2,0:T(8,128)(2,1)S(1)}, u32[]{:S(2)}, u32[]{:S(2)}) collective-permute-start(bf16[3,128,256]{1,2,0:T(8,128)(2,1)S(1)} %collective-permute-done.2), channel_id=1, source_target_pairs={{0,56},{8,0},{16,8},{24,16},{32,24},{40,32},{48,40},{56,48},{64,12... | collective-permute-start | bytes 589832 | tf_op jit(solution)/shard_map/ppermute | solution.py:81
  28.8 9.2 %collective-permute-start.7 = (bf16[3,128,256]{1,2,0:T(8,128)(2,1)S(1)}, bf16[3,128,256]{1,2,0:T(8,128)(2,1)S(1)}, u32[]{:S(2)}, u32[]{:S(2)}) collective-permute-start(bf16[3,128,256]{1,2,0:T(8,128)(2,1)S(1)} %collective-permute-done.6), channel_id=1, source_target_pairs={{0,8},{8,16},{16,24},{24,32},{32,40},{40,48},{48,56},{56,0},{64,72... | collective-permute-start | bytes 589832 | tf_op jit(solution)/shard_map/ppermute | solution.py:81
  34.5 5.4 %collective-permute-start.4 = (bf16[2,128,256]{1,2,0:T(8,128)(2,1)S(1)}, bf16[2,128,256]{1,2,0:T(8,128)(2,1)S(1)}, u32[]{:S(2)}, u32[]{:S(2)}) collective-permute-start(bf16[2,128,256]{1,2,0:T(8,128)(2,1)S(1)} %constant_dynamic-slice_fusion.2), channel_id=1, source_target_pairs={{0,56},{8,0},{16,8},{24,16},{32,24},{40,32},{48,40},{56,48},{64,12... | collective-permute-start | bytes 393224 | tf_op jit(solution)/shard_map/ppermute | solution.py:81
  38.0 5.1 %collective-permute-start.8 = (bf16[2,128,256]{1,2,0:T(8,128)(2,1)S(1)}, bf16[2,128,256]{1,2,0:T(8,128)(2,1)S(1)}, u32[]{:S(2)}, u32[]{:S(2)}) collective-permute-start(bf16[2,128,256]{1,2,0:T(8,128)(2,1)S(1)} %constant_dynamic-slice_fusion), channel_id=1, source_target_pairs={{0,8},{8,16},{16,24},{24,32},{32,40},{40,48},{48,56},{56,0},{64,72... | collective-permute-start | bytes 393224 | tf_op jit(solution)/shard_map/ppermute | solution.py:81
  46.0 3.9 %collective-permute-start.9 = (bf16[128,512]{0,1:T(8,128)(2,1)S(1)}, bf16[128,512]{0,1:T(8,128)(2,1)S(1)}, u32[]{:S(2)}, u32[]{:S(2)}) collective-permute-start(bf16[128,512]{0,1:T(8,128)(2,1)S(1)} %bitcast.100), channel_id=1, source_target_pairs={{0,1},{1,0},{2,3},{3,2},{4,5},{5,4},{6,7},{7,6},{8,9},{9,8},{10,11... | collective-permute-start | bytes 393224 | tf_op jit(solution)/shard_map/ppermute | solution.py:123
  50.0 8.8 %collective-permute-start.10 = (bf16[128,1024]{0,1:T(8,128)(2,1)S(1)}, bf16[128,1024]{0,1:T(8,128)(2,1)S(1)}, u32[]{:S(2)}, u32[]{:S(2)}) collective-permute-start(bf16[128,1024]{0,1:T(8,128)(2,1)S(1)} %maximum_select_fusion), channel_id=1, source_target_pairs={{0,2},{1,3},{2,4},{3,5},{4,6},{5,7},{6,0},{7,1},{8,10},{9,11},{10,... | collective-permute-start | bytes 786440 | tf_op jit(solution)/shard_map/ppermute | solution.py:129
  51.3 7.5 %collective-permute-start.11 = (bf16[128,1024]{0,1:T(8,128)(2,1)S(1)}, bf16[128,1024]{0,1:T(8,128)(2,1)S(1)}, u32[]{:S(2)}, u32[]{:S(2)}) collective-permute-start(bf16[128,1024]{0,1:T(8,128)(2,1)S(1)} %maximum_select_fusion), channel_id=1, source_target_pairs={{0,6},{1,7},{2,0},{3,1},{4,2},{5,3},{6,4},{7,5},{8,14},{9,15},{10,... | collective-permute-start | bytes 786440 | tf_op jit(solution)/shard_map/ppermute | solution.py:130
  58.8 6.6 %collective-permute-start.12 = (bf16[128,1024]{0,1:T(8,128)(2,1)S(1)}, bf16[128,1024]{0,1:T(8,128)(2,1)S(1)}, u32[]{:S(2)}, u32[]{:S(2)}) collective-permute-start(bf16[128,1024]{0,1:T(8,128)(2,1)S(1)} %broadcast_select_fusion), channel_id=1, source_target_pairs={{0,2},{1,7},{2,4},{3,1},{4,6},{5,3},{6,0},{7,5},{8,10},{9,15},{10,... | collective-permute-start | bytes 786440 | tf_op jit(solution)/shard_map/ppermute | solution.py:132

commit v12 on v8

--- a/solution.py
+++ b/solution.py
@@ -64,16 +64,7 @@
         z = ctx % row
         n_rows = n_ctx // row
         chains, direct = relay_plan(row, rows_back)
-        if direct:
-            half = row // 2
-            lo = jnp.where((z + half) % row < half, 1, 0)
-            got = lax.ppermute(
-                lax.dynamic_slice_in_dim(bundle, lo, rows_back, 0),
-                "ctx",
-                [(r * row + s, r * row + (s + half) % row) for r in range(n_rows) for s in range(row)],
-            )
-            for m in range(rows_back):
-                blocks[half + row * m] = got[m]
+        first_round = []
         for chain in chains:
             packet = bundle
             for step in chain:
@@ -83,10 +74,23 @@
                     "ctx",
                     [(r * row + s, r * row + (s + step["dir"]) % row) for r in range(n_rows) for s in range(row)],
                 )
+                if not first_round:
+                    first_round.append(packet)
                 at = pick(step["take"], z)
                 got = lax.dynamic_slice_in_dim(packet, at, len(step["blocks"]), 0)
                 for i, blk in enumerate(step["blocks"]):
                     blocks[blk] = got[i]
+        if direct:
+            half = row // 2
+            lo = jnp.where((z + half) % row < half, 1, 0)
+            payload, _ = lax.optimization_barrier((lax.dynamic_slice_in_dim(bundle, lo, rows_back, 0), first_round[0]))
+            got = lax.ppermute(
+                payload,
+                "ctx",
+                [(r * row + s, r * row + (s + half) % row) for r in range(n_rows) for s in range(row)],
+            )
+            for m in range(rows_back):
+                blocks[half + row * m] = got[m]
         window = jnp.concatenate([blocks[span - k] for k in range(span + 1)], axis=0)
         key_count = window.shape[0]
         key_block = window[:, :kv_width].reshape(key_count, kv_local, HD)

time: 63.9 us -> 66.8 us (1.045)
  starting transfers between devices: 35.9 us -> 40.7 us
  waiting for transfers between devices: 14.3 us -> 12.5 us
    ppermute x1, starting transfers between devices: 3.32 us -> 7.39 us  [on_device(): partner = lax.ppermute(attended, 'head', swap)]
    ppermute x6, starting transfers between devices: 12.5 us -> 14.6 us  [on_device(): lax.ppermute(lax.dynamic_slice_in_dim(packet, lo, step['width'], 0), 'ctx...]
    ppermute x6, waiting for transfers between devices: 12.5 us -> 10.7 us  [on_device(): lax.ppermute(lax.dynamic_slice_in_dim(packet, lo, step['width'], 0), 'ctx...]
    ppermute x1, starting transfers between devices: 2.86 us -> 1.56 us  [on_device(): lax.ppermute(payload, 'ctx', [(r * row + s, r * row + (s + half) % row) f...]
  transfers between devices with their start and end apart: 15 -> 15, of which waited for: 5 -> 7; matrix products, arithmetic and copies ran while one was open for 7% -> 7% of each run, Pallas kernels for 0% -> 0%
where the time goes in v12:
time: 66.8 us; the launch traced here: 66.6 us
  starting transfers between devices  40.7 us (61%)
  waiting for transfers between devices  12.5 us (19%)
  matrix products  5.18 us (8%)
  other arithmetic  4.11 us (6%)
  local copies, waits for them, and re-layouts  3.42 us (5%)
    ppermute x6, starting transfers between devices, on_device(): lax.ppermute(lax.dynamic_slice_in_dim(packet, lo, step['width'], 0), 'ctx...  14.6 us
    ppermute x6, waiting for transfers between devices, on_device(): lax.ppermute(lax.dynamic_slice_in_dim(packet, lo, step['width'], 0), 'ctx...  10.7 us
    ppermute x2, starting transfers between devices, on_device(): lax.ppermute(own, 'ctx', [(s, s + shift) for s in range(n_ctx - shift)])  8.55 us
    ppermute x1, starting transfers between devices, on_device(): partner = lax.ppermute(attended, 'head', swap)  7.39 us
    ppermute x1, starting transfers between devices, on_device(): lax.ppermute(jnp.where(core == 1, up, down), 'head', cross_pairs)  4.26 us
    dot_general x8, matrix products, project(): return jnp.dot(piece, rows, preferred_element_type=jnp.float32)  3.43 us
    unnamed x25, local copies, waits for them, and re-layouts  3.36 us
    ppermute x1, waiting for transfers between devices, on_device(): lax.ppermute(jnp.where(core == 1, up, down), 'head', cross_pairs)  1.82 us
  transfers between devices with their start and end apart: 15, of which 7 were waited for; matrix products, arithmetic and copies ran while one was open for 7% of the time, Pallas kernels for 0%

profile of v12, /device:TPU:1, one launch (start us, length us, event | category | flops | bytes accessed | tf_op | source)
XLA Modules:
  0.0 66.6 jit_solution(4568731083574923864)
XLA Ops:
  1.5 0.9 %copy.18 = bf16[128,128]{0,1:T(8,128)(2,1)S(1)} copy(bf16[128,128]{1,0:T(8,128)(2,1)} %param.6) | data formatting | bytes 65536 | tf_op args[1]
  2.4 0.9 %copy.19 = bf16[128,128]{0,1:T(8,128)(2,1)S(1)} copy(bf16[128,128]{1,0:T(8,128)(2,1)} %param.7) | data formatting | bytes 65536 | tf_op args[2]
  3.6 4.0 %collective-permute-start.1 = (bf16[128,256]{0,1:T(8,128)(2,1)S(1)}, bf16[128,256]{0,1:T(8,128)(2,1)S(1)}, u32[]{:S(2)}, u32[]{:S(2)}) collective-permute-start(bf16[128,256]{0,1:T(8,128)(2,1)S(1)} %get-tuple-element.16), channel_id=1, source_target_pairs={{0,64},{8,72},{16,80},{24,88},{32,96},{40,104},{48,112},{56,120},{... | collective-permute-start | bytes 196616 | tf_op jit(solution)/shard_map/ppermute | solution.py:61
  7.6 4.5 %collective-permute-start = (bf16[128,256]{0,1:T(8,128)(2,1)S(1)}, bf16[128,256]{0,1:T(8,128)(2,1)S(1)}, u32[]{:S(2)}, u32[]{:S(2)}) collective-permute-start(bf16[128,256]{0,1:T(8,128)(2,1)S(1)} %get-tuple-element.16), channel_id=1, source_target_pairs={{0,128},{8,136},{16,144},{24,152},{32,160},{40,168},{48,176},{56,1... | collective-permute-start | bytes 196616 | tf_op jit(solution)/shard_map/ppermute | solution.py:61
  12.1 1.0 %copy.20 = bf16[128,512]{0,1:T(8,128)(2,1)S(1)} copy(bf16[128,512]{1,0:T(8,128)(2,1)} %param.5) | data formatting | bytes 262144 | tf_op args[0]
  13.2 1.0 %compare_and_fusion = pred[128,2176]{0,1:T(8,128)(4,1)S(1)} fusion(s32[128]{0:T(128)S(1)} %select_reduce_fusion, s32[128]{0:T(128)S(1)} %iota_add_fusion.1, s32[2176]{0:T(1024)S(1)} %iota_add_fusion), kind=kLoop, calls=%fused_computation.19 | loop fusion | flops 835584 | bytes 288256 | tf_op jit(solution)/shard_map/and | solution.py:103
  14.9 5.7 %collective-permute-start.2 = (bf16[3,128,256]{1,2,0:T(8,128)(2,1)S(1)}, bf16[3,128,256]{1,2,0:T(8,128)(2,1)S(1)}, u32[]{:S(2)}, u32[]{:S(2)}) collective-permute-start(bf16[3,128,256]{1,2,0:T(8,128)(2,1)S(1)} %pad_maximum_fusion.1), channel_id=1, source_target_pairs={{0,56},{8,0},{16,8},{24,16},{32,24},{40,32},{48,40},{56,48},{64,12... | collective-permute-start | bytes 589832 | tf_op jit(solution)/shard_map/ppermute | solution.py:72
  20.9 2.6 %collective-permute-done.2 = bf16[3,128,256]{1,2,0:T(8,128)(2,1)S(1)} collective-permute-done((bf16[3,128,256]{1,2,0:T(8,128)(2,1)S(1)}, bf16[3,128,256]{1,2,0:T(8,128)(2,1)S(1)}, u32[]{:S(2)}, u32[]{:S(2)}) %collective-permute-start.2) | collective-permute-done | bytes 196640 | tf_op jit(solution)/shard_map/ppermute | solution.py:72
  23.6 3.4 %collective-permute-start.3 = (bf16[3,128,256]{1,2,0:T(8,128)(2,1)S(1)}, bf16[3,128,256]{1,2,0:T(8,128)(2,1)S(1)}, u32[]{:S(2)}, u32[]{:S(2)}) collective-permute-start(bf16[3,128,256]{1,2,0:T(8,128)(2,1)S(1)} %collective-permute-done.2), channel_id=1, source_target_pairs={{0,56},{8,0},{16,8},{24,16},{32,24},{40,32},{48,40},{56,48},{64,12... | collective-permute-start | bytes 589832 | tf_op jit(solution)/shard_map/ppermute | solution.py:72
  27.0 1.6 %collective-permute-start.6 = (bf16[2,128,256]{1,2,0:T(8,128)(2,1)S(1)}, bf16[2,128,256]{1,2,0:T(8,128)(2,1)S(1)}, u32[]{:S(2)}, u32[]{:S(2)}) collective-permute-start(bf16[2,128,256]{1,2,0:T(8,128)(2,1)S(1)} %constant_dynamic-slice_fusion.1), channel_id=1, source_target_pairs={{0,32},{8,40},{16,48},{24,56},{32,0},{40,8},{48,16},{56,24},{64,96... | collective-permute-start | bytes 393224 | tf_op jit(solution)/shard_map/ppermute | solution.py:87
  28.7 1.4 %collective-permute-done.3 = bf16[3,128,256]{1,2,0:T(8,128)(2,1)S(1)} collective-permute-done((bf16[3,128,256]{1,2,0:T(8,128)(2,1)S(1)}, bf16[3,128,256]{1,2,0:T(8,128)(2,1)S(1)}, u32[]{:S(2)}, u32[]{:S(2)}) %collective-permute-start.3) | collective-permute-done | bytes 196640 | tf_op jit(solution)/shard_map/ppermute | solution.py:72
  30.1 3.8 %collective-permute-start.4 = (bf16[2,128,256]{1,2,0:T(8,128)(2,1)S(1)}, bf16[2,128,256]{1,2,0:T(8,128)(2,1)S(1)}, u32[]{:S(2)}, u32[]{:S(2)}) collective-permute-start(bf16[2,128,256]{1,2,0:T(8,128)(2,1)S(1)} %constant_dynamic-slice_fusion.2), channel_id=1, source_target_pairs={{0,56},{8,0},{16,8},{24,16},{32,24},{40,32},{48,40},{56,48},{64,12... | collective-permute-start | bytes 393224 | tf_op jit(solution)/shard_map/ppermute | solution.py:72
  33.9 2.7 %collective-permute-done.7 = bf16[3,128,256]{1,2,0:T(8,128)(2,1)S(1)} collective-permute-done((bf16[3,128,256]{1,2,0:T(8,128)(2,1)S(1)}, bf16[3,128,256]{1,2,0:T(8,128)(2,1)S(1)}, u32[]{:S(2)}, u32[]{:S(2)}) %collective-permute-start.7) | collective-permute-done | bytes 196640 | tf_op jit(solution)/shard_map/ppermute | solution.py:72
  36.6 1.6 %collective-permute-start.8 = (bf16[2,128,256]{1,2,0:T(8,128)(2,1)S(1)}, bf16[2,128,256]{1,2,0:T(8,128)(2,1)S(1)}, u32[]{:S(2)}, u32[]{:S(2)}) collective-permute-start(bf16[2,128,256]{1,2,0:T(8,128)(2,1)S(1)} %constant_dynamic-slice_fusion), channel_id=1, source_target_pairs={{0,8},{8,16},{16,24},{24,32},{32,40},{40,48},{48,56},{56,0},{64,72... | collective-permute-start | bytes 393224 | tf_op jit(solution)/shard_map/ppermute | solution.py:72
  38.8 3.4 %collective-permute-done.8 = bf16[2,128,256]{1,2,0:T(8,128)(2,1)S(1)} collective-permute-done((bf16[2,128,256]{1,2,0:T(8,128)(2,1)S(1)}, bf16[2,128,256]{1,2,0:T(8,128)(2,1)S(1)}, u32[]{:S(2)}, u32[]{:S(2)}) %collective-permute-start.8) | collective-permute-done | bytes 131104 | tf_op jit(solution)/shard_map/ppermute | solution.py:72
  42.5 0.8 %fusion.73 = (f32[4,128]{1,0:T(4,128)S(1)}, f32[1,4,128,2176]{2,3,1,0:T(8,128)S(1)}) fusion(bf16[128,4,64]{2,0,1:T(8,128)(2,1)S(1)} %get-tuple-element.8, bf16[128,4,64]{2,0,1:T(8,128)(2,1)S(1)} %get-tuple-element.7, bf16[2176,256]{0,1:T(8,128)(2,1)S(1)} %constant_dynamic-update-slice_fusion, pred[128,2176]{0,1:T(8,128)(4,1)S(1)} %compare_and_fusion), kind=kOutput, calls=%fused_computation.117 | convolution fusion | flops 288816640 | bytes 5556224 | tf_op jit(solution)/shard_map/tkgd,nkd->kgtn/dot_general | solution.py:99
  44.2 0.9 %fusion.19 = bf16[4,128,128]{1,2,0:T(8,128)(2,1)S(1)} fusion(f32[1,4,128,2176]{2,3,1,0:T(8,128)S(1)} %get-tuple-element.20, f32[4,128]{1,0:T(4,128)S(1)} %get-tuple-element.19, pred[128,2176]{0,1:T(8,128)(4,1)S(1)} %compare_and_fusion, bf16[2176,256]{0,1:T(8,128)(2,1)S(1)} %constant_dynamic-update-slice_fusion, f32[4,128]{1,0:T(4,128)S(1)} %fusion.2), kind=kOutput, calls=%fused_computation.21 | convolution fusion | flops 288686080 | bytes 5427200 | tf_op jit(solution)/shard_map/kgtn,nkd->kgtd/dot_general | solution.py:108
  45.1 1.3 %collective-permute-start.9 = (bf16[128,512]{0,1:T(8,128)(2,1)S(1)}, bf16[128,512]{0,1:T(8,128)(2,1)S(1)}, u32[]{:S(2)}, u32[]{:S(2)}) collective-permute-start(bf16[128,512]{0,1:T(8,128)(2,1)S(1)} %bitcast.114), channel_id=1, source_target_pairs={{0,2},{1,3},{2,4},{3,5},{4,6},{5,7},{6,0},{7,1},{8,10},{9,11},{10,... | collective-permute-start | bytes 393224 | tf_op jit(solution)/shard_map/ppermute | solution.py:125
  46.4 1.5 %collective-permute-start.10 = (bf16[128,512]{0,1:T(8,128)(2,1)S(1)}, bf16[128,512]{0,1:T(8,128)(2,1)S(1)}, u32[]{:S(2)}, u32[]{:S(2)}) collective-permute-start(bf16[128,512]{0,1:T(8,128)(2,1)S(1)} %bitcast.115), channel_id=1, source_target_pairs={{0,6},{1,7},{2,0},{3,1},{4,2},{5,3},{6,4},{7,5},{8,14},{9,15},{10,... | collective-permute-start | bytes 393224 | tf_op jit(solution)/shard_map/ppermute | solution.py:126
  47.9 7.4 %collective-permute-start.11 = (bf16[128,512]{0,1:T(8,128)(2,1)S(1)}, bf16[128,512]{0,1:T(8,128)(2,1)S(1)}, u32[]{:S(2)}, u32[]{:S(2)}) collective-permute-start(bf16[128,512]{0,1:T(8,128)(2,1)S(1)} %bitcast.116), channel_id=1, source_target_pairs={{0,1},{1,0},{2,3},{3,2},{4,5},{5,4},{6,7},{7,6},{8,9},{9,8},{10,11... | collective-permute-start | bytes 393224 | tf_op jit(solution)/shard_map/ppermute | solution.py:128
  55.6 1.5 %collective-permute-start.12 = (bf16[128,512]{0,1:T(8,128)(2,1)S(1)}, bf16[128,512]{0,1:T(8,128)(2,1)S(1)}, u32[]{:S(2)}, u32[]{:S(2)}) collective-permute-start(bf16[128,512]{0,1:T(8,128)(2,1)S(1)} %get-tuple-element.9), channel_id=1, source_target_pairs={{0,2},{1,7},{2,4},{3,1},{4,6},{5,3},{6,0},{7,5},{8,10},{9,15},{10,... | collective-permute-start | bytes 393224 | tf_op jit(solution)/shard_map/ppermute | solution.py:130
  57.2 4.3 %collective-permute-start.13 = (bf16[128,512]{0,1:T(8,128)(2,1)S(1)}, bf16[128,512]{0,1:T(8,128)(2,1)S(1)}, u32[]{:S(2)}, u32[]{:S(2)}) collective-permute-start(bf16[128,512]{0,1:T(8,128)(2,1)S(1)} %get-tuple-element.10), channel_id=1, source_target_pairs={{0,7},{1,2},{2,1},{3,4},{4,3},{5,6},{6,5},{7,0},{8,15},{9,10},{10,... | collective-permute-start | bytes 393224 | tf_op jit(solution)/shard_map/ppermute | solution.py:132
  62.6 1.8 %collective-permute-done.13 = bf16[128,512]{0,1:T(8,128)(2,1)S(1)} collective-permute-done((bf16[128,512]{0,1:T(8,128)(2,1)S(1)}, bf16[128,512]{0,1:T(8,128)(2,1)S(1)}, u32[]{:S(2)}, u32[]{:S(2)}) %collective-permute-start.13) | collective-permute-done | bytes 131104 | tf_op jit(solution)/shard_map/ppermute | solution.py:132
  65.4 1.1 %fusion.15 = bf16[128,1024]{1,0:T(8,128)(2,1)} fusion(f32[128,1024]{1,0:T(8,128)S(1)} %fusion.22, f32[128,1024]{1,0:T(8,128)S(1)} %fusion.24, f32[128,1024]{1,0:T(8,128)S(1)} %fusion.26, f32[128,1024]{1,0:T(8,128)S(1)} %fusion.28, f32[128,1024]{1,0:T(8,128)S(1)} %fusion.30, f32[128,1024]{1,0:T(8,128)S(1)} %convolution_add_fusion.1, ...), kind=kOutput, calls=%fused_computation.18 | convolution fusion | flops 135135232 | bytes 4587524 | tf_op jit(solution)/shard_map/dot_general | solution.py:123
  (64 shorter events, 6.8 us)
Async XLA Ops:
  3.6 11.3 %collective-permute-start.1 = (bf16[128,256]{0,1:T(8,128)(2,1)S(1)}, bf16[128,256]{0,1:T(8,128)(2,1)S(1)}, u32[]{:S(2)}, u32[]{:S(2)}) collective-permute-start(bf16[128,256]{0,1:T(8,128)(2,1)S(1)} %get-tuple-element.16), channel_id=1, source_target_pairs={{0,64},{8,72},{16,80},{24,88},{32,96},{40,104},{48,112},{56,120},{... | collective-permute-start | bytes 196616 | tf_op jit(solution)/shard_map/ppermute | solution.py:61
  7.6 7.3 %collective-permute-start = (bf16[128,256]{0,1:T(8,128)(2,1)S(1)}, bf16[128,256]{0,1:T(8,128)(2,1)S(1)}, u32[]{:S(2)}, u32[]{:S(2)}) collective-permute-start(bf16[128,256]{0,1:T(8,128)(2,1)S(1)} %get-tuple-element.16), channel_id=1, source_target_pairs={{0,128},{8,136},{16,144},{24,152},{32,160},{40,168},{48,176},{56,1... | collective-permute-start | bytes 196616 | tf_op jit(solution)/shard_map/ppermute | solution.py:61
  14.9 8.7 %collective-permute-start.2 = (bf16[3,128,256]{1,2,0:T(8,128)(2,1)S(1)}, bf16[3,128,256]{1,2,0:T(8,128)(2,1)S(1)}, u32[]{:S(2)}, u32[]{:S(2)}) collective-permute-start(bf16[3,128,256]{1,2,0:T(8,128)(2,1)S(1)} %pad_maximum_fusion.1), channel_id=1, source_target_pairs={{0,56},{8,0},{16,8},{24,16},{32,24},{40,32},{48,40},{56,48},{64,12... | collective-permute-start | bytes 589832 | tf_op jit(solution)/shard_map/ppermute | solution.py:72
  20.8 6.2 %collective-permute-start.5 = (bf16[3,128,256]{1,2,0:T(8,128)(2,1)S(1)}, bf16[3,128,256]{1,2,0:T(8,128)(2,1)S(1)}, u32[]{:S(2)}, u32[]{:S(2)}) collective-permute-start(bf16[3,128,256]{1,2,0:T(8,128)(2,1)S(1)} %pad_maximum_fusion.1), channel_id=1, source_target_pairs={{0,8},{8,16},{16,24},{24,32},{32,40},{40,48},{48,56},{56,0},{64,72... | collective-permute-start | bytes 589832 | tf_op jit(solution)/shard_map/ppermute | solution.py:72
  23.6 6.6 %collective-permute-start.3 = (bf16[3,128,256]{1,2,0:T(8,128)(2,1)S(1)}, bf16[3,128,256]{1,2,0:T(8,128)(2,1)S(1)}, u32[]{:S(2)}, u32[]{:S(2)}) collective-permute-start(bf16[3,128,256]{1,2,0:T(8,128)(2,1)S(1)} %collective-permute-done.2), channel_id=1, source_target_pairs={{0,56},{8,0},{16,8},{24,16},{32,24},{40,32},{48,40},{56,48},{64,12... | collective-permute-start | bytes 589832 | tf_op jit(solution)/shard_map/ppermute | solution.py:72
  27.0 11.7 %collective-permute-start.6 = (bf16[2,128,256]{1,2,0:T(8,128)(2,1)S(1)}, bf16[2,128,256]{1,2,0:T(8,128)(2,1)S(1)}, u32[]{:S(2)}, u32[]{:S(2)}) collective-permute-start(bf16[2,128,256]{1,2,0:T(8,128)(2,1)S(1)} %constant_dynamic-slice_fusion.1), channel_id=1, source_target_pairs={{0,32},{8,40},{16,48},{24,56},{32,0},{40,8},{48,16},{56,24},{64,96... | collective-permute-start | bytes 393224 | tf_op jit(solution)/shard_map/ppermute | solution.py:87
  28.6 8.0 %collective-permute-start.7 = (bf16[3,128,256]{1,2,0:T(8,128)(2,1)S(1)}, bf16[3,128,256]{1,2,0:T(8,128)(2,1)S(1)}, u32[]{:S(2)}, u32[]{:S(2)}) collective-permute-start(bf16[3,128,256]{1,2,0:T(8,128)(2,1)S(1)} %collective-permute-done.5), channel_id=1, source_target_pairs={{0,8},{8,16},{16,24},{24,32},{32,40},{40,48},{48,56},{56,0},{64,72... | collective-permute-start | bytes 589832 | tf_op jit(solution)/shard_map/ppermute | solution.py:72
  30.1 8.6 %collective-permute-start.4 = (bf16[2,128,256]{1,2,0:T(8,128)(2,1)S(1)}, bf16[2,128,256]{1,2,0:T(8,128)(2,1)S(1)}, u32[]{:S(2)}, u32[]{:S(2)}) collective-permute-start(bf16[2,128,256]{1,2,0:T(8,128)(2,1)S(1)} %constant_dynamic-slice_fusion.2), channel_id=1, source_target_pairs={{0,56},{8,0},{16,8},{24,16},{32,24},{40,32},{48,40},{56,48},{64,12... | collective-permute-start | bytes 393224 | tf_op jit(solution)/shard_map/ppermute | solution.py:72
  36.6 5.5 %collective-permute-start.8 = (bf16[2,128,256]{1,2,0:T(8,128)(2,1)S(1)}, bf16[2,128,256]{1,2,0:T(8,128)(2,1)S(1)}, u32[]{:S(2)}, u32[]{:S(2)}) collective-permute-start(bf16[2,128,256]{1,2,0:T(8,128)(2,1)S(1)} %constant_dynamic-slice_fusion), channel_id=1, source_target_pairs={{0,8},{8,16},{16,24},{24,32},{32,40},{40,48},{48,56},{56,0},{64,72... | collective-permute-start | bytes 393224 | tf_op jit(solution)/shard_map/ppermute | solution.py:72
  42.5 12.8 %slice-start = ((s8[8388608]{0:T(1024)(128)(4,1)}), s8[4194304]{0:T(1024)(128)(4,1)S(1)}, s32[]{:S(2)}) async-start(s8[8388608]{0:T(1024)(128)(4,1)} %bitcast.107), calls=%async_computation | async-start | bytes 8388608
  43.4 11.9 %slice-start.1 = ((s8[8388608]{0:T(1024)(128)(4,1)}), s8[4194304]{0:T(1024)(128)(4,1)S(1)}, s32[]{:S(2)}) async-start(s8[8388608]{0:T(1024)(128)(4,1)} %bitcast.107), calls=%async_computation.1 | async-start | bytes 8388608
  45.1 10.5 %collective-permute-start.9 = (bf16[128,512]{0,1:T(8,128)(2,1)S(1)}, bf16[128,512]{0,1:T(8,128)(2,1)S(1)}, u32[]{:S(2)}, u32[]{:S(2)}) collective-permute-start(bf16[128,512]{0,1:T(8,128)(2,1)S(1)} %bitcast.114), channel_id=1, source_target_pairs={{0,2},{1,3},{2,4},{3,5},{4,6},{5,7},{6,0},{7,1},{8,10},{9,11},{10,... | collective-permute-start | bytes 393224 | tf_op jit(solution)/shard_map/ppermute | solution.py:125
  46.4 9.2 %collective-permute-start.10 = (bf16[128,512]{0,1:T(8,128)(2,1)S(1)}, bf16[128,512]{0,1:T(8,128)(2,1)S(1)}, u32[]{:S(2)}, u32[]{:S(2)}) collective-permute-start(bf16[128,512]{0,1:T(8,128)(2,1)S(1)} %bitcast.115), channel_id=1, source_target_pairs={{0,6},{1,7},{2,0},{3,1},{4,2},{5,3},{6,4},{7,5},{8,14},{9,15},{10,... | collective-permute-start | bytes 393224 | tf_op jit(solution)/shard_map/ppermute | solution.py:126
  47.9 14.0 %collective-permute-start.11 = (bf16[128,512]{0,1:T(8,128)(2,1)S(1)}, bf16[128,512]{0,1:T(8,128)(2,1)S(1)}, u32[]{:S(2)}, u32[]{:S(2)}) collective-permute-start(bf16[128,512]{0,1:T(8,128)(2,1)S(1)} %bitcast.116), channel_id=1, source_target_pairs={{0,1},{1,0},{2,3},{3,2},{4,5},{5,4},{6,7},{7,6},{8,9},{9,8},{10,11... | collective-permute-start | bytes 393224 | tf_op jit(solution)/shard_map/ppermute | solution.py:128
  55.6 6.6 %collective-permute-start.12 = (bf16[128,512]{0,1:T(8,128)(2,1)S(1)}, bf16[128,512]{0,1:T(8,128)(2,1)S(1)}, u32[]{:S(2)}, u32[]{:S(2)}) collective-permute-start(bf16[128,512]{0,1:T(8,128)(2,1)S(1)} %get-tuple-element.9), channel_id=1, source_target_pairs={{0,2},{1,7},{2,4},{3,1},{4,6},{5,3},{6,0},{7,5},{8,10},{9,15},{10,... | collective-permute-start | bytes 393224 | tf_op jit(solution)/shard_map/ppermute | solution.py:130
  57.2 7.3 %collective-permute-start.13 = (bf16[128,512]{0,1:T(8,128)(2,1)S(1)}, bf16[128,512]{0,1:T(8,128)(2,1)S(1)}, u32[]{:S(2)}, u32[]{:S(2)}) collective-permute-start(bf16[128,512]{0,1:T(8,128)(2,1)S(1)} %get-tuple-element.10), channel_id=1, source_target_pairs={{0,7},{1,2},{2,1},{3,4},{4,3},{5,6},{6,5},{7,0},{8,15},{9,10},{10,... | collective-permute-start | bytes 393224 | tf_op jit(solution)/shard_map/ppermute | solution.py:132
  61.5 3.3 %collective-permute-start.14 = (bf16[2,128,512]{1,2,0:T(8,128)(2,1)S(1)}, bf16[2,128,512]{1,2,0:T(8,128)(2,1)S(1)}, u32[]{:S(2)}, u32[]{:S(2)}) collective-permute-start(bf16[2,128,512]{1,2,0:T(8,128)(2,1)S(1)} %pad_maximum_fusion), channel_id=1, source_target_pairs={{0,1},{1,0},{2,3},{3,2},{4,5},{5,4},{6,7},{7,6},{8,9},{9,8},{10,11... | collective-permute-start | bytes 786440 | tf_op jit(solution)/shard_map/ppermute | solution.py:133

commit v13 on v8

--- a/solution.py
+++ b/solution.py
@@ -47,18 +47,22 @@
         rows_back = -(-back // row)
         span = rows_back * row
         ctx = lax.axis_index("ctx")
+        raw = jnp.concatenate([key_proj, value_proj], axis=1)
+        raw, lengths = lax.optimization_barrier((raw, lengths))
         first_row = ctx * tok_rows
         positions = first_row + jnp.arange(tok_rows, dtype=jnp.int32)
         starts = doc_starts(lengths, positions)
         offsets = positions - starts
         q_rot = rotary(queries, offsets, HD).reshape(tok_rows, kv_local, query_group, HD)
-        k_rot = rotary(key_proj, offsets, HD)
-        own = jnp.concatenate([k_rot, value_proj], axis=1)
+        own = jnp.concatenate([rotary(key_proj, offsets, HD), value_proj], axis=1)
 
         bundle = [own]
         for m in range(1, rows_back + 1):
             shift = row * m
-            bundle.append(lax.ppermute(own, "ctx", [(s, s + shift) for s in range(n_ctx - shift)]))
+            got = lax.ppermute(raw, "ctx", [(s, s + shift) for s in range(n_ctx - shift)])
+            pos = (ctx - shift) * tok_rows + jnp.arange(tok_rows, dtype=jnp.int32)
+            k_rot = rotary(got[:, :kv_width], pos - doc_starts(lengths, pos), HD)
+            bundle.append(jnp.concatenate([k_rot, got[:, kv_width:]], axis=1))
         blocks = {row * m: bundle[m] for m in range(rows_back + 1)}
         bundle = jnp.stack(bundle)
         z = ctx % row

time: 63.9 us -> 66.6 us (1.042)
  starting transfers between devices: 35.9 us -> 41.3 us
  waiting for transfers between devices: 14.3 us -> 11.9 us
    ppermute x1, starting transfers between devices: 3.32 us -> 7.74 us  [on_device(): partner = lax.ppermute(attended, 'head', swap)]
    ppermute x6, waiting for transfers between devices: 12.5 us -> 10.1 us  [on_device(): lax.ppermute(lax.dynamic_slice_in_dim(packet, lo, step['width'], 0), 'ctx...]
    ppermute x6, starting transfers between devices: 12.5 us -> 14.8 us  [on_device(): lax.ppermute(lax.dynamic_slice_in_dim(packet, lo, step['width'], 0), 'ctx...]
    ppermute x1, starting transfers between devices: 2.86 us -> 1.61 us  [on_device(): lax.ppermute(lax.dynamic_slice_in_dim(bundle, lo, rows_back, 0), 'ctx', [...]
  transfers between devices with their start and end apart: 15 -> 15, of which waited for: 5 -> 6; matrix products, arithmetic and copies ran while one was open for 7% -> 8% of each run, Pallas kernels for 0% -> 0%
where the time goes in v13:
time: 66.6 us; the launch traced here: 66.3 us
  starting transfers between devices  41.3 us (62%)
  waiting for transfers between devices  11.9 us (18%)
  matrix products  5.19 us (8%)
  other arithmetic  3.78 us (6%)
  local copies, waits for them, and re-layouts  3.41 us (5%)
  between operations  0.71 us (1%)
    ppermute x6, starting transfers between devices, on_device(): lax.ppermute(lax.dynamic_slice_in_dim(packet, lo, step['width'], 0), 'ctx...  14.8 us
    ppermute x6, waiting for transfers between devices, on_device(): lax.ppermute(lax.dynamic_slice_in_dim(packet, lo, step['width'], 0), 'ctx...  10.1 us
    ppermute x2, starting transfers between devices, on_device(): lax.ppermute(raw, 'ctx', [(s, s + shift) for s in range(n_ctx - shift)])  8.55 us
    ppermute x1, starting transfers between devices, on_device(): partner = lax.ppermute(attended, 'head', swap)  7.74 us
    ppermute x1, starting transfers between devices, on_device(): lax.ppermute(jnp.where(core == 1, up, down), 'head', cross_pairs)  4.44 us
    dot_general x8, matrix products, project(): return jnp.dot(piece, rows, preferred_element_type=jnp.float32)  3.43 us
    unnamed x25, local copies, waits for them, and re-layouts  3.36 us
    ppermute x1, waiting for transfers between devices, on_device(): lax.ppermute(jnp.where(core == 1, up, down), 'head', cross_pairs)  1.81 us
  transfers between devices with their start and end apart: 15, of which 6 were waited for; matrix products, arithmetic and copies ran while one was open for 8% of the time, Pallas kernels for 0%

profile of v13, /device:TPU:1, one launch (start us, length us, event | category | flops | bytes accessed | tf_op | source)
XLA Modules:
  0.0 66.3 jit_solution(13110483540209019254)
XLA Ops:
  0.0 0.9 %copy.19 = bf16[128,128]{0,1:T(8,128)(2,1)S(1)} copy(bf16[128,128]{1,0:T(8,128)(2,1)} %param.7) | data formatting | bytes 65536 | tf_op args[2]
  0.9 0.9 %copy.18 = bf16[128,128]{0,1:T(8,128)(2,1)S(1)} copy(bf16[128,128]{1,0:T(8,128)(2,1)} %param.6) | data formatting | bytes 65536 | tf_op args[1]
  1.8 4.0 %collective-permute-start.1 = (bf16[128,256]{0,1:T(8,128)(2,1)S(1)}, bf16[128,256]{0,1:T(8,128)(2,1)S(1)}, u32[]{:S(2)}, u32[]{:S(2)}) collective-permute-start(bf16[128,256]{0,1:T(8,128)(2,1)S(1)} %pad_maximum_fusion.3), channel_id=1, source_target_pairs={{0,64},{8,72},{16,80},{24,88},{32,96},{40,104},{48,112},{56,120},{... | collective-permute-start | bytes 196616 | tf_op jit(solution)/shard_map/ppermute | solution.py:62
  5.8 4.5 %collective-permute-start = (bf16[128,256]{0,1:T(8,128)(2,1)S(1)}, bf16[128,256]{0,1:T(8,128)(2,1)S(1)}, u32[]{:S(2)}, u32[]{:S(2)}) collective-permute-start(bf16[128,256]{0,1:T(8,128)(2,1)S(1)} %pad_maximum_fusion.3), channel_id=1, source_target_pairs={{0,128},{8,136},{16,144},{24,152},{32,160},{40,168},{48,176},{56,1... | collective-permute-start | bytes 196616 | tf_op jit(solution)/shard_map/ppermute | solution.py:62
  11.2 1.0 %copy.22 = bf16[128,512]{0,1:T(8,128)(2,1)S(1)} copy(bf16[128,512]{1,0:T(8,128)(2,1)} %param.5) | data formatting | bytes 262144 | tf_op args[0]
  12.4 1.0 %compare_and_fusion = pred[128,2176]{0,1:T(8,128)(4,1)S(1)} fusion(s32[128]{0:T(128)S(1)} %get-tuple-element.11, s32[128]{0:T(128)S(1)} %iota_add_fusion.3, s32[2176]{0:T(1024)S(1)} %iota_add_fusion), kind=kLoop, calls=%fused_computation.19 | loop fusion | flops 835584 | bytes 288256 | tf_op jit(solution)/shard_map/and | solution.py:103
  14.7 5.7 %collective-permute-start.2 = (bf16[3,128,256]{1,2,0:T(8,128)(2,1)S(1)}, bf16[3,128,256]{1,2,0:T(8,128)(2,1)S(1)}, u32[]{:S(2)}, u32[]{:S(2)}) collective-permute-start(bf16[3,128,256]{1,2,0:T(8,128)(2,1)S(1)} %pad_maximum_fusion.1), channel_id=1, source_target_pairs={{0,56},{8,0},{16,8},{24,16},{32,24},{40,32},{48,40},{56,48},{64,12... | collective-permute-start | bytes 589832 | tf_op jit(solution)/shard_map/ppermute | solution.py:85
  20.6 2.7 %collective-permute-done.2 = bf16[3,128,256]{1,2,0:T(8,128)(2,1)S(1)} collective-permute-done((bf16[3,128,256]{1,2,0:T(8,128)(2,1)S(1)}, bf16[3,128,256]{1,2,0:T(8,128)(2,1)S(1)}, u32[]{:S(2)}, u32[]{:S(2)}) %collective-permute-start.2) | collective-permute-done | bytes 196640 | tf_op jit(solution)/shard_map/ppermute | solution.py:85
  23.3 3.4 %collective-permute-start.3 = (bf16[3,128,256]{1,2,0:T(8,128)(2,1)S(1)}, bf16[3,128,256]{1,2,0:T(8,128)(2,1)S(1)}, u32[]{:S(2)}, u32[]{:S(2)}) collective-permute-start(bf16[3,128,256]{1,2,0:T(8,128)(2,1)S(1)} %collective-permute-done.2), channel_id=1, source_target_pairs={{0,56},{8,0},{16,8},{24,16},{32,24},{40,32},{48,40},{56,48},{64,12... | collective-permute-start | bytes 589832 | tf_op jit(solution)/shard_map/ppermute | solution.py:85
  26.8 1.6 %collective-permute-start.5 = (bf16[2,128,256]{1,2,0:T(8,128)(2,1)S(1)}, bf16[2,128,256]{1,2,0:T(8,128)(2,1)S(1)}, u32[]{:S(2)}, u32[]{:S(2)}) collective-permute-start(bf16[2,128,256]{1,2,0:T(8,128)(2,1)S(1)} %constant_dynamic-slice_fusion.1), channel_id=1, source_target_pairs={{0,32},{8,40},{16,48},{24,56},{32,0},{40,8},{48,16},{56,24},{64,96... | collective-permute-start | bytes 393224 | tf_op jit(solution)/shard_map/ppermute | solution.py:74
  28.5 1.5 %collective-permute-done.3 = bf16[3,128,256]{1,2,0:T(8,128)(2,1)S(1)} collective-permute-done((bf16[3,128,256]{1,2,0:T(8,128)(2,1)S(1)}, bf16[3,128,256]{1,2,0:T(8,128)(2,1)S(1)}, u32[]{:S(2)}, u32[]{:S(2)}) %collective-permute-start.3) | collective-permute-done | bytes 196640 | tf_op jit(solution)/shard_map/ppermute | solution.py:85
  29.9 4.1 %collective-permute-start.4 = (bf16[2,128,256]{1,2,0:T(8,128)(2,1)S(1)}, bf16[2,128,256]{1,2,0:T(8,128)(2,1)S(1)}, u32[]{:S(2)}, u32[]{:S(2)}) collective-permute-start(bf16[2,128,256]{1,2,0:T(8,128)(2,1)S(1)} %constant_dynamic-slice_fusion.2), channel_id=1, source_target_pairs={{0,56},{8,0},{16,8},{24,16},{32,24},{40,32},{48,40},{56,48},{64,12... | collective-permute-start | bytes 393224 | tf_op jit(solution)/shard_map/ppermute | solution.py:85
  34.0 2.4 %collective-permute-done.7 = bf16[3,128,256]{1,2,0:T(8,128)(2,1)S(1)} collective-permute-done((bf16[3,128,256]{1,2,0:T(8,128)(2,1)S(1)}, bf16[3,128,256]{1,2,0:T(8,128)(2,1)S(1)}, u32[]{:S(2)}, u32[]{:S(2)}) %collective-permute-start.7) | collective-permute-done | bytes 196640 | tf_op jit(solution)/shard_map/ppermute | solution.py:85
  36.5 1.5 %collective-permute-start.8 = (bf16[2,128,256]{1,2,0:T(8,128)(2,1)S(1)}, bf16[2,128,256]{1,2,0:T(8,128)(2,1)S(1)}, u32[]{:S(2)}, u32[]{:S(2)}) collective-permute-start(bf16[2,128,256]{1,2,0:T(8,128)(2,1)S(1)} %constant_dynamic-slice_fusion), channel_id=1, source_target_pairs={{0,8},{8,16},{16,24},{24,32},{32,40},{40,48},{48,56},{56,0},{64,72... | collective-permute-start | bytes 393224 | tf_op jit(solution)/shard_map/ppermute | solution.py:85
  38.5 3.0 %collective-permute-done.8 = bf16[2,128,256]{1,2,0:T(8,128)(2,1)S(1)} collective-permute-done((bf16[2,128,256]{1,2,0:T(8,128)(2,1)S(1)}, bf16[2,128,256]{1,2,0:T(8,128)(2,1)S(1)}, u32[]{:S(2)}, u32[]{:S(2)}) %collective-permute-start.8) | collective-permute-done | bytes 131104 | tf_op jit(solution)/shard_map/ppermute | solution.py:85
  41.9 0.8 %fusion.96 = (f32[4,128]{1,0:T(4,128)S(1)}, f32[1,4,128,2176]{2,3,1,0:T(8,128)S(1)}) fusion(bf16[128,4,64]{2,0,1:T(8,128)(2,1)S(1)} %get-tuple-element.13, bf16[128,4,64]{2,0,1:T(8,128)(2,1)S(1)} %get-tuple-element.12, bf16[2176,256]{0,1:T(8,128)(2,1)S(1)} %fusion.69, pred[128,2176]{0,1:T(8,128)(4,1)S(1)} %compare_and_fusion), kind=kOutput, calls=%fused_computation.154 | convolution fusion | flops 288816640 | bytes 5556224 | tf_op jit(solution)/shard_map/tkgd,nkd->kgtn/dot_general | solution.py:99
  43.6 0.9 %fusion.19 = bf16[4,128,128]{1,2,0:T(8,128)(2,1)S(1)} fusion(f32[1,4,128,2176]{2,3,1,0:T(8,128)S(1)} %get-tuple-element.37, f32[4,128]{1,0:T(4,128)S(1)} %get-tuple-element.36, pred[128,2176]{0,1:T(8,128)(4,1)S(1)} %compare_and_fusion, bf16[2176,256]{0,1:T(8,128)(2,1)S(1)} %fusion.69, f32[4,128]{1,0:T(4,128)S(1)} %fusion.2), kind=kOutput, calls=%fused_computation.21 | convolution fusion | flops 288686080 | bytes 5427200 | tf_op jit(solution)/shard_map/kgtn,nkd->kgtd/dot_general | solution.py:108
  44.5 1.3 %collective-permute-start.9 = (bf16[128,512]{0,1:T(8,128)(2,1)S(1)}, bf16[128,512]{0,1:T(8,128)(2,1)S(1)}, u32[]{:S(2)}, u32[]{:S(2)}) collective-permute-start(bf16[128,512]{0,1:T(8,128)(2,1)S(1)} %bitcast.128), channel_id=1, source_target_pairs={{0,2},{1,3},{2,4},{3,5},{4,6},{5,7},{6,0},{7,1},{8,10},{9,11},{10,... | collective-permute-start | bytes 393224 | tf_op jit(solution)/shard_map/ppermute | solution.py:125
  45.8 1.5 %collective-permute-start.10 = (bf16[128,512]{0,1:T(8,128)(2,1)S(1)}, bf16[128,512]{0,1:T(8,128)(2,1)S(1)}, u32[]{:S(2)}, u32[]{:S(2)}) collective-permute-start(bf16[128,512]{0,1:T(8,128)(2,1)S(1)} %bitcast.129), channel_id=1, source_target_pairs={{0,6},{1,7},{2,0},{3,1},{4,2},{5,3},{6,4},{7,5},{8,14},{9,15},{10,... | collective-permute-start | bytes 393224 | tf_op jit(solution)/shard_map/ppermute | solution.py:126
  47.3 7.7 %collective-permute-start.11 = (bf16[128,512]{0,1:T(8,128)(2,1)S(1)}, bf16[128,512]{0,1:T(8,128)(2,1)S(1)}, u32[]{:S(2)}, u32[]{:S(2)}) collective-permute-start(bf16[128,512]{0,1:T(8,128)(2,1)S(1)} %bitcast.130), channel_id=1, source_target_pairs={{0,1},{1,0},{2,3},{3,2},{4,5},{5,4},{6,7},{7,6},{8,9},{9,8},{10,11... | collective-permute-start | bytes 393224 | tf_op jit(solution)/shard_map/ppermute | solution.py:128
  55.4 1.3 %collective-permute-start.12 = (bf16[128,512]{0,1:T(8,128)(2,1)S(1)}, bf16[128,512]{0,1:T(8,128)(2,1)S(1)}, u32[]{:S(2)}, u32[]{:S(2)}) collective-permute-start(bf16[128,512]{0,1:T(8,128)(2,1)S(1)} %get-tuple-element.14), channel_id=1, source_target_pairs={{0,2},{1,7},{2,4},{3,1},{4,6},{5,3},{6,0},{7,5},{8,10},{9,15},{10,... | collective-permute-start | bytes 393224 | tf_op jit(solution)/shard_map/ppermute | solution.py:130
  56.8 4.4 %collective-permute-start.13 = (bf16[128,512]{0,1:T(8,128)(2,1)S(1)}, bf16[128,512]{0,1:T(8,128)(2,1)S(1)}, u32[]{:S(2)}, u32[]{:S(2)}) collective-permute-start(bf16[128,512]{0,1:T(8,128)(2,1)S(1)} %get-tuple-element.15), channel_id=1, source_target_pairs={{0,7},{1,2},{2,1},{3,4},{4,3},{5,6},{6,5},{7,0},{8,15},{9,10},{10,... | collective-permute-start | bytes 393224 | tf_op jit(solution)/shard_map/ppermute | solution.py:132
  62.4 1.8 %collective-permute-done.13 = bf16[128,512]{0,1:T(8,128)(2,1)S(1)} collective-permute-done((bf16[128,512]{0,1:T(8,128)(2,1)S(1)}, bf16[128,512]{0,1:T(8,128)(2,1)S(1)}, u32[]{:S(2)}, u32[]{:S(2)}) %collective-permute-start.13) | collective-permute-done | bytes 131104 | tf_op jit(solution)/shard_map/ppermute | solution.py:132
  65.2 1.1 %fusion.15 = bf16[128,1024]{1,0:T(8,128)(2,1)} fusion(f32[128,1024]{1,0:T(8,128)S(1)} %fusion.22, f32[128,1024]{1,0:T(8,128)S(1)} %fusion.24, f32[128,1024]{1,0:T(8,128)S(1)} %fusion.26, f32[128,1024]{1,0:T(8,128)S(1)} %fusion.28, f32[128,1024]{1,0:T(8,128)S(1)} %fusion.30, f32[128,1024]{1,0:T(8,128)S(1)} %convolution_add_fusion.1, ...), kind=kOutput, calls=%fused_computation.18 | convolution fusion | flops 135135232 | bytes 4587524 | tf_op jit(solution)/shard_map/dot_general | solution.py:123
  (75 shorter events, 6.3 us)
Async XLA Ops:
  0.0 12.3 %copy-start = (s32[32]{0:T(128)S(1)}, s32[32]{0:T(128)}, u32[]{:S(2)}) copy-start(s32[32]{0:T(128)} %param.8) | copy-start | bytes 388
  1.8 12.3 %collective-permute-start.1 = (bf16[128,256]{0,1:T(8,128)(2,1)S(1)}, bf16[128,256]{0,1:T(8,128)(2,1)S(1)}, u32[]{:S(2)}, u32[]{:S(2)}) collective-permute-start(bf16[128,256]{0,1:T(8,128)(2,1)S(1)} %pad_maximum_fusion.3), channel_id=1, source_target_pairs={{0,64},{8,72},{16,80},{24,88},{32,96},{40,104},{48,112},{56,120},{... | collective-permute-start | bytes 196616 | tf_op jit(solution)/shard_map/ppermute | solution.py:62
  5.8 8.3 %collective-permute-start = (bf16[128,256]{0,1:T(8,128)(2,1)S(1)}, bf16[128,256]{0,1:T(8,128)(2,1)S(1)}, u32[]{:S(2)}, u32[]{:S(2)}) collective-permute-start(bf16[128,256]{0,1:T(8,128)(2,1)S(1)} %pad_maximum_fusion.3), channel_id=1, source_target_pairs={{0,128},{8,136},{16,144},{24,152},{32,160},{40,168},{48,176},{56,1... | collective-permute-start | bytes 196616 | tf_op jit(solution)/shard_map/ppermute | solution.py:62
  14.7 8.7 %collective-permute-start.2 = (bf16[3,128,256]{1,2,0:T(8,128)(2,1)S(1)}, bf16[3,128,256]{1,2,0:T(8,128)(2,1)S(1)}, u32[]{:S(2)}, u32[]{:S(2)}) collective-permute-start(bf16[3,128,256]{1,2,0:T(8,128)(2,1)S(1)} %pad_maximum_fusion.1), channel_id=1, source_target_pairs={{0,56},{8,0},{16,8},{24,16},{32,24},{40,32},{48,40},{56,48},{64,12... | collective-permute-start | bytes 589832 | tf_op jit(solution)/shard_map/ppermute | solution.py:85
  20.3 8.1 %collective-permute-start.6 = (bf16[3,128,256]{1,2,0:T(8,128)(2,1)S(1)}, bf16[3,128,256]{1,2,0:T(8,128)(2,1)S(1)}, u32[]{:S(2)}, u32[]{:S(2)}) collective-permute-start(bf16[3,128,256]{1,2,0:T(8,128)(2,1)S(1)} %pad_maximum_fusion.1), channel_id=1, source_target_pairs={{0,8},{8,16},{16,24},{24,32},{32,40},{40,48},{48,56},{56,0},{64,72... | collective-permute-start | bytes 589832 | tf_op jit(solution)/shard_map/ppermute | solution.py:85
  23.3 6.6 %collective-permute-start.3 = (bf16[3,128,256]{1,2,0:T(8,128)(2,1)S(1)}, bf16[3,128,256]{1,2,0:T(8,128)(2,1)S(1)}, u32[]{:S(2)}, u32[]{:S(2)}) collective-permute-start(bf16[3,128,256]{1,2,0:T(8,128)(2,1)S(1)} %collective-permute-done.2), channel_id=1, source_target_pairs={{0,56},{8,0},{16,8},{24,16},{32,24},{40,32},{48,40},{56,48},{64,12... | collective-permute-start | bytes 589832 | tf_op jit(solution)/shard_map/ppermute | solution.py:85
  26.8 11.8 %collective-permute-start.5 = (bf16[2,128,256]{1,2,0:T(8,128)(2,1)S(1)}, bf16[2,128,256]{1,2,0:T(8,128)(2,1)S(1)}, u32[]{:S(2)}, u32[]{:S(2)}) collective-permute-start(bf16[2,128,256]{1,2,0:T(8,128)(2,1)S(1)} %constant_dynamic-slice_fusion.1), channel_id=1, source_target_pairs={{0,32},{8,40},{16,48},{24,56},{32,0},{40,8},{48,16},{56,24},{64,96... | collective-permute-start | bytes 393224 | tf_op jit(solution)/shard_map/ppermute | solution.py:74
  28.4 8.1 %collective-permute-start.7 = (bf16[3,128,256]{1,2,0:T(8,128)(2,1)S(1)}, bf16[3,128,256]{1,2,0:T(8,128)(2,1)S(1)}, u32[]{:S(2)}, u32[]{:S(2)}) collective-permute-start(bf16[3,128,256]{1,2,0:T(8,128)(2,1)S(1)} %collective-permute-done.6), channel_id=1, source_target_pairs={{0,8},{8,16},{16,24},{24,32},{32,40},{40,48},{48,56},{56,0},{64,72... | collective-permute-start | bytes 589832 | tf_op jit(solution)/shard_map/ppermute | solution.py:85
  29.9 8.6 %collective-permute-start.4 = (bf16[2,128,256]{1,2,0:T(8,128)(2,1)S(1)}, bf16[2,128,256]{1,2,0:T(8,128)(2,1)S(1)}, u32[]{:S(2)}, u32[]{:S(2)}) collective-permute-start(bf16[2,128,256]{1,2,0:T(8,128)(2,1)S(1)} %constant_dynamic-slice_fusion.2), channel_id=1, source_target_pairs={{0,56},{8,0},{16,8},{24,16},{32,24},{40,32},{48,40},{56,48},{64,12... | collective-permute-start | bytes 393224 | tf_op jit(solution)/shard_map/ppermute | solution.py:85
  36.5 5.1 %collective-permute-start.8 = (bf16[2,128,256]{1,2,0:T(8,128)(2,1)S(1)}, bf16[2,128,256]{1,2,0:T(8,128)(2,1)S(1)}, u32[]{:S(2)}, u32[]{:S(2)}) collective-permute-start(bf16[2,128,256]{1,2,0:T(8,128)(2,1)S(1)} %constant_dynamic-slice_fusion), channel_id=1, source_target_pairs={{0,8},{8,16},{16,24},{24,32},{32,40},{40,48},{48,56},{56,0},{64,72... | collective-permute-start | bytes 393224 | tf_op jit(solution)/shard_map/ppermute | solution.py:85
  41.9 13.1 %slice-start = ((s8[8388608]{0:T(1024)(128)(4,1)}), s8[4194304]{0:T(1024)(128)(4,1)S(1)}, s32[]{:S(2)}) async-start(s8[8388608]{0:T(1024)(128)(4,1)} %bitcast.123), calls=%async_computation | async-start | bytes 8388608
  42.8 12.3 %slice-start.1 = ((s8[8388608]{0:T(1024)(128)(4,1)}), s8[4194304]{0:T(1024)(128)(4,1)S(1)}, s32[]{:S(2)}) async-start(s8[8388608]{0:T(1024)(128)(4,1)} %bitcast.123), calls=%async_computation.1 | async-start | bytes 8388608
  44.5 10.8 %collective-permute-start.9 = (bf16[128,512]{0,1:T(8,128)(2,1)S(1)}, bf16[128,512]{0,1:T(8,128)(2,1)S(1)}, u32[]{:S(2)}, u32[]{:S(2)}) collective-permute-start(bf16[128,512]{0,1:T(8,128)(2,1)S(1)} %bitcast.128), channel_id=1, source_target_pairs={{0,2},{1,3},{2,4},{3,5},{4,6},{5,7},{6,0},{7,1},{8,10},{9,11},{10,... | collective-permute-start | bytes 393224 | tf_op jit(solution)/shard_map/ppermute | solution.py:125
  45.8 9.6 %collective-permute-start.10 = (bf16[128,512]{0,1:T(8,128)(2,1)S(1)}, bf16[128,512]{0,1:T(8,128)(2,1)S(1)}, u32[]{:S(2)}, u32[]{:S(2)}) collective-permute-start(bf16[128,512]{0,1:T(8,128)(2,1)S(1)} %bitcast.129), channel_id=1, source_target_pairs={{0,6},{1,7},{2,0},{3,1},{4,2},{5,3},{6,4},{7,5},{8,14},{9,15},{10,... | collective-permute-start | bytes 393224 | tf_op jit(solution)/shard_map/ppermute | solution.py:126
  47.3 14.4 %collective-permute-start.11 = (bf16[128,512]{0,1:T(8,128)(2,1)S(1)}, bf16[128,512]{0,1:T(8,128)(2,1)S(1)}, u32[]{:S(2)}, u32[]{:S(2)}) collective-permute-start(bf16[128,512]{0,1:T(8,128)(2,1)S(1)} %bitcast.130), channel_id=1, source_target_pairs={{0,1},{1,0},{2,3},{3,2},{4,5},{5,4},{6,7},{7,6},{8,9},{9,8},{10,11... | collective-permute-start | bytes 393224 | tf_op jit(solution)/shard_map/ppermute | solution.py:128
  55.4 6.6 %collective-permute-start.12 = (bf16[128,512]{0,1:T(8,128)(2,1)S(1)}, bf16[128,512]{0,1:T(8,128)(2,1)S(1)}, u32[]{:S(2)}, u32[]{:S(2)}) collective-permute-start(bf16[128,512]{0,1:T(8,128)(2,1)S(1)} %get-tuple-element.14), channel_id=1, source_target_pairs={{0,2},{1,7},{2,4},{3,1},{4,6},{5,3},{6,0},{7,5},{8,10},{9,15},{10,... | collective-permute-start | bytes 393224 | tf_op jit(solution)/shard_map/ppermute | solution.py:130
  56.8 7.4 %collective-permute-start.13 = (bf16[128,512]{0,1:T(8,128)(2,1)S(1)}, bf16[128,512]{0,1:T(8,128)(2,1)S(1)}, u32[]{:S(2)}, u32[]{:S(2)}) collective-permute-start(bf16[128,512]{0,1:T(8,128)(2,1)S(1)} %get-tuple-element.15), channel_id=1, source_target_pairs={{0,7},{1,2},{2,1},{3,4},{4,3},{5,6},{6,5},{7,0},{8,15},{9,10},{10,... | collective-permute-start | bytes 393224 | tf_op jit(solution)/shard_map/ppermute | solution.py:132
  61.2 3.3 %collective-permute-start.14 = (bf16[2,128,512]{1,2,0:T(8,128)(2,1)S(1)}, bf16[2,128,512]{1,2,0:T(8,128)(2,1)S(1)}, u32[]{:S(2)}, u32[]{:S(2)}) collective-permute-start(bf16[2,128,512]{1,2,0:T(8,128)(2,1)S(1)} %pad_maximum_fusion), channel_id=1, source_target_pairs={{0,1},{1,0},{2,3},{3,2},{4,5},{5,4},{6,7},{7,6},{8,9},{9,8},{10,11... | collective-permute-start | bytes 786440 | tf_op jit(solution)/shard_map/ppermute | solution.py:133

commit v14 on v8

--- a/solution.py
+++ b/solution.py
@@ -122,20 +122,20 @@
         down = lax.ppermute(attended, "head", [(s, (s - 2) % n_head) for s in range(n_head)])
         swap = [(s, s ^ 1) for s in range(n_head)]
         partner = lax.ppermute(attended, "head", swap)
+        cross = lax.ppermute(attended, "head", [(s, (s + 1) % n_head) if s % 2 else (s, (s - 1) % n_head) for s in range(n_head)])
         same_pairs = [(s, (s + 2) % n_head) if s % 2 == 0 else (s, (s - 2) % n_head) for s in range(n_head)]
-        far = lax.ppermute(jnp.where(core == 0, up, down), "head", same_pairs)
-        cross_pairs = [(s, (s + 1) % n_head) if s % 2 == 1 else (s, (s - 1) % n_head) for s in range(n_head)]
-        far_cross = lax.ppermute(jnp.where(core == 1, up, down), "head", cross_pairs)
-        near_other = lax.ppermute(jnp.stack([up, down]), "head", swap)
-        other = head ^ 1
+        far = lax.ppermute(
+            jnp.where(core == 0, jnp.stack([up, cross]), jnp.stack([down, cross])), "head", same_pairs
+        )
+        other = lax.ppermute(jnp.where(core == 0, up, down), "head", swap)
         total = project(attended, head)
         total = total + project(up, (head - 2) % n_head)
         total = total + project(down, (head + 2) % n_head)
-        total = total + project(partner, other)
-        total = total + project(far, (head + 4) % n_head)
-        total = total + project(far_cross, jnp.where(core == 0, head - 3, head + 3) % n_head)
-        total = total + project(near_other[0], (other - 2) % n_head)
-        total = total + project(near_other[1], (other + 2) % n_head)
+        total = total + project(partner, head ^ 1)
+        total = total + project(cross, jnp.where(core == 0, head - 1, head + 1) % n_head)
+        total = total + project(far[0], (head + 4) % n_head)
+        total = total + project(far[1], jnp.where(core == 0, head + 5, head + 3) % n_head)
+        total = total + project(other, jnp.where(core == 0, head + 3, head - 3) % n_head)
         return total.astype(jnp.bfloat16)
 
     return on_device

time: 63.9 us -> 65.4 us (1.023)
  waiting for transfers between devices: 14.3 us -> 18.4 us
  starting transfers between devices: 35.9 us -> 32.8 us
    ppermute x1, starting transfers between devices: 3.32 us -> 0.01 us  [on_device(): partner = lax.ppermute(attended, 'head', swap)]
    ppermute x1, waiting for transfers between devices: 0.01 us -> 2.34 us  [on_device(): lax.ppermute(attended, 'head', [(s, (s - 2) % n_head) for s in range(n_he...]
    ppermute x3, waiting for transfers between devices: 1.82 us -> 3.57 us  [the longest x1 1.98 us: on_device(): lax.ppermute(jnp.where(core == 0, jnp.stack([up, cross]), jnp.stack([down...]
  transfers between devices with their start and end apart: 15 -> 15, of which waited for: 5 -> 8; matrix products, arithmetic and copies ran while one was open for 7% -> 7% of each run, Pallas kernels for 0% -> 0%
where the time goes in v14:
time: 65.4 us; the launch traced here: 64.5 us
  starting transfers between devices  32.8 us (50%)
  waiting for transfers between devices  18.4 us (28%)
  matrix products  5.18 us (8%)
  other arithmetic  4.11 us (6%)
  local copies, waits for them, and re-layouts  3.43 us (5%)
    ppermute x6, waiting for transfers between devices, on_device(): lax.ppermute(lax.dynamic_slice_in_dim(packet, lo, step['width'], 0), 'ctx...  12.5 us
    ppermute x6, starting transfers between devices, on_device(): lax.ppermute(lax.dynamic_slice_in_dim(packet, lo, step['width'], 0), 'ctx...  12.5 us
    ppermute x2, starting transfers between devices, on_device(): lax.ppermute(own, 'ctx', [(s, s + shift) for s in range(n_ctx - shift)])  8.55 us
    ppermute x1, starting transfers between devices, on_device(): lax.ppermute(attended, 'head', [(s, (s + 1) % n_head) if s % 2 else (s, (...  4.14 us
    dot_general x8, matrix products, project(): return jnp.dot(piece, rows, preferred_element_type=jnp.float32)  3.43 us
    unnamed x25, local copies, waits for them, and re-layouts  3.37 us
    ppermute x1, starting transfers between devices, on_device(): lax.ppermute(lax.dynamic_slice_in_dim(bundle, lo, rows_back, 0), 'ctx', [...  2.86 us
    ppermute x1, waiting for transfers between devices, on_device(): lax.ppermute(attended, 'head', [(s, (s - 2) % n_head) for s in range(n_he...  2.34 us
  transfers between devices with their start and end apart: 15, of which 8 were waited for; matrix products, arithmetic and copies ran while one was open for 7% of the time, Pallas kernels for 0%

profile of v14, /device:TPU:1, one launch (start us, length us, event | category | flops | bytes accessed | tf_op | source)
XLA Modules:
  0.0 64.5 jit_solution(4799973351195564726)
XLA Ops:
  1.5 0.9 %copy.18 = bf16[128,128]{0,1:T(8,128)(2,1)S(1)} copy(bf16[128,128]{1,0:T(8,128)(2,1)} %param.6) | data formatting | bytes 65536 | tf_op args[1]
  2.4 0.9 %copy.19 = bf16[128,128]{0,1:T(8,128)(2,1)S(1)} copy(bf16[128,128]{1,0:T(8,128)(2,1)} %param.7) | data formatting | bytes 65536 | tf_op args[2]
  3.6 4.0 %collective-permute-start.1 = (bf16[128,256]{0,1:T(8,128)(2,1)S(1)}, bf16[128,256]{0,1:T(8,128)(2,1)S(1)}, u32[]{:S(2)}, u32[]{:S(2)}) collective-permute-start(bf16[128,256]{0,1:T(8,128)(2,1)S(1)} %get-tuple-element.12), channel_id=1, source_target_pairs={{0,64},{8,72},{16,80},{24,88},{32,96},{40,104},{48,112},{56,120},{... | collective-permute-start | bytes 196616 | tf_op jit(solution)/shard_map/ppermute | solution.py:61
  7.6 4.5 %collective-permute-start = (bf16[128,256]{0,1:T(8,128)(2,1)S(1)}, bf16[128,256]{0,1:T(8,128)(2,1)S(1)}, u32[]{:S(2)}, u32[]{:S(2)}) collective-permute-start(bf16[128,256]{0,1:T(8,128)(2,1)S(1)} %get-tuple-element.12), channel_id=1, source_target_pairs={{0,128},{8,136},{16,144},{24,152},{32,160},{40,168},{48,176},{56,1... | collective-permute-start | bytes 196616 | tf_op jit(solution)/shard_map/ppermute | solution.py:61
  12.1 1.0 %copy.20 = bf16[128,512]{0,1:T(8,128)(2,1)S(1)} copy(bf16[128,512]{1,0:T(8,128)(2,1)} %param.5) | data formatting | bytes 262144 | tf_op args[0]
  13.2 1.0 %compare_and_fusion = pred[128,2176]{0,1:T(8,128)(4,1)S(1)} fusion(s32[128]{0:T(128)S(1)} %select_reduce_fusion, s32[128]{0:T(128)S(1)} %iota_add_fusion.1, s32[2176]{0:T(1024)S(1)} %iota_add_fusion), kind=kLoop, calls=%fused_computation.19 | loop fusion | flops 835584 | bytes 288256 | tf_op jit(solution)/shard_map/and | solution.py:99
  14.9 5.7 %collective-permute-start.2 = (bf16[3,128,256]{1,2,0:T(8,128)(2,1)S(1)}, bf16[3,128,256]{1,2,0:T(8,128)(2,1)S(1)}, u32[]{:S(2)}, u32[]{:S(2)}) collective-permute-start(bf16[3,128,256]{1,2,0:T(8,128)(2,1)S(1)} %pad_maximum_fusion.2), channel_id=1, source_target_pairs={{0,56},{8,0},{16,8},{24,16},{32,24},{40,32},{48,40},{56,48},{64,12... | collective-permute-start | bytes 589832 | tf_op jit(solution)/shard_map/ppermute | solution.py:81
  20.9 2.9 %collective-permute-start.5 = (bf16[2,128,256]{1,2,0:T(8,128)(2,1)S(1)}, bf16[2,128,256]{1,2,0:T(8,128)(2,1)S(1)}, u32[]{:S(2)}, u32[]{:S(2)}) collective-permute-start(bf16[2,128,256]{1,2,0:T(8,128)(2,1)S(1)} %constant_dynamic-slice_fusion.1), channel_id=1, source_target_pairs={{0,32},{8,40},{16,48},{24,56},{32,0},{40,8},{48,16},{56,24},{64,96... | collective-permute-start | bytes 393224 | tf_op jit(solution)/shard_map/ppermute | solution.py:70
  23.8 3.2 %collective-permute-start.3 = (bf16[3,128,256]{1,2,0:T(8,128)(2,1)S(1)}, bf16[3,128,256]{1,2,0:T(8,128)(2,1)S(1)}, u32[]{:S(2)}, u32[]{:S(2)}) collective-permute-start(bf16[3,128,256]{1,2,0:T(8,128)(2,1)S(1)} %collective-permute-done.2), channel_id=1, source_target_pairs={{0,56},{8,0},{16,8},{24,16},{32,24},{40,32},{48,40},{56,48},{64,12... | collective-permute-start | bytes 589832 | tf_op jit(solution)/shard_map/ppermute | solution.py:81
  27.0 2.0 %collective-permute-done.6 = bf16[3,128,256]{1,2,0:T(8,128)(2,1)S(1)} collective-permute-done((bf16[3,128,256]{1,2,0:T(8,128)(2,1)S(1)}, bf16[3,128,256]{1,2,0:T(8,128)(2,1)S(1)}, u32[]{:S(2)}, u32[]{:S(2)}) %collective-permute-start.6) | collective-permute-done | bytes 196640 | tf_op jit(solution)/shard_map/ppermute | solution.py:81
  29.0 5.6 %collective-permute-done.3 = bf16[3,128,256]{1,2,0:T(8,128)(2,1)S(1)} collective-permute-done((bf16[3,128,256]{1,2,0:T(8,128)(2,1)S(1)}, bf16[3,128,256]{1,2,0:T(8,128)(2,1)S(1)}, u32[]{:S(2)}, u32[]{:S(2)}) %collective-permute-start.3) | collective-permute-done | bytes 196640 | tf_op jit(solution)/shard_map/ppermute | solution.py:81
  34.6 3.5 %collective-permute-start.4 = (bf16[2,128,256]{1,2,0:T(8,128)(2,1)S(1)}, bf16[2,128,256]{1,2,0:T(8,128)(2,1)S(1)}, u32[]{:S(2)}, u32[]{:S(2)}) collective-permute-start(bf16[2,128,256]{1,2,0:T(8,128)(2,1)S(1)} %constant_dynamic-slice_fusion.2), channel_id=1, source_target_pairs={{0,56},{8,0},{16,8},{24,16},{32,24},{40,32},{48,40},{56,48},{64,12... | collective-permute-start | bytes 393224 | tf_op jit(solution)/shard_map/ppermute | solution.py:81
  38.2 1.8 %collective-permute-done.4 = bf16[2,128,256]{1,2,0:T(8,128)(2,1)S(1)} collective-permute-done((bf16[2,128,256]{1,2,0:T(8,128)(2,1)S(1)}, bf16[2,128,256]{1,2,0:T(8,128)(2,1)S(1)}, u32[]{:S(2)}, u32[]{:S(2)}) %collective-permute-start.4) | collective-permute-done | bytes 131104 | tf_op jit(solution)/shard_map/ppermute | solution.py:81
  40.1 3.1 %collective-permute-done.8 = bf16[2,128,256]{1,2,0:T(8,128)(2,1)S(1)} collective-permute-done((bf16[2,128,256]{1,2,0:T(8,128)(2,1)S(1)}, bf16[2,128,256]{1,2,0:T(8,128)(2,1)S(1)}, u32[]{:S(2)}, u32[]{:S(2)}) %collective-permute-start.8) | collective-permute-done | bytes 131104 | tf_op jit(solution)/shard_map/ppermute | solution.py:81
  43.6 0.8 %fusion.74 = (f32[4,128]{1,0:T(4,128)S(1)}, f32[1,4,128,2176]{2,3,1,0:T(8,128)S(1)}) fusion(bf16[128,4,64]{2,0,1:T(8,128)(2,1)S(1)} %get-tuple-element.6, bf16[128,4,64]{2,0,1:T(8,128)(2,1)S(1)} %get-tuple-element.5, bf16[2176,256]{0,1:T(8,128)(2,1)S(1)} %constant_dynamic-update-slice_fusion, pred[128,2176]{0,1:T(8,128)(4,1)S(1)} %compare_and_fusion), kind=kOutput, calls=%fused_computation.118 | convolution fusion | flops 288816640 | bytes 5556224 | tf_op jit(solution)/shard_map/tkgd,nkd->kgtn/dot_general | solution.py:95
  45.2 0.9 %fusion.19 = bf16[4,128,128]{1,2,0:T(8,128)(2,1)S(1)} fusion(f32[1,4,128,2176]{2,3,1,0:T(8,128)S(1)} %get-tuple-element.16, f32[4,128]{1,0:T(4,128)S(1)} %get-tuple-element.15, pred[128,2176]{0,1:T(8,128)(4,1)S(1)} %compare_and_fusion, bf16[2176,256]{0,1:T(8,128)(2,1)S(1)} %constant_dynamic-update-slice_fusion, f32[4,128]{1,0:T(4,128)S(1)} %fusion.2), kind=kOutput, calls=%fused_computation.21 | convolution fusion | flops 288686080 | bytes 5427200 | tf_op jit(solution)/shard_map/kgtn,nkd->kgtd/dot_general | solution.py:104
  46.2 1.3 %collective-permute-start.9 = (bf16[128,512]{0,1:T(8,128)(2,1)S(1)}, bf16[128,512]{0,1:T(8,128)(2,1)S(1)}, u32[]{:S(2)}, u32[]{:S(2)}) collective-permute-start(bf16[128,512]{0,1:T(8,128)(2,1)S(1)} %bitcast.116), channel_id=1, source_target_pairs={{0,2},{1,3},{2,4},{3,5},{4,6},{5,7},{6,0},{7,1},{8,10},{9,11},{10,... | collective-permute-start | bytes 393224 | tf_op jit(solution)/shard_map/ppermute | solution.py:121
  47.5 4.1 %collective-permute-start.12 = (bf16[128,512]{0,1:T(8,128)(2,1)S(1)}, bf16[128,512]{0,1:T(8,128)(2,1)S(1)}, u32[]{:S(2)}, u32[]{:S(2)}) collective-permute-start(bf16[128,512]{0,1:T(8,128)(2,1)S(1)} %bitcast.117), channel_id=1, source_target_pairs={{0,7},{1,2},{2,1},{3,4},{4,3},{5,6},{6,5},{7,0},{8,15},{9,10},{10,... | collective-permute-start | bytes 393224 | tf_op jit(solution)/shard_map/ppermute | solution.py:125
  51.6 1.5 %collective-permute-start.10 = (bf16[128,512]{0,1:T(8,128)(2,1)S(1)}, bf16[128,512]{0,1:T(8,128)(2,1)S(1)}, u32[]{:S(2)}, u32[]{:S(2)}) collective-permute-start(bf16[128,512]{0,1:T(8,128)(2,1)S(1)} %bitcast.118), channel_id=1, source_target_pairs={{0,6},{1,7},{2,0},{3,1},{4,2},{5,3},{6,4},{7,5},{8,14},{9,15},{10,... | collective-permute-start | bytes 393224 | tf_op jit(solution)/shard_map/ppermute | solution.py:122
  53.4 1.3 %collective-permute-done.12 = bf16[128,512]{0,1:T(8,128)(2,1)S(1)} collective-permute-done((bf16[128,512]{0,1:T(8,128)(2,1)S(1)}, bf16[128,512]{0,1:T(8,128)(2,1)S(1)}, u32[]{:S(2)}, u32[]{:S(2)}) %collective-permute-start.12) | collective-permute-done | bytes 131104 | tf_op jit(solution)/shard_map/ppermute | solution.py:125
  54.8 2.3 %collective-permute-done.10 = bf16[128,512]{0,1:T(8,128)(2,1)S(1)} collective-permute-done((bf16[128,512]{0,1:T(8,128)(2,1)S(1)}, bf16[128,512]{0,1:T(8,128)(2,1)S(1)}, u32[]{:S(2)}, u32[]{:S(2)}) %collective-permute-start.10) | collective-permute-done | bytes 131104 | tf_op jit(solution)/shard_map/ppermute | solution.py:122
  57.2 1.8 %collective-permute-start.13 = (bf16[2,128,512]{1,2,0:T(8,128)(2,1)S(1)}, bf16[2,128,512]{1,2,0:T(8,128)(2,1)S(1)}, u32[]{:S(2)}, u32[]{:S(2)}) collective-permute-start(bf16[2,128,512]{1,2,0:T(8,128)(2,1)S(1)} %fusion.36), channel_id=1, source_target_pairs={{0,2},{1,7},{2,4},{3,1},{4,6},{5,3},{6,0},{7,5},{8,10},{9,15},{10,... | collective-permute-start | bytes 786440 | tf_op jit(solution)/shard_map/ppermute | solution.py:127
  60.8 2.0 %collective-permute-done.13 = bf16[2,128,512]{1,2,0:T(8,128)(2,1)S(1)} collective-permute-done((bf16[2,128,512]{1,2,0:T(8,128)(2,1)S(1)}, bf16[2,128,512]{1,2,0:T(8,128)(2,1)S(1)}, u32[]{:S(2)}, u32[]{:S(2)}) %collective-permute-start.13) | collective-permute-done | bytes 262176 | tf_op jit(solution)/shard_map/ppermute | solution.py:127
  63.4 1.1 %fusion.15 = bf16[128,1024]{1,0:T(8,128)(2,1)} fusion(f32[128,1024]{1,0:T(8,128)S(1)} %fusion.22, f32[128,1024]{1,0:T(8,128)S(1)} %fusion.24, f32[128,1024]{1,0:T(8,128)S(1)} %fusion.26, f32[128,1024]{1,0:T(8,128)S(1)} %fusion.28, f32[128,1024]{1,0:T(8,128)S(1)} %fusion.30, f32[128,1024]{1,0:T(8,128)S(1)} %convolution_add_fusion.1, ...), kind=kOutput, calls=%fused_computation.18 | convolution fusion | flops 135135232 | bytes 4587524 | tf_op jit(solution)/shard_map/dot_general | solution.py:119
  (64 shorter events, 6.7 us)
Async XLA Ops:
  3.6 11.3 %collective-permute-start.1 = (bf16[128,256]{0,1:T(8,128)(2,1)S(1)}, bf16[128,256]{0,1:T(8,128)(2,1)S(1)}, u32[]{:S(2)}, u32[]{:S(2)}) collective-permute-start(bf16[128,256]{0,1:T(8,128)(2,1)S(1)} %get-tuple-element.12), channel_id=1, source_target_pairs={{0,64},{8,72},{16,80},{24,88},{32,96},{40,104},{48,112},{56,120},{... | collective-permute-start | bytes 196616 | tf_op jit(solution)/shard_map/ppermute | solution.py:61
  7.6 7.3 %collective-permute-start = (bf16[128,256]{0,1:T(8,128)(2,1)S(1)}, bf16[128,256]{0,1:T(8,128)(2,1)S(1)}, u32[]{:S(2)}, u32[]{:S(2)}) collective-permute-start(bf16[128,256]{0,1:T(8,128)(2,1)S(1)} %get-tuple-element.12), channel_id=1, source_target_pairs={{0,128},{8,136},{16,144},{24,152},{32,160},{40,168},{48,176},{56,1... | collective-permute-start | bytes 196616 | tf_op jit(solution)/shard_map/ppermute | solution.py:61
  14.9 8.9 %collective-permute-start.2 = (bf16[3,128,256]{1,2,0:T(8,128)(2,1)S(1)}, bf16[3,128,256]{1,2,0:T(8,128)(2,1)S(1)}, u32[]{:S(2)}, u32[]{:S(2)}) collective-permute-start(bf16[3,128,256]{1,2,0:T(8,128)(2,1)S(1)} %pad_maximum_fusion.2), channel_id=1, source_target_pairs={{0,56},{8,0},{16,8},{24,16},{32,24},{40,32},{48,40},{56,48},{64,12... | collective-permute-start | bytes 589832 | tf_op jit(solution)/shard_map/ppermute | solution.py:81
  20.8 8.2 %collective-permute-start.6 = (bf16[3,128,256]{1,2,0:T(8,128)(2,1)S(1)}, bf16[3,128,256]{1,2,0:T(8,128)(2,1)S(1)}, u32[]{:S(2)}, u32[]{:S(2)}) collective-permute-start(bf16[3,128,256]{1,2,0:T(8,128)(2,1)S(1)} %pad_maximum_fusion.2), channel_id=1, source_target_pairs={{0,8},{8,16},{16,24},{24,32},{32,40},{40,48},{48,56},{56,0},{64,72... | collective-permute-start | bytes 589832 | tf_op jit(solution)/shard_map/ppermute | solution.py:81
  20.9 19.1 %collective-permute-start.5 = (bf16[2,128,256]{1,2,0:T(8,128)(2,1)S(1)}, bf16[2,128,256]{1,2,0:T(8,128)(2,1)S(1)}, u32[]{:S(2)}, u32[]{:S(2)}) collective-permute-start(bf16[2,128,256]{1,2,0:T(8,128)(2,1)S(1)} %constant_dynamic-slice_fusion.1), channel_id=1, source_target_pairs={{0,32},{8,40},{16,48},{24,56},{32,0},{40,8},{48,16},{56,24},{64,96... | collective-permute-start | bytes 393224 | tf_op jit(solution)/shard_map/ppermute | solution.py:70
  23.8 10.8 %collective-permute-start.3 = (bf16[3,128,256]{1,2,0:T(8,128)(2,1)S(1)}, bf16[3,128,256]{1,2,0:T(8,128)(2,1)S(1)}, u32[]{:S(2)}, u32[]{:S(2)}) collective-permute-start(bf16[3,128,256]{1,2,0:T(8,128)(2,1)S(1)} %collective-permute-done.2), channel_id=1, source_target_pairs={{0,56},{8,0},{16,8},{24,16},{32,24},{40,32},{48,40},{56,48},{64,12... | collective-permute-start | bytes 589832 | tf_op jit(solution)/shard_map/ppermute | solution.py:81
  29.0 9.1 %collective-permute-start.7 = (bf16[3,128,256]{1,2,0:T(8,128)(2,1)S(1)}, bf16[3,128,256]{1,2,0:T(8,128)(2,1)S(1)}, u32[]{:S(2)}, u32[]{:S(2)}) collective-permute-start(bf16[3,128,256]{1,2,0:T(8,128)(2,1)S(1)} %collective-permute-done.6), channel_id=1, source_target_pairs={{0,8},{8,16},{16,24},{24,32},{32,40},{40,48},{48,56},{56,0},{64,72... | collective-permute-start | bytes 589832 | tf_op jit(solution)/shard_map/ppermute | solution.py:81
  34.6 5.4 %collective-permute-start.4 = (bf16[2,128,256]{1,2,0:T(8,128)(2,1)S(1)}, bf16[2,128,256]{1,2,0:T(8,128)(2,1)S(1)}, u32[]{:S(2)}, u32[]{:S(2)}) collective-permute-start(bf16[2,128,256]{1,2,0:T(8,128)(2,1)S(1)} %constant_dynamic-slice_fusion.2), channel_id=1, source_target_pairs={{0,56},{8,0},{16,8},{24,16},{32,24},{40,32},{48,40},{56,48},{64,12... | collective-permute-start | bytes 393224 | tf_op jit(solution)/shard_map/ppermute | solution.py:81
  38.1 5.1 %collective-permute-start.8 = (bf16[2,128,256]{1,2,0:T(8,128)(2,1)S(1)}, bf16[2,128,256]{1,2,0:T(8,128)(2,1)S(1)}, u32[]{:S(2)}, u32[]{:S(2)}) collective-permute-start(bf16[2,128,256]{1,2,0:T(8,128)(2,1)S(1)} %constant_dynamic-slice_fusion), channel_id=1, source_target_pairs={{0,8},{8,16},{16,24},{24,32},{32,40},{40,48},{48,56},{56,0},{64,72... | collective-permute-start | bytes 393224 | tf_op jit(solution)/shard_map/ppermute | solution.py:81
  43.6 9.5 %slice-start = ((s8[8388608]{0:T(1024)(128)(4,1)}), s8[4194304]{0:T(1024)(128)(4,1)S(1)}, s32[]{:S(2)}) async-start(s8[8388608]{0:T(1024)(128)(4,1)} %bitcast.108), calls=%async_computation | async-start | bytes 8388608
  44.4 8.7 %slice-start.1 = ((s8[8388608]{0:T(1024)(128)(4,1)}), s8[4194304]{0:T(1024)(128)(4,1)S(1)}, s32[]{:S(2)}) async-start(s8[8388608]{0:T(1024)(128)(4,1)} %bitcast.108), calls=%async_computation.1 | async-start | bytes 8388608
  46.2 7.3 %collective-permute-start.9 = (bf16[128,512]{0,1:T(8,128)(2,1)S(1)}, bf16[128,512]{0,1:T(8,128)(2,1)S(1)}, u32[]{:S(2)}, u32[]{:S(2)}) collective-permute-start(bf16[128,512]{0,1:T(8,128)(2,1)S(1)} %bitcast.116), channel_id=1, source_target_pairs={{0,2},{1,3},{2,4},{3,5},{4,6},{5,7},{6,0},{7,1},{8,10},{9,11},{10,... | collective-permute-start | bytes 393224 | tf_op jit(solution)/shard_map/ppermute | solution.py:121
  47.5 7.3 %collective-permute-start.12 = (bf16[128,512]{0,1:T(8,128)(2,1)S(1)}, bf16[128,512]{0,1:T(8,128)(2,1)S(1)}, u32[]{:S(2)}, u32[]{:S(2)}) collective-permute-start(bf16[128,512]{0,1:T(8,128)(2,1)S(1)} %bitcast.117), channel_id=1, source_target_pairs={{0,7},{1,2},{2,1},{3,4},{4,3},{5,6},{6,5},{7,0},{8,15},{9,10},{10,... | collective-permute-start | bytes 393224 | tf_op jit(solution)/shard_map/ppermute | solution.py:125
  51.6 5.5 %collective-permute-start.10 = (bf16[128,512]{0,1:T(8,128)(2,1)S(1)}, bf16[128,512]{0,1:T(8,128)(2,1)S(1)}, u32[]{:S(2)}, u32[]{:S(2)}) collective-permute-start(bf16[128,512]{0,1:T(8,128)(2,1)S(1)} %bitcast.118), channel_id=1, source_target_pairs={{0,6},{1,7},{2,0},{3,1},{4,2},{5,3},{6,4},{7,5},{8,14},{9,15},{10,... | collective-permute-start | bytes 393224 | tf_op jit(solution)/shard_map/ppermute | solution.py:122
  53.1 6.8 %collective-permute-start.11 = (bf16[128,512]{0,1:T(8,128)(2,1)S(1)}, bf16[128,512]{0,1:T(8,128)(2,1)S(1)}, u32[]{:S(2)}, u32[]{:S(2)}) collective-permute-start(bf16[128,512]{0,1:T(8,128)(2,1)S(1)} %bitcast.119), channel_id=1, source_target_pairs={{0,1},{1,0},{2,3},{3,2},{4,5},{5,4},{6,7},{7,6},{8,9},{9,8},{10,11... | collective-permute-start | bytes 393224 | tf_op jit(solution)/shard_map/ppermute | solution.py:124
  57.2 5.6 %collective-permute-start.13 = (bf16[2,128,512]{1,2,0:T(8,128)(2,1)S(1)}, bf16[2,128,512]{1,2,0:T(8,128)(2,1)S(1)}, u32[]{:S(2)}, u32[]{:S(2)}) collective-permute-start(bf16[2,128,512]{1,2,0:T(8,128)(2,1)S(1)} %fusion.36), channel_id=1, source_target_pairs={{0,2},{1,7},{2,4},{3,1},{4,6},{5,3},{6,0},{7,5},{8,10},{9,15},{10,... | collective-permute-start | bytes 786440 | tf_op jit(solution)/shard_map/ppermute | solution.py:127
  59.0 1.4 %collective-permute-start.14 = (bf16[128,512]{0,1:T(8,128)(2,1)S(1)}, bf16[128,512]{0,1:T(8,128)(2,1)S(1)}, u32[]{:S(2)}, u32[]{:S(2)}) collective-permute-start(bf16[128,512]{0,1:T(8,128)(2,1)S(1)} %broadcast_select_fusion), channel_id=1, source_target_pairs={{0,1},{1,0},{2,3},{3,2},{4,5},{5,4},{6,7},{7,6},{8,9},{9,8},{10,11... | collective-permute-start | bytes 393224 | tf_op jit(solution)/shard_map/ppermute | solution.py:130

commit v15 on v8

--- a/solution.py
+++ b/solution.py
@@ -129,13 +129,13 @@
         near_other = lax.ppermute(jnp.stack([up, down]), "head", swap)
         other = head ^ 1
         total = project(attended, head)
-        total = total + project(up, (head - 2) % n_head)
-        total = total + project(down, (head + 2) % n_head)
-        total = total + project(partner, other)
-        total = total + project(far, (head + 4) % n_head)
-        total = total + project(far_cross, jnp.where(core == 0, head - 3, head + 3) % n_head)
-        total = total + project(near_other[0], (other - 2) % n_head)
-        total = total + project(near_other[1], (other + 2) % n_head)
+        total = lax.optimization_barrier(total) + project(up, (head - 2) % n_head)
+        total = lax.optimization_barrier(total) + project(down, (head + 2) % n_head)
+        total = lax.optimization_barrier(total) + project(partner, other)
+        total = lax.optimization_barrier(total) + project(far, (head + 4) % n_head)
+        total = lax.optimization_barrier(total) + project(far_cross, jnp.where(core == 0, head - 3, head + 3) % n_head)
+        total = lax.optimization_barrier(total) + project(near_other[0], (other - 2) % n_head)
+        total = lax.optimization_barrier(total) + project(near_other[1], (other + 2) % n_head)
         return total.astype(jnp.bfloat16)
 
     return on_device

time: 63.9 us -> 65.7 us (1.028)
  the two profiles are of different devices: /device:TPU:1 before, /device:TPU:16 now
where the time goes in v15:
time: 65.7 us; the launch traced here: 65.4 us
  starting transfers between devices  29.6 us (45%)
  waiting for transfers between devices  22.1 us (34%)
  other arithmetic  5.2 us (8%)
  matrix products  4.39 us (7%)
  local copies, waits for them, and re-layouts  3.43 us (5%)
  between operations  0.66 us (1%)
    ppermute x6, starting transfers between devices, on_device(): lax.ppermute(lax.dynamic_slice_in_dim(packet, lo, step['width'], 0), 'ctx...  14.9 us
    ppermute x6, waiting for transfers between devices, on_device(): lax.ppermute(lax.dynamic_slice_in_dim(packet, lo, step['width'], 0), 'ctx...  10.6 us
    ppermute x1, waiting for transfers between devices, on_device(): far = lax.ppermute(jnp.where(core == 0, up, down), 'head', same_pairs)  5 us
    ppermute x2, starting transfers between devices, on_device(): lax.ppermute(own, 'ctx', [(s, s + shift) for s in range(n_ctx - shift)])  4.48 us
    ppermute x2, waiting for transfers between devices, on_device(): lax.ppermute(own, 'ctx', [(s, s + shift) for s in range(n_ctx - shift)])  3.65 us
    ppermute x1, starting transfers between devices, on_device(): lax.ppermute(lax.dynamic_slice_in_dim(bundle, lo, rows_back, 0), 'ctx', [...  3.42 us
    unnamed x25, local copies, waits for them, and re-layouts  3.37 us
    ppermute x1, starting transfers between devices, on_device(): lax.ppermute(jnp.where(core == 1, up, down), 'head', cross_pairs)  3.13 us
  transfers between devices with their start and end apart: 15, of which 10 were waited for; matrix products, arithmetic and copies ran while one was open for 8% of the time, Pallas kernels for 0%

profile of v15, /device:TPU:16, one launch (start us, length us, event | category | flops | bytes accessed | tf_op | source)
XLA Modules:
  0.0 65.4 jit_solution(15656152265641783909)
XLA Ops:
  0.0 0.8 %select_reduce_fusion.1 = s32[32]{0:T(128)S(1)} fusion(s32[32]{0:T(128)} %param.8), kind=kLoop, calls=%fused_computation.91 | loop fusion | flops 3040 | bytes 256 | tf_op jit(solution)/shard_map/reduce_sum | solution.py:15
  1.5 0.9 %copy.18 = bf16[128,128]{0,1:T(8,128)(2,1)S(1)} copy(bf16[128,128]{1,0:T(8,128)(2,1)} %param.6) | data formatting | bytes 65536 | tf_op args[1]
  2.4 0.9 %copy.19 = bf16[128,128]{0,1:T(8,128)(2,1)S(1)} copy(bf16[128,128]{1,0:T(8,128)(2,1)} %param.7) | data formatting | bytes 65536 | tf_op args[2]
  3.6 3.2 %collective-permute-start.1 = (bf16[128,256]{0,1:T(8,128)(2,1)S(1)}, bf16[128,256]{0,1:T(8,128)(2,1)S(1)}, u32[]{:S(2)}, u32[]{:S(2)}) collective-permute-start(bf16[128,256]{0,1:T(8,128)(2,1)S(1)} %get-tuple-element.14), channel_id=1, source_target_pairs={{0,64},{8,72},{16,80},{24,88},{32,96},{40,104},{48,112},{56,120},{... | collective-permute-start | bytes 196616 | tf_op jit(solution)/shard_map/ppermute | solution.py:61
  6.7 1.3 %collective-permute-start = (bf16[128,256]{0,1:T(8,128)(2,1)S(1)}, bf16[128,256]{0,1:T(8,128)(2,1)S(1)}, u32[]{:S(2)}, u32[]{:S(2)}) collective-permute-start(bf16[128,256]{0,1:T(8,128)(2,1)S(1)} %get-tuple-element.14), channel_id=1, source_target_pairs={{0,128},{8,136},{16,144},{24,152},{32,160},{40,168},{48,176},{56,1... | collective-permute-start | bytes 196616 | tf_op jit(solution)/shard_map/ppermute | solution.py:61
  8.0 1.0 %copy.20 = bf16[128,512]{0,1:T(8,128)(2,1)S(1)} copy(bf16[128,512]{1,0:T(8,128)(2,1)} %param.5) | data formatting | bytes 262144 | tf_op args[0]
  9.1 1.0 %compare_and_fusion = pred[128,2176]{0,1:T(8,128)(4,1)S(1)} fusion(s32[128]{0:T(128)S(1)} %select_reduce_fusion, s32[128]{0:T(128)S(1)} %iota_add_fusion.1, s32[2176]{0:T(1024)S(1)} %iota_add_fusion), kind=kLoop, calls=%fused_computation.12 | loop fusion | flops 835584 | bytes 288256 | tf_op jit(solution)/shard_map/and | solution.py:99
  10.8 3.6 %collective-permute-done = bf16[128,256]{0,1:T(8,128)(2,1)S(1)} collective-permute-done((bf16[128,256]{0,1:T(8,128)(2,1)S(1)}, bf16[128,256]{0,1:T(8,128)(2,1)S(1)}, u32[]{:S(2)}, u32[]{:S(2)}) %collective-permute-start) | collective-permute-done | bytes 65568 | tf_op jit(solution)/shard_map/ppermute | solution.py:61
  14.4 5.9 %collective-permute-start.2 = (bf16[3,128,256]{1,2,0:T(8,128)(2,1)S(1)}, bf16[3,128,256]{1,2,0:T(8,128)(2,1)S(1)}, u32[]{:S(2)}, u32[]{:S(2)}) collective-permute-start(bf16[3,128,256]{1,2,0:T(8,128)(2,1)S(1)} %pad_maximum_fusion.1), channel_id=1, source_target_pairs={{0,56},{8,0},{16,8},{24,16},{32,24},{40,32},{48,40},{56,48},{64,12... | collective-permute-start | bytes 589832 | tf_op jit(solution)/shard_map/ppermute | solution.py:81
  20.8 3.4 %collective-permute-start.5 = (bf16[2,128,256]{1,2,0:T(8,128)(2,1)S(1)}, bf16[2,128,256]{1,2,0:T(8,128)(2,1)S(1)}, u32[]{:S(2)}, u32[]{:S(2)}) collective-permute-start(bf16[2,128,256]{1,2,0:T(8,128)(2,1)S(1)} %constant_dynamic-slice_fusion.1), channel_id=1, source_target_pairs={{0,32},{8,40},{16,48},{24,56},{32,0},{40,8},{48,16},{56,24},{64,96... | collective-permute-start | bytes 393224 | tf_op jit(solution)/shard_map/ppermute | solution.py:70
  24.2 1.2 %collective-permute-done.2 = bf16[3,128,256]{1,2,0:T(8,128)(2,1)S(1)} collective-permute-done((bf16[3,128,256]{1,2,0:T(8,128)(2,1)S(1)}, bf16[3,128,256]{1,2,0:T(8,128)(2,1)S(1)}, u32[]{:S(2)}, u32[]{:S(2)}) %collective-permute-start.2) | collective-permute-done | bytes 196640 | tf_op jit(solution)/shard_map/ppermute | solution.py:81
  25.4 5.1 %collective-permute-start.3 = (bf16[3,128,256]{1,2,0:T(8,128)(2,1)S(1)}, bf16[3,128,256]{1,2,0:T(8,128)(2,1)S(1)}, u32[]{:S(2)}, u32[]{:S(2)}) collective-permute-start(bf16[3,128,256]{1,2,0:T(8,128)(2,1)S(1)} %collective-permute-done.2), channel_id=1, source_target_pairs={{0,56},{8,0},{16,8},{24,16},{32,24},{40,32},{48,40},{56,48},{64,12... | collective-permute-start | bytes 589832 | tf_op jit(solution)/shard_map/ppermute | solution.py:81
  30.8 2.9 %collective-permute-done.3 = bf16[3,128,256]{1,2,0:T(8,128)(2,1)S(1)} collective-permute-done((bf16[3,128,256]{1,2,0:T(8,128)(2,1)S(1)}, bf16[3,128,256]{1,2,0:T(8,128)(2,1)S(1)}, u32[]{:S(2)}, u32[]{:S(2)}) %collective-permute-start.3) | collective-permute-done | bytes 196640 | tf_op jit(solution)/shard_map/ppermute | solution.py:81
  33.7 3.8 %collective-permute-start.4 = (bf16[2,128,256]{1,2,0:T(8,128)(2,1)S(1)}, bf16[2,128,256]{1,2,0:T(8,128)(2,1)S(1)}, u32[]{:S(2)}, u32[]{:S(2)}) collective-permute-start(bf16[2,128,256]{1,2,0:T(8,128)(2,1)S(1)} %constant_dynamic-slice_fusion.2), channel_id=1, source_target_pairs={{0,56},{8,0},{16,8},{24,16},{32,24},{40,32},{48,40},{56,48},{64,12... | collective-permute-start | bytes 393224 | tf_op jit(solution)/shard_map/ppermute | solution.py:81
  37.8 2.2 %collective-permute-done.4 = bf16[2,128,256]{1,2,0:T(8,128)(2,1)S(1)} collective-permute-done((bf16[2,128,256]{1,2,0:T(8,128)(2,1)S(1)}, bf16[2,128,256]{1,2,0:T(8,128)(2,1)S(1)}, u32[]{:S(2)}, u32[]{:S(2)}) %collective-permute-start.4) | collective-permute-done | bytes 131104 | tf_op jit(solution)/shard_map/ppermute | solution.py:81
  40.0 3.9 %collective-permute-done.8 = bf16[2,128,256]{1,2,0:T(8,128)(2,1)S(1)} collective-permute-done((bf16[2,128,256]{1,2,0:T(8,128)(2,1)S(1)}, bf16[2,128,256]{1,2,0:T(8,128)(2,1)S(1)}, u32[]{:S(2)}, u32[]{:S(2)}) %collective-permute-start.8) | collective-permute-done | bytes 131104 | tf_op jit(solution)/shard_map/ppermute | solution.py:81
  44.3 0.8 %fusion.68 = (f32[4,128]{1,0:T(4,128)S(1)}, f32[1,4,128,2176]{2,3,1,0:T(8,128)S(1)}) fusion(bf16[128,4,64]{2,0,1:T(8,128)(2,1)S(1)} %get-tuple-element.6, bf16[128,4,64]{2,0,1:T(8,128)(2,1)S(1)} %get-tuple-element.5, bf16[2176,256]{0,1:T(8,128)(2,1)S(1)} %constant_dynamic-update-slice_fusion, pred[128,2176]{0,1:T(8,128)(4,1)S(1)} %compare_and_fusion), kind=kOutput, calls=%fused_computation.112 | convolution fusion | flops 288816640 | bytes 5556224 | tf_op jit(solution)/shard_map/tkgd,nkd->kgtn/dot_general | solution.py:95
  45.1 0.8 %fusion.2 = f32[4,128]{1,0:T(4,128)S(1)} fusion(f32[1,4,128,2176]{2,3,1,0:T(8,128)S(1)} %get-tuple-element.18, f32[4,128]{1,0:T(4,128)S(1)} %get-tuple-element.17, pred[128,2176]{0,1:T(8,128)(4,1)S(1)} %compare_and_fusion), kind=kLoop, calls=%fused_computation.4 | loop fusion | flops 3341824 | bytes 4739072 | tf_op jit(solution)/shard_map/reduce_sum | solution.py:103
  45.9 0.9 %fusion.13 = bf16[4,128,128]{1,2,0:T(8,128)(2,1)S(1)} fusion(f32[1,4,128,2176]{2,3,1,0:T(8,128)S(1)} %get-tuple-element.18, f32[4,128]{1,0:T(4,128)S(1)} %get-tuple-element.17, pred[128,2176]{0,1:T(8,128)(4,1)S(1)} %compare_and_fusion, bf16[2176,256]{0,1:T(8,128)(2,1)S(1)} %constant_dynamic-update-slice_fusion, f32[4,128]{1,0:T(4,128)S(1)} %fusion.2), kind=kOutput, calls=%fused_computation.14 | convolution fusion | flops 288686080 | bytes 5427200 | tf_op jit(solution)/shard_map/kgtn,nkd->kgtd/dot_general | solution.py:104
  46.8 1.6 %collective-permute-start.9 = (bf16[128,512]{0,1:T(8,128)(2,1)S(1)}, bf16[128,512]{0,1:T(8,128)(2,1)S(1)}, u32[]{:S(2)}, u32[]{:S(2)}) collective-permute-start(bf16[128,512]{0,1:T(8,128)(2,1)S(1)} %bitcast.114), channel_id=1, source_target_pairs={{0,2},{1,3},{2,4},{3,5},{4,6},{5,7},{6,0},{7,1},{8,10},{9,11},{10,... | collective-permute-start | bytes 393224 | tf_op jit(solution)/shard_map/ppermute | solution.py:121
  48.4 1.7 %collective-permute-start.10 = (bf16[128,512]{0,1:T(8,128)(2,1)S(1)}, bf16[128,512]{0,1:T(8,128)(2,1)S(1)}, u32[]{:S(2)}, u32[]{:S(2)}) collective-permute-start(bf16[128,512]{0,1:T(8,128)(2,1)S(1)} %bitcast.115), channel_id=1, source_target_pairs={{0,6},{1,7},{2,0},{3,1},{4,2},{5,3},{6,4},{7,5},{8,14},{9,15},{10,... | collective-permute-start | bytes 393224 | tf_op jit(solution)/shard_map/ppermute | solution.py:122
  50.5 2.6 %collective-permute-done.9 = bf16[128,512]{0,1:T(8,128)(2,1)S(1)} collective-permute-done((bf16[128,512]{0,1:T(8,128)(2,1)S(1)}, bf16[128,512]{0,1:T(8,128)(2,1)S(1)}, u32[]{:S(2)}, u32[]{:S(2)}) %collective-permute-start.9) | collective-permute-done | bytes 131104 | tf_op jit(solution)/shard_map/ppermute | solution.py:121
  53.7 3.1 %collective-permute-start.13 = (bf16[128,512]{0,1:T(8,128)(2,1)S(1)}, bf16[128,512]{0,1:T(8,128)(2,1)S(1)}, u32[]{:S(2)}, u32[]{:S(2)}) collective-permute-start(bf16[128,512]{0,1:T(8,128)(2,1)S(1)} %get-tuple-element.7), channel_id=1, source_target_pairs={{0,7},{1,2},{2,1},{3,4},{4,3},{5,6},{6,5},{7,0},{8,15},{9,10},{10,... | collective-permute-start | bytes 393224 | tf_op jit(solution)/shard_map/ppermute | solution.py:128
  58.0 5.0 %collective-permute-done.12 = bf16[128,512]{0,1:T(8,128)(2,1)S(1)} collective-permute-done((bf16[128,512]{0,1:T(8,128)(2,1)S(1)}, bf16[128,512]{0,1:T(8,128)(2,1)S(1)}, u32[]{:S(2)}, u32[]{:S(2)}) %collective-permute-start.12) | collective-permute-done | bytes 131104 | tf_op jit(solution)/shard_map/ppermute | solution.py:126
  (70 shorter events, 7.1 us)
Async XLA Ops:
  3.6 7.2 %collective-permute-start.1 = (bf16[128,256]{0,1:T(8,128)(2,1)S(1)}, bf16[128,256]{0,1:T(8,128)(2,1)S(1)}, u32[]{:S(2)}, u32[]{:S(2)}) collective-permute-start(bf16[128,256]{0,1:T(8,128)(2,1)S(1)} %get-tuple-element.14), channel_id=1, source_target_pairs={{0,64},{8,72},{16,80},{24,88},{32,96},{40,104},{48,112},{56,120},{... | collective-permute-start | bytes 196616 | tf_op jit(solution)/shard_map/ppermute | solution.py:61
  6.7 7.7 %collective-permute-start = (bf16[128,256]{0,1:T(8,128)(2,1)S(1)}, bf16[128,256]{0,1:T(8,128)(2,1)S(1)}, u32[]{:S(2)}, u32[]{:S(2)}) collective-permute-start(bf16[128,256]{0,1:T(8,128)(2,1)S(1)} %get-tuple-element.14), channel_id=1, source_target_pairs={{0,128},{8,136},{16,144},{24,152},{32,160},{40,168},{48,176},{56,1... | collective-permute-start | bytes 196616 | tf_op jit(solution)/shard_map/ppermute | solution.py:61
  14.4 10.9 %collective-permute-start.2 = (bf16[3,128,256]{1,2,0:T(8,128)(2,1)S(1)}, bf16[3,128,256]{1,2,0:T(8,128)(2,1)S(1)}, u32[]{:S(2)}, u32[]{:S(2)}) collective-permute-start(bf16[3,128,256]{1,2,0:T(8,128)(2,1)S(1)} %pad_maximum_fusion.1), channel_id=1, source_target_pairs={{0,56},{8,0},{16,8},{24,16},{32,24},{40,32},{48,40},{56,48},{64,12... | collective-permute-start | bytes 589832 | tf_op jit(solution)/shard_map/ppermute | solution.py:81
  20.7 10.1 %collective-permute-start.6 = (bf16[3,128,256]{1,2,0:T(8,128)(2,1)S(1)}, bf16[3,128,256]{1,2,0:T(8,128)(2,1)S(1)}, u32[]{:S(2)}, u32[]{:S(2)}) collective-permute-start(bf16[3,128,256]{1,2,0:T(8,128)(2,1)S(1)} %pad_maximum_fusion.1), channel_id=1, source_target_pairs={{0,8},{8,16},{16,24},{24,32},{32,40},{40,48},{48,56},{56,0},{64,72... | collective-permute-start | bytes 589832 | tf_op jit(solution)/shard_map/ppermute | solution.py:81
  20.8 19.2 %collective-permute-start.5 = (bf16[2,128,256]{1,2,0:T(8,128)(2,1)S(1)}, bf16[2,128,256]{1,2,0:T(8,128)(2,1)S(1)}, u32[]{:S(2)}, u32[]{:S(2)}) collective-permute-start(bf16[2,128,256]{1,2,0:T(8,128)(2,1)S(1)} %constant_dynamic-slice_fusion.1), channel_id=1, source_target_pairs={{0,32},{8,40},{16,48},{24,56},{32,0},{40,8},{48,16},{56,24},{64,96... | collective-permute-start | bytes 393224 | tf_op jit(solution)/shard_map/ppermute | solution.py:70
  25.4 8.3 %collective-permute-start.3 = (bf16[3,128,256]{1,2,0:T(8,128)(2,1)S(1)}, bf16[3,128,256]{1,2,0:T(8,128)(2,1)S(1)}, u32[]{:S(2)}, u32[]{:S(2)}) collective-permute-start(bf16[3,128,256]{1,2,0:T(8,128)(2,1)S(1)} %collective-permute-done.2), channel_id=1, source_target_pairs={{0,56},{8,0},{16,8},{24,16},{32,24},{40,32},{48,40},{56,48},{64,12... | collective-permute-start | bytes 589832 | tf_op jit(solution)/shard_map/ppermute | solution.py:81
  30.7 6.9 %collective-permute-start.7 = (bf16[3,128,256]{1,2,0:T(8,128)(2,1)S(1)}, bf16[3,128,256]{1,2,0:T(8,128)(2,1)S(1)}, u32[]{:S(2)}, u32[]{:S(2)}) collective-permute-start(bf16[3,128,256]{1,2,0:T(8,128)(2,1)S(1)} %collective-permute-done.6), channel_id=1, source_target_pairs={{0,8},{8,16},{16,24},{24,32},{32,40},{40,48},{48,56},{56,0},{64,72... | collective-permute-start | bytes 589832 | tf_op jit(solution)/shard_map/ppermute | solution.py:81
  33.7 6.3 %collective-permute-start.4 = (bf16[2,128,256]{1,2,0:T(8,128)(2,1)S(1)}, bf16[2,128,256]{1,2,0:T(8,128)(2,1)S(1)}, u32[]{:S(2)}, u32[]{:S(2)}) collective-permute-start(bf16[2,128,256]{1,2,0:T(8,128)(2,1)S(1)} %constant_dynamic-slice_fusion.2), channel_id=1, source_target_pairs={{0,56},{8,0},{16,8},{24,16},{32,24},{40,32},{48,40},{56,48},{64,12... | collective-permute-start | bytes 393224 | tf_op jit(solution)/shard_map/ppermute | solution.py:81
  37.6 6.3 %collective-permute-start.8 = (bf16[2,128,256]{1,2,0:T(8,128)(2,1)S(1)}, bf16[2,128,256]{1,2,0:T(8,128)(2,1)S(1)}, u32[]{:S(2)}, u32[]{:S(2)}) collective-permute-start(bf16[2,128,256]{1,2,0:T(8,128)(2,1)S(1)} %constant_dynamic-slice_fusion), channel_id=1, source_target_pairs={{0,8},{8,16},{16,24},{24,32},{32,40},{40,48},{48,56},{56,0},{64,72... | collective-permute-start | bytes 393224 | tf_op jit(solution)/shard_map/ppermute | solution.py:81
  44.2 5.9 %slice-start = ((s8[8388608]{0:T(1024)(128)(4,1)}), s8[4194304]{0:T(1024)(128)(4,1)S(1)}, s32[]{:S(2)}) async-start(s8[8388608]{0:T(1024)(128)(4,1)} %bitcast.107), calls=%async_computation | async-start | bytes 8388608
  45.1 5.1 %slice-start.1 = ((s8[8388608]{0:T(1024)(128)(4,1)}), s8[4194304]{0:T(1024)(128)(4,1)S(1)}, s32[]{:S(2)}) async-start(s8[8388608]{0:T(1024)(128)(4,1)} %bitcast.107), calls=%async_computation.1 | async-start | bytes 8388608
  46.8 6.3 %collective-permute-start.9 = (bf16[128,512]{0,1:T(8,128)(2,1)S(1)}, bf16[128,512]{0,1:T(8,128)(2,1)S(1)}, u32[]{:S(2)}, u32[]{:S(2)}) collective-permute-start(bf16[128,512]{0,1:T(8,128)(2,1)S(1)} %bitcast.114), channel_id=1, source_target_pairs={{0,2},{1,3},{2,4},{3,5},{4,6},{5,7},{6,0},{7,1},{8,10},{9,11},{10,... | collective-permute-start | bytes 393224 | tf_op jit(solution)/shard_map/ppermute | solution.py:121
  48.4 5.0 %collective-permute-start.10 = (bf16[128,512]{0,1:T(8,128)(2,1)S(1)}, bf16[128,512]{0,1:T(8,128)(2,1)S(1)}, u32[]{:S(2)}, u32[]{:S(2)}) collective-permute-start(bf16[128,512]{0,1:T(8,128)(2,1)S(1)} %bitcast.115), channel_id=1, source_target_pairs={{0,6},{1,7},{2,0},{3,1},{4,2},{5,3},{6,4},{7,5},{8,14},{9,15},{10,... | collective-permute-start | bytes 393224 | tf_op jit(solution)/shard_map/ppermute | solution.py:122
  50.2 7.5 %collective-permute-start.11 = (bf16[128,512]{0,1:T(8,128)(2,1)S(1)}, bf16[128,512]{0,1:T(8,128)(2,1)S(1)}, u32[]{:S(2)}, u32[]{:S(2)}) collective-permute-start(bf16[128,512]{0,1:T(8,128)(2,1)S(1)} %bitcast.116), channel_id=1, source_target_pairs={{0,1},{1,0},{2,3},{3,2},{4,5},{5,4},{6,7},{7,6},{8,9},{9,8},{10,11... | collective-permute-start | bytes 393224 | tf_op jit(solution)/shard_map/ppermute | solution.py:124
  53.4 10.4 %collective-permute-start.14 = (bf16[2,128,512]{1,2,0:T(8,128)(2,1)S(1)}, bf16[2,128,512]{1,2,0:T(8,128)(2,1)S(1)}, u32[]{:S(2)}, u32[]{:S(2)}) collective-permute-start(bf16[2,128,512]{1,2,0:T(8,128)(2,1)S(1)} %pad_maximum_fusion), channel_id=1, source_target_pairs={{0,1},{1,0},{2,3},{3,2},{4,5},{5,4},{6,7},{7,6},{8,9},{9,8},{10,11... | collective-permute-start | bytes 786440 | tf_op jit(solution)/shard_map/ppermute | solution.py:129
  53.7 9.7 %collective-permute-start.13 = (bf16[128,512]{0,1:T(8,128)(2,1)S(1)}, bf16[128,512]{0,1:T(8,128)(2,1)S(1)}, u32[]{:S(2)}, u32[]{:S(2)}) collective-permute-start(bf16[128,512]{0,1:T(8,128)(2,1)S(1)} %get-tuple-element.7), channel_id=1, source_target_pairs={{0,7},{1,2},{2,1},{3,4},{4,3},{5,6},{6,5},{7,0},{8,15},{9,10},{10,... | collective-permute-start | bytes 393224 | tf_op jit(solution)/shard_map/ppermute | solution.py:128
  56.9 6.2 %collective-permute-start.12 = (bf16[128,512]{0,1:T(8,128)(2,1)S(1)}, bf16[128,512]{0,1:T(8,128)(2,1)S(1)}, u32[]{:S(2)}, u32[]{:S(2)}) collective-permute-start(bf16[128,512]{0,1:T(8,128)(2,1)S(1)} %get-tuple-element.8), channel_id=1, source_target_pairs={{0,2},{1,7},{2,4},{3,1},{4,6},{5,3},{6,0},{7,5},{8,10},{9,15},{10,... | collective-permute-start | bytes 393224 | tf_op jit(solution)/shard_map/ppermute | solution.py:126

commit v16 on v8

--- a/solution.py
+++ b/solution.py
@@ -99,7 +99,7 @@
         allowed = (key_pos[None, :] <= positions[:, None]) & (key_pos[None, :] >= starts[:, None])
         scores = jnp.where(allowed, scores, -1e30)
         row_max = jnp.max(scores, axis=-1)
-        weights = jnp.where(allowed, jnp.exp(scores - row_max[..., None]), 0.0)
+        weights = jnp.exp(scores - row_max[..., None])
         row_sum = jnp.sum(weights, axis=-1)
         weighted = jnp.einsum(
             "kgtn,nkd->kgtd",

time: 63.9 us -> 63.6 us (level)
  no operation moved by 1% of the time
where the time goes in v16:
time: 63.6 us; the launch traced here: 63.3 us
  starting transfers between devices  35.8 us (56%)
  waiting for transfers between devices  14.3 us (22%)
  matrix products  5.17 us (8%)
  other arithmetic  3.9 us (6%)
  local copies, waits for them, and re-layouts  3.43 us (5%)
    ppermute x6, waiting for transfers between devices, on_device(): lax.ppermute(lax.dynamic_slice_in_dim(packet, lo, step['width'], 0), 'ctx...  12.5 us
    ppermute x6, starting transfers between devices, on_device(): lax.ppermute(lax.dynamic_slice_in_dim(packet, lo, step['width'], 0), 'ctx...  12.5 us
    ppermute x2, starting transfers between devices, on_device(): lax.ppermute(own, 'ctx', [(s, s + shift) for s in range(n_ctx - shift)])  8.55 us
    ppermute x1, starting transfers between devices, on_device(): lax.ppermute(jnp.where(core == 1, up, down), 'head', cross_pairs)  4.19 us
    dot_general x8, matrix products, project(): return jnp.dot(piece, rows, preferred_element_type=jnp.float32)  3.43 us
    unnamed x25, local copies, waits for them, and re-layouts  3.37 us
    ppermute x1, starting transfers between devices, on_device(): partner = lax.ppermute(attended, 'head', swap)  3.32 us
    ppermute x1, starting transfers between devices, on_device(): lax.ppermute(lax.dynamic_slice_in_dim(bundle, lo, rows_back, 0), 'ctx', [...  2.86 us
  transfers between devices with their start and end apart: 15, of which 5 were waited for; matrix products, arithmetic and copies ran while one was open for 7% of the time, Pallas kernels for 0%

profile of v16, /device:TPU:1, one launch (start us, length us, event | category | flops | bytes accessed | tf_op | source)
XLA Modules:
  0.0 63.3 jit_solution(11117685000263764768)
XLA Ops:
  0.0 0.8 %select_reduce_fusion.1 = s32[32]{0:T(128)S(1)} fusion(s32[32]{0:T(128)} %param.8), kind=kLoop, calls=%fused_computation.94 | loop fusion | flops 3040 | bytes 256 | tf_op jit(solution)/shard_map/reduce_sum | solution.py:15
  1.5 0.9 %copy.18 = bf16[128,128]{0,1:T(8,128)(2,1)S(1)} copy(bf16[128,128]{1,0:T(8,128)(2,1)} %param.6) | data formatting | bytes 65536 | tf_op args[1]
  2.4 0.9 %copy.19 = bf16[128,128]{0,1:T(8,128)(2,1)S(1)} copy(bf16[128,128]{1,0:T(8,128)(2,1)} %param.7) | data formatting | bytes 65536 | tf_op args[2]
  3.6 4.0 %collective-permute-start.1 = (bf16[128,256]{0,1:T(8,128)(2,1)S(1)}, bf16[128,256]{0,1:T(8,128)(2,1)S(1)}, u32[]{:S(2)}, u32[]{:S(2)}) collective-permute-start(bf16[128,256]{0,1:T(8,128)(2,1)S(1)} %get-tuple-element.14), channel_id=1, source_target_pairs={{0,64},{8,72},{16,80},{24,88},{32,96},{40,104},{48,112},{56,120},{... | collective-permute-start | bytes 196616 | tf_op jit(solution)/shard_map/ppermute | solution.py:61
  7.6 4.5 %collective-permute-start = (bf16[128,256]{0,1:T(8,128)(2,1)S(1)}, bf16[128,256]{0,1:T(8,128)(2,1)S(1)}, u32[]{:S(2)}, u32[]{:S(2)}) collective-permute-start(bf16[128,256]{0,1:T(8,128)(2,1)S(1)} %get-tuple-element.14), channel_id=1, source_target_pairs={{0,128},{8,136},{16,144},{24,152},{32,160},{40,168},{48,176},{56,1... | collective-permute-start | bytes 196616 | tf_op jit(solution)/shard_map/ppermute | solution.py:61
  12.1 1.0 %copy.20 = bf16[128,512]{0,1:T(8,128)(2,1)S(1)} copy(bf16[128,512]{1,0:T(8,128)(2,1)} %param.5) | data formatting | bytes 262144 | tf_op args[0]
  13.2 1.0 %compare_and_fusion = pred[128,2176]{0,1:T(8,128)(4,1)S(1)} fusion(s32[128]{0:T(128)S(1)} %select_reduce_fusion, s32[128]{0:T(128)S(1)} %iota_add_fusion.1, s32[2176]{0:T(1024)S(1)} %iota_add_fusion), kind=kLoop, calls=%fused_computation.19 | loop fusion | flops 835584 | bytes 288256 | tf_op jit(solution)/shard_map/and | solution.py:99
  14.9 5.7 %collective-permute-start.2 = (bf16[3,128,256]{1,2,0:T(8,128)(2,1)S(1)}, bf16[3,128,256]{1,2,0:T(8,128)(2,1)S(1)}, u32[]{:S(2)}, u32[]{:S(2)}) collective-permute-start(bf16[3,128,256]{1,2,0:T(8,128)(2,1)S(1)} %pad_maximum_fusion.1), channel_id=1, source_target_pairs={{0,56},{8,0},{16,8},{24,16},{32,24},{40,32},{48,40},{56,48},{64,12... | collective-permute-start | bytes 589832 | tf_op jit(solution)/shard_map/ppermute | solution.py:81
  20.9 2.9 %collective-permute-start.5 = (bf16[2,128,256]{1,2,0:T(8,128)(2,1)S(1)}, bf16[2,128,256]{1,2,0:T(8,128)(2,1)S(1)}, u32[]{:S(2)}, u32[]{:S(2)}) collective-permute-start(bf16[2,128,256]{1,2,0:T(8,128)(2,1)S(1)} %constant_dynamic-slice_fusion.1), channel_id=1, source_target_pairs={{0,32},{8,40},{16,48},{24,56},{32,0},{40,8},{48,16},{56,24},{64,96... | collective-permute-start | bytes 393224 | tf_op jit(solution)/shard_map/ppermute | solution.py:70
  23.8 3.2 %collective-permute-start.3 = (bf16[3,128,256]{1,2,0:T(8,128)(2,1)S(1)}, bf16[3,128,256]{1,2,0:T(8,128)(2,1)S(1)}, u32[]{:S(2)}, u32[]{:S(2)}) collective-permute-start(bf16[3,128,256]{1,2,0:T(8,128)(2,1)S(1)} %collective-permute-done.2), channel_id=1, source_target_pairs={{0,56},{8,0},{16,8},{24,16},{32,24},{40,32},{48,40},{56,48},{64,12... | collective-permute-start | bytes 589832 | tf_op jit(solution)/shard_map/ppermute | solution.py:81
  27.0 2.0 %collective-permute-done.6 = bf16[3,128,256]{1,2,0:T(8,128)(2,1)S(1)} collective-permute-done((bf16[3,128,256]{1,2,0:T(8,128)(2,1)S(1)}, bf16[3,128,256]{1,2,0:T(8,128)(2,1)S(1)}, u32[]{:S(2)}, u32[]{:S(2)}) %collective-permute-start.6) | collective-permute-done | bytes 196640 | tf_op jit(solution)/shard_map/ppermute | solution.py:81
  29.0 5.6 %collective-permute-done.3 = bf16[3,128,256]{1,2,0:T(8,128)(2,1)S(1)} collective-permute-done((bf16[3,128,256]{1,2,0:T(8,128)(2,1)S(1)}, bf16[3,128,256]{1,2,0:T(8,128)(2,1)S(1)}, u32[]{:S(2)}, u32[]{:S(2)}) %collective-permute-start.3) | collective-permute-done | bytes 196640 | tf_op jit(solution)/shard_map/ppermute | solution.py:81
  34.6 3.5 %collective-permute-start.4 = (bf16[2,128,256]{1,2,0:T(8,128)(2,1)S(1)}, bf16[2,128,256]{1,2,0:T(8,128)(2,1)S(1)}, u32[]{:S(2)}, u32[]{:S(2)}) collective-permute-start(bf16[2,128,256]{1,2,0:T(8,128)(2,1)S(1)} %constant_dynamic-slice_fusion.2), channel_id=1, source_target_pairs={{0,56},{8,0},{16,8},{24,16},{32,24},{40,32},{48,40},{56,48},{64,12... | collective-permute-start | bytes 393224 | tf_op jit(solution)/shard_map/ppermute | solution.py:81
  38.2 1.8 %collective-permute-done.4 = bf16[2,128,256]{1,2,0:T(8,128)(2,1)S(1)} collective-permute-done((bf16[2,128,256]{1,2,0:T(8,128)(2,1)S(1)}, bf16[2,128,256]{1,2,0:T(8,128)(2,1)S(1)}, u32[]{:S(2)}, u32[]{:S(2)}) %collective-permute-start.4) | collective-permute-done | bytes 131104 | tf_op jit(solution)/shard_map/ppermute | solution.py:81
  40.1 3.1 %collective-permute-done.8 = bf16[2,128,256]{1,2,0:T(8,128)(2,1)S(1)} collective-permute-done((bf16[2,128,256]{1,2,0:T(8,128)(2,1)S(1)}, bf16[2,128,256]{1,2,0:T(8,128)(2,1)S(1)}, u32[]{:S(2)}, u32[]{:S(2)}) %collective-permute-start.8) | collective-permute-done | bytes 131104 | tf_op jit(solution)/shard_map/ppermute | solution.py:81
  43.6 0.8 %fusion.70 = (f32[4,128]{1,0:T(4,128)S(1)}, f32[1,4,128,2176]{2,3,1,0:T(8,128)S(1)}) fusion(bf16[128,4,64]{2,0,1:T(8,128)(2,1)S(1)} %get-tuple-element.6, bf16[128,4,64]{2,0,1:T(8,128)(2,1)S(1)} %get-tuple-element.5, bf16[2176,256]{0,1:T(8,128)(2,1)S(1)} %constant_dynamic-update-slice_fusion, pred[128,2176]{0,1:T(8,128)(4,1)S(1)} %compare_and_fusion), kind=kOutput, calls=%fused_computation.114 | convolution fusion | flops 288816640 | bytes 5556224 | tf_op jit(solution)/shard_map/tkgd,nkd->kgtn/dot_general | solution.py:95
  45.0 0.9 %fusion.17 = bf16[4,128,128]{1,2,0:T(8,128)(2,1)S(1)} fusion(f32[1,4,128,2176]{2,3,1,0:T(8,128)S(1)} %get-tuple-element.18, f32[4,128]{1,0:T(4,128)S(1)} %get-tuple-element.17, bf16[2176,256]{0,1:T(8,128)(2,1)S(1)} %constant_dynamic-update-slice_fusion, f32[4,128]{1,0:T(4,128)S(1)} %fusion.2), kind=kOutput, calls=%fused_computation.18 | convolution fusion | flops 287571968 | bytes 5148672 | tf_op jit(solution)/shard_map/kgtn,nkd->kgtd/dot_general | solution.py:104
  45.9 1.3 %collective-permute-start.9 = (bf16[128,512]{0,1:T(8,128)(2,1)S(1)}, bf16[128,512]{0,1:T(8,128)(2,1)S(1)}, u32[]{:S(2)}, u32[]{:S(2)}) collective-permute-start(bf16[128,512]{0,1:T(8,128)(2,1)S(1)} %bitcast.112), channel_id=1, source_target_pairs={{0,2},{1,3},{2,4},{3,5},{4,6},{5,7},{6,0},{7,1},{8,10},{9,11},{10,... | collective-permute-start | bytes 393224 | tf_op jit(solution)/shard_map/ppermute | solution.py:121
  47.2 1.5 %collective-permute-start.10 = (bf16[128,512]{0,1:T(8,128)(2,1)S(1)}, bf16[128,512]{0,1:T(8,128)(2,1)S(1)}, u32[]{:S(2)}, u32[]{:S(2)}) collective-permute-start(bf16[128,512]{0,1:T(8,128)(2,1)S(1)} %bitcast.113), channel_id=1, source_target_pairs={{0,6},{1,7},{2,0},{3,1},{4,2},{5,3},{6,4},{7,5},{8,14},{9,15},{10,... | collective-permute-start | bytes 393224 | tf_op jit(solution)/shard_map/ppermute | solution.py:122
  48.7 3.3 %collective-permute-start.11 = (bf16[128,512]{0,1:T(8,128)(2,1)S(1)}, bf16[128,512]{0,1:T(8,128)(2,1)S(1)}, u32[]{:S(2)}, u32[]{:S(2)}) collective-permute-start(bf16[128,512]{0,1:T(8,128)(2,1)S(1)} %bitcast.114), channel_id=1, source_target_pairs={{0,1},{1,0},{2,3},{3,2},{4,5},{5,4},{6,7},{7,6},{8,9},{9,8},{10,11... | collective-permute-start | bytes 393224 | tf_op jit(solution)/shard_map/ppermute | solution.py:124
  52.4 1.6 %collective-permute-start.12 = (bf16[128,512]{0,1:T(8,128)(2,1)S(1)}, bf16[128,512]{0,1:T(8,128)(2,1)S(1)}, u32[]{:S(2)}, u32[]{:S(2)}) collective-permute-start(bf16[128,512]{0,1:T(8,128)(2,1)S(1)} %get-tuple-element.7), channel_id=1, source_target_pairs={{0,2},{1,7},{2,4},{3,1},{4,6},{5,3},{6,0},{7,5},{8,10},{9,15},{10,... | collective-permute-start | bytes 393224 | tf_op jit(solution)/shard_map/ppermute | solution.py:126
  54.0 4.2 %collective-permute-start.13 = (bf16[128,512]{0,1:T(8,128)(2,1)S(1)}, bf16[128,512]{0,1:T(8,128)(2,1)S(1)}, u32[]{:S(2)}, u32[]{:S(2)}) collective-permute-start(bf16[128,512]{0,1:T(8,128)(2,1)S(1)} %get-tuple-element.8), channel_id=1, source_target_pairs={{0,7},{1,2},{2,1},{3,4},{4,3},{5,6},{6,5},{7,0},{8,15},{9,10},{10,... | collective-permute-start | bytes 393224 | tf_op jit(solution)/shard_map/ppermute | solution.py:128
  59.4 1.8 %collective-permute-done.13 = bf16[128,512]{0,1:T(8,128)(2,1)S(1)} collective-permute-done((bf16[128,512]{0,1:T(8,128)(2,1)S(1)}, bf16[128,512]{0,1:T(8,128)(2,1)S(1)}, u32[]{:S(2)}, u32[]{:S(2)}) %collective-permute-start.13) | collective-permute-done | bytes 131104 | tf_op jit(solution)/shard_map/ppermute | solution.py:128
  62.2 1.1 %fusion.13 = bf16[128,1024]{1,0:T(8,128)(2,1)} fusion(f32[128,1024]{1,0:T(8,128)S(1)} %fusion.20, f32[128,1024]{1,0:T(8,128)S(1)} %fusion.22, f32[128,1024]{1,0:T(8,128)S(1)} %fusion.24, f32[128,1024]{1,0:T(8,128)S(1)} %fusion.26, f32[128,1024]{1,0:T(8,128)S(1)} %fusion.28, f32[128,1024]{1,0:T(8,128)S(1)} %convolution_add_fusion.1, ...), kind=kOutput, calls=%fused_computation.16 | convolution fusion | flops 135135232 | bytes 4587524 | tf_op jit(solution)/shard_map/dot_general | solution.py:119
  (64 shorter events, 5.4 us)
Async XLA Ops:
  3.6 11.3 %collective-permute-start.1 = (bf16[128,256]{0,1:T(8,128)(2,1)S(1)}, bf16[128,256]{0,1:T(8,128)(2,1)S(1)}, u32[]{:S(2)}, u32[]{:S(2)}) collective-permute-start(bf16[128,256]{0,1:T(8,128)(2,1)S(1)} %get-tuple-element.14), channel_id=1, source_target_pairs={{0,64},{8,72},{16,80},{24,88},{32,96},{40,104},{48,112},{56,120},{... | collective-permute-start | bytes 196616 | tf_op jit(solution)/shard_map/ppermute | solution.py:61
  7.6 7.3 %collective-permute-start = (bf16[128,256]{0,1:T(8,128)(2,1)S(1)}, bf16[128,256]{0,1:T(8,128)(2,1)S(1)}, u32[]{:S(2)}, u32[]{:S(2)}) collective-permute-start(bf16[128,256]{0,1:T(8,128)(2,1)S(1)} %get-tuple-element.14), channel_id=1, source_target_pairs={{0,128},{8,136},{16,144},{24,152},{32,160},{40,168},{48,176},{56,1... | collective-permute-start | bytes 196616 | tf_op jit(solution)/shard_map/ppermute | solution.py:61
  14.9 8.9 %collective-permute-start.2 = (bf16[3,128,256]{1,2,0:T(8,128)(2,1)S(1)}, bf16[3,128,256]{1,2,0:T(8,128)(2,1)S(1)}, u32[]{:S(2)}, u32[]{:S(2)}) collective-permute-start(bf16[3,128,256]{1,2,0:T(8,128)(2,1)S(1)} %pad_maximum_fusion.1), channel_id=1, source_target_pairs={{0,56},{8,0},{16,8},{24,16},{32,24},{40,32},{48,40},{56,48},{64,12... | collective-permute-start | bytes 589832 | tf_op jit(solution)/shard_map/ppermute | solution.py:81
  20.8 8.2 %collective-permute-start.6 = (bf16[3,128,256]{1,2,0:T(8,128)(2,1)S(1)}, bf16[3,128,256]{1,2,0:T(8,128)(2,1)S(1)}, u32[]{:S(2)}, u32[]{:S(2)}) collective-permute-start(bf16[3,128,256]{1,2,0:T(8,128)(2,1)S(1)} %pad_maximum_fusion.1), channel_id=1, source_target_pairs={{0,8},{8,16},{16,24},{24,32},{32,40},{40,48},{48,56},{56,0},{64,72... | collective-permute-start | bytes 589832 | tf_op jit(solution)/shard_map/ppermute | solution.py:81
  20.9 19.1 %collective-permute-start.5 = (bf16[2,128,256]{1,2,0:T(8,128)(2,1)S(1)}, bf16[2,128,256]{1,2,0:T(8,128)(2,1)S(1)}, u32[]{:S(2)}, u32[]{:S(2)}) collective-permute-start(bf16[2,128,256]{1,2,0:T(8,128)(2,1)S(1)} %constant_dynamic-slice_fusion.1), channel_id=1, source_target_pairs={{0,32},{8,40},{16,48},{24,56},{32,0},{40,8},{48,16},{56,24},{64,96... | collective-permute-start | bytes 393224 | tf_op jit(solution)/shard_map/ppermute | solution.py:70
  23.8 10.8 %collective-permute-start.3 = (bf16[3,128,256]{1,2,0:T(8,128)(2,1)S(1)}, bf16[3,128,256]{1,2,0:T(8,128)(2,1)S(1)}, u32[]{:S(2)}, u32[]{:S(2)}) collective-permute-start(bf16[3,128,256]{1,2,0:T(8,128)(2,1)S(1)} %collective-permute-done.2), channel_id=1, source_target_pairs={{0,56},{8,0},{16,8},{24,16},{32,24},{40,32},{48,40},{56,48},{64,12... | collective-permute-start | bytes 589832 | tf_op jit(solution)/shard_map/ppermute | solution.py:81
  29.0 9.1 %collective-permute-start.7 = (bf16[3,128,256]{1,2,0:T(8,128)(2,1)S(1)}, bf16[3,128,256]{1,2,0:T(8,128)(2,1)S(1)}, u32[]{:S(2)}, u32[]{:S(2)}) collective-permute-start(bf16[3,128,256]{1,2,0:T(8,128)(2,1)S(1)} %collective-permute-done.6), channel_id=1, source_target_pairs={{0,8},{8,16},{16,24},{24,32},{32,40},{40,48},{48,56},{56,0},{64,72... | collective-permute-start | bytes 589832 | tf_op jit(solution)/shard_map/ppermute | solution.py:81
  34.6 5.4 %collective-permute-start.4 = (bf16[2,128,256]{1,2,0:T(8,128)(2,1)S(1)}, bf16[2,128,256]{1,2,0:T(8,128)(2,1)S(1)}, u32[]{:S(2)}, u32[]{:S(2)}) collective-permute-start(bf16[2,128,256]{1,2,0:T(8,128)(2,1)S(1)} %constant_dynamic-slice_fusion.2), channel_id=1, source_target_pairs={{0,56},{8,0},{16,8},{24,16},{32,24},{40,32},{48,40},{56,48},{64,12... | collective-permute-start | bytes 393224 | tf_op jit(solution)/shard_map/ppermute | solution.py:81
  38.1 5.1 %collective-permute-start.8 = (bf16[2,128,256]{1,2,0:T(8,128)(2,1)S(1)}, bf16[2,128,256]{1,2,0:T(8,128)(2,1)S(1)}, u32[]{:S(2)}, u32[]{:S(2)}) collective-permute-start(bf16[2,128,256]{1,2,0:T(8,128)(2,1)S(1)} %constant_dynamic-slice_fusion), channel_id=1, source_target_pairs={{0,8},{8,16},{16,24},{24,32},{32,40},{40,48},{48,56},{56,0},{64,72... | collective-permute-start | bytes 393224 | tf_op jit(solution)/shard_map/ppermute | solution.py:81
  43.6 8.5 %slice-start = ((s8[8388608]{0:T(1024)(128)(4,1)}), s8[4194304]{0:T(1024)(128)(4,1)S(1)}, s32[]{:S(2)}) async-start(s8[8388608]{0:T(1024)(128)(4,1)} %bitcast.107), calls=%async_computation | async-start | bytes 8388608
  44.4 7.6 %slice-start.1 = ((s8[8388608]{0:T(1024)(128)(4,1)}), s8[4194304]{0:T(1024)(128)(4,1)S(1)}, s32[]{:S(2)}) async-start(s8[8388608]{0:T(1024)(128)(4,1)} %bitcast.107), calls=%async_computation.1 | async-start | bytes 8388608
  45.9 6.4 %collective-permute-start.9 = (bf16[128,512]{0,1:T(8,128)(2,1)S(1)}, bf16[128,512]{0,1:T(8,128)(2,1)S(1)}, u32[]{:S(2)}, u32[]{:S(2)}) collective-permute-start(bf16[128,512]{0,1:T(8,128)(2,1)S(1)} %bitcast.112), channel_id=1, source_target_pairs={{0,2},{1,3},{2,4},{3,5},{4,6},{5,7},{6,0},{7,1},{8,10},{9,11},{10,... | collective-permute-start | bytes 393224 | tf_op jit(solution)/shard_map/ppermute | solution.py:121
  47.2 5.1 %collective-permute-start.10 = (bf16[128,512]{0,1:T(8,128)(2,1)S(1)}, bf16[128,512]{0,1:T(8,128)(2,1)S(1)}, u32[]{:S(2)}, u32[]{:S(2)}) collective-permute-start(bf16[128,512]{0,1:T(8,128)(2,1)S(1)} %bitcast.113), channel_id=1, source_target_pairs={{0,6},{1,7},{2,0},{3,1},{4,2},{5,3},{6,4},{7,5},{8,14},{9,15},{10,... | collective-permute-start | bytes 393224 | tf_op jit(solution)/shard_map/ppermute | solution.py:122
  48.7 10.0 %collective-permute-start.11 = (bf16[128,512]{0,1:T(8,128)(2,1)S(1)}, bf16[128,512]{0,1:T(8,128)(2,1)S(1)}, u32[]{:S(2)}, u32[]{:S(2)}) collective-permute-start(bf16[128,512]{0,1:T(8,128)(2,1)S(1)} %bitcast.114), channel_id=1, source_target_pairs={{0,1},{1,0},{2,3},{3,2},{4,5},{5,4},{6,7},{7,6},{8,9},{9,8},{10,11... | collective-permute-start | bytes 393224 | tf_op jit(solution)/shard_map/ppermute | solution.py:124
  52.4 6.6 %collective-permute-start.12 = (bf16[128,512]{0,1:T(8,128)(2,1)S(1)}, bf16[128,512]{0,1:T(8,128)(2,1)S(1)}, u32[]{:S(2)}, u32[]{:S(2)}) collective-permute-start(bf16[128,512]{0,1:T(8,128)(2,1)S(1)} %get-tuple-element.7), channel_id=1, source_target_pairs={{0,2},{1,7},{2,4},{3,1},{4,6},{5,3},{6,0},{7,5},{8,10},{9,15},{10,... | collective-permute-start | bytes 393224 | tf_op jit(solution)/shard_map/ppermute | solution.py:126
  54.0 7.2 %collective-permute-start.13 = (bf16[128,512]{0,1:T(8,128)(2,1)S(1)}, bf16[128,512]{0,1:T(8,128)(2,1)S(1)}, u32[]{:S(2)}, u32[]{:S(2)}) collective-permute-start(bf16[128,512]{0,1:T(8,128)(2,1)S(1)} %get-tuple-element.8), channel_id=1, source_target_pairs={{0,7},{1,2},{2,1},{3,4},{4,3},{5,6},{6,5},{7,0},{8,15},{9,10},{10,... | collective-permute-start | bytes 393224 | tf_op jit(solution)/shard_map/ppermute | solution.py:128
  58.2 3.3 %collective-permute-start.14 = (bf16[2,128,512]{1,2,0:T(8,128)(2,1)S(1)}, bf16[2,128,512]{1,2,0:T(8,128)(2,1)S(1)}, u32[]{:S(2)}, u32[]{:S(2)}) collective-permute-start(bf16[2,128,512]{1,2,0:T(8,128)(2,1)S(1)} %pad_maximum_fusion), channel_id=1, source_target_pairs={{0,1},{1,0},{2,3},{3,2},{4,5},{5,4},{6,7},{7,6},{8,9},{9,8},{10,11... | collective-permute-start | bytes 786440 | tf_op jit(solution)/shard_map/ppermute | solution.py:129

commit v17 on v16

--- a/solution.py
+++ b/solution.py
@@ -64,6 +64,7 @@
         z = ctx % row
         n_rows = n_ctx // row
         chains, direct = relay_plan(row, rows_back)
+        late = []
         if direct:
             half = row // 2
             lo = jnp.where((z + half) % row < half, 1, 0)
@@ -74,6 +75,7 @@
             )
             for m in range(rows_back):
                 blocks[half + row * m] = got[m]
+                late.append(half + row * m)
         for chain in chains:
             packet = bundle
             for step in chain:
@@ -87,26 +89,36 @@
                 got = lax.dynamic_slice_in_dim(packet, at, len(step["blocks"]), 0)
                 for i, blk in enumerate(step["blocks"]):
                     blocks[blk] = got[i]
-        window = jnp.concatenate([blocks[span - k] for k in range(span + 1)], axis=0)
-        key_count = window.shape[0]
-        key_block = window[:, :kv_width].reshape(key_count, kv_local, HD)
-        value_block = window[:, kv_width:].reshape(key_count, kv_local, HD)
-
-        scores = jnp.einsum(
-            "tkgd,nkd->kgtn", q_rot, key_block, preferred_element_type=jnp.float32
-        ) / jnp.sqrt(jnp.float32(HD))
-        key_pos = (ctx - span) * tok_rows + jnp.arange(key_count, dtype=jnp.int32)
-        allowed = (key_pos[None, :] <= positions[:, None]) & (key_pos[None, :] >= starts[:, None])
-        scores = jnp.where(allowed, scores, -1e30)
-        row_max = jnp.max(scores, axis=-1)
-        weights = jnp.exp(scores - row_max[..., None])
-        row_sum = jnp.sum(weights, axis=-1)
-        weighted = jnp.einsum(
-            "kgtn,nkd->kgtd",
-            weights.astype(jnp.bfloat16),
-            value_block,
-            preferred_element_type=jnp.float32,
-        )
+                    if step is chain[-1]:
+                        late.append(blk)
+        def scored(backs):
+            window = jnp.concatenate([blocks[b] for b in backs], axis=0)
+            key_count = window.shape[0]
+            key_block = window[:, :kv_width].reshape(key_count, kv_local, HD)
+            value_block = window[:, kv_width:].reshape(key_count, kv_local, HD)
+            scores = jnp.einsum(
+                "tkgd,nkd->kgtn", q_rot, key_block, preferred_element_type=jnp.float32
+            ) / jnp.sqrt(jnp.float32(HD))
+            key_pos = jnp.concatenate(
+                [(ctx - b) * tok_rows + jnp.arange(tok_rows, dtype=jnp.int32) for b in backs]
+            )
+            allowed = (key_pos[None, :] <= positions[:, None]) & (key_pos[None, :] >= starts[:, None])
+            return jnp.where(allowed, scores, -1e30), value_block
+
+        early = [b for b in range(span + 1) if b not in late]
+        parts = [scored(early), scored(sorted(late))]
+        row_max = jnp.maximum(jnp.max(parts[0][0], axis=-1), jnp.max(parts[1][0], axis=-1))
+        row_sum = 0.0
+        weighted = 0.0
+        for scores, value_block in parts:
+            weights = jnp.exp(scores - row_max[..., None])
+            row_sum = row_sum + jnp.sum(weights, axis=-1)
+            weighted = weighted + jnp.einsum(
+                "kgtn,nkd->kgtd",
+                weights.astype(jnp.bfloat16),
+                value_block,
+                preferred_element_type=jnp.float32,
+            )
         normed = (weighted / row_sum[..., None]).astype(jnp.bfloat16)
         attended = jnp.transpose(normed, (2, 0, 1, 3)).reshape(tok_rows, kv_local * query_group * HD)
 

time: 63.6 us -> 65.8 us (1.035)
  waiting for transfers between devices: 14.3 us -> 16.6 us
    ppermute x6, waiting for transfers between devices: 12.5 us -> 14.8 us  [on_device(): lax.ppermute(lax.dynamic_slice_in_dim(packet, lo, step['width'], 0), 'ctx...]
    ppermute x1, starting transfers between devices: 2.86 us -> 3.73 us  [on_device(): lax.ppermute(lax.dynamic_slice_in_dim(bundle, lo, rows_back, 0), 'ctx', [...]
    unnamed x25 -> x23, local copies, waits for them, and re-layouts: 3.37 us -> 3.34 us
  transfers between devices with their start and end apart: 15 -> 15, of which waited for: 5 -> 4; matrix products, arithmetic and copies ran while one was open for 7% -> 7% of each run, Pallas kernels for 0% -> 0%
where the time goes in v17:
time: 65.8 us; the launch traced here: 65.5 us
  starting transfers between devices  35.7 us (54%)
  waiting for transfers between devices  16.6 us (25%)
  matrix products  5.58 us (8%)
  local copies, waits for them, and re-layouts  3.44 us (5%)
  other arithmetic  3.4 us (5%)
  between operations  0.84 us (1%)
    ppermute x6, waiting for transfers between devices, on_device(): lax.ppermute(lax.dynamic_slice_in_dim(packet, lo, step['width'], 0), 'ctx...  14.8 us
    ppermute x6, starting transfers between devices, on_device(): lax.ppermute(lax.dynamic_slice_in_dim(packet, lo, step['width'], 0), 'ctx...  12 us
    ppermute x2, starting transfers between devices, on_device(): lax.ppermute(own, 'ctx', [(s, s + shift) for s in range(n_ctx - shift)])  8.55 us
    ppermute x1, starting transfers between devices, on_device(): lax.ppermute(jnp.where(core == 1, up, down), 'head', cross_pairs)  3.83 us
    ppermute x1, starting transfers between devices, on_device(): lax.ppermute(lax.dynamic_slice_in_dim(bundle, lo, rows_back, 0), 'ctx', [...  3.73 us
    dot_general x8, matrix products, project(): return jnp.dot(piece, rows, preferred_element_type=jnp.float32)  3.43 us
    unnamed x23, local copies, waits for them, and re-layouts  3.34 us
    ppermute x1, starting transfers between devices, on_device(): partner = lax.ppermute(attended, 'head', swap)  2.84 us
  transfers between devices with their start and end apart: 15, of which 4 were waited for; matrix products, arithmetic and copies ran while one was open for 7% of the time, Pallas kernels for 0%

profile of v17, /device:TPU:1, one launch (start us, length us, event | category | flops | bytes accessed | tf_op | source)
XLA Modules:
  0.0 65.5 jit_solution(12395150262161760911)
XLA Ops:
  0.0 0.8 %select_reduce_fusion.1 = s32[32]{0:T(128)S(1)} fusion(s32[32]{0:T(128)} %param.8), kind=kLoop, calls=%fused_computation.105 | loop fusion | flops 3040 | bytes 256 | tf_op jit(solution)/shard_map/reduce_sum | solution.py:15
  0.8 0.9 %copy.24 = bf16[128,128]{0,1:T(8,128)(2,1)S(1)} copy(bf16[128,128]{1,0:T(8,128)(2,1)} %param.6) | data formatting | bytes 65536 | tf_op args[1]
  1.7 0.9 %copy.25 = bf16[128,128]{0,1:T(8,128)(2,1)S(1)} copy(bf16[128,128]{1,0:T(8,128)(2,1)} %param.7) | data formatting | bytes 65536 | tf_op args[2]
  2.6 0.8 %select_reduce_fusion = s32[128]{0:T(128)S(1)} fusion(s32[32]{0:T(128)} %param.8, s32[128]{0:T(128)S(1)} %iota_add_fusion, s32[32]{0:T(128)S(1)} %select_reduce_fusion.1), kind=kLoop, calls=%fused_computation.104 | loop fusion | flops 12160 | bytes 1280 | tf_op jit(solution)/shard_map/reduce_sum | solution.py:17
  3.6 4.0 %collective-permute-start = (bf16[128,256]{0,1:T(8,128)(2,1)S(1)}, bf16[128,256]{0,1:T(8,128)(2,1)S(1)}, u32[]{:S(2)}, u32[]{:S(2)}) collective-permute-start(bf16[128,256]{0,1:T(8,128)(2,1)S(1)} %get-tuple-element.15), channel_id=1, source_target_pairs={{0,64},{8,72},{16,80},{24,88},{32,96},{40,104},{48,112},{56,120},{... | collective-permute-start | bytes 196616 | tf_op jit(solution)/shard_map/ppermute | solution.py:61
  7.6 4.5 %collective-permute-start.1 = (bf16[128,256]{0,1:T(8,128)(2,1)S(1)}, bf16[128,256]{0,1:T(8,128)(2,1)S(1)}, u32[]{:S(2)}, u32[]{:S(2)}) collective-permute-start(bf16[128,256]{0,1:T(8,128)(2,1)S(1)} %get-tuple-element.15), channel_id=1, source_target_pairs={{0,128},{8,136},{16,144},{24,152},{32,160},{40,168},{48,176},{56,1... | collective-permute-start | bytes 196616 | tf_op jit(solution)/shard_map/ppermute | solution.py:61
  12.9 1.0 %copy.26 = bf16[128,512]{0,1:T(8,128)(2,1)S(1)} copy(bf16[128,512]{1,0:T(8,128)(2,1)} %param.5) | data formatting | bytes 262144 | tf_op args[0]
  14.4 1.7 %collective-permute-start.2 = (bf16[3,128,256]{1,2,0:T(8,128)(2,1)S(1)}, bf16[3,128,256]{1,2,0:T(8,128)(2,1)S(1)}, u32[]{:S(2)}, u32[]{:S(2)}) collective-permute-start(bf16[3,128,256]{1,2,0:T(8,128)(2,1)S(1)} %pad_maximum_fusion.1), channel_id=1, source_target_pairs={{0,8},{8,16},{16,24},{24,32},{32,40},{40,48},{48,56},{56,0},{64,72... | collective-permute-start | bytes 589832 | tf_op jit(solution)/shard_map/ppermute | solution.py:83
  16.2 4.0 %collective-permute-start.4 = (bf16[3,128,256]{1,2,0:T(8,128)(2,1)S(1)}, bf16[3,128,256]{1,2,0:T(8,128)(2,1)S(1)}, u32[]{:S(2)}, u32[]{:S(2)}) collective-permute-start(bf16[3,128,256]{1,2,0:T(8,128)(2,1)S(1)} %pad_maximum_fusion.1), channel_id=1, source_target_pairs={{0,56},{8,0},{16,8},{24,16},{32,24},{40,32},{48,40},{56,48},{64,12... | collective-permute-start | bytes 589832 | tf_op jit(solution)/shard_map/ppermute | solution.py:83
  20.6 2.6 %collective-permute-done.4 = bf16[3,128,256]{1,2,0:T(8,128)(2,1)S(1)} collective-permute-done((bf16[3,128,256]{1,2,0:T(8,128)(2,1)S(1)}, bf16[3,128,256]{1,2,0:T(8,128)(2,1)S(1)}, u32[]{:S(2)}, u32[]{:S(2)}) %collective-permute-start.4) | collective-permute-done | bytes 196640 | tf_op jit(solution)/shard_map/ppermute | solution.py:83
  23.2 3.4 %collective-permute-start.5 = (bf16[3,128,256]{1,2,0:T(8,128)(2,1)S(1)}, bf16[3,128,256]{1,2,0:T(8,128)(2,1)S(1)}, u32[]{:S(2)}, u32[]{:S(2)}) collective-permute-start(bf16[3,128,256]{1,2,0:T(8,128)(2,1)S(1)} %collective-permute-done.4), channel_id=1, source_target_pairs={{0,56},{8,0},{16,8},{24,16},{32,24},{40,32},{48,40},{56,48},{64,12... | collective-permute-start | bytes 589832 | tf_op jit(solution)/shard_map/ppermute | solution.py:83
  26.6 3.7 %collective-permute-start.7 = (bf16[2,128,256]{1,2,0:T(8,128)(2,1)S(1)}, bf16[2,128,256]{1,2,0:T(8,128)(2,1)S(1)}, u32[]{:S(2)}, u32[]{:S(2)}) collective-permute-start(bf16[2,128,256]{1,2,0:T(8,128)(2,1)S(1)} %constant_dynamic-slice_fusion.1), channel_id=1, source_target_pairs={{0,32},{8,40},{16,48},{24,56},{32,0},{40,8},{48,16},{56,24},{64,96... | collective-permute-start | bytes 393224 | tf_op jit(solution)/shard_map/ppermute | solution.py:71
  30.4 2.7 %collective-permute-start.8 = (bf16[2,128,256]{1,2,0:T(8,128)(2,1)S(1)}, bf16[2,128,256]{1,2,0:T(8,128)(2,1)S(1)}, u32[]{:S(2)}, u32[]{:S(2)}) collective-permute-start(bf16[2,128,256]{1,2,0:T(8,128)(2,1)S(1)} %constant_dynamic-slice_fusion), channel_id=1, source_target_pairs={{0,56},{8,0},{16,8},{24,16},{32,24},{40,32},{48,40},{56,48},{64,12... | collective-permute-start | bytes 393224 | tf_op jit(solution)/shard_map/ppermute | solution.py:83
  33.2 8.1 %collective-permute-done.3 = bf16[3,128,256]{1,2,0:T(8,128)(2,1)S(1)} collective-permute-done((bf16[3,128,256]{1,2,0:T(8,128)(2,1)S(1)}, bf16[3,128,256]{1,2,0:T(8,128)(2,1)S(1)}, u32[]{:S(2)}, u32[]{:S(2)}) %collective-permute-start.3) | collective-permute-done | bytes 196640 | tf_op jit(solution)/shard_map/ppermute | solution.py:83
  41.6 0.6 fusion.77
  42.3 4.1 %collective-permute-done.6 = bf16[2,128,256]{1,2,0:T(8,128)(2,1)S(1)} collective-permute-done((bf16[2,128,256]{1,2,0:T(8,128)(2,1)S(1)}, bf16[2,128,256]{1,2,0:T(8,128)(2,1)S(1)}, u32[]{:S(2)}, u32[]{:S(2)}) %collective-permute-start.6) | collective-permute-done | bytes 131104 | tf_op jit(solution)/shard_map/ppermute | solution.py:83
  48.1 0.6 fusion.22
  48.7 1.3 %collective-permute-start.9 = (bf16[128,512]{0,1:T(8,128)(2,1)S(1)}, bf16[128,512]{0,1:T(8,128)(2,1)S(1)}, u32[]{:S(2)}, u32[]{:S(2)}) collective-permute-start(bf16[128,512]{0,1:T(8,128)(2,1)S(1)} %bitcast.129), channel_id=1, source_target_pairs={{0,2},{1,3},{2,4},{3,5},{4,6},{5,7},{6,0},{7,1},{8,10},{9,11},{10,... | collective-permute-start | bytes 393224 | tf_op jit(solution)/shard_map/ppermute | solution.py:133
  50.0 1.5 %collective-permute-start.10 = (bf16[128,512]{0,1:T(8,128)(2,1)S(1)}, bf16[128,512]{0,1:T(8,128)(2,1)S(1)}, u32[]{:S(2)}, u32[]{:S(2)}) collective-permute-start(bf16[128,512]{0,1:T(8,128)(2,1)S(1)} %bitcast.130), channel_id=1, source_target_pairs={{0,6},{1,7},{2,0},{3,1},{4,2},{5,3},{6,4},{7,5},{8,14},{9,15},{10,... | collective-permute-start | bytes 393224 | tf_op jit(solution)/shard_map/ppermute | solution.py:134
  51.5 2.8 %collective-permute-start.11 = (bf16[128,512]{0,1:T(8,128)(2,1)S(1)}, bf16[128,512]{0,1:T(8,128)(2,1)S(1)}, u32[]{:S(2)}, u32[]{:S(2)}) collective-permute-start(bf16[128,512]{0,1:T(8,128)(2,1)S(1)} %bitcast.131), channel_id=1, source_target_pairs={{0,1},{1,0},{2,3},{3,2},{4,5},{5,4},{6,7},{7,6},{8,9},{9,8},{10,11... | collective-permute-start | bytes 393224 | tf_op jit(solution)/shard_map/ppermute | solution.py:136
  54.7 1.9 %collective-permute-start.12 = (bf16[128,512]{0,1:T(8,128)(2,1)S(1)}, bf16[128,512]{0,1:T(8,128)(2,1)S(1)}, u32[]{:S(2)}, u32[]{:S(2)}) collective-permute-start(bf16[128,512]{0,1:T(8,128)(2,1)S(1)} %get-tuple-element.7), channel_id=1, source_target_pairs={{0,2},{1,7},{2,4},{3,1},{4,6},{5,3},{6,0},{7,5},{8,10},{9,15},{10,... | collective-permute-start | bytes 393224 | tf_op jit(solution)/shard_map/ppermute | solution.py:138
  56.6 3.8 %collective-permute-start.13 = (bf16[128,512]{0,1:T(8,128)(2,1)S(1)}, bf16[128,512]{0,1:T(8,128)(2,1)S(1)}, u32[]{:S(2)}, u32[]{:S(2)}) collective-permute-start(bf16[128,512]{0,1:T(8,128)(2,1)S(1)} %get-tuple-element.8), channel_id=1, source_target_pairs={{0,7},{1,2},{2,1},{3,4},{4,3},{5,6},{6,5},{7,0},{8,15},{9,10},{10,... | collective-permute-start | bytes 393224 | tf_op jit(solution)/shard_map/ppermute | solution.py:140
  61.6 1.8 %collective-permute-done.13 = bf16[128,512]{0,1:T(8,128)(2,1)S(1)} collective-permute-done((bf16[128,512]{0,1:T(8,128)(2,1)S(1)}, bf16[128,512]{0,1:T(8,128)(2,1)S(1)}, u32[]{:S(2)}, u32[]{:S(2)}) %collective-permute-start.13) | collective-permute-done | bytes 131104 | tf_op jit(solution)/shard_map/ppermute | solution.py:140
  64.4 1.1 %fusion.15 = bf16[128,1024]{1,0:T(8,128)(2,1)} fusion(f32[128,1024]{1,0:T(8,128)S(1)} %fusion.25, f32[128,1024]{1,0:T(8,128)S(1)} %fusion.27, f32[128,1024]{1,0:T(8,128)S(1)} %fusion.29, f32[128,1024]{1,0:T(8,128)S(1)} %fusion.31, f32[128,1024]{1,0:T(8,128)S(1)} %fusion.33, f32[128,1024]{1,0:T(8,128)S(1)} %convolution_add_fusion.1, ...), kind=kOutput, calls=%fused_computation.20 | convolution fusion | flops 135135232 | bytes 4587524 | tf_op jit(solution)/shard_map/dot_general | solution.py:131
  (86 shorter events, 5.9 us)
Async XLA Ops:
  3.6 10.8 %collective-permute-start = (bf16[128,256]{0,1:T(8,128)(2,1)S(1)}, bf16[128,256]{0,1:T(8,128)(2,1)S(1)}, u32[]{:S(2)}, u32[]{:S(2)}) collective-permute-start(bf16[128,256]{0,1:T(8,128)(2,1)S(1)} %get-tuple-element.15), channel_id=1, source_target_pairs={{0,64},{8,72},{16,80},{24,88},{32,96},{40,104},{48,112},{56,120},{... | collective-permute-start | bytes 196616 | tf_op jit(solution)/shard_map/ppermute | solution.py:61
  7.6 6.8 %collective-permute-start.1 = (bf16[128,256]{0,1:T(8,128)(2,1)S(1)}, bf16[128,256]{0,1:T(8,128)(2,1)S(1)}, u32[]{:S(2)}, u32[]{:S(2)}) collective-permute-start(bf16[128,256]{0,1:T(8,128)(2,1)S(1)} %get-tuple-element.15), channel_id=1, source_target_pairs={{0,128},{8,136},{16,144},{24,152},{32,160},{40,168},{48,176},{56,1... | collective-permute-start | bytes 196616 | tf_op jit(solution)/shard_map/ppermute | solution.py:61
  14.4 15.9 %collective-permute-start.2 = (bf16[3,128,256]{1,2,0:T(8,128)(2,1)S(1)}, bf16[3,128,256]{1,2,0:T(8,128)(2,1)S(1)}, u32[]{:S(2)}, u32[]{:S(2)}) collective-permute-start(bf16[3,128,256]{1,2,0:T(8,128)(2,1)S(1)} %pad_maximum_fusion.1), channel_id=1, source_target_pairs={{0,8},{8,16},{16,24},{24,32},{32,40},{40,48},{48,56},{56,0},{64,72... | collective-permute-start | bytes 589832 | tf_op jit(solution)/shard_map/ppermute | solution.py:83
  16.2 7.0 %collective-permute-start.4 = (bf16[3,128,256]{1,2,0:T(8,128)(2,1)S(1)}, bf16[3,128,256]{1,2,0:T(8,128)(2,1)S(1)}, u32[]{:S(2)}, u32[]{:S(2)}) collective-permute-start(bf16[3,128,256]{1,2,0:T(8,128)(2,1)S(1)} %pad_maximum_fusion.1), channel_id=1, source_target_pairs={{0,56},{8,0},{16,8},{24,16},{32,24},{40,32},{48,40},{56,48},{64,12... | collective-permute-start | bytes 589832 | tf_op jit(solution)/shard_map/ppermute | solution.py:83
  23.2 7.2 %collective-permute-start.5 = (bf16[3,128,256]{1,2,0:T(8,128)(2,1)S(1)}, bf16[3,128,256]{1,2,0:T(8,128)(2,1)S(1)}, u32[]{:S(2)}, u32[]{:S(2)}) collective-permute-start(bf16[3,128,256]{1,2,0:T(8,128)(2,1)S(1)} %collective-permute-done.4), channel_id=1, source_target_pairs={{0,56},{8,0},{16,8},{24,16},{32,24},{40,32},{48,40},{56,48},{64,12... | collective-permute-start | bytes 589832 | tf_op jit(solution)/shard_map/ppermute | solution.py:83
  26.6 19.7 %collective-permute-start.7 = (bf16[2,128,256]{1,2,0:T(8,128)(2,1)S(1)}, bf16[2,128,256]{1,2,0:T(8,128)(2,1)S(1)}, u32[]{:S(2)}, u32[]{:S(2)}) collective-permute-start(bf16[2,128,256]{1,2,0:T(8,128)(2,1)S(1)} %constant_dynamic-slice_fusion.1), channel_id=1, source_target_pairs={{0,32},{8,40},{16,48},{24,56},{32,0},{40,8},{48,16},{56,24},{64,96... | collective-permute-start | bytes 393224 | tf_op jit(solution)/shard_map/ppermute | solution.py:71
  30.4 10.9 %collective-permute-start.3 = (bf16[3,128,256]{1,2,0:T(8,128)(2,1)S(1)}, bf16[3,128,256]{1,2,0:T(8,128)(2,1)S(1)}, u32[]{:S(2)}, u32[]{:S(2)}) collective-permute-start(bf16[3,128,256]{1,2,0:T(8,128)(2,1)S(1)} %collective-permute-done.2), channel_id=1, source_target_pairs={{0,8},{8,16},{16,24},{24,32},{32,40},{40,48},{48,56},{56,0},{64,72... | collective-permute-start | bytes 589832 | tf_op jit(solution)/shard_map/ppermute | solution.py:83
  30.4 16.0 %collective-permute-start.8 = (bf16[2,128,256]{1,2,0:T(8,128)(2,1)S(1)}, bf16[2,128,256]{1,2,0:T(8,128)(2,1)S(1)}, u32[]{:S(2)}, u32[]{:S(2)}) collective-permute-start(bf16[2,128,256]{1,2,0:T(8,128)(2,1)S(1)} %constant_dynamic-slice_fusion), channel_id=1, source_target_pairs={{0,56},{8,0},{16,8},{24,16},{32,24},{40,32},{48,40},{56,48},{64,12... | collective-permute-start | bytes 393224 | tf_op jit(solution)/shard_map/ppermute | solution.py:83
  41.2 5.1 %collective-permute-start.6 = (bf16[2,128,256]{1,2,0:T(8,128)(2,1)S(1)}, bf16[2,128,256]{1,2,0:T(8,128)(2,1)S(1)}, u32[]{:S(2)}, u32[]{:S(2)}) collective-permute-start(bf16[2,128,256]{1,2,0:T(8,128)(2,1)S(1)} %constant_dynamic-slice_fusion.2), channel_id=1, source_target_pairs={{0,8},{8,16},{16,24},{24,32},{32,40},{40,48},{48,56},{56,0},{64,72... | collective-permute-start | bytes 393224 | tf_op jit(solution)/shard_map/ppermute | solution.py:83
  41.6 12.7 %slice-start = ((s8[8388608]{0:T(1024)(128)(4,1)}), s8[4194304]{0:T(1024)(128)(4,1)S(1)}, s32[]{:S(2)}) async-start(s8[8388608]{0:T(1024)(128)(4,1)} %bitcast.124), calls=%async_computation | async-start | bytes 8388608
  47.2 7.1 %slice-start.1 = ((s8[8388608]{0:T(1024)(128)(4,1)}), s8[4194304]{0:T(1024)(128)(4,1)S(1)}, s32[]{:S(2)}) async-start(s8[8388608]{0:T(1024)(128)(4,1)} %bitcast.124), calls=%async_computation.1 | async-start | bytes 8388608
  48.7 5.9 %collective-permute-start.9 = (bf16[128,512]{0,1:T(8,128)(2,1)S(1)}, bf16[128,512]{0,1:T(8,128)(2,1)S(1)}, u32[]{:S(2)}, u32[]{:S(2)}) collective-permute-start(bf16[128,512]{0,1:T(8,128)(2,1)S(1)} %bitcast.129), channel_id=1, source_target_pairs={{0,2},{1,3},{2,4},{3,5},{4,6},{5,7},{6,0},{7,1},{8,10},{9,11},{10,... | collective-permute-start | bytes 393224 | tf_op jit(solution)/shard_map/ppermute | solution.py:133
  50.0 4.7 %collective-permute-start.10 = (bf16[128,512]{0,1:T(8,128)(2,1)S(1)}, bf16[128,512]{0,1:T(8,128)(2,1)S(1)}, u32[]{:S(2)}, u32[]{:S(2)}) collective-permute-start(bf16[128,512]{0,1:T(8,128)(2,1)S(1)} %bitcast.130), channel_id=1, source_target_pairs={{0,6},{1,7},{2,0},{3,1},{4,2},{5,3},{6,4},{7,5},{8,14},{9,15},{10,... | collective-permute-start | bytes 393224 | tf_op jit(solution)/shard_map/ppermute | solution.py:134
  51.5 9.4 %collective-permute-start.11 = (bf16[128,512]{0,1:T(8,128)(2,1)S(1)}, bf16[128,512]{0,1:T(8,128)(2,1)S(1)}, u32[]{:S(2)}, u32[]{:S(2)}) collective-permute-start(bf16[128,512]{0,1:T(8,128)(2,1)S(1)} %bitcast.131), channel_id=1, source_target_pairs={{0,1},{1,0},{2,3},{3,2},{4,5},{5,4},{6,7},{7,6},{8,9},{9,8},{10,11... | collective-permute-start | bytes 393224 | tf_op jit(solution)/shard_map/ppermute | solution.py:136
  54.7 6.6 %collective-permute-start.12 = (bf16[128,512]{0,1:T(8,128)(2,1)S(1)}, bf16[128,512]{0,1:T(8,128)(2,1)S(1)}, u32[]{:S(2)}, u32[]{:S(2)}) collective-permute-start(bf16[128,512]{0,1:T(8,128)(2,1)S(1)} %get-tuple-element.7), channel_id=1, source_target_pairs={{0,2},{1,7},{2,4},{3,1},{4,6},{5,3},{6,0},{7,5},{8,10},{9,15},{10,... | collective-permute-start | bytes 393224 | tf_op jit(solution)/shard_map/ppermute | solution.py:138
  56.6 6.8 %collective-permute-start.13 = (bf16[128,512]{0,1:T(8,128)(2,1)S(1)}, bf16[128,512]{0,1:T(8,128)(2,1)S(1)}, u32[]{:S(2)}, u32[]{:S(2)}) collective-permute-start(bf16[128,512]{0,1:T(8,128)(2,1)S(1)} %get-tuple-element.8), channel_id=1, source_target_pairs={{0,7},{1,2},{2,1},{3,4},{4,3},{5,6},{6,5},{7,0},{8,15},{9,10},{10,... | collective-permute-start | bytes 393224 | tf_op jit(solution)/shard_map/ppermute | solution.py:140
  60.5 3.3 %collective-permute-start.14 = (bf16[2,128,512]{1,2,0:T(8,128)(2,1)S(1)}, bf16[2,128,512]{1,2,0:T(8,128)(2,1)S(1)}, u32[]{:S(2)}, u32[]{:S(2)}) collective-permute-start(bf16[2,128,512]{1,2,0:T(8,128)(2,1)S(1)} %pad_maximum_fusion), channel_id=1, source_target_pairs={{0,1},{1,0},{2,3},{3,2},{4,5},{5,4},{6,7},{7,6},{8,9},{9,8},{10,11... | collective-permute-start | bytes 786440 | tf_op jit(solution)/shard_map/ppermute | solution.py:141
